TPU v7x, 32 devices: a whole 2x2x4 slice. The times are simulated.
32 devices in a mesh: groups: 2 (over y), dp: 16 (over z, x, core).
Axes of the slice: x: 2, y: 2, z: 4, core: 2. Of those that a mesh axis runs over, the one named last changes fastest.
Arguments:
- queries: bfloat16 [8192, 2048], P(('groups', 'dp')), parts along dimension 0, may hold values from -6 to 6
- grad_out: bfloat16 [8192, 2048], P(('groups', 'dp')), parts along dimension 0, may hold values from -60 to 60
- params: float32 [4096, 2048], P(('groups', 'dp')), parts along dimension 0, may hold values from -0.0625 to 0.0625
- first_moment: float32 [4096, 2048], P(('groups', 'dp')), parts along dimension 0, may hold values from -6 to 6
- second_moment: float32 [4096, 2048], P(('groups', 'dp')), parts along dimension 0, may hold values from 0.05 to 0.08
- key_params: float32 [4096, 2048], P(('groups', 'dp')), parts along dimension 0, may hold values from -0.0625 to 0.0625
- keys: bfloat16 [4096, 2048], P(('groups', 'dp')), parts along dimension 0, may hold values from -6 to 6
- perm: int32 [4096], P('groups'), parts along dimension 0, may hold values from 0 to 2047, as said below
- inv_perm: int32 [4096], P('groups'), parts along dimension 0, may hold values from 0 to 2047, as said below
- bn_gain: float32 [4096], P('groups'), parts along dimension 0, may hold values from 0.25 to 1.75
- bn_shift: float32 [4096], P('groups'), parts along dimension 0, may hold values from -3 to 3
- queue: bfloat16 [16, 2048, 2048], P('groups', 'dp'), parts along dimension 0, may hold values from -6 to 6
- slot: int32 [1], replicated, may hold values from 0 to 7
Outputs:
- new_params: float32 [4096, 2048], P(('groups', 'dp')), parts along dimension 0
- new_first: float32 [4096, 2048], P(('groups', 'dp')), parts along dimension 0
- new_second: float32 [4096, 2048], P(('groups', 'dp')), parts along dimension 0
- new_key: float32 [4096, 2048], P(('groups', 'dp')), parts along dimension 0
- new_queue: bfloat16 [16, 2048, 2048], P('groups', 'dp'), parts along dimension 0
There are 2 independent parts, one for each index of `groups`. A program takes and returns all parts, laid end to end along the dimension named above; an argument that names none is the same for every part. Nothing has to cross between parts.
Inputs may be any that keep to these rules, and one draw needn't show every extreme that they name: perm is a permutation of 0 to 2047; each aligned block of 128 of its entries holds exactly 8 values from every aligned block of 128 values. inv_perm[perm[i]] = i for every i.
All inputs are finite; a program needn't handle non-finite values.
Results may differ from a plain program's by a relative error of at most 0.0025.
Values may be sent and summed in bfloat16 or wider, within the bound.
No kernel may reach another device: no remote copies, remote signals or barrier semaphores. Data moves between devices by JAX's collectives and lax.ppermute only.
A program may use at most 128 MiB of HBM per device.

v0:
```python
import jax
import jax.numpy as jnp
from jax import lax
from jax.sharding import PartitionSpec as P

norm_epsilon = 1e-05
adam_epsilon = 1e-08
bias_first = 1.0 - 0.9**10
bias_second = 1.0 - 0.999**10


def route(mapping, position, block_rows, per_peer):
    members = mapping.shape[0] // block_rows
    layout = mapping.reshape(members, block_rows)
    owned = (layout // block_rows == position).astype(jnp.int32)
    ordinal = jnp.cumsum(owned, axis=1) - 1
    destination = jnp.arange(members, dtype=jnp.int32)[:, None] * per_peer + ordinal
    destination = jnp.where(owned == 1, destination, members * per_peer)
    offsets = jnp.where(owned == 1, layout - position * block_rows, 0)
    send_index = (
        jnp.zeros((members * per_peer + 1,), jnp.int32)
        .at[destination.reshape(-1)]
        .set(offsets.reshape(-1))[: members * per_peer]
    )
    own_block = lax.dynamic_slice_in_dim(mapping, position * block_rows, block_rows)
    anchor = own_block // block_rows
    indicator = (anchor[:, None] == jnp.arange(members, dtype=jnp.int32)[None, :]).astype(jnp.int32)
    arrival = jnp.sum((jnp.cumsum(indicator, axis=0) - 1) * indicator, axis=1)
    return (send_index, anchor * per_peer + arrival)


def grad_term(queries, grad_out):
    return lax.dot_general(
        queries, grad_out, (((0,), (0,)), ((), ())), preferred_element_type=jnp.float32
    )


def adamw(gradient, params, first_moment, second_moment, key_params):
    new_first = 0.9 * first_moment + 0.1 * gradient
    new_second = 0.999 * second_moment + 0.001 * gradient * gradient
    update = new_first / bias_first / (jnp.sqrt(new_second / bias_second) + adam_epsilon)
    new_params = params - 0.05 * (update + 0.1 * params)
    new_key = 0.99 * key_params + 0.01 * new_params
    return (new_params, new_first, new_second, new_key)


def batch_norm(codes, bn_gain, bn_shift):
    values = codes.astype(jnp.float32)
    center = jnp.mean(values, axis=0)
    spread = jnp.mean(jnp.square(values - center), axis=0)
    return jax.nn.relu(
        (values - center) * lax.rsqrt(spread + norm_epsilon) * bn_gain + bn_shift
    ).astype(jnp.bfloat16)


def per_device(
    queries,
    grad_out,
    params,
    first_moment,
    second_moment,
    key_params,
    keys,
    perm,
    inv_perm,
    bn_gain,
    bn_shift,
    queue,
    slot,
):
    position = lax.axis_index("dp")
    members = lax.axis_size("dp")
    block_rows = keys.shape[0]
    per_peer = block_rows // members
    scaling = 1.0 / jnp.sqrt(jnp.float32(queries.shape[0] * members))
    send_forward, receive_forward = route(perm, position, block_rows, per_peer)
    send_back, receive_back = route(inv_perm, position, block_rows, per_peer)
    moved = lax.all_to_all(
        jnp.take(keys, send_forward, axis=0), "dp", split_axis=0, concat_axis=0, tiled=True
    )
    encoded_rows = jnp.take(moved, receive_forward, axis=0)
    gradient = (
        lax.psum_scatter(grad_term(queries, grad_out), "dp", scatter_dimension=0, tiled=True)
        * scaling
    )
    new_params, new_first, new_second, new_key = adamw(
        gradient, params, first_moment, second_moment, key_params
    )
    codes = jnp.dot(
        encoded_rows,
        lax.all_gather(new_key.astype(jnp.bfloat16), "dp", axis=0, tiled=True),
        preferred_element_type=jnp.float32,
    )
    codes = codes.astype(jnp.bfloat16)
    normed = batch_norm(codes, bn_gain, bn_shift)
    returned = lax.all_to_all(
        jnp.take(normed, send_back, axis=0), "dp", split_axis=0, concat_axis=0, tiled=True
    )
    restored = jnp.take(returned, receive_back, axis=0)
    new_queue = lax.dynamic_update_slice(
        queue, restored[None], (slot[0], jnp.int32(0), jnp.int32(0))
    )
    return (new_params, new_first, new_second, new_key, new_queue)


def solution(mesh):
    in_specs = (
        P(("groups", "dp"), None),
        P(("groups", "dp"), None),
        P(("groups", "dp"), None),
        P(("groups", "dp"), None),
        P(("groups", "dp"), None),
        P(("groups", "dp"), None),
        P(("groups", "dp"), None),
        P("groups"),
        P("groups"),
        P("groups"),
        P("groups"),
        P("groups", "dp", None),
        P(),
    )
    out_specs = (
        P(("groups", "dp"), None),
        P(("groups", "dp"), None),
        P(("groups", "dp"), None),
        P(("groups", "dp"), None),
        P("groups", "dp", None),
    )
    return jax.shard_map(
        per_device, mesh=mesh, in_specs=in_specs, out_specs=out_specs, check_vma=False
    )
```

profile of v0, /device:TPU:0, one launch (start us, length us, event | category | flops | bytes accessed | tf_op | source)
XLA Modules:
  0.0 325.0 jit_solution(14405362757740360536)
XLA Ops:
  7.2 4.9 %copy.21 = bf16[8,128,2048]{2,1,0:T(8,128)(2,1)} copy(bf16[8,128,2048]{2,1,0:T(8,128)(2,1)} %param.26) | data formatting | bytes 8388608
  12.2 8.1 %fusion.29 = f32[2048,2048]{1,0:T(8,128)} fusion(bf16[256,2048]{1,0:T(8,128)(2,1)S(1)} %copy-done, bf16[256,2048]{1,0:T(8,128)(2,1)S(1)} %copy-done.2), kind=kOutput, calls=%fused_computation.102 | convolution fusion | flops 2147483648 | bytes 18874368 | tf_op jit(solution)/shard_map/dot_general | solution.py:33
  20.3 0.0 all-gather.2.cloned.1.call-start
  20.4 181.3 %reduce-scatter.2.cloned.1.call-done = f32[128,2048]{1,0:T(8,128)} async-done(((f32[2048,2048]{1,0:T(8,128)}), f32[128,2048]{1,0:T(8,128)}) %reduce-scatter.2.cloned.1.call-update) | async-done | bytes 1048592 | tf_op jit(solution)/shard_map/reduce_scatter | solution.py:83
  201.7 5.1 %fusion.27 = (bf16[128,2048]{1,0:T(8,128)(2,1)}, f32[128,2048]{1,0:T(8,128)}, f32[128,2048]{1,0:T(8,128)}, f32[128,2048]{1,0:T(8,128)}, f32[128,2048]{1,0:T(8,128)}) fusion(f32[128,2048]{1,0:T(8,128)S(1)} %copy-done.3, f32[128,2048]{1,0:T(8,128)} %param.17, f32[128,2048]{1,0:T(8,128)} %reduce-scatter.2.cloned.1.call-done, f32[128,2048]{1,0:T(8,128)} %param.18, ...), kind=kLoop, calls=%fused_computation.100 | loop fusion | flops 5242880 | bytes 9961472 | tf_op jit(solution)/shard_map/convert_element_type | solution.py:91
  206.9 0.3 reduce_window_sum.34
  207.2 0.3 reduce_window_sum.36
  207.4 0.1 subtract_select_fusion
  207.5 8.0 %scatter_custom_fusion = s32[129]{0:T(256)S(1)} fusion(s32[2048]{0:T(1024)S(1)} %get-tuple-element.25, s32[2048]{0:T(1024)S(1)} %get-tuple-element.26, s32[]{:T(128)} %constant.105.clone.1), kind=kCustom, calls=%fused_computation.97 | custom fusion | bytes 520 | tf_op jit(solution)/shard_map/scatter | solution.py:23
  215.6 0.9 gather_fusion
  216.5 1.0 select_bitcast_fusion.1
  217.5 3.7 %all-to-all-start = ((bf16[16,8,2048]{2,1,0:T(8,128)(2,1)}), bf16[16,8,2048]{2,1,0:T(8,128)(2,1)S(1)}, u32[]{:S(2)}, u32[]{:S(2)}) async-start(bf16[16,8,2048]{2,1,0:T(8,128)(2,1)} %select_bitcast_fusion.1), calls=%async_computation.1 | async-start | bytes 1048576 | tf_op jit(solution)/shard_map/all_to_all | solution.py:78
  221.2 0.1 and_select_fusion
  221.3 0.1 fusion.5
  221.4 0.2 reduce_window_sum.35
  221.6 8.0 %scatter_custom_fusion.1 = s32[129]{0:T(256)S(1)} fusion(s32[2048]{0:T(1024)S(1)} %get-tuple-element.20, s32[2048]{0:T(1024)S(1)} %get-tuple-element.19, s32[]{:T(128)} %constant.105.clone.1), kind=kCustom, calls=%fused_computation.95 | custom fusion | bytes 520 | tf_op jit(solution)/shard_map/scatter | solution.py:23
  229.6 0.2 select_reduce_fusion.1
  229.8 14.4 %all-to-all-done = bf16[16,8,2048]{2,1,0:T(8,128)(2,1)S(1)} async-done(((bf16[16,8,2048]{2,1,0:T(8,128)(2,1)}), bf16[16,8,2048]{2,1,0:T(8,128)(2,1)S(1)}, u32[]{:S(2)}, u32[]{:S(2)}) %all-to-all-start) | async-done | bytes 524320 | tf_op jit(solution)/shard_map/all_to_all | solution.py:78
  244.2 0.9 gather_fusion.1
  245.2 46.1 %all-gather.2.cloned.1.call-done = bf16[2048,2048]{1,0:T(8,128)(2,1)} async-done(((bf16[128,2048]{1,0:T(8,128)(2,1)}), bf16[2048,2048]{1,0:T(8,128)(2,1)}) %all-gather.2.cloned.1.call-update) | async-done | bytes 8388624 | tf_op jit(solution)/shard_map/all_gather | solution.py:91
  291.3 4.7 %fusion.28 = (f32[2048]{0:T(1024)S(1)}, f32[128,2048]{1,0:T(8,128)S(1)}) fusion(bf16[2048,2048]{1,0:T(8,128)(2,1)} %all-gather.2.cloned.1.call-done, bf16[128,2048]{1,0:T(8,128)(2,1)S(1)} %gather_fusion.1, pred[128]{0:T(512)(128)(4,1)S(1)} %get-tuple-element.10), kind=kOutput, calls=%fused_computation.101 | convolution fusion | flops 1074788352 | bytes 9969792 | tf_op jit(solution)/shard_map/dot_general | solution.py:89
  296.0 0.1 multiply_reduce_fusion
  296.2 0.2 maximum_convert_fusion
  296.4 0.9 gather_fusion.2
  297.4 0.9 select_bitcast_fusion
  298.3 3.6 %all-to-all-start.1 = ((bf16[16,8,2048]{2,1,0:T(8,128)(2,1)}), bf16[16,8,2048]{2,1,0:T(8,128)(2,1)S(1)}, u32[]{:S(2)}, u32[]{:S(2)}) async-start(bf16[16,8,2048]{2,1,0:T(8,128)(2,1)} %select_bitcast_fusion), calls=%async_computation.2 | async-start | bytes 1048576 | tf_op jit(solution)/shard_map/all_to_all | solution.py:96
  301.8 0.1 fusion.4
  301.9 0.2 reduce_window_sum.37
  302.8 0.2 select_reduce_fusion
  303.0 13.3 %all-to-all-done.1 = bf16[16,8,2048]{2,1,0:T(8,128)(2,1)S(1)} async-done(((bf16[16,8,2048]{2,1,0:T(8,128)(2,1)}), bf16[16,8,2048]{2,1,0:T(8,128)(2,1)S(1)}, u32[]{:S(2)}, u32[]{:S(2)}) %all-to-all-start.1) | async-done | bytes 524320 | tf_op jit(solution)/shard_map/all_to_all | solution.py:96
  316.3 0.9 gather_fusion.3
  317.2 1.0 bitcast_dynamic-update-slice_fusion
  (32 shorter events, 0.2 us)
Async XLA Ops:
  7.2 5.0 %copy-start = (bf16[256,2048]{1,0:T(8,128)(2,1)S(1)}, bf16[256,2048]{1,0:T(8,128)(2,1)}, u32[]{:S(2)}) copy-start(bf16[256,2048]{1,0:T(8,128)(2,1)} %param.15) | copy-start | bytes 3145732
  7.2 5.0 %copy-start.2 = (bf16[256,2048]{1,0:T(8,128)(2,1)S(1)}, bf16[256,2048]{1,0:T(8,128)(2,1)}, u32[]{:S(2)}) copy-start(bf16[256,2048]{1,0:T(8,128)(2,1)} %param.16) | copy-start | bytes 3145732
  7.2 194.5 %reduce-scatter.2.cloned.1.call-start = ((), (), s32[]{:S(2)}) async-start(), calls=%async_computation.3 | async-start | bytes 17825792 | tf_op jit(solution)/shard_map/reduce_scatter | solution.py:83
  20.3 181.4 %copy-start.3 = (f32[128,2048]{1,0:T(8,128)S(1)}, f32[128,2048]{1,0:T(8,128)}, u32[]{:S(2)}) copy-start(f32[128,2048]{1,0:T(8,128)} %param.20) | copy-start | bytes 3145732
  20.3 186.5 %copy-start.5 = (s32[2048]{0:T(1024)S(1)}, s32[2048]{0:T(1024)}, u32[]{:S(2)}) copy-start(s32[2048]{0:T(1024)} %param.22) | copy-start | bytes 24580
  20.3 186.8 %copy-start.4 = (s32[2048]{0:T(1024)S(1)}, s32[2048]{0:T(1024)}, u32[]{:S(2)}) copy-start(s32[2048]{0:T(1024)} %param.23) | copy-start | bytes 24580
  20.3 195.3 %copy-start.1 = (bf16[128,2048]{1,0:T(8,128)(2,1)S(1)}, bf16[128,2048]{1,0:T(8,128)(2,1)}, u32[]{:S(2)}) copy-start(bf16[128,2048]{1,0:T(8,128)(2,1)} %param.21) | copy-start | bytes 1572868
  20.3 270.9 %all-gather.2.cloned.1.call-start = ((), (), s32[]{:S(2)}) async-start(), calls=%async_computation.4 | async-start | bytes 8912896 | tf_op jit(solution)/shard_map/all_gather | solution.py:91
  217.5 26.7 %all-to-all-start = ((bf16[16,8,2048]{2,1,0:T(8,128)(2,1)}), bf16[16,8,2048]{2,1,0:T(8,128)(2,1)S(1)}, u32[]{:S(2)}, u32[]{:S(2)}) async-start(bf16[16,8,2048]{2,1,0:T(8,128)(2,1)} %select_bitcast_fusion.1), calls=%async_computation.1 | async-start | bytes 1048576 | tf_op jit(solution)/shard_map/all_to_all | solution.py:78
  291.3 4.9 %copy-start.6 = (f32[2048]{0:T(1024)S(1)}, f32[2048]{0:T(1024)}, u32[]{:S(2)}) copy-start(f32[2048]{0:T(1024)} %param.25) | copy-start | bytes 24580
  291.3 4.9 %copy-start.7 = (f32[2048]{0:T(1024)S(1)}, f32[2048]{0:T(1024)}, u32[]{:S(2)}) copy-start(f32[2048]{0:T(1024)} %param.24) | copy-start | bytes 24580
  298.3 18.0 %all-to-all-start.1 = ((bf16[16,8,2048]{2,1,0:T(8,128)(2,1)}), bf16[16,8,2048]{2,1,0:T(8,128)(2,1)S(1)}, u32[]{:S(2)}, u32[]{:S(2)}) async-start(bf16[16,8,2048]{2,1,0:T(8,128)(2,1)} %select_bitcast_fusion), calls=%async_computation.2 | async-start | bytes 1048576 | tf_op jit(solution)/shard_map/all_to_all | solution.py:96
Sparse Core Ops, SparseCore 0:
  20.4 181.2 reduce-scatter.1
  206.9 84.2 all-gather.1
where the time goes:
time: 325 us
  waiting for transfers between devices  255 us (78%)
  local copies, waits for them, and re-layouts  24.8 us (8%)
  between operations  14.9 us (5%)
  matrix products  12.8 us (4%)
  other arithmetic  9.96 us (3%)
  starting transfers between devices  7.34 us (2%)
    reduce_scatter x1, waiting for transfers between devices, per_device(): lax.psum_scatter(grad_term(queries, grad_out), 'dp', scatter_dimension=0,...  181 us
    all_gather x1, waiting for transfers between devices, per_device(): lax.all_gather(new_key.astype(jnp.bfloat16), 'dp', axis=0, tiled=True)  46.1 us
    scatter x2, local copies, waits for them, and re-layouts, route(): send_index = jnp.zeros((members * per_peer + 1,), jnp.int32).at[destinati...  16.1 us
    all_to_all x1, waiting for transfers between devices, per_device(): lax.all_to_all(jnp.take(keys, send_forward, axis=0), 'dp', split_axis=0,...  14.4 us
    all_to_all x1, waiting for transfers between devices, per_device(): lax.all_to_all(jnp.take(normed, send_back, axis=0), 'dp', split_axis=0, c...  13.3 us
    dot_general x1, matrix products, grad_term(): lax.dot_general(queries, grad_out, (((0,), (0,)), ((), ())), preferred_el...  8.1 us
  transfers between devices with their start and end apart: 4, of which 4 were waited for; matrix products, arithmetic and copies ran while one was open for 6% of the time, Pallas kernels for 0%

commit v1 on v0

--- a/solution.py
+++ b/solution.py
@@ -1,12 +1,15 @@
 import jax
 import jax.numpy as jnp
 from jax import lax
+from jax.sharding import Mesh
 from jax.sharding import PartitionSpec as P
 
 norm_epsilon = 1e-05
 adam_epsilon = 1e-08
 bias_first = 1.0 - 0.9**10
 bias_second = 1.0 - 0.999**10
+
+DP = ("zo", "xl", "c")
 
 
 def route(mapping, position, block_rows, per_peer):
@@ -29,10 +32,23 @@
     return (send_index, anchor * per_peer + arrival)
 
 
-def grad_term(queries, grad_out):
-    return lax.dot_general(
-        queries, grad_out, (((0,), (0,)), ((), ())), preferred_element_type=jnp.float32
+def pair_gradient(queries, grad_out):
+    tokens, width = queries.shape
+    zo = lax.axis_size("zo")
+    x = lax.axis_index("xl")
+    blocks = queries.reshape(tokens, zo, 2, 2, width // (4 * zo))
+    mine = lax.dynamic_index_in_dim(blocks, x, axis=2, keepdims=False)
+    theirs = lax.dynamic_index_in_dim(blocks, 1 - x, axis=2, keepdims=False)
+    mine = mine.reshape(tokens, width // 2)
+    theirs = theirs.reshape(tokens, width // 2)
+    swap = [(0, 1), (1, 0)]
+    got_queries, got_grad = lax.ppermute((theirs, grad_out), "xl", swap)
+    both_queries = jnp.concatenate([mine, got_queries], axis=0)
+    both_grad = jnp.concatenate([grad_out, got_grad], axis=0)
+    partial = lax.dot_general(
+        both_queries, both_grad, (((0,), (0,)), ((), ())), preferred_element_type=jnp.float32
     )
+    return lax.psum_scatter(partial, ("zo", "c"), scatter_dimension=0, tiled=True)
 
 
 def adamw(gradient, params, first_moment, second_moment, key_params):
@@ -68,33 +84,30 @@
     queue,
     slot,
 ):
-    position = lax.axis_index("dp")
-    members = lax.axis_size("dp")
+    position = lax.axis_index(DP)
+    members = lax.axis_size(DP)
     block_rows = keys.shape[0]
     per_peer = block_rows // members
     scaling = 1.0 / jnp.sqrt(jnp.float32(queries.shape[0] * members))
     send_forward, receive_forward = route(perm, position, block_rows, per_peer)
     send_back, receive_back = route(inv_perm, position, block_rows, per_peer)
     moved = lax.all_to_all(
-        jnp.take(keys, send_forward, axis=0), "dp", split_axis=0, concat_axis=0, tiled=True
+        jnp.take(keys, send_forward, axis=0), DP, split_axis=0, concat_axis=0, tiled=True
     )
     encoded_rows = jnp.take(moved, receive_forward, axis=0)
-    gradient = (
-        lax.psum_scatter(grad_term(queries, grad_out), "dp", scatter_dimension=0, tiled=True)
-        * scaling
-    )
+    gradient = pair_gradient(queries, grad_out) * scaling
     new_params, new_first, new_second, new_key = adamw(
         gradient, params, first_moment, second_moment, key_params
     )
     codes = jnp.dot(
         encoded_rows,
-        lax.all_gather(new_key.astype(jnp.bfloat16), "dp", axis=0, tiled=True),
+        lax.all_gather(new_key.astype(jnp.bfloat16), DP, axis=0, tiled=True),
         preferred_element_type=jnp.float32,
     )
     codes = codes.astype(jnp.bfloat16)
     normed = batch_norm(codes, bn_gain, bn_shift)
     returned = lax.all_to_all(
-        jnp.take(normed, send_back, axis=0), "dp", split_axis=0, concat_axis=0, tiled=True
+        jnp.take(normed, send_back, axis=0), DP, split_axis=0, concat_axis=0, tiled=True
     )
     restored = jnp.take(returned, receive_back, axis=0)
     new_queue = lax.dynamic_update_slice(
@@ -104,28 +117,25 @@
 
 
 def solution(mesh):
+    groups, dp = mesh.devices.shape
+    grid = Mesh(mesh.devices.reshape(groups, dp // 4, 2, 2), ("groups",) + DP)
+    rows = P(("groups",) + DP, None)
     in_specs = (
-        P(("groups", "dp"), None),
-        P(("groups", "dp"), None),
-        P(("groups", "dp"), None),
-        P(("groups", "dp"), None),
-        P(("groups", "dp"), None),
-        P(("groups", "dp"), None),
-        P(("groups", "dp"), None),
+        rows,
+        rows,
+        rows,
+        rows,
+        rows,
+        rows,
+        rows,
         P("groups"),
         P("groups"),
         P("groups"),
         P("groups"),
-        P("groups", "dp", None),
+        P("groups", DP, None),
         P(),
     )
-    out_specs = (
-        P(("groups", "dp"), None),
-        P(("groups", "dp"), None),
-        P(("groups", "dp"), None),
-        P(("groups", "dp"), None),
-        P("groups", "dp", None),
+    out_specs = (rows, rows, rows, rows, P("groups", DP, None))
+    return jax.shard_map(
+        per_device, mesh=grid, in_specs=in_specs, out_specs=out_specs, check_vma=False
     )
-    return jax.shard_map(
-        per_device, mesh=mesh, in_specs=in_specs, out_specs=out_specs, check_vma=False
-    )

time: 325 us -> 271 us (0.83)
  waiting for transfers between devices: 255 us -> 197 us
    reduce_scatter x1, waiting for transfers between devices: 181 us -> 91.2 us  [pair_gradient(): lax.psum_scatter(partial, ('zo', 'c'), scatter_dimension=0, tiled=True)]
    ppermute x0 -> x2, waiting for transfers between devices: none -> 32.3 us  [pair_gradient(): got_queries, got_grad = lax.ppermute((theirs, grad_out), 'xl', swap)]
  transfers between devices with their start and end apart: 4 -> 6, of which waited for: 4 -> 5; matrix products, arithmetic and copies ran while one was open for 6% -> 8% of each run, Pallas kernels for 0% -> 0%
where the time goes in v1:
time: 271 us; the launch traced here: 270 us
  waiting for transfers between devices  197 us (73%)
  local copies, waits for them, and re-layouts  26.9 us (10%)
  between operations  15 us (6%)
  matrix products  11.9 us (4%)
  starting transfers between devices  10.2 us (4%)
  other arithmetic  9.59 us (4%)
    reduce_scatter x1, waiting for transfers between devices, pair_gradient(): lax.psum_scatter(partial, ('zo', 'c'), scatter_dimension=0, tiled=True)  91.2 us
    all_gather x1, waiting for transfers between devices, per_device(): lax.all_gather(new_key.astype(jnp.bfloat16), DP, axis=0, tiled=True)  45.4 us
    ppermute x2, waiting for transfers between devices, pair_gradient(): got_queries, got_grad = lax.ppermute((theirs, grad_out), 'xl', swap)  32.3 us
    scatter x2, local copies, waits for them, and re-layouts, route(): send_index = jnp.zeros((members * per_peer + 1,), jnp.int32).at[destinati...  16.1 us
    all_to_all x1, waiting for transfers between devices, per_device(): lax.all_to_all(jnp.take(keys, send_forward, axis=0), DP, split_axis=0, co...  14.3 us
    all_to_all x1, waiting for transfers between devices, per_device(): lax.all_to_all(jnp.take(normed, send_back, axis=0), DP, split_axis=0, con...  13.3 us
    dot_general x1, matrix products, pair_gradient(): lax.dot_general(both_queries, both_grad, (((0,), (0,)), ((), ())), prefer...  7.15 us
  transfers between devices with their start and end apart: 6, of which 5 were waited for; matrix products, arithmetic and copies ran while one was open for 8% of the time, Pallas kernels for 0%

profile of v1, /device:TPU:0, one launch (start us, length us, event | category | flops | bytes accessed | tf_op | source)
XLA Modules:
  0.0 270.2 jit_solution(5281522540189356939)
XLA Ops:
  7.2 4.9 %copy.21 = bf16[8,128,2048]{2,1,0:T(8,128)(2,1)} copy(bf16[8,128,2048]{2,1,0:T(8,128)(2,1)} %param.26) | data formatting | bytes 8388608
  12.1 2.9 %collective-permute-start.1 = (bf16[256,2048]{1,0:T(8,128)(2,1)}, bf16[256,2048]{1,0:T(8,128)(2,1)}, u32[]{:S(2)}, u32[]{:S(2)}) collective-permute-start(bf16[256,2048]{1,0:T(8,128)(2,1)} %param.16), channel_id=1, source_target_pairs={{0,2},{2,0},{1,3},{3,1},{4,6},{6,4},{5,7},{7,5},{8,10},{10,8},{9,1... | collective-permute-start | bytes 3145736 | tf_op jit(solution)/shard_map/ppermute | solution.py:45
  15.1 0.7 reshape.67
  15.8 0.7 constant_dynamic-slice_fusion.1
  16.6 0.4 reshape.69
  17.0 0.4 reshape.68
  17.4 32.3 %collective-permute-done = bf16[256,1024]{1,0:T(8,128)(2,1)S(1)} collective-permute-done((bf16[256,1024]{1,0:T(8,128)(2,1)S(1)}, bf16[256,1024]{1,0:T(8,128)(2,1)S(1)}, u32[]{:S(2)}, u32[]{:S(2)}) %collective-permute-start) | collective-permute-done | bytes 524320 | tf_op jit(solution)/shard_map/ppermute | solution.py:45
  49.7 7.1 %fusion.1 = f32[1024,2048]{1,0:T(8,128)} fusion(bf16[256,2048]{1,0:T(8,128)(2,1)} %collective-permute-done.1, bf16[256,2048]{1,0:T(8,128)(2,1)} %param.16, bf16[256,1024]{1,0:T(8,128)(2,1)S(1)} %collective-permute-done, bf16[256,1024]{1,0:T(8,128)(2,1)S(1)} %reshape.68), kind=kOutput, calls=%fused_computation.8 | convolution fusion | flops 2153775104 | bytes 11534336 | tf_op jit(solution)/shard_map/dot_general | solution.py:48
  56.9 91.2 %reduce-scatter.2.cloned.1.call-done = f32[128,2048]{1,0:T(8,128)} async-done(((f32[1024,2048]{1,0:T(8,128)}), f32[128,2048]{1,0:T(8,128)}) %reduce-scatter.2.cloned.1.call-update) | async-done | bytes 1048592 | tf_op jit(solution)/shard_map/reduce_scatter | solution.py:51
  148.1 4.7 %fusion.35 = (bf16[128,2048]{1,0:T(8,128)(2,1)}, f32[128,2048]{1,0:T(8,128)}, f32[128,2048]{1,0:T(8,128)}, f32[128,2048]{1,0:T(8,128)}, f32[128,2048]{1,0:T(8,128)}) fusion(f32[128,2048]{1,0:T(8,128)S(1)} %copy-done.1, f32[128,2048]{1,0:T(8,128)S(1)} %copy-done.2, f32[128,2048]{1,0:T(8,128)} %reduce-scatter.2.cloned.1.call-done, f32[128,2048]{1,0:T(8,128)} %param.18, ...), kind=kLoop, calls=%fused_computation.110 | loop fusion | flops 5242880 | bytes 9961472 | tf_op jit(solution)/shard_map/convert_element_type | solution.py:104
  152.9 0.3 reduce_window_sum.34
  153.2 0.3 reduce_window_sum.36
  153.6 8.0 %scatter_custom_fusion = s32[129]{0:T(256)S(1)} fusion(s32[2048]{0:T(1024)S(1)} %get-tuple-element.29, s32[2048]{0:T(1024)S(1)} %get-tuple-element.30, s32[]{:T(128)} %constant.109.clone.1), kind=kCustom, calls=%fused_computation.106 | custom fusion | bytes 520 | tf_op jit(solution)/shard_map/scatter | solution.py:26
  161.7 0.9 gather_fusion
  162.6 1.0 select_bitcast_fusion.1
  163.6 3.6 %all-to-all-start = ((bf16[16,8,2048]{2,1,0:T(8,128)(2,1)}), bf16[16,8,2048]{2,1,0:T(8,128)(2,1)S(1)}, u32[]{:S(2)}, u32[]{:S(2)}) async-start(bf16[16,8,2048]{2,1,0:T(8,128)(2,1)} %select_bitcast_fusion.1), calls=%async_computation.1 | async-start | bytes 1048576 | tf_op jit(solution)/shard_map/all_to_all | solution.py:94
  167.3 0.2 reduce_window_sum.35
  167.5 8.0 %scatter_custom_fusion.1 = s32[129]{0:T(256)S(1)} fusion(s32[2048]{0:T(1024)S(1)} %get-tuple-element.22, s32[2048]{0:T(1024)S(1)} %get-tuple-element.21, s32[]{:T(128)} %constant.109.clone.1), kind=kCustom, calls=%fused_computation.104 | custom fusion | bytes 520 | tf_op jit(solution)/shard_map/scatter | solution.py:26
  175.6 0.2 select_reduce_fusion.1
  175.8 14.3 %all-to-all-done = bf16[16,8,2048]{2,1,0:T(8,128)(2,1)S(1)} async-done(((bf16[16,8,2048]{2,1,0:T(8,128)(2,1)}), bf16[16,8,2048]{2,1,0:T(8,128)(2,1)S(1)}, u32[]{:S(2)}, u32[]{:S(2)}) %all-to-all-start) | async-done | bytes 524320 | tf_op jit(solution)/shard_map/all_to_all | solution.py:94
  190.1 0.9 gather_fusion.1
  191.1 45.4 %all-gather.2.cloned.1.call-done = bf16[2048,2048]{1,0:T(8,128)(2,1)} async-done(((bf16[128,2048]{1,0:T(8,128)(2,1)}), bf16[2048,2048]{1,0:T(8,128)(2,1)}) %all-gather.2.cloned.1.call-update) | async-done | bytes 8388624 | tf_op jit(solution)/shard_map/all_gather | solution.py:104
  236.5 4.7 %fusion.36 = (f32[2048]{0:T(1024)S(1)}, f32[128,2048]{1,0:T(8,128)S(1)}) fusion(bf16[2048,2048]{1,0:T(8,128)(2,1)} %all-gather.2.cloned.1.call-done, bf16[128,2048]{1,0:T(8,128)(2,1)S(1)} %gather_fusion.1, pred[128]{0:T(512)(128)(4,1)S(1)} %get-tuple-element.10), kind=kOutput, calls=%fused_computation.111 | convolution fusion | flops 1074788352 | bytes 9969792 | tf_op jit(solution)/shard_map/dot_general | solution.py:102
  241.4 0.2 maximum_convert_fusion
  241.6 0.9 gather_fusion.2
  242.5 0.9 select_bitcast_fusion
  243.4 3.6 %all-to-all-start.1 = ((bf16[16,8,2048]{2,1,0:T(8,128)(2,1)}), bf16[16,8,2048]{2,1,0:T(8,128)(2,1)S(1)}, u32[]{:S(2)}, u32[]{:S(2)}) async-start(bf16[16,8,2048]{2,1,0:T(8,128)(2,1)} %select_bitcast_fusion), calls=%async_computation.2 | async-start | bytes 1048576 | tf_op jit(solution)/shard_map/all_to_all | solution.py:109
  247.1 0.2 reduce_window_sum.37
  247.9 0.2 select_reduce_fusion
  248.2 13.3 %all-to-all-done.1 = bf16[16,8,2048]{2,1,0:T(8,128)(2,1)S(1)} async-done(((bf16[16,8,2048]{2,1,0:T(8,128)(2,1)}), bf16[16,8,2048]{2,1,0:T(8,128)(2,1)S(1)}, u32[]{:S(2)}, u32[]{:S(2)}) %all-to-all-start.1) | async-done | bytes 524320 | tf_op jit(solution)/shard_map/all_to_all | solution.py:109
  261.5 0.9 gather_fusion.3
  262.4 1.0 bitcast_dynamic-update-slice_fusion
  (40 shorter events, 0.8 us)
Async XLA Ops:
  7.2 154.5 %copy-start = (bf16[128,2048]{1,0:T(8,128)(2,1)S(1)}, bf16[128,2048]{1,0:T(8,128)(2,1)}, u32[]{:S(2)}) copy-start(bf16[128,2048]{1,0:T(8,128)(2,1)} %param.21) | copy-start | bytes 1572868
  7.2 7.9 %copy-start.3 = (bf16[256,2048]{1,0:T(8,128)(2,1)S(1)}, bf16[256,2048]{1,0:T(8,128)(2,1)}, u32[]{:S(2)}) copy-start(bf16[256,2048]{1,0:T(8,128)(2,1)} %param.15) | copy-start | bytes 3145732
  7.2 140.9 %reduce-scatter.2.cloned.1.call-start = ((), (), s32[]{:S(2)}) async-start(), calls=%async_computation.3 | async-start | bytes 9437184 | tf_op jit(solution)/shard_map/reduce_scatter | solution.py:51
  12.1 37.5 %collective-permute-start.1 = (bf16[256,2048]{1,0:T(8,128)(2,1)}, bf16[256,2048]{1,0:T(8,128)(2,1)}, u32[]{:S(2)}, u32[]{:S(2)}) collective-permute-start(bf16[256,2048]{1,0:T(8,128)(2,1)} %param.16), channel_id=1, source_target_pairs={{0,2},{2,0},{1,3},{3,1},{4,6},{6,4},{5,7},{7,5},{8,10},{10,8},{9,1... | collective-permute-start | bytes 3145736 | tf_op jit(solution)/shard_map/ppermute | solution.py:45
  16.9 32.7 %collective-permute-start = (bf16[256,1024]{1,0:T(8,128)(2,1)S(1)}, bf16[256,1024]{1,0:T(8,128)(2,1)S(1)}, u32[]{:S(2)}, u32[]{:S(2)}) collective-permute-start(bf16[256,1024]{1,0:T(8,128)(2,1)S(1)} %reshape.69), channel_id=1, source_target_pairs={{0,2},{2,0},{1,3},{3,1},{4,6},{6,4},{5,7},{7,5},{8,10},{10,8},{9,1... | collective-permute-start | bytes 1572872 | tf_op jit(solution)/shard_map/ppermute | solution.py:45
  56.8 91.3 %copy-start.1 = (f32[128,2048]{1,0:T(8,128)S(1)}, f32[128,2048]{1,0:T(8,128)}, u32[]{:S(2)}) copy-start(f32[128,2048]{1,0:T(8,128)} %param.20) | copy-start | bytes 3145732
  56.8 91.3 %copy-start.2 = (f32[128,2048]{1,0:T(8,128)S(1)}, f32[128,2048]{1,0:T(8,128)}, u32[]{:S(2)}) copy-start(f32[128,2048]{1,0:T(8,128)} %param.17) | copy-start | bytes 3145732
  56.9 96.0 %copy-start.5 = (s32[2048]{0:T(1024)S(1)}, s32[2048]{0:T(1024)}, u32[]{:S(2)}) copy-start(s32[2048]{0:T(1024)} %param.22) | copy-start | bytes 24580
  56.9 96.3 %copy-start.4 = (s32[2048]{0:T(1024)S(1)}, s32[2048]{0:T(1024)}, u32[]{:S(2)}) copy-start(s32[2048]{0:T(1024)} %param.23) | copy-start | bytes 24580
  56.9 179.6 %all-gather.2.cloned.1.call-start = ((), (), s32[]{:S(2)}) async-start(), calls=%async_computation.4 | async-start | bytes 8912896 | tf_op jit(solution)/shard_map/all_gather | solution.py:104
  163.6 26.6 %all-to-all-start = ((bf16[16,8,2048]{2,1,0:T(8,128)(2,1)}), bf16[16,8,2048]{2,1,0:T(8,128)(2,1)S(1)}, u32[]{:S(2)}, u32[]{:S(2)}) async-start(bf16[16,8,2048]{2,1,0:T(8,128)(2,1)} %select_bitcast_fusion.1), calls=%async_computation.1 | async-start | bytes 1048576 | tf_op jit(solution)/shard_map/all_to_all | solution.py:94
  236.5 4.9 %copy-start.6 = (f32[2048]{0:T(1024)S(1)}, f32[2048]{0:T(1024)}, u32[]{:S(2)}) copy-start(f32[2048]{0:T(1024)} %param.25) | copy-start | bytes 24580
  236.5 4.9 %copy-start.7 = (f32[2048]{0:T(1024)S(1)}, f32[2048]{0:T(1024)}, u32[]{:S(2)}) copy-start(f32[2048]{0:T(1024)} %param.24) | copy-start | bytes 24580
  243.4 18.0 %all-to-all-start.1 = ((bf16[16,8,2048]{2,1,0:T(8,128)(2,1)}), bf16[16,8,2048]{2,1,0:T(8,128)(2,1)S(1)}, u32[]{:S(2)}, u32[]{:S(2)}) async-start(bf16[16,8,2048]{2,1,0:T(8,128)(2,1)} %select_bitcast_fusion), calls=%async_computation.2 | async-start | bytes 1048576 | tf_op jit(solution)/shard_map/all_to_all | solution.py:109
Sparse Core Ops, SparseCore 0:
  57.0 91.1 reduce-scatter.1
  153.0 83.4 all-gather.1

commit v2 on v1

--- a/solution.py
+++ b/solution.py
@@ -15,16 +15,12 @@
 def route(mapping, position, block_rows, per_peer):
     members = mapping.shape[0] // block_rows
     layout = mapping.reshape(members, block_rows)
-    owned = (layout // block_rows == position).astype(jnp.int32)
-    ordinal = jnp.cumsum(owned, axis=1) - 1
-    destination = jnp.arange(members, dtype=jnp.int32)[:, None] * per_peer + ordinal
-    destination = jnp.where(owned == 1, destination, members * per_peer)
-    offsets = jnp.where(owned == 1, layout - position * block_rows, 0)
-    send_index = (
-        jnp.zeros((members * per_peer + 1,), jnp.int32)
-        .at[destination.reshape(-1)]
-        .set(offsets.reshape(-1))[: members * per_peer]
-    )
+    owned = layout // block_rows == position
+    ordinal = jnp.cumsum(owned.astype(jnp.int32), axis=1) - 1
+    offsets = layout - position * block_rows
+    slots = jnp.arange(per_peer, dtype=jnp.int32)[None, :, None]
+    hit = owned[:, None, :] & (ordinal[:, None, :] == slots)
+    send_index = jnp.sum(jnp.where(hit, offsets[:, None, :], 0), axis=2).reshape(-1)
     own_block = lax.dynamic_slice_in_dim(mapping, position * block_rows, block_rows)
     anchor = own_block // block_rows
     indicator = (anchor[:, None] == jnp.arange(members, dtype=jnp.int32)[None, :]).astype(jnp.int32)
@@ -32,23 +28,25 @@
     return (send_index, anchor * per_peer + arrival)
 
 
-def pair_gradient(queries, grad_out):
+def pair_gradient(queries, grad_out, early):
     tokens, width = queries.shape
     zo = lax.axis_size("zo")
     x = lax.axis_index("xl")
-    blocks = queries.reshape(tokens, zo, 2, 2, width // (4 * zo))
-    mine = lax.dynamic_index_in_dim(blocks, x, axis=2, keepdims=False)
-    theirs = lax.dynamic_index_in_dim(blocks, 1 - x, axis=2, keepdims=False)
+    blocks = queries.reshape(tokens, zo, 2, 2, width // (4 * zo)).transpose(0, 2, 3, 1, 4)
+    mine = lax.dynamic_index_in_dim(blocks, x, axis=1, keepdims=False)
+    theirs = lax.dynamic_index_in_dim(blocks, 1 - x, axis=1, keepdims=False)
     mine = mine.reshape(tokens, width // 2)
     theirs = theirs.reshape(tokens, width // 2)
     swap = [(0, 1), (1, 0)]
     got_queries, got_grad = lax.ppermute((theirs, grad_out), "xl", swap)
+    (got_queries, got_grad), early = lax.optimization_barrier(((got_queries, got_grad), early))
     both_queries = jnp.concatenate([mine, got_queries], axis=0)
     both_grad = jnp.concatenate([grad_out, got_grad], axis=0)
     partial = lax.dot_general(
         both_queries, both_grad, (((0,), (0,)), ((), ())), preferred_element_type=jnp.float32
     )
-    return lax.psum_scatter(partial, ("zo", "c"), scatter_dimension=0, tiled=True)
+    partial = lax.psum_scatter(partial, "c", scatter_dimension=0, tiled=True)
+    return lax.psum_scatter(partial, "zo", scatter_dimension=0, tiled=True), early
 
 
 def adamw(gradient, params, first_moment, second_moment, key_params):
@@ -95,14 +93,18 @@
         jnp.take(keys, send_forward, axis=0), DP, split_axis=0, concat_axis=0, tiled=True
     )
     encoded_rows = jnp.take(moved, receive_forward, axis=0)
-    gradient = pair_gradient(queries, grad_out) * scaling
+    gradient, (encoded_rows, send_back, receive_back) = pair_gradient(
+        queries, grad_out, (encoded_rows, send_back, receive_back)
+    )
     new_params, new_first, new_second, new_key = adamw(
-        gradient, params, first_moment, second_moment, key_params
+        gradient * scaling, params, first_moment, second_moment, key_params
     )
+    zo = lax.axis_size("zo")
+    weight = lax.all_gather(new_key.astype(jnp.bfloat16), ("zo", "xl"), axis=0, tiled=True)
+    weight = lax.all_gather(weight, "c", axis=0, tiled=True)
+    columns = encoded_rows.reshape(block_rows, zo, 2, 2, -1).transpose(0, 3, 1, 2, 4)
     codes = jnp.dot(
-        encoded_rows,
-        lax.all_gather(new_key.astype(jnp.bfloat16), DP, axis=0, tiled=True),
-        preferred_element_type=jnp.float32,
+        columns.reshape(block_rows, -1), weight, preferred_element_type=jnp.float32
     )
     codes = codes.astype(jnp.bfloat16)
     normed = batch_norm(codes, bn_gain, bn_shift)

time: 271 us -> 304 us (1.12)
  waiting for transfers between devices: 197 us -> 240 us
  local copies, waits for them, and re-layouts: 26.9 us -> 11.4 us
  starting transfers between devices: 10.2 us -> 15.5 us
    all_gather x1 -> x2, waiting for transfers between devices: 45.4 us -> 92.6 us  [the longest x1 74 us: per_device(): lax.all_gather(new_key.astype(jnp.bfloat16), ('zo', 'xl'), axis=0, tiled=...]
    scatter x2 -> x0, local copies, waits for them, and re-layouts: 16.1 us -> none  [route(): send_index = jnp.zeros((members * per_peer + 1,), jnp.int32).at[destinati...]
    reduce_scatter x1 -> x2, waiting for transfers between devices: 91.2 us -> 97.5 us  [the longest x1 80.4 us: pair_gradient(): lax.psum_scatter(partial, 'zo', scatter_dimension=0, tiled=True)]
    all_to_all x1, waiting for transfers between devices: 14.3 us -> 8.85 us  [per_device(): lax.all_to_all(jnp.take(keys, send_forward, axis=0), DP, split_axis=0, co...]
    ppermute x2, waiting for transfers between devices: 32.3 us -> 27 us  [pair_gradient(): got_queries, got_grad = lax.ppermute((theirs, grad_out), 'xl', swap)]
    all_to_all x1, starting transfers between devices: 3.57 us -> 7.36 us  [per_device(): lax.all_to_all(jnp.take(keys, send_forward, axis=0), DP, split_axis=0, co...]
    unnamed x17 -> x16, local copies, waits for them, and re-layouts: 4.94 us -> 6.37 us
  transfers between devices with their start and end apart: 6 -> 8, of which waited for: 5 -> 8; matrix products, arithmetic and copies ran while one was open for 8% -> 2% of each run, Pallas kernels for 0% -> 0%
where the time goes in v2:
time: 304 us
  waiting for transfers between devices  240 us (79%)
  starting transfers between devices  15.5 us (5%)
  between operations  14.7 us (5%)
  matrix products  12 us (4%)
  local copies, waits for them, and re-layouts  11.4 us (4%)
  other arithmetic  10.5 us (3%)
    reduce_scatter x1, waiting for transfers between devices, pair_gradient(): lax.psum_scatter(partial, 'zo', scatter_dimension=0, tiled=True)  80.4 us
    all_gather x1, waiting for transfers between devices, per_device(): lax.all_gather(new_key.astype(jnp.bfloat16), ('zo', 'xl'), axis=0, tiled=...  74 us
    ppermute x2, waiting for transfers between devices, pair_gradient(): got_queries, got_grad = lax.ppermute((theirs, grad_out), 'xl', swap)  27 us
    all_gather x1, waiting for transfers between devices, per_device(): weight = lax.all_gather(weight, 'c', axis=0, tiled=True)  18.6 us
    reduce_scatter x1, waiting for transfers between devices, pair_gradient(): partial = lax.psum_scatter(partial, 'c', scatter_dimension=0, tiled=True)  17.1 us
    all_to_all x1, waiting for transfers between devices, per_device(): lax.all_to_all(jnp.take(normed, send_back, axis=0), DP, split_axis=0, con...  13.8 us
    all_to_all x1, waiting for transfers between devices, per_device(): lax.all_to_all(jnp.take(keys, send_forward, axis=0), DP, split_axis=0, co...  8.85 us
    all_to_all x1, starting transfers between devices, per_device(): lax.all_to_all(jnp.take(keys, send_forward, axis=0), DP, split_axis=0, co...  7.36 us
  transfers between devices with their start and end apart: 8, of which 8 were waited for; matrix products, arithmetic and copies ran while one was open for 2% of the time, Pallas kernels for 0%

profile of v2, /device:TPU:0, one launch (start us, length us, event | category | flops | bytes accessed | tf_op | source)
XLA Modules:
  0.0 303.8 jit_solution(17909300407234767059)
XLA Ops:
  7.2 4.8 %copy.30 = bf16[8,128,2048]{2,1,0:T(8,128)(2,1)} copy(bf16[8,128,2048]{2,1,0:T(8,128)(2,1)} %param.26) | data formatting | bytes 8388608
  12.1 0.3 reduce_window_sum.34
  12.4 0.3 select_reduce_fusion.3
  12.9 0.9 gather_fusion
  13.9 0.9 select_bitcast_fusion.1
  14.8 7.4 %all-to-all-start = ((bf16[16,8,2048]{2,1,0:T(8,128)(2,1)}), bf16[16,8,2048]{2,1,0:T(8,128)(2,1)S(1)}, u32[]{:S(2)}, u32[]{:S(2)}) async-start(bf16[16,8,2048]{2,1,0:T(8,128)(2,1)} %select_bitcast_fusion.1), calls=%async_computation | async-start | bytes 1048576 | tf_op jit(solution)/shard_map/all_to_all | solution.py:92
  22.2 1.5 copy.23
  23.8 2.0 collective-permute-start
  26.1 0.2 reduce_window_sum.35
  26.6 0.2 reduce_window_sum.37
  26.7 0.3 reduce_window_sum.36
  27.2 0.3 select_reduce_fusion.1
  27.8 8.8 %all-to-all-done = bf16[16,8,2048]{2,1,0:T(8,128)(2,1)S(1)} async-done(((bf16[16,8,2048]{2,1,0:T(8,128)(2,1)}), bf16[16,8,2048]{2,1,0:T(8,128)(2,1)S(1)}, u32[]{:S(2)}, u32[]{:S(2)}) %all-to-all-start) | async-done | bytes 524320 | tf_op jit(solution)/shard_map/all_to_all | solution.py:92
  36.7 0.9 gather_fusion.1
  37.7 4.8 %collective-permute-done = bf16[256,1024]{0,1:T(8,128)(2,1)} collective-permute-done((bf16[256,1024]{0,1:T(8,128)(2,1)S(1)}, bf16[256,1024]{0,1:T(8,128)(2,1)}, u32[]{:S(2)}, u32[]{:S(2)}) %collective-permute-start) | collective-permute-done | bytes 524320 | tf_op jit(solution)/shard_map/ppermute | solution.py:41
  42.5 22.2 %collective-permute-done.1 = bf16[256,2048]{1,0:T(8,128)(2,1)} collective-permute-done((bf16[256,2048]{1,0:T(8,128)(2,1)}, bf16[256,2048]{1,0:T(8,128)(2,1)}, u32[]{:S(2)}, u32[]{:S(2)}) %collective-permute-start.1) | collective-permute-done | bytes 1048608 | tf_op jit(solution)/shard_map/ppermute | solution.py:41
  64.7 7.3 %fusion.1 = f32[1024,2048]{1,0:T(8,128)} fusion(bf16[256,2048]{1,0:T(8,128)(2,1)} %collective-permute-done.1, bf16[256,2048]{1,0:T(8,128)(2,1)} %param.16, bf16[256,1024]{0,1:T(8,128)(2,1)} %collective-permute-done, bf16[256,1024]{0,1:T(8,128)(2,1)S(1)} %bitcast.65), kind=kOutput, calls=%fused_computation.6 | convolution fusion | flops 2153775104 | bytes 11534336 | tf_op jit(solution)/shard_map/dot_general | solution.py:45
  72.1 17.1 %reduce-scatter.3.cloned.1.call-done = f32[512,2048]{1,0:T(8,128)} async-done(((f32[1024,2048]{1,0:T(8,128)}), f32[512,2048]{1,0:T(8,128)}) %reduce-scatter.3.cloned.1.call-update) | async-done | bytes 4194320 | tf_op jit(solution)/shard_map/reduce_scatter | solution.py:48
  89.3 80.4 %reduce-scatter.5.cloned.1.call-done = f32[128,2048]{1,0:T(8,128)} async-done(((f32[512,2048]{1,0:T(8,128)}), f32[128,2048]{1,0:T(8,128)}) %reduce-scatter.5.cloned.1.call-update) | async-done | bytes 1048592 | tf_op jit(solution)/shard_map/reduce_scatter | solution.py:49
  169.7 4.8 %fusion.21 = (bf16[128,2048]{1,0:T(8,128)(2,1)}, f32[128,2048]{1,0:T(8,128)}, f32[128,2048]{1,0:T(8,128)}, f32[128,2048]{1,0:T(8,128)}, f32[128,2048]{1,0:T(8,128)}) fusion(f32[128,2048]{1,0:T(8,128)S(1)} %copy-done.1, f32[128,2048]{1,0:T(8,128)S(1)} %copy-done.2, f32[128,2048]{1,0:T(8,128)} %reduce-scatter.5.cloned.1.call-done, f32[128,2048]{1,0:T(8,128)} %param.18, ...), kind=kLoop, calls=%fused_computation.85 | loop fusion | flops 5242880 | bytes 9961472 | tf_op jit(solution)/shard_map/convert_element_type | solution.py:103
  174.5 74.0 %all-gather.3.cloned.1.call-done = bf16[1024,2048]{1,0:T(8,128)(2,1)} async-done(((bf16[128,2048]{1,0:T(8,128)(2,1)}), bf16[1024,2048]{1,0:T(8,128)(2,1)}) %all-gather.3.cloned.1.call-update) | async-done | bytes 4194320 | tf_op jit(solution)/shard_map/all_gather | solution.py:103
  248.6 0.4 reshape.207
  248.9 0.5 copy.26
  249.5 18.6 %all-gather.5.cloned.1.call-done = bf16[2048,2048]{1,0:T(8,128)(2,1)} async-done(((bf16[1024,2048]{1,0:T(8,128)(2,1)}), bf16[2048,2048]{1,0:T(8,128)(2,1)}) %all-gather.5.cloned.1.call-update) | async-done | bytes 8388624 | tf_op jit(solution)/shard_map/all_gather | solution.py:104
  268.1 4.7 %fusion.26 = (f32[2048]{0:T(1024)S(1)}, f32[128,2048]{1,0:T(8,128)S(1)}) fusion(bf16[128,2048]{0,1:T(8,128)(2,1)S(1)} %bitcast.63, bf16[2048,2048]{1,0:T(8,128)(2,1)} %all-gather.5.cloned.1.call-done), kind=kOutput, calls=%fused_computation.88 | convolution fusion | flops 1074526208 | bytes 9969664 | tf_op jit(solution)/shard_map/dot_general | solution.py:106
  273.0 0.2 maximum_convert_fusion
  273.2 0.9 gather_fusion.2
  274.1 0.9 select_bitcast_fusion
  275.0 5.9 %all-to-all-start.1 = ((bf16[16,8,2048]{2,1,0:T(8,128)(2,1)}), bf16[16,8,2048]{2,1,0:T(8,128)(2,1)S(1)}, u32[]{:S(2)}, u32[]{:S(2)}) async-start(bf16[16,8,2048]{2,1,0:T(8,128)(2,1)} %select_bitcast_fusion), calls=%async_computation.3 | async-start | bytes 1048576 | tf_op jit(solution)/shard_map/all_to_all | solution.py:111
  281.6 13.8 %all-to-all-done.1 = bf16[16,8,2048]{2,1,0:T(8,128)(2,1)S(1)} async-done(((bf16[16,8,2048]{2,1,0:T(8,128)(2,1)}), bf16[16,8,2048]{2,1,0:T(8,128)(2,1)S(1)}, u32[]{:S(2)}, u32[]{:S(2)}) %all-to-all-start.1) | async-done | bytes 524320 | tf_op jit(solution)/shard_map/all_to_all | solution.py:111
  295.4 0.9 gather_fusion.3
  296.3 1.0 bitcast_dynamic-update-slice_fusion
  (55 shorter events, 1.8 us)
Async XLA Ops:
  7.2 5.8 %copy-start = (bf16[128,2048]{1,0:T(8,128)(2,1)S(1)}, bf16[128,2048]{1,0:T(8,128)(2,1)}, u32[]{:S(2)}) copy-start(bf16[128,2048]{1,0:T(8,128)(2,1)} %param.21) | copy-start | bytes 1572868
  7.2 4.9 %copy-start.3 = (s32[2048]{0:T(1024)S(1)}, s32[2048]{0:T(1024)}, u32[]{:S(2)}) copy-start(s32[2048]{0:T(1024)} %param.22) | copy-start | bytes 24580
  13.9 12.1 %copy-start.4 = (s32[2048]{0:T(1024)S(1)}, s32[2048]{0:T(1024)}, u32[]{:S(2)}) copy-start(s32[2048]{0:T(1024)} %param.23) | copy-start | bytes 24580
  14.8 21.9 %all-to-all-start = ((bf16[16,8,2048]{2,1,0:T(8,128)(2,1)}), bf16[16,8,2048]{2,1,0:T(8,128)(2,1)S(1)}, u32[]{:S(2)}, u32[]{:S(2)}) async-start(bf16[16,8,2048]{2,1,0:T(8,128)(2,1)} %select_bitcast_fusion.1), calls=%async_computation | async-start | bytes 1048576 | tf_op jit(solution)/shard_map/all_to_all | solution.py:92
  22.2 67.1 %reduce-scatter.3.cloned.1.call-start = ((), (), s32[]{:S(2)}) async-start(), calls=%async_computation.4 | async-start | bytes 12582912 | tf_op jit(solution)/shard_map/reduce_scatter | solution.py:48
  23.8 18.6 %collective-permute-start = (bf16[256,1024]{0,1:T(8,128)(2,1)S(1)}, bf16[256,1024]{0,1:T(8,128)(2,1)}, u32[]{:S(2)}, u32[]{:S(2)}) collective-permute-start(bf16[256,1024]{0,1:T(8,128)(2,1)S(1)} %bitcast.64), channel_id=1, source_target_pairs={{0,2},{2,0},{1,3},{3,1},{4,6},{6,4},{5,7},{7,5},{8,10},{10,8},{9,1... | collective-permute-start | bytes 1572872 | tf_op jit(solution)/shard_map/ppermute | solution.py:41
  25.8 38.9 %collective-permute-start.1 = (bf16[256,2048]{1,0:T(8,128)(2,1)}, bf16[256,2048]{1,0:T(8,128)(2,1)}, u32[]{:S(2)}, u32[]{:S(2)}) collective-permute-start(bf16[256,2048]{1,0:T(8,128)(2,1)} %param.16), channel_id=1, source_target_pairs={{0,2},{2,0},{1,3},{3,1},{4,6},{6,4},{5,7},{7,5},{8,10},{10,8},{9,1... | collective-permute-start | bytes 3145736 | tf_op jit(solution)/shard_map/ppermute | solution.py:41
  72.0 97.7 %copy-start.1 = (f32[128,2048]{1,0:T(8,128)S(1)}, f32[128,2048]{1,0:T(8,128)}, u32[]{:S(2)}) copy-start(f32[128,2048]{1,0:T(8,128)} %param.20) | copy-start | bytes 3145732
  72.0 97.7 %copy-start.2 = (f32[128,2048]{1,0:T(8,128)S(1)}, f32[128,2048]{1,0:T(8,128)}, u32[]{:S(2)}) copy-start(f32[128,2048]{1,0:T(8,128)} %param.17) | copy-start | bytes 3145732
  72.0 97.6 %reduce-scatter.5.cloned.1.call-start = ((), (), s32[]{:S(2)}) async-start(), calls=%async_computation.5 | async-start | bytes 5242880 | tf_op jit(solution)/shard_map/reduce_scatter | solution.py:49
  89.2 159.3 %all-gather.3.cloned.1.call-start = ((), (), s32[]{:S(2)}) async-start(), calls=%async_computation.6 | async-start | bytes 4718592 | tf_op jit(solution)/shard_map/all_gather | solution.py:103
  174.5 93.6 %all-gather.5.cloned.1.call-start = ((), (), s32[]{:S(2)}) async-start(), calls=%async_computation.7 | async-start | bytes 12582912 | tf_op jit(solution)/shard_map/all_gather | solution.py:104
  268.1 4.9 %copy-start.5 = (f32[2048]{0:T(1024)S(1)}, f32[2048]{0:T(1024)}, u32[]{:S(2)}) copy-start(f32[2048]{0:T(1024)} %param.25) | copy-start | bytes 24580
  268.1 4.9 %copy-start.6 = (f32[2048]{0:T(1024)S(1)}, f32[2048]{0:T(1024)}, u32[]{:S(2)}) copy-start(f32[2048]{0:T(1024)} %param.24) | copy-start | bytes 24580
  275.0 20.3 %all-to-all-start.1 = ((bf16[16,8,2048]{2,1,0:T(8,128)(2,1)}), bf16[16,8,2048]{2,1,0:T(8,128)(2,1)S(1)}, u32[]{:S(2)}, u32[]{:S(2)}) async-start(bf16[16,8,2048]{2,1,0:T(8,128)(2,1)} %select_bitcast_fusion), calls=%async_computation.3 | async-start | bytes 1048576 | tf_op jit(solution)/shard_map/all_to_all | solution.py:111
Sparse Core Ops, SparseCore 0:
  72.1 17.0 reduce-scatter.2
  91.6 78.0 reduce-scatter.4
  174.6 73.9 all-gather.2
  249.9 18.1 all-gather.4

commit v3 on v1

--- a/solution.py
+++ b/solution.py
@@ -15,16 +15,12 @@
 def route(mapping, position, block_rows, per_peer):
     members = mapping.shape[0] // block_rows
     layout = mapping.reshape(members, block_rows)
-    owned = (layout // block_rows == position).astype(jnp.int32)
-    ordinal = jnp.cumsum(owned, axis=1) - 1
-    destination = jnp.arange(members, dtype=jnp.int32)[:, None] * per_peer + ordinal
-    destination = jnp.where(owned == 1, destination, members * per_peer)
-    offsets = jnp.where(owned == 1, layout - position * block_rows, 0)
-    send_index = (
-        jnp.zeros((members * per_peer + 1,), jnp.int32)
-        .at[destination.reshape(-1)]
-        .set(offsets.reshape(-1))[: members * per_peer]
-    )
+    owned = layout // block_rows == position
+    ordinal = jnp.cumsum(owned.astype(jnp.int32), axis=1) - 1
+    offsets = layout - position * block_rows
+    slots = jnp.arange(per_peer, dtype=jnp.int32)[None, :, None]
+    hit = owned[:, None, :] & (ordinal[:, None, :] == slots)
+    send_index = jnp.sum(jnp.where(hit, offsets[:, None, :], 0), axis=2).reshape(-1)
     own_block = lax.dynamic_slice_in_dim(mapping, position * block_rows, block_rows)
     anchor = own_block // block_rows
     indicator = (anchor[:, None] == jnp.arange(members, dtype=jnp.int32)[None, :]).astype(jnp.int32)
@@ -49,6 +45,67 @@
         both_queries, both_grad, (((0,), (0,)), ((), ())), preferred_element_type=jnp.float32
     )
     return lax.psum_scatter(partial, ("zo", "c"), scatter_dimension=0, tiled=True)
+
+
+def ring_codes(weight, rows):
+    zo_size = lax.axis_size("zo")
+    length = 2 * zo_size
+    block = weight.shape[0]
+
+    def where(q):
+        return (q if q < zo_size else length - 1 - q, 0 if q < zo_size else 1)
+
+    def index(zo, xl, c):
+        return (zo * 2 + xl) * 2 + c
+
+    def pairs(step):
+        return [
+            (index(*where(q), c), index(*where((q + step) % length), c))
+            for q in range(length)
+            for c in (0, 1)
+        ]
+
+    forward, backward = pairs(1), pairs(length - 1)
+    partner = [
+        (index(zo, xl, c), index(zo, xl, 1 - c))
+        for zo in range(zo_size)
+        for xl in (0, 1)
+        for c in (0, 1)
+    ]
+    zo = lax.axis_index("zo")
+    xl = lax.axis_index("xl")
+    c = lax.axis_index("c")
+    here = jnp.where(xl == 0, zo, length - 1 - zo)
+
+    def columns(offset, cls):
+        q = (here + offset) % length
+        source = jnp.where(q < zo_size, q, length - 1 - q)
+        source = (source * 2 + (q >= zo_size).astype(jnp.int32)) * 2 + cls
+        return lax.dynamic_slice_in_dim(rows, source * block, block, axis=1)
+
+    def add(total, offset, cls, shard):
+        part = jnp.dot(columns(offset, cls), shard, preferred_element_type=jnp.float32)
+        return part if total is None else total + part
+
+    total = add(None, 0, c, weight)
+    ahead, behind = weight, weight
+    handed = [(0, weight)]
+    for step in range(1, length // 2 + 1):
+        sent = lax.ppermute(tuple(s for _, s in handed), DP, partner)
+        for (offset, _), shard in zip(handed, sent):
+            total = add(total, offset, 1 - c, shard)
+        handed = []
+        ahead = lax.ppermute(ahead, DP, forward)
+        total = add(total, -step, c, ahead)
+        handed.append((-step, ahead))
+        if step < length // 2:
+            behind = lax.ppermute(behind, DP, backward)
+            total = add(total, step, c, behind)
+            handed.append((step, behind))
+    sent = lax.ppermute(tuple(s for _, s in handed), DP, partner)
+    for (offset, _), shard in zip(handed, sent):
+        total = add(total, offset, 1 - c, shard)
+    return total
 
 
 def adamw(gradient, params, first_moment, second_moment, key_params):
@@ -96,14 +153,13 @@
     )
     encoded_rows = jnp.take(moved, receive_forward, axis=0)
     gradient = pair_gradient(queries, grad_out) * scaling
+    gradient, (encoded_rows, send_back, receive_back) = lax.optimization_barrier(
+        (gradient, (encoded_rows, send_back, receive_back))
+    )
     new_params, new_first, new_second, new_key = adamw(
         gradient, params, first_moment, second_moment, key_params
     )
-    codes = jnp.dot(
-        encoded_rows,
-        lax.all_gather(new_key.astype(jnp.bfloat16), DP, axis=0, tiled=True),
-        preferred_element_type=jnp.float32,
-    )
+    codes = ring_codes(new_key.astype(jnp.bfloat16), encoded_rows)
     codes = codes.astype(jnp.bfloat16)
     normed = batch_norm(codes, bn_gain, bn_shift)
     returned = lax.all_to_all(

time: 271 us -> 253 us (0.934)
  waiting for transfers between devices: 197 us -> 181 us
  local copies, waits for them, and re-layouts: 26.9 us -> 11.7 us
  starting transfers between devices: 10.2 us -> 20.2 us
    ppermute x0 -> x15, waiting for transfers between devices: none -> 48.3 us  [the longest x4 24.2 us: ring_codes(): ahead = lax.ppermute(ahead, DP, forward)]
    all_gather x1 -> x0, waiting for transfers between devices: 45.4 us -> none  [per_device(): lax.all_gather(new_key.astype(jnp.bfloat16), DP, axis=0, tiled=True)]
    reduce_scatter x1, waiting for transfers between devices: 91.2 us -> 66.1 us  [pair_gradient(): lax.psum_scatter(partial, ('zo', 'c'), scatter_dimension=0, tiled=True)]
    scatter x2 -> x0, local copies, waits for them, and re-layouts: 16.1 us -> none  [route(): send_index = jnp.zeros((members * per_peer + 1,), jnp.int32).at[destinati...]
    ppermute x0 -> x15, starting transfers between devices: none -> 7.39 us  [the longest x4 3.69 us: ring_codes(): ahead = lax.ppermute(ahead, DP, forward)]
    all_to_all x1, waiting for transfers between devices: 14.3 us -> 20.8 us  [per_device(): lax.all_to_all(jnp.take(keys, send_forward, axis=0), DP, split_axis=0, co...]
    unnamed x17 -> x15, local copies, waits for them, and re-layouts: 4.94 us -> 5.58 us
  transfers between devices with their start and end apart: 6 -> 20, of which waited for: 5 -> 11; matrix products, arithmetic and copies ran while one was open for 8% -> 5% of each run, Pallas kernels for 0% -> 0%
where the time goes in v3:
time: 253 us; the launch traced here: 252 us
  waiting for transfers between devices  181 us (72%)
  starting transfers between devices  20.2 us (8%)
  between operations  15.5 us (6%)
  matrix products  11.8 us (5%)
  local copies, waits for them, and re-layouts  11.7 us (5%)
  other arithmetic  11.6 us (5%)
    reduce_scatter x1, waiting for transfers between devices, pair_gradient(): lax.psum_scatter(partial, ('zo', 'c'), scatter_dimension=0, tiled=True)  66.1 us
    ppermute x2, waiting for transfers between devices, pair_gradient(): got_queries, got_grad = lax.ppermute((theirs, grad_out), 'xl', swap)  32.3 us
    ppermute x4, waiting for transfers between devices, ring_codes(): ahead = lax.ppermute(ahead, DP, forward)  24.2 us
    ppermute x3, waiting for transfers between devices, ring_codes(): behind = lax.ppermute(behind, DP, backward)  23.2 us
    all_to_all x1, waiting for transfers between devices, per_device(): lax.all_to_all(jnp.take(keys, send_forward, axis=0), DP, split_axis=0, co...  20.8 us
    all_to_all x1, waiting for transfers between devices, per_device(): lax.all_to_all(jnp.take(normed, send_back, axis=0), DP, split_axis=0, con...  13.7 us
    dot_general x1, matrix products, pair_gradient(): lax.dot_general(both_queries, both_grad, (((0,), (0,)), ((), ())), prefer...  7.16 us
    all_to_all x1, starting transfers between devices, per_device(): lax.all_to_all(jnp.take(keys, send_forward, axis=0), DP, split_axis=0, co...  6.16 us
  transfers between devices with their start and end apart: 20, of which 11 were waited for; matrix products, arithmetic and copies ran while one was open for 5% of the time, Pallas kernels for 0%

profile of v3, /device:TPU:0, one launch (start us, length us, event | category | flops | bytes accessed | tf_op | source)
XLA Modules:
  0.0 252.1 jit_solution(12929853300064101138)
XLA Ops:
  7.2 4.9 %copy.21 = bf16[8,128,2048]{2,1,0:T(8,128)(2,1)} copy(bf16[8,128,2048]{2,1,0:T(8,128)(2,1)} %param.26) | data formatting | bytes 8388608
  12.1 2.9 %collective-permute-start.1 = (bf16[256,2048]{1,0:T(8,128)(2,1)}, bf16[256,2048]{1,0:T(8,128)(2,1)}, u32[]{:S(2)}, u32[]{:S(2)}) collective-permute-start(bf16[256,2048]{1,0:T(8,128)(2,1)} %param.16), channel_id=1, source_target_pairs={{0,2},{2,0},{1,3},{3,1},{4,6},{6,4},{5,7},{7,5},{8,10},{10,8},{9,1... | collective-permute-start | bytes 3145736 | tf_op jit(solution)/shard_map/ppermute | solution.py:41
  15.1 0.7 reshape.194
  15.8 0.7 constant_dynamic-slice_fusion.1
  17.4 32.3 %collective-permute-done = bf16[256,1024]{1,0:T(8,128)(2,1)S(1)} collective-permute-done((bf16[256,1024]{1,0:T(8,128)(2,1)S(1)}, bf16[256,1024]{1,0:T(8,128)(2,1)S(1)}, u32[]{:S(2)}, u32[]{:S(2)}) %collective-permute-start) | collective-permute-done | bytes 524320 | tf_op jit(solution)/shard_map/ppermute | solution.py:41
  49.7 7.2 %fusion.11 = f32[1024,2048]{1,0:T(8,128)} fusion(bf16[256,2048]{1,0:T(8,128)(2,1)} %collective-permute-done.1, bf16[256,2048]{1,0:T(8,128)(2,1)} %param.16, bf16[256,1024]{1,0:T(8,128)(2,1)S(1)} %collective-permute-done, bf16[256,1024]{1,0:T(8,128)(2,1)S(1)} %reshape.195), kind=kOutput, calls=%fused_computation.21 | convolution fusion | flops 2153775104 | bytes 11534336 | tf_op jit(solution)/shard_map/dot_general | solution.py:44
  56.9 0.6 copy-done.3
  58.4 0.9 gather_fusion
  59.3 0.9 select_bitcast_fusion.1
  60.2 6.2 %all-to-all-start = ((bf16[16,8,2048]{2,1,0:T(8,128)(2,1)}), bf16[16,8,2048]{2,1,0:T(8,128)(2,1)S(1)}, u32[]{:S(2)}, u32[]{:S(2)}) async-start(bf16[16,8,2048]{2,1,0:T(8,128)(2,1)} %select_bitcast_fusion.1), calls=%async_computation.1 | async-start | bytes 1048576 | tf_op jit(solution)/shard_map/all_to_all | solution.py:151
  68.6 20.8 %all-to-all-done = bf16[16,8,2048]{2,1,0:T(8,128)(2,1)S(1)} async-done(((bf16[16,8,2048]{2,1,0:T(8,128)(2,1)}), bf16[16,8,2048]{2,1,0:T(8,128)(2,1)S(1)}, u32[]{:S(2)}, u32[]{:S(2)}) %all-to-all-start) | async-done | bytes 524320 | tf_op jit(solution)/shard_map/all_to_all | solution.py:151
  89.4 0.9 gather_fusion.1
  90.5 66.1 %reduce-scatter.2.cloned.1.call-done = f32[128,2048]{1,0:T(8,128)} async-done(((f32[1024,2048]{1,0:T(8,128)}), f32[128,2048]{1,0:T(8,128)}) %reduce-scatter.2.cloned.1.call-update) | async-done | bytes 1048592 | tf_op jit(solution)/shard_map/reduce_scatter | solution.py:47
  156.6 1.3 broadcast_multiply_fusion
  157.9 4.6 %fusion.74 = (bf16[128,2048]{1,0:T(8,128)(2,1)S(1)}, f32[128,2048]{1,0:T(8,128)}, f32[128,2048]{1,0:T(8,128)}, f32[128,2048]{1,0:T(8,128)}, f32[128,2048]{1,0:T(8,128)}) fusion(f32[128,2048]{1,0:T(8,128)S(1)} %copy-done.1, f32[128,2048]{1,0:T(8,128)} %param.17, f32[128,2048]{1,0:T(8,128)S(1)} %broadcast_multiply_fusion, f32[128,2048]{1,0:T(8,128)} %param.18, ...), kind=kLoop, calls=%fused_computation.144 | loop fusion | flops 4980736 | bytes 9961472 | tf_op jit(solution)/shard_map/convert_element_type | solution.py:162
  162.5 1.5 collective-permute-start.4
  163.9 1.4 collective-permute-start.3
  165.7 11.8 %collective-permute-done.4 = bf16[128,2048]{1,0:T(8,128)(2,1)S(1)} collective-permute-done((bf16[128,2048]{1,0:T(8,128)(2,1)S(1)}, bf16[128,2048]{1,0:T(8,128)(2,1)S(1)}, u32[]{:S(2)}, u32[]{:S(2)}) %collective-permute-start.4) | collective-permute-done | bytes 524320 | tf_op jit(solution)/shard_map/ppermute | solution.py:102
  177.4 0.8 collective-permute-start.8
  178.6 0.8 collective-permute-start.7
  180.4 11.4 %collective-permute-done.8 = bf16[128,2048]{1,0:T(8,128)(2,1)S(1)} collective-permute-done((bf16[128,2048]{1,0:T(8,128)(2,1)S(1)}, bf16[128,2048]{1,0:T(8,128)(2,1)S(1)}, u32[]{:S(2)}, u32[]{:S(2)}) %collective-permute-start.8) | collective-permute-done | bytes 524320 | tf_op jit(solution)/shard_map/ppermute | solution.py:102
  191.8 0.8 collective-permute-start.12
  193.0 0.8 collective-permute-start.11
  195.1 12.2 %collective-permute-done.11 = bf16[128,2048]{1,0:T(8,128)(2,1)S(1)} collective-permute-done((bf16[128,2048]{1,0:T(8,128)(2,1)S(1)}, bf16[128,2048]{1,0:T(8,128)(2,1)S(1)}, u32[]{:S(2)}, u32[]{:S(2)}) %collective-permute-start.11) | collective-permute-done | bytes 524320 | tf_op jit(solution)/shard_map/ppermute | solution.py:98
  209.6 11.2 %collective-permute-done.15 = bf16[128,2048]{1,0:T(8,128)(2,1)S(1)} collective-permute-done((bf16[128,2048]{1,0:T(8,128)(2,1)S(1)}, bf16[128,2048]{1,0:T(8,128)(2,1)S(1)}, u32[]{:S(2)}, u32[]{:S(2)}) %collective-permute-start.15) | collective-permute-done | bytes 524320 | tf_op jit(solution)/shard_map/ppermute | solution.py:98
  221.8 1.0 collective-permute-done.16
  223.5 0.9 gather_fusion.2
  224.4 0.9 select_bitcast_fusion
  225.3 3.6 %all-to-all-start.1 = ((bf16[16,8,2048]{2,1,0:T(8,128)(2,1)}), bf16[16,8,2048]{2,1,0:T(8,128)(2,1)S(1)}, u32[]{:S(2)}, u32[]{:S(2)}) async-start(bf16[16,8,2048]{2,1,0:T(8,128)(2,1)} %select_bitcast_fusion), calls=%async_computation.2 | async-start | bytes 1048576 | tf_op jit(solution)/shard_map/all_to_all | solution.py:165
  229.6 13.7 %all-to-all-done.1 = bf16[16,8,2048]{2,1,0:T(8,128)(2,1)S(1)} async-done(((bf16[16,8,2048]{2,1,0:T(8,128)(2,1)}), bf16[16,8,2048]{2,1,0:T(8,128)(2,1)S(1)}, u32[]{:S(2)}, u32[]{:S(2)}) %all-to-all-start.1) | async-done | bytes 524320 | tf_op jit(solution)/shard_map/all_to_all | solution.py:165
  243.3 0.9 gather_fusion.3
  244.2 1.0 bitcast_dynamic-update-slice_fusion
  (90 shorter events, 10.6 us)
Async XLA Ops:
  7.2 51.2 %copy-start = (bf16[128,2048]{1,0:T(8,128)(2,1)S(1)}, bf16[128,2048]{1,0:T(8,128)(2,1)}, u32[]{:S(2)}) copy-start(bf16[128,2048]{1,0:T(8,128)(2,1)} %param.21) | copy-start | bytes 1572868
  7.2 7.9 %copy-start.2 = (bf16[256,2048]{1,0:T(8,128)(2,1)S(1)}, bf16[256,2048]{1,0:T(8,128)(2,1)}, u32[]{:S(2)}) copy-start(bf16[256,2048]{1,0:T(8,128)(2,1)} %param.15) | copy-start | bytes 3145732
  7.2 149.4 %reduce-scatter.2.cloned.1.call-start = ((), (), s32[]{:S(2)}) async-start(), calls=%async_computation.3 | async-start | bytes 9437184 | tf_op jit(solution)/shard_map/reduce_scatter | solution.py:47
  12.1 37.5 %collective-permute-start.1 = (bf16[256,2048]{1,0:T(8,128)(2,1)}, bf16[256,2048]{1,0:T(8,128)(2,1)}, u32[]{:S(2)}, u32[]{:S(2)}) collective-permute-start(bf16[256,2048]{1,0:T(8,128)(2,1)} %param.16), channel_id=1, source_target_pairs={{0,2},{2,0},{1,3},{3,1},{4,6},{6,4},{5,7},{7,5},{8,10},{10,8},{9,1... | collective-permute-start | bytes 3145736 | tf_op jit(solution)/shard_map/ppermute | solution.py:41
  16.9 32.7 %collective-permute-start = (bf16[256,1024]{1,0:T(8,128)(2,1)S(1)}, bf16[256,1024]{1,0:T(8,128)(2,1)S(1)}, u32[]{:S(2)}, u32[]{:S(2)}) collective-permute-start(bf16[256,1024]{1,0:T(8,128)(2,1)S(1)} %reshape.196), channel_id=1, source_target_pairs={{0,2},{2,0},{1,3},{3,1},{4,6},{6,4},{5,7},{7,5},{8,10},{10,8},{9,1... | collective-permute-start | bytes 1572872 | tf_op jit(solution)/shard_map/ppermute | solution.py:41
  56.8 0.7 copy-start.3
  56.9 9.6 %copy-start.4 = (s32[2048]{0:T(1024)S(1)}, s32[2048]{0:T(1024)}, u32[]{:S(2)}) copy-start(s32[2048]{0:T(1024)} %param.23) | copy-start | bytes 24580
  60.2 29.2 %all-to-all-start = ((bf16[16,8,2048]{2,1,0:T(8,128)(2,1)}), bf16[16,8,2048]{2,1,0:T(8,128)(2,1)S(1)}, u32[]{:S(2)}, u32[]{:S(2)}) async-start(bf16[16,8,2048]{2,1,0:T(8,128)(2,1)} %select_bitcast_fusion.1), calls=%async_computation.1 | async-start | bytes 1048576 | tf_op jit(solution)/shard_map/all_to_all | solution.py:151
  67.2 90.6 %copy-start.1 = (f32[128,2048]{1,0:T(8,128)S(1)}, f32[128,2048]{1,0:T(8,128)}, u32[]{:S(2)}) copy-start(f32[128,2048]{1,0:T(8,128)} %param.20) | copy-start | bytes 3145732
  162.5 17.0 %collective-permute-start.2 = (bf16[128,2048]{1,0:T(8,128)(2,1)S(1)}, bf16[128,2048]{1,0:T(8,128)(2,1)S(1)}, u32[]{:S(2)}, u32[]{:S(2)}) collective-permute-start(bf16[128,2048]{1,0:T(8,128)(2,1)S(1)} %get-tuple-element.14), channel_id=1, source_target_pairs={{0,1},{1,0},{2,3},{3,2},{4,5},{5,4},{6,7},{7,6},{8,9},{9,8},{10,11... | collective-permute-start | bytes 1572872 | tf_op jit(solution)/shard_map/ppermute | solution.py:94
  162.5 15.0 %collective-permute-start.4 = (bf16[128,2048]{1,0:T(8,128)(2,1)S(1)}, bf16[128,2048]{1,0:T(8,128)(2,1)S(1)}, u32[]{:S(2)}, u32[]{:S(2)}) collective-permute-start(bf16[128,2048]{1,0:T(8,128)(2,1)S(1)} %get-tuple-element.14), channel_id=1, source_target_pairs={{0,2},{1,3},{4,0},{5,1},{8,4},{9,5},{12,8},{13,9},{14,12},{15,13},... | collective-permute-start | bytes 1572872 | tf_op jit(solution)/shard_map/ppermute | solution.py:102
  163.9 14.7 %collective-permute-start.3 = (bf16[128,2048]{1,0:T(8,128)(2,1)S(1)}, bf16[128,2048]{1,0:T(8,128)(2,1)S(1)}, u32[]{:S(2)}, u32[]{:S(2)}) collective-permute-start(bf16[128,2048]{1,0:T(8,128)(2,1)S(1)} %get-tuple-element.14), channel_id=1, source_target_pairs={{0,4},{1,5},{4,8},{5,9},{8,12},{9,13},{12,14},{13,15},{14,10},{15,... | collective-permute-start | bytes 1572872 | tf_op jit(solution)/shard_map/ppermute | solution.py:98
  177.4 17.0 %collective-permute-start.6 = (bf16[128,2048]{1,0:T(8,128)(2,1)S(1)}, bf16[128,2048]{1,0:T(8,128)(2,1)S(1)}, u32[]{:S(2)}, u32[]{:S(2)}) collective-permute-start(bf16[128,2048]{1,0:T(8,128)(2,1)S(1)} %collective-permute-done.4), channel_id=1, source_target_pairs={{0,1},{1,0},{2,3},{3,2},{4,5},{5,4},{6,7},{7,6},{8,9},{9,8},{10,11... | collective-permute-start | bytes 1572872 | tf_op jit(solution)/shard_map/ppermute | solution.py:94
  177.4 14.3 %collective-permute-start.8 = (bf16[128,2048]{1,0:T(8,128)(2,1)S(1)}, bf16[128,2048]{1,0:T(8,128)(2,1)S(1)}, u32[]{:S(2)}, u32[]{:S(2)}) collective-permute-start(bf16[128,2048]{1,0:T(8,128)(2,1)S(1)} %collective-permute-done.4), channel_id=1, source_target_pairs={{0,2},{1,3},{4,0},{5,1},{8,4},{9,5},{12,8},{13,9},{14,12},{15,13},... | collective-permute-start | bytes 1572872 | tf_op jit(solution)/shard_map/ppermute | solution.py:102
  178.6 14.3 %collective-permute-start.7 = (bf16[128,2048]{1,0:T(8,128)(2,1)S(1)}, bf16[128,2048]{1,0:T(8,128)(2,1)S(1)}, u32[]{:S(2)}, u32[]{:S(2)}) collective-permute-start(bf16[128,2048]{1,0:T(8,128)(2,1)S(1)} %collective-permute-done.3), channel_id=1, source_target_pairs={{0,4},{1,5},{4,8},{5,9},{8,12},{9,13},{12,14},{13,15},{14,10},{15,... | collective-permute-start | bytes 1572872 | tf_op jit(solution)/shard_map/ppermute | solution.py:98
  179.5 15.3 %collective-permute-start.5 = (bf16[128,2048]{1,0:T(8,128)(2,1)S(1)}, bf16[128,2048]{1,0:T(8,128)(2,1)S(1)}, u32[]{:S(2)}, u32[]{:S(2)}) collective-permute-start(bf16[128,2048]{1,0:T(8,128)(2,1)S(1)} %collective-permute-done.3), channel_id=1, source_target_pairs={{0,1},{1,0},{2,3},{3,2},{4,5},{5,4},{6,7},{7,6},{8,9},{9,8},{10,11... | collective-permute-start | bytes 1572872 | tf_op jit(solution)/shard_map/ppermute | solution.py:94
  191.8 17.2 %collective-permute-start.10 = (bf16[128,2048]{1,0:T(8,128)(2,1)S(1)}, bf16[128,2048]{1,0:T(8,128)(2,1)S(1)}, u32[]{:S(2)}, u32[]{:S(2)}) collective-permute-start(bf16[128,2048]{1,0:T(8,128)(2,1)S(1)} %collective-permute-done.8), channel_id=1, source_target_pairs={{0,1},{1,0},{2,3},{3,2},{4,5},{5,4},{6,7},{7,6},{8,9},{9,8},{10,11... | collective-permute-start | bytes 1572872 | tf_op jit(solution)/shard_map/ppermute | solution.py:94
  191.8 16.1 %collective-permute-start.12 = (bf16[128,2048]{1,0:T(8,128)(2,1)S(1)}, bf16[128,2048]{1,0:T(8,128)(2,1)S(1)}, u32[]{:S(2)}, u32[]{:S(2)}) collective-permute-start(bf16[128,2048]{1,0:T(8,128)(2,1)S(1)} %collective-permute-done.8), channel_id=1, source_target_pairs={{0,2},{1,3},{4,0},{5,1},{8,4},{9,5},{12,8},{13,9},{14,12},{15,13},... | collective-permute-start | bytes 1572872 | tf_op jit(solution)/shard_map/ppermute | solution.py:102
  193.0 14.3 %collective-permute-start.11 = (bf16[128,2048]{1,0:T(8,128)(2,1)S(1)}, bf16[128,2048]{1,0:T(8,128)(2,1)S(1)}, u32[]{:S(2)}, u32[]{:S(2)}) collective-permute-start(bf16[128,2048]{1,0:T(8,128)(2,1)S(1)} %collective-permute-done.7), channel_id=1, source_target_pairs={{0,4},{1,5},{4,8},{5,9},{8,12},{9,13},{12,14},{13,15},{14,10},{15,... | collective-permute-start | bytes 1572872 | tf_op jit(solution)/shard_map/ppermute | solution.py:98
  194.4 14.9 %collective-permute-start.9 = (bf16[128,2048]{1,0:T(8,128)(2,1)S(1)}, bf16[128,2048]{1,0:T(8,128)(2,1)S(1)}, u32[]{:S(2)}, u32[]{:S(2)}) collective-permute-start(bf16[128,2048]{1,0:T(8,128)(2,1)S(1)} %collective-permute-done.7), channel_id=1, source_target_pairs={{0,1},{1,0},{2,3},{3,2},{4,5},{5,4},{6,7},{7,6},{8,9},{9,8},{10,11... | collective-permute-start | bytes 1572872 | tf_op jit(solution)/shard_map/ppermute | solution.py:94
  207.3 13.6 %collective-permute-start.15 = (bf16[128,2048]{1,0:T(8,128)(2,1)S(1)}, bf16[128,2048]{1,0:T(8,128)(2,1)S(1)}, u32[]{:S(2)}, u32[]{:S(2)}) collective-permute-start(bf16[128,2048]{1,0:T(8,128)(2,1)S(1)} %collective-permute-done.11), channel_id=1, source_target_pairs={{0,4},{1,5},{4,8},{5,9},{8,12},{9,13},{12,14},{13,15},{14,10},{15,... | collective-permute-start | bytes 1572872 | tf_op jit(solution)/shard_map/ppermute | solution.py:98
  207.9 13.6 %collective-permute-start.13 = (bf16[128,2048]{1,0:T(8,128)(2,1)S(1)}, bf16[128,2048]{1,0:T(8,128)(2,1)S(1)}, u32[]{:S(2)}, u32[]{:S(2)}) collective-permute-start(bf16[128,2048]{1,0:T(8,128)(2,1)S(1)} %collective-permute-done.11), channel_id=1, source_target_pairs={{0,1},{1,0},{2,3},{3,2},{4,5},{5,4},{6,7},{7,6},{8,9},{9,8},{10,11... | collective-permute-start | bytes 1572872 | tf_op jit(solution)/shard_map/ppermute | solution.py:94
  207.9 13.3 %collective-permute-start.14 = (bf16[128,2048]{1,0:T(8,128)(2,1)S(1)}, bf16[128,2048]{1,0:T(8,128)(2,1)S(1)}, u32[]{:S(2)}, u32[]{:S(2)}) collective-permute-start(bf16[128,2048]{1,0:T(8,128)(2,1)S(1)} %collective-permute-done.12), channel_id=1, source_target_pairs={{0,1},{1,0},{2,3},{3,2},{4,5},{5,4},{6,7},{7,6},{8,9},{9,8},{10,11... | collective-permute-start | bytes 1572872 | tf_op jit(solution)/shard_map/ppermute | solution.py:94
  220.9 1.9 collective-permute-start.16
  221.5 1.8 copy-start.5
  221.5 1.8 copy-start.6
  225.3 18.0 %all-to-all-start.1 = ((bf16[16,8,2048]{2,1,0:T(8,128)(2,1)}), bf16[16,8,2048]{2,1,0:T(8,128)(2,1)S(1)}, u32[]{:S(2)}, u32[]{:S(2)}) async-start(bf16[16,8,2048]{2,1,0:T(8,128)(2,1)} %select_bitcast_fusion), calls=%async_computation.2 | async-start | bytes 1048576 | tf_op jit(solution)/shard_map/all_to_all | solution.py:165
Sparse Core Ops, SparseCore 0:
  57.0 99.5 reduce-scatter.1

commit v4 on v3

--- a/solution.py
+++ b/solution.py
@@ -38,13 +38,20 @@
     mine = mine.reshape(tokens, width // 2)
     theirs = theirs.reshape(tokens, width // 2)
     swap = [(0, 1), (1, 0)]
-    got_queries, got_grad = lax.ppermute((theirs, grad_out), "xl", swap)
+    half = grad_out.shape[1] // 2
+    got_queries, got_first = lax.ppermute((theirs, grad_out[:, :half]), "xl", swap)
+    got_second = lax.ppermute(grad_out[:, half:], "xl", swap)
     both_queries = jnp.concatenate([mine, got_queries], axis=0)
-    both_grad = jnp.concatenate([grad_out, got_grad], axis=0)
-    partial = lax.dot_general(
-        both_queries, both_grad, (((0,), (0,)), ((), ())), preferred_element_type=jnp.float32
-    )
-    return lax.psum_scatter(partial, ("zo", "c"), scatter_dimension=0, tiled=True)
+    parts = []
+    for own, got in ((grad_out[:, :half], got_first), (grad_out[:, half:], got_second)):
+        partial = lax.dot_general(
+            both_queries,
+            jnp.concatenate([own, got], axis=0),
+            (((0,), (0,)), ((), ())),
+            preferred_element_type=jnp.float32,
+        )
+        parts.append(lax.psum_scatter(partial, ("zo", "c"), scatter_dimension=0, tiled=True))
+    return jnp.concatenate(parts, axis=1)
 
 
 def ring_codes(weight, rows):

time: 253 us -> 252 us (level)
  waiting for transfers between devices: 181 us -> 177 us
  local copies, waits for them, and re-layouts: 11.7 us -> 14.3 us
    reduce_scatter x1 -> x2, waiting for transfers between devices: 66.1 us -> 63.7 us  [pair_gradient(): lax.psum_scatter(partial, ('zo', 'c'), scatter_dimension=0, tiled=True)]
    ppermute x2 -> x3, waiting for transfers between devices: 32.3 us -> 31.1 us  [the longest x2 19.7 us: pair_gradient(): lax.ppermute((theirs, grad_out[:, :half]), 'xl', swap)]
    unnamed x15 -> x20, local copies, waits for them, and re-layouts: 5.58 us -> 4.99 us
    dot_general x1 -> x2, matrix products: 7.16 us -> 7.71 us  [pair_gradient(): lax.dot_general(both_queries, jnp.concatenate([own, got], axis=0), (((0,)...]
  transfers between devices with their start and end apart: 20 -> 22, of which waited for: 11 -> 12; matrix products, arithmetic and copies ran while one was open for 5% -> 7% of each run, Pallas kernels for 0% -> 0%
where the time goes in v4:
time: 252 us
  waiting for transfers between devices  177 us (70%)
  starting transfers between devices  21.5 us (9%)
  between operations  15.6 us (6%)
  local copies, waits for them, and re-layouts  14.3 us (6%)
  matrix products  12.4 us (5%)
  other arithmetic  11.2 us (4%)
    reduce_scatter x2, waiting for transfers between devices, pair_gradient(): lax.psum_scatter(partial, ('zo', 'c'), scatter_dimension=0, tiled=True)  63.7 us
    ppermute x3, waiting for transfers between devices, ring_codes(): behind = lax.ppermute(behind, DP, backward)  23.4 us
    ppermute x4, waiting for transfers between devices, ring_codes(): ahead = lax.ppermute(ahead, DP, forward)  23.2 us
    all_to_all x1, waiting for transfers between devices, per_device(): lax.all_to_all(jnp.take(keys, send_forward, axis=0), DP, split_axis=0, co...  20.9 us
    ppermute x2, waiting for transfers between devices, pair_gradient(): lax.ppermute((theirs, grad_out[:, :half]), 'xl', swap)  19.7 us
    all_to_all x1, waiting for transfers between devices, per_device(): lax.all_to_all(jnp.take(normed, send_back, axis=0), DP, split_axis=0, con...  13.7 us
    ppermute x1, waiting for transfers between devices, pair_gradient(): got_second = lax.ppermute(grad_out[:, half:], 'xl', swap)  11.4 us
    dot_general x2, matrix products, pair_gradient(): lax.dot_general(both_queries, jnp.concatenate([own, got], axis=0), (((0,)...  7.71 us
  transfers between devices with their start and end apart: 22, of which 12 were waited for; matrix products, arithmetic and copies ran while one was open for 7% of the time, Pallas kernels for 0%

profile of v4, /device:TPU:0, one launch (start us, length us, event | category | flops | bytes accessed | tf_op | source)
XLA Modules:
  0.0 252.0 jit_solution(8856600784633385790)
XLA Ops:
  7.2 4.9 %copy.22 = bf16[8,128,2048]{2,1,0:T(8,128)(2,1)} copy(bf16[8,128,2048]{2,1,0:T(8,128)(2,1)} %param.26) | data formatting | bytes 8388608
  14.0 3.0 %collective-permute-start = (bf16[256,1024]{1,0:T(8,128)(2,1)S(1)}, bf16[256,1024]{1,0:T(8,128)(2,1)}, u32[]{:S(2)}, u32[]{:S(2)}) collective-permute-start(bf16[256,1024]{1,0:T(8,128)(2,1)S(1)} %reshape.196), channel_id=1, source_target_pairs={{0,2},{2,0},{1,3},{3,1},{4,6},{6,4},{5,7},{7,5},{8,10},{10,8},{9,1... | collective-permute-start | bytes 1572872 | tf_op jit(solution)/shard_map/ppermute | solution.py:42
  17.0 2.1 fusion.82
  19.5 10.4 %collective-permute-done = bf16[256,1024]{1,0:T(8,128)(2,1)} collective-permute-done((bf16[256,1024]{1,0:T(8,128)(2,1)S(1)}, bf16[256,1024]{1,0:T(8,128)(2,1)}, u32[]{:S(2)}, u32[]{:S(2)}) %collective-permute-start) | collective-permute-done | bytes 524320 | tf_op jit(solution)/shard_map/ppermute | solution.py:42
  29.9 1.1 constant_dynamic-update-slice_fusion
  30.9 9.3 %collective-permute-done.1 = bf16[256,1024]{1,0:T(8,128)(2,1)} collective-permute-done((bf16[256,1024]{1,0:T(8,128)(2,1)}, bf16[256,1024]{1,0:T(8,128)(2,1)}, u32[]{:S(2)}, u32[]{:S(2)}) %collective-permute-start.1) | collective-permute-done | bytes 524320 | tf_op jit(solution)/shard_map/ppermute | solution.py:42
  40.3 4.4 %fusion.12 = f32[1024,1024]{1,0:T(8,128)} fusion(bf16[512,1024]{1,0:T(8,128)(2,1)S(1)} %constant_dynamic-update-slice_fusion, bf16[256,1024]{1,0:T(8,128)(2,1)} %collective-permute-done.1, bf16[256,1024]{1,0:T(8,128)(2,1)} %get-tuple-element.25), kind=kOutput, calls=%fused_computation.23 | convolution fusion | flops 1075838976 | bytes 6291456 | tf_op jit(solution)/shard_map/dot_general | solution.py:47
  44.8 1.8 collective-permute-start.2
  46.6 11.4 %collective-permute-done.2 = bf16[256,1024]{1,0:T(8,128)(2,1)S(1)} collective-permute-done((bf16[256,1024]{1,0:T(8,128)(2,1)S(1)}, bf16[256,1024]{1,0:T(8,128)(2,1)S(1)}, u32[]{:S(2)}, u32[]{:S(2)}) %collective-permute-start.2) | collective-permute-done | bytes 524320 | tf_op jit(solution)/shard_map/ppermute | solution.py:43
  58.0 3.3 %fusion.16 = f32[1024,1024]{1,0:T(8,128)} fusion(bf16[512,1024]{1,0:T(8,128)(2,1)S(1)} %constant_dynamic-update-slice_fusion, bf16[256,1024]{1,0:T(8,128)(2,1)S(1)} %collective-permute-done.2, bf16[256,1024]{1,0:T(8,128)(2,1)S(1)} %get-tuple-element.26), kind=kOutput, calls=%fused_computation.27 | convolution fusion | flops 1075838976 | bytes 6291456 | tf_op jit(solution)/shard_map/dot_general | solution.py:47
  62.2 0.9 gather_fusion
  64.0 5.8 %all-to-all-start = ((bf16[16,8,2048]{2,1,0:T(8,128)(2,1)}), bf16[16,8,2048]{2,1,0:T(8,128)(2,1)S(1)}, u32[]{:S(2)}, u32[]{:S(2)}) async-start(bf16[16,8,2048]{2,1,0:T(8,128)(2,1)} %select_bitcast_fusion.1), calls=%async_computation.2 | async-start | bytes 1048576 | tf_op jit(solution)/shard_map/all_to_all | solution.py:158
  72.1 20.9 %all-to-all-done = bf16[16,8,2048]{2,1,0:T(8,128)(2,1)S(1)} async-done(((bf16[16,8,2048]{2,1,0:T(8,128)(2,1)}), bf16[16,8,2048]{2,1,0:T(8,128)(2,1)S(1)}, u32[]{:S(2)}, u32[]{:S(2)}) %all-to-all-start) | async-done | bytes 524320 | tf_op jit(solution)/shard_map/all_to_all | solution.py:158
  93.0 0.9 gather_fusion.1
  94.0 10.8 %reduce-scatter.3.cloned.1.call-done = f32[128,1024]{1,0:T(8,128)} async-done(((f32[1024,1024]{1,0:T(8,128)}), f32[128,1024]{1,0:T(8,128)}) %reduce-scatter.3.cloned.1.call-update) | async-done | bytes 524304 | tf_op jit(solution)/shard_map/reduce_scatter | solution.py:53
  104.8 53.0 %reduce-scatter.5.cloned.1.call-done = f32[128,1024]{1,0:T(8,128)} async-done(((f32[1024,1024]{1,0:T(8,128)}), f32[128,1024]{1,0:T(8,128)}) %reduce-scatter.5.cloned.1.call-update) | async-done | bytes 524304 | tf_op jit(solution)/shard_map/reduce_scatter | solution.py:53
  157.8 1.3 maximum_multiply_fusion
  159.1 4.3 %fusion.76 = (bf16[128,2048]{1,0:T(8,128)(2,1)S(1)}, f32[128,2048]{1,0:T(8,128)}, f32[128,2048]{1,0:T(8,128)}, f32[128,2048]{1,0:T(8,128)}, f32[128,2048]{1,0:T(8,128)}) fusion(f32[128,2048]{1,0:T(8,128)S(1)} %copy-done.2, f32[128,2048]{1,0:T(8,128)S(1)} %copy-done.3, f32[128,2048]{1,0:T(8,128)S(1)} %maximum_multiply_fusion, f32[128,2048]{1,0:T(8,128)} %param.18, ...), kind=kLoop, calls=%fused_computation.148 | loop fusion | flops 4980736 | bytes 9961472 | tf_op jit(solution)/shard_map/convert_element_type | solution.py:169
  163.3 1.5 collective-permute-start.5
  165.7 12.0 %collective-permute-done.5 = bf16[128,2048]{1,0:T(8,128)(2,1)S(1)} collective-permute-done((bf16[128,2048]{1,0:T(8,128)(2,1)S(1)}, bf16[128,2048]{1,0:T(8,128)(2,1)S(1)}, u32[]{:S(2)}, u32[]{:S(2)}) %collective-permute-start.5) | collective-permute-done | bytes 524320 | tf_op jit(solution)/shard_map/ppermute | solution.py:109
  177.7 1.5 collective-permute-start.9
  180.6 11.4 %collective-permute-done.9 = bf16[128,2048]{1,0:T(8,128)(2,1)S(1)} collective-permute-done((bf16[128,2048]{1,0:T(8,128)(2,1)S(1)}, bf16[128,2048]{1,0:T(8,128)(2,1)S(1)}, u32[]{:S(2)}, u32[]{:S(2)}) %collective-permute-start.9) | collective-permute-done | bytes 524320 | tf_op jit(solution)/shard_map/ppermute | solution.py:109
  192.0 1.5 collective-permute-start.13
  195.4 12.2 %collective-permute-done.12 = bf16[128,2048]{1,0:T(8,128)(2,1)S(1)} collective-permute-done((bf16[128,2048]{1,0:T(8,128)(2,1)S(1)}, bf16[128,2048]{1,0:T(8,128)(2,1)S(1)}, u32[]{:S(2)}, u32[]{:S(2)}) %collective-permute-start.12) | collective-permute-done | bytes 524320 | tf_op jit(solution)/shard_map/ppermute | solution.py:105
  209.9 11.0 %collective-permute-done.16 = bf16[128,2048]{1,0:T(8,128)(2,1)S(1)} collective-permute-done((bf16[128,2048]{1,0:T(8,128)(2,1)S(1)}, bf16[128,2048]{1,0:T(8,128)(2,1)S(1)}, u32[]{:S(2)}, u32[]{:S(2)}) %collective-permute-start.16) | collective-permute-done | bytes 524320 | tf_op jit(solution)/shard_map/ppermute | solution.py:105
  221.7 1.0 collective-permute-done.17
  223.4 0.9 gather_fusion.2
  224.4 0.9 select_bitcast_fusion
  225.3 3.6 %all-to-all-start.1 = ((bf16[16,8,2048]{2,1,0:T(8,128)(2,1)}), bf16[16,8,2048]{2,1,0:T(8,128)(2,1)S(1)}, u32[]{:S(2)}, u32[]{:S(2)}) async-start(bf16[16,8,2048]{2,1,0:T(8,128)(2,1)} %select_bitcast_fusion), calls=%async_computation.3 | async-start | bytes 1048576 | tf_op jit(solution)/shard_map/all_to_all | solution.py:172
  229.5 13.7 %all-to-all-done.1 = bf16[16,8,2048]{2,1,0:T(8,128)(2,1)S(1)} async-done(((bf16[16,8,2048]{2,1,0:T(8,128)(2,1)}), bf16[16,8,2048]{2,1,0:T(8,128)(2,1)S(1)}, u32[]{:S(2)}, u32[]{:S(2)}) %all-to-all-start.1) | async-done | bytes 524320 | tf_op jit(solution)/shard_map/all_to_all | solution.py:172
  243.3 0.9 gather_fusion.3
  244.2 1.0 bitcast_dynamic-update-slice_fusion
  (103 shorter events, 13.9 us)
Async XLA Ops:
  7.2 55.0 %copy-start = (bf16[128,2048]{1,0:T(8,128)(2,1)S(1)}, bf16[128,2048]{1,0:T(8,128)(2,1)}, u32[]{:S(2)}) copy-start(bf16[128,2048]{1,0:T(8,128)(2,1)} %param.21) | copy-start | bytes 1572868
  7.2 5.0 %copy-start.4 = (bf16[256,2048]{1,0:T(8,128)(2,1)S(1)}, bf16[256,2048]{1,0:T(8,128)(2,1)}, u32[]{:S(2)}) copy-start(bf16[256,2048]{1,0:T(8,128)(2,1)} %param.15) | copy-start | bytes 3145732
  7.2 97.6 %reduce-scatter.3.cloned.1.call-start = ((), (), s32[]{:S(2)}) async-start(), calls=%async_computation.4 | async-start | bytes 4718592 | tf_op jit(solution)/shard_map/reduce_scatter | solution.py:53
  14.0 15.9 %collective-permute-start = (bf16[256,1024]{1,0:T(8,128)(2,1)S(1)}, bf16[256,1024]{1,0:T(8,128)(2,1)}, u32[]{:S(2)}, u32[]{:S(2)}) collective-permute-start(bf16[256,1024]{1,0:T(8,128)(2,1)S(1)} %reshape.196), channel_id=1, source_target_pairs={{0,2},{2,0},{1,3},{3,1},{4,6},{6,4},{5,7},{7,5},{8,10},{10,8},{9,1... | collective-permute-start | bytes 1572872 | tf_op jit(solution)/shard_map/ppermute | solution.py:42
  19.1 21.2 %collective-permute-start.1 = (bf16[256,1024]{1,0:T(8,128)(2,1)}, bf16[256,1024]{1,0:T(8,128)(2,1)}, u32[]{:S(2)}, u32[]{:S(2)}) collective-permute-start(bf16[256,1024]{1,0:T(8,128)(2,1)} %get-tuple-element.25), channel_id=1, source_target_pairs={{0,2},{2,0},{1,3},{3,1},{4,6},{6,4},{5,7},{7,5},{8,10},{10,8},{9,1... | collective-permute-start | bytes 1572872 | tf_op jit(solution)/shard_map/ppermute | solution.py:42
  44.7 113.0 %reduce-scatter.5.cloned.1.call-start = ((), (), s32[]{:S(2)}) async-start(), calls=%async_computation.5 | async-start | bytes 4718592 | tf_op jit(solution)/shard_map/reduce_scatter | solution.py:53
  44.8 16.5 %copy-start.5 = (s32[2048]{0:T(1024)S(1)}, s32[2048]{0:T(1024)}, u32[]{:S(2)}) copy-start(s32[2048]{0:T(1024)} %param.22) | copy-start | bytes 24580
  44.8 13.2 %collective-permute-start.2 = (bf16[256,1024]{1,0:T(8,128)(2,1)S(1)}, bf16[256,1024]{1,0:T(8,128)(2,1)S(1)}, u32[]{:S(2)}, u32[]{:S(2)}) collective-permute-start(bf16[256,1024]{1,0:T(8,128)(2,1)S(1)} %get-tuple-element.26), channel_id=1, source_target_pairs={{0,2},{2,0},{1,3},{3,1},{4,6},{6,4},{5,7},{7,5},{8,10},{10,8},{9,1... | collective-permute-start | bytes 1572872 | tf_op jit(solution)/shard_map/ppermute | solution.py:43
  61.3 8.6 %copy-start.6 = (s32[2048]{0:T(1024)S(1)}, s32[2048]{0:T(1024)}, u32[]{:S(2)}) copy-start(s32[2048]{0:T(1024)} %param.23) | copy-start | bytes 24580
  64.0 28.9 %all-to-all-start = ((bf16[16,8,2048]{2,1,0:T(8,128)(2,1)}), bf16[16,8,2048]{2,1,0:T(8,128)(2,1)S(1)}, u32[]{:S(2)}, u32[]{:S(2)}) async-start(bf16[16,8,2048]{2,1,0:T(8,128)(2,1)} %select_bitcast_fusion.1), calls=%async_computation.2 | async-start | bytes 1048576 | tf_op jit(solution)/shard_map/all_to_all | solution.py:158
  70.7 88.4 %copy-start.2 = (f32[128,2048]{1,0:T(8,128)S(1)}, f32[128,2048]{1,0:T(8,128)}, u32[]{:S(2)}) copy-start(f32[128,2048]{1,0:T(8,128)} %param.20) | copy-start | bytes 3145732
  70.7 88.4 %copy-start.3 = (f32[128,2048]{1,0:T(8,128)S(1)}, f32[128,2048]{1,0:T(8,128)}, u32[]{:S(2)}) copy-start(f32[128,2048]{1,0:T(8,128)} %param.17) | copy-start | bytes 3145732
  163.3 16.4 %collective-permute-start.3 = (bf16[128,2048]{1,0:T(8,128)(2,1)S(1)}, bf16[128,2048]{1,0:T(8,128)(2,1)S(1)}, u32[]{:S(2)}, u32[]{:S(2)}) collective-permute-start(bf16[128,2048]{1,0:T(8,128)(2,1)S(1)} %get-tuple-element.14), channel_id=1, source_target_pairs={{0,1},{1,0},{2,3},{3,2},{4,5},{5,4},{6,7},{7,6},{8,9},{9,8},{10,11... | collective-permute-start | bytes 1572872 | tf_op jit(solution)/shard_map/ppermute | solution.py:101
  163.3 14.3 %collective-permute-start.5 = (bf16[128,2048]{1,0:T(8,128)(2,1)S(1)}, bf16[128,2048]{1,0:T(8,128)(2,1)S(1)}, u32[]{:S(2)}, u32[]{:S(2)}) collective-permute-start(bf16[128,2048]{1,0:T(8,128)(2,1)S(1)} %get-tuple-element.14), channel_id=1, source_target_pairs={{0,2},{1,3},{4,0},{5,1},{8,4},{9,5},{12,8},{13,9},{14,12},{15,13},... | collective-permute-start | bytes 1572872 | tf_op jit(solution)/shard_map/ppermute | solution.py:109
  164.8 14.3 %collective-permute-start.4 = (bf16[128,2048]{1,0:T(8,128)(2,1)S(1)}, bf16[128,2048]{1,0:T(8,128)(2,1)S(1)}, u32[]{:S(2)}, u32[]{:S(2)}) collective-permute-start(bf16[128,2048]{1,0:T(8,128)(2,1)S(1)} %get-tuple-element.14), channel_id=1, source_target_pairs={{0,4},{1,5},{4,8},{5,9},{8,12},{9,13},{12,14},{13,15},{14,10},{15,... | collective-permute-start | bytes 1572872 | tf_op jit(solution)/shard_map/ppermute | solution.py:105
  177.7 17.0 %collective-permute-start.7 = (bf16[128,2048]{1,0:T(8,128)(2,1)S(1)}, bf16[128,2048]{1,0:T(8,128)(2,1)S(1)}, u32[]{:S(2)}, u32[]{:S(2)}) collective-permute-start(bf16[128,2048]{1,0:T(8,128)(2,1)S(1)} %collective-permute-done.5), channel_id=1, source_target_pairs={{0,1},{1,0},{2,3},{3,2},{4,5},{5,4},{6,7},{7,6},{8,9},{9,8},{10,11... | collective-permute-start | bytes 1572872 | tf_op jit(solution)/shard_map/ppermute | solution.py:101
  177.7 14.3 %collective-permute-start.9 = (bf16[128,2048]{1,0:T(8,128)(2,1)S(1)}, bf16[128,2048]{1,0:T(8,128)(2,1)S(1)}, u32[]{:S(2)}, u32[]{:S(2)}) collective-permute-start(bf16[128,2048]{1,0:T(8,128)(2,1)S(1)} %collective-permute-done.5), channel_id=1, source_target_pairs={{0,2},{1,3},{4,0},{5,1},{8,4},{9,5},{12,8},{13,9},{14,12},{15,13},... | collective-permute-start | bytes 1572872 | tf_op jit(solution)/shard_map/ppermute | solution.py:109
  179.2 14.3 %collective-permute-start.8 = (bf16[128,2048]{1,0:T(8,128)(2,1)S(1)}, bf16[128,2048]{1,0:T(8,128)(2,1)S(1)}, u32[]{:S(2)}, u32[]{:S(2)}) collective-permute-start(bf16[128,2048]{1,0:T(8,128)(2,1)S(1)} %collective-permute-done.4), channel_id=1, source_target_pairs={{0,4},{1,5},{4,8},{5,9},{8,12},{9,13},{12,14},{13,15},{14,10},{15,... | collective-permute-start | bytes 1572872 | tf_op jit(solution)/shard_map/ppermute | solution.py:105
  179.7 15.3 %collective-permute-start.6 = (bf16[128,2048]{1,0:T(8,128)(2,1)S(1)}, bf16[128,2048]{1,0:T(8,128)(2,1)S(1)}, u32[]{:S(2)}, u32[]{:S(2)}) collective-permute-start(bf16[128,2048]{1,0:T(8,128)(2,1)S(1)} %collective-permute-done.4), channel_id=1, source_target_pairs={{0,1},{1,0},{2,3},{3,2},{4,5},{5,4},{6,7},{7,6},{8,9},{9,8},{10,11... | collective-permute-start | bytes 1572872 | tf_op jit(solution)/shard_map/ppermute | solution.py:101
  192.0 17.2 %collective-permute-start.11 = (bf16[128,2048]{1,0:T(8,128)(2,1)S(1)}, bf16[128,2048]{1,0:T(8,128)(2,1)S(1)}, u32[]{:S(2)}, u32[]{:S(2)}) collective-permute-start(bf16[128,2048]{1,0:T(8,128)(2,1)S(1)} %collective-permute-done.9), channel_id=1, source_target_pairs={{0,1},{1,0},{2,3},{3,2},{4,5},{5,4},{6,7},{7,6},{8,9},{9,8},{10,11... | collective-permute-start | bytes 1572872 | tf_op jit(solution)/shard_map/ppermute | solution.py:101
  192.0 16.1 %collective-permute-start.13 = (bf16[128,2048]{1,0:T(8,128)(2,1)S(1)}, bf16[128,2048]{1,0:T(8,128)(2,1)S(1)}, u32[]{:S(2)}, u32[]{:S(2)}) collective-permute-start(bf16[128,2048]{1,0:T(8,128)(2,1)S(1)} %collective-permute-done.9), channel_id=1, source_target_pairs={{0,2},{1,3},{4,0},{5,1},{8,4},{9,5},{12,8},{13,9},{14,12},{15,13},... | collective-permute-start | bytes 1572872 | tf_op jit(solution)/shard_map/ppermute | solution.py:109
  193.5 14.1 %collective-permute-start.12 = (bf16[128,2048]{1,0:T(8,128)(2,1)S(1)}, bf16[128,2048]{1,0:T(8,128)(2,1)S(1)}, u32[]{:S(2)}, u32[]{:S(2)}) collective-permute-start(bf16[128,2048]{1,0:T(8,128)(2,1)S(1)} %collective-permute-done.8), channel_id=1, source_target_pairs={{0,4},{1,5},{4,8},{5,9},{8,12},{9,13},{12,14},{13,15},{14,10},{15,... | collective-permute-start | bytes 1572872 | tf_op jit(solution)/shard_map/ppermute | solution.py:105
  194.6 14.9 %collective-permute-start.10 = (bf16[128,2048]{1,0:T(8,128)(2,1)S(1)}, bf16[128,2048]{1,0:T(8,128)(2,1)S(1)}, u32[]{:S(2)}, u32[]{:S(2)}) collective-permute-start(bf16[128,2048]{1,0:T(8,128)(2,1)S(1)} %collective-permute-done.8), channel_id=1, source_target_pairs={{0,1},{1,0},{2,3},{3,2},{4,5},{5,4},{6,7},{7,6},{8,9},{9,8},{10,11... | collective-permute-start | bytes 1572872 | tf_op jit(solution)/shard_map/ppermute | solution.py:101
  207.6 13.2 %collective-permute-start.16 = (bf16[128,2048]{1,0:T(8,128)(2,1)S(1)}, bf16[128,2048]{1,0:T(8,128)(2,1)S(1)}, u32[]{:S(2)}, u32[]{:S(2)}) collective-permute-start(bf16[128,2048]{1,0:T(8,128)(2,1)S(1)} %collective-permute-done.12), channel_id=1, source_target_pairs={{0,4},{1,5},{4,8},{5,9},{8,12},{9,13},{12,14},{13,15},{14,10},{15,... | collective-permute-start | bytes 1572872 | tf_op jit(solution)/shard_map/ppermute | solution.py:105
  208.1 13.3 %collective-permute-start.14 = (bf16[128,2048]{1,0:T(8,128)(2,1)S(1)}, bf16[128,2048]{1,0:T(8,128)(2,1)S(1)}, u32[]{:S(2)}, u32[]{:S(2)}) collective-permute-start(bf16[128,2048]{1,0:T(8,128)(2,1)S(1)} %collective-permute-done.12), channel_id=1, source_target_pairs={{0,1},{1,0},{2,3},{3,2},{4,5},{5,4},{6,7},{7,6},{8,9},{9,8},{10,11... | collective-permute-start | bytes 1572872 | tf_op jit(solution)/shard_map/ppermute | solution.py:101
  208.1 13.0 %collective-permute-start.15 = (bf16[128,2048]{1,0:T(8,128)(2,1)S(1)}, bf16[128,2048]{1,0:T(8,128)(2,1)S(1)}, u32[]{:S(2)}, u32[]{:S(2)}) collective-permute-start(bf16[128,2048]{1,0:T(8,128)(2,1)S(1)} %collective-permute-done.13), channel_id=1, source_target_pairs={{0,1},{1,0},{2,3},{3,2},{4,5},{5,4},{6,7},{7,6},{8,9},{9,8},{10,11... | collective-permute-start | bytes 1572872 | tf_op jit(solution)/shard_map/ppermute | solution.py:101
  220.8 1.9 collective-permute-start.17
  221.4 1.8 copy-start.7
  221.4 1.8 copy-start.8
  223.4 21.8 %copy-start.1 = (bf16[128,2048]{1,0:T(8,128)(2,1)S(1)}, bf16[128,2048]{1,0:T(8,128)(2,1)}, u32[]{:S(2)}) copy-start(bf16[128,2048]{1,0:T(8,128)(2,1)} %param.21) | copy-start | bytes 1572868
  225.3 18.0 %all-to-all-start.1 = ((bf16[16,8,2048]{2,1,0:T(8,128)(2,1)}), bf16[16,8,2048]{2,1,0:T(8,128)(2,1)S(1)}, u32[]{:S(2)}, u32[]{:S(2)}) async-start(bf16[16,8,2048]{2,1,0:T(8,128)(2,1)} %select_bitcast_fusion), calls=%async_computation.3 | async-start | bytes 1048576 | tf_op jit(solution)/shard_map/all_to_all | solution.py:172
Sparse Core Ops, SparseCore 0:
  44.9 59.9 reduce-scatter.2
  107.1 50.6 reduce-scatter.4

commit v5 on v3

--- a/solution.py
+++ b/solution.py
@@ -117,15 +117,6 @@
     return (new_params, new_first, new_second, new_key)
 
 
-def batch_norm(codes, bn_gain, bn_shift):
-    values = codes.astype(jnp.float32)
-    center = jnp.mean(values, axis=0)
-    spread = jnp.mean(jnp.square(values - center), axis=0)
-    return jax.nn.relu(
-        (values - center) * lax.rsqrt(spread + norm_epsilon) * bn_gain + bn_shift
-    ).astype(jnp.bfloat16)
-
-
 def per_device(
     queries,
     grad_out,
@@ -147,25 +138,27 @@
     per_peer = block_rows // members
     scaling = 1.0 / jnp.sqrt(jnp.float32(queries.shape[0] * members))
     send_forward, receive_forward = route(perm, position, block_rows, per_peer)
-    send_back, receive_back = route(inv_perm, position, block_rows, per_peer)
     moved = lax.all_to_all(
         jnp.take(keys, send_forward, axis=0), DP, split_axis=0, concat_axis=0, tiled=True
     )
     encoded_rows = jnp.take(moved, receive_forward, axis=0)
     gradient = pair_gradient(queries, grad_out) * scaling
-    gradient, (encoded_rows, send_back, receive_back) = lax.optimization_barrier(
-        (gradient, (encoded_rows, send_back, receive_back))
-    )
+    gradient, encoded_rows = lax.optimization_barrier((gradient, encoded_rows))
     new_params, new_first, new_second, new_key = adamw(
         gradient, params, first_moment, second_moment, key_params
     )
-    codes = ring_codes(new_key.astype(jnp.bfloat16), encoded_rows)
-    codes = codes.astype(jnp.bfloat16)
-    normed = batch_norm(codes, bn_gain, bn_shift)
-    returned = lax.all_to_all(
-        jnp.take(normed, send_back, axis=0), DP, split_axis=0, concat_axis=0, tiled=True
-    )
-    restored = jnp.take(returned, receive_back, axis=0)
+    codes = ring_codes(
+        new_key.astype(jnp.bfloat16), jnp.concatenate([encoded_rows, keys], axis=0)
+    ).astype(jnp.bfloat16)
+    values = codes[:block_rows].astype(jnp.float32)
+    center = jnp.mean(values, axis=0)
+    scale = lax.rsqrt(jnp.mean(jnp.square(values - center), axis=0) + norm_epsilon)
+    stats = lax.all_gather(jnp.stack([center, scale])[None], DP, axis=0, tiled=True)
+    own = lax.dynamic_slice_in_dim(inv_perm, position * block_rows, block_rows)
+    stats = jnp.take(stats, own // block_rows, axis=0)
+    restored = jax.nn.relu(
+        (codes[block_rows:].astype(jnp.float32) - stats[:, 0]) * stats[:, 1] * bn_gain + bn_shift
+    ).astype(jnp.bfloat16)
     new_queue = lax.dynamic_update_slice(
         queue, restored[None], (slot[0], jnp.int32(0), jnp.int32(0))
     )

time: 253 us -> 253 us (level)
  blocking collectives: 0 us -> 19.5 us
  waiting for transfers between devices: 181 us -> 165 us
  starting transfers between devices: 20.2 us -> 16.8 us
    all_gather x0 -> x1, blocking collectives: none -> 19.5 us  [per_device(): lax.all_gather(jnp.stack([center, scale])[None], DP, axis=0, tiled=True)]
    all_to_all x1 -> x0, waiting for transfers between devices: 13.7 us -> none  [per_device(): lax.all_to_all(jnp.take(normed, send_back, axis=0), DP, split_axis=0, con...]
    all_to_all x1 -> x0, starting transfers between devices: 3.57 us -> none  [per_device(): lax.all_to_all(jnp.take(normed, send_back, axis=0), DP, split_axis=0, con...]
    unnamed x15 -> x19, local copies, waits for them, and re-layouts: 5.58 us -> 4.79 us
  transfers between devices with their start and end apart: 20 -> 19, of which waited for: 11 -> 10; matrix products, arithmetic and copies ran while one was open for 5% -> 6% of each run, Pallas kernels for 0% -> 0%
where the time goes in v5:
time: 253 us
  waiting for transfers between devices  165 us (65%)
  blocking collectives  19.5 us (8%)
  starting transfers between devices  16.8 us (7%)
  between operations  15.4 us (6%)
  matrix products  14 us (6%)
  local copies, waits for them, and re-layouts  11.8 us (5%)
  other arithmetic  10.8 us (4%)
    reduce_scatter x1, waiting for transfers between devices, pair_gradient(): lax.psum_scatter(partial, ('zo', 'c'), scatter_dimension=0, tiled=True)  66.1 us
    ppermute x2, waiting for transfers between devices, pair_gradient(): got_queries, got_grad = lax.ppermute((theirs, grad_out), 'xl', swap)  31.9 us
    ppermute x4, waiting for transfers between devices, ring_codes(): ahead = lax.ppermute(ahead, DP, forward)  22.8 us
    ppermute x3, waiting for transfers between devices, ring_codes(): behind = lax.ppermute(behind, DP, backward)  22.6 us
    all_to_all x1, waiting for transfers between devices, per_device(): lax.all_to_all(jnp.take(keys, send_forward, axis=0), DP, split_axis=0, co...  20.8 us
    all_gather x1, blocking collectives, per_device(): lax.all_gather(jnp.stack([center, scale])[None], DP, axis=0, tiled=True)  19.5 us
    dot_general x16, matrix products, add(): jnp.dot(columns(offset, cls), shard, preferred_element_type=jnp.float32)  7.21 us
    dot_general x1, matrix products, pair_gradient(): lax.dot_general(both_queries, both_grad, (((0,), (0,)), ((), ())), prefer...  6.84 us
  transfers between devices with their start and end apart: 19, of which 10 were waited for; matrix products, arithmetic and copies ran while one was open for 6% of the time, Pallas kernels for 0%

profile of v5, /device:TPU:0, one launch (start us, length us, event | category | flops | bytes accessed | tf_op | source)
XLA Modules:
  0.0 253.0 jit_solution(14860024307359664963)
XLA Ops:
  7.2 1.3 copy-done.8
  8.5 2.9 %collective-permute-start.1 = (bf16[256,2048]{1,0:T(8,128)(2,1)S(1)}, bf16[256,2048]{1,0:T(8,128)(2,1)}, u32[]{:S(2)}, u32[]{:S(2)}) collective-permute-start(bf16[256,2048]{1,0:T(8,128)(2,1)S(1)} %copy-done.8), channel_id=1, source_target_pairs={{0,2},{2,0},{1,3},{3,1},{4,6},{6,4},{5,7},{7,5},{8,10},{10,8},{9,1... | collective-permute-start | bytes 3145736 | tf_op jit(solution)/shard_map/ppermute | solution.py:41
  11.4 0.7 reshape.139
  12.2 0.7 constant_dynamic-slice_fusion.1
  13.9 31.9 %collective-permute-done = bf16[256,1024]{1,0:T(8,128)(2,1)S(1)} collective-permute-done((bf16[256,1024]{1,0:T(8,128)(2,1)S(1)}, bf16[256,1024]{1,0:T(8,128)(2,1)S(1)}, u32[]{:S(2)}, u32[]{:S(2)}) %collective-permute-start) | collective-permute-done | bytes 524320 | tf_op jit(solution)/shard_map/ppermute | solution.py:41
  45.8 6.8 %fusion.10 = f32[1024,2048]{1,0:T(8,128)} fusion(bf16[256,2048]{1,0:T(8,128)(2,1)} %collective-permute-done.1, bf16[256,2048]{1,0:T(8,128)(2,1)S(1)} %copy-done.8, bf16[256,1024]{1,0:T(8,128)(2,1)S(1)} %collective-permute-done, bf16[256,1024]{1,0:T(8,128)(2,1)S(1)} %reshape.140), kind=kOutput, calls=%fused_computation.19 | convolution fusion | flops 2153775104 | bytes 11534336 | tf_op jit(solution)/shard_map/dot_general | solution.py:44
  52.7 0.7 copy-done.5
  54.2 0.9 gather_fusion.1
  55.2 0.9 select_bitcast_fusion
  56.1 6.2 %all-to-all-start = ((bf16[16,8,2048]{2,1,0:T(8,128)(2,1)}), bf16[16,8,2048]{2,1,0:T(8,128)(2,1)S(1)}, u32[]{:S(2)}, u32[]{:S(2)}) async-start(bf16[16,8,2048]{2,1,0:T(8,128)(2,1)} %select_bitcast_fusion), calls=%async_computation.1 | async-start | bytes 1048576 | tf_op jit(solution)/shard_map/all_to_all | solution.py:141
  63.5 0.8 compare_and_fusion.2
  64.5 20.8 %all-to-all-done = bf16[16,8,2048]{2,1,0:T(8,128)(2,1)S(1)} async-done(((bf16[16,8,2048]{2,1,0:T(8,128)(2,1)}), bf16[16,8,2048]{2,1,0:T(8,128)(2,1)S(1)}, u32[]{:S(2)}, u32[]{:S(2)}) %all-to-all-start) | async-done | bytes 524320 | tf_op jit(solution)/shard_map/all_to_all | solution.py:141
  85.3 0.9 gather_fusion.2
  86.3 66.1 %reduce-scatter.2.cloned.1.call-done = f32[128,2048]{1,0:T(8,128)} async-done(((f32[1024,2048]{1,0:T(8,128)}), f32[128,2048]{1,0:T(8,128)}) %reduce-scatter.2.cloned.1.call-update) | async-done | bytes 1048592 | tf_op jit(solution)/shard_map/reduce_scatter | solution.py:47
  152.4 1.3 broadcast_multiply_fusion
  153.7 4.6 %fusion.77 = (bf16[128,2048]{1,0:T(8,128)(2,1)S(1)}, f32[128,2048]{1,0:T(8,128)}, f32[128,2048]{1,0:T(8,128)}, f32[128,2048]{1,0:T(8,128)}, f32[128,2048]{1,0:T(8,128)}) fusion(f32[128,2048]{1,0:T(8,128)S(1)} %copy-done.3, f32[128,2048]{1,0:T(8,128)} %param.17, f32[128,2048]{1,0:T(8,128)S(1)} %broadcast_multiply_fusion, f32[128,2048]{1,0:T(8,128)} %param.18, ...), kind=kLoop, calls=%fused_computation.134 | loop fusion | flops 4980736 | bytes 9961472 | tf_op jit(solution)/shard_map/convert_element_type | solution.py:151
  158.3 1.5 collective-permute-start.4
  159.8 1.4 collective-permute-start.3
  161.7 11.6 %collective-permute-done.4 = bf16[128,2048]{1,0:T(8,128)(2,1)S(1)} collective-permute-done((bf16[128,2048]{1,0:T(8,128)(2,1)S(1)}, bf16[128,2048]{1,0:T(8,128)(2,1)S(1)}, u32[]{:S(2)}, u32[]{:S(2)}) %collective-permute-start.4) | collective-permute-done | bytes 524320 | tf_op jit(solution)/shard_map/ppermute | solution.py:102
  173.3 0.8 collective-permute-start.8
  174.5 0.9 collective-permute-start.7
  176.6 11.0 %collective-permute-done.8 = bf16[128,2048]{1,0:T(8,128)(2,1)S(1)} collective-permute-done((bf16[128,2048]{1,0:T(8,128)(2,1)S(1)}, bf16[128,2048]{1,0:T(8,128)(2,1)S(1)}, u32[]{:S(2)}, u32[]{:S(2)}) %collective-permute-start.8) | collective-permute-done | bytes 524320 | tf_op jit(solution)/shard_map/ppermute | solution.py:102
  187.6 0.8 collective-permute-start.12
  188.8 0.8 collective-permute-start.11
  191.6 11.6 %collective-permute-done.11 = bf16[128,2048]{1,0:T(8,128)(2,1)S(1)} collective-permute-done((bf16[128,2048]{1,0:T(8,128)(2,1)S(1)}, bf16[128,2048]{1,0:T(8,128)(2,1)S(1)}, u32[]{:S(2)}, u32[]{:S(2)}) %collective-permute-start.11) | collective-permute-done | bytes 524320 | tf_op jit(solution)/shard_map/ppermute | solution.py:98
  205.5 0.7 fusion.4
  206.2 10.5 %collective-permute-done.15 = bf16[128,2048]{1,0:T(8,128)(2,1)S(1)} collective-permute-done((bf16[128,2048]{1,0:T(8,128)(2,1)S(1)}, bf16[128,2048]{1,0:T(8,128)(2,1)S(1)}, u32[]{:S(2)}, u32[]{:S(2)}) %collective-permute-start.15) | collective-permute-done | bytes 524320 | tf_op jit(solution)/shard_map/ppermute | solution.py:98
  219.4 19.5 %all-gather.1 = f32[16,2,2048]{2,1,0:T(2,128)S(1)} all-gather(f32[1,2,2048]{2,1,0:T(2,128)S(1)} %maximum_bitcast_fusion), channel_id=2, replica_groups=mesh['groups'=2,'zo'=4,'xl'=2,'c'=2] {'zo','xl','c'}, dimensions={0}, use_global_device_ids=true | all-gather | bytes 278528 | tf_op jit(solution)/shard_map/all_gather | solution.py:156
  238.9 2.8 %gather_fusion = f32[128,2,2048]{2,1,0:T(2,128)S(1)} fusion(f32[16,2,2048]{2,1,0:T(2,128)S(1)} %all-gather.1, s32[1024]{0:T(1024)S(1)} %pad_clamp_fusion), kind=kCustom, calls=%fused_computation.2 | custom fusion | bytes 4194816 | tf_op jit(solution)/shard_map/jit(_take)/gather | solution.py:158
  241.7 1.4 copy_select_fusion
  243.1 0.8 copy-done.2
  244.2 2.0 copy-done.1
  (79 shorter events, 12.2 us)
Async XLA Ops:
  7.2 4.3 %copy-start.4 = (bf16[256,2048]{1,0:T(8,128)(2,1)S(1)}, bf16[256,2048]{1,0:T(8,128)(2,1)}, u32[]{:S(2)}) copy-start(bf16[256,2048]{1,0:T(8,128)(2,1)} %param.15) | copy-start | bytes 3145732
  7.2 1.3 copy-start.8
  7.2 145.2 %reduce-scatter.2.cloned.1.call-start = ((), (), s32[]{:S(2)}) async-start(), calls=%async_computation.2 | async-start | bytes 9437184 | tf_op jit(solution)/shard_map/reduce_scatter | solution.py:47
  8.5 37.3 %collective-permute-start.1 = (bf16[256,2048]{1,0:T(8,128)(2,1)S(1)}, bf16[256,2048]{1,0:T(8,128)(2,1)}, u32[]{:S(2)}, u32[]{:S(2)}) collective-permute-start(bf16[256,2048]{1,0:T(8,128)(2,1)S(1)} %copy-done.8), channel_id=1, source_target_pairs={{0,2},{2,0},{1,3},{3,1},{4,6},{6,4},{5,7},{7,5},{8,10},{10,8},{9,1... | collective-permute-start | bytes 3145736 | tf_op jit(solution)/shard_map/ppermute | solution.py:41
  13.3 32.5 %collective-permute-start = (bf16[256,1024]{1,0:T(8,128)(2,1)S(1)}, bf16[256,1024]{1,0:T(8,128)(2,1)S(1)}, u32[]{:S(2)}, u32[]{:S(2)}) collective-permute-start(bf16[256,1024]{1,0:T(8,128)(2,1)S(1)} %reshape.141), channel_id=1, source_target_pairs={{0,2},{2,0},{1,3},{3,1},{4,6},{6,4},{5,7},{7,5},{8,10},{10,8},{9,1... | collective-permute-start | bytes 1572872 | tf_op jit(solution)/shard_map/ppermute | solution.py:41
  52.7 0.7 copy-start.5
  52.7 1.5 copy-start
  56.1 29.2 %all-to-all-start = ((bf16[16,8,2048]{2,1,0:T(8,128)(2,1)}), bf16[16,8,2048]{2,1,0:T(8,128)(2,1)S(1)}, u32[]{:S(2)}, u32[]{:S(2)}) async-start(bf16[16,8,2048]{2,1,0:T(8,128)(2,1)} %select_bitcast_fusion), calls=%async_computation.1 | async-start | bytes 1048576 | tf_op jit(solution)/shard_map/all_to_all | solution.py:141
  86.2 67.5 %copy-start.3 = (f32[128,2048]{1,0:T(8,128)S(1)}, f32[128,2048]{1,0:T(8,128)}, u32[]{:S(2)}) copy-start(f32[128,2048]{1,0:T(8,128)} %param.20) | copy-start | bytes 3145732
  158.3 17.0 %collective-permute-start.2 = (bf16[128,2048]{1,0:T(8,128)(2,1)S(1)}, bf16[128,2048]{1,0:T(8,128)(2,1)S(1)}, u32[]{:S(2)}, u32[]{:S(2)}) collective-permute-start(bf16[128,2048]{1,0:T(8,128)(2,1)S(1)} %get-tuple-element.12), channel_id=1, source_target_pairs={{0,1},{1,0},{2,3},{3,2},{4,5},{5,4},{6,7},{7,6},{8,9},{9,8},{10,11... | collective-permute-start | bytes 1572872 | tf_op jit(solution)/shard_map/ppermute | solution.py:94
  158.3 15.0 %collective-permute-start.4 = (bf16[128,2048]{1,0:T(8,128)(2,1)S(1)}, bf16[128,2048]{1,0:T(8,128)(2,1)S(1)}, u32[]{:S(2)}, u32[]{:S(2)}) collective-permute-start(bf16[128,2048]{1,0:T(8,128)(2,1)S(1)} %get-tuple-element.12), channel_id=1, source_target_pairs={{0,2},{1,3},{4,0},{5,1},{8,4},{9,5},{12,8},{13,9},{14,12},{15,13},... | collective-permute-start | bytes 1572872 | tf_op jit(solution)/shard_map/ppermute | solution.py:102
  159.8 14.7 %collective-permute-start.3 = (bf16[128,2048]{1,0:T(8,128)(2,1)S(1)}, bf16[128,2048]{1,0:T(8,128)(2,1)S(1)}, u32[]{:S(2)}, u32[]{:S(2)}) collective-permute-start(bf16[128,2048]{1,0:T(8,128)(2,1)S(1)} %get-tuple-element.12), channel_id=1, source_target_pairs={{0,4},{1,5},{4,8},{5,9},{8,12},{9,13},{12,14},{13,15},{14,10},{15,... | collective-permute-start | bytes 1572872 | tf_op jit(solution)/shard_map/ppermute | solution.py:98
  173.3 17.2 %collective-permute-start.6 = (bf16[128,2048]{1,0:T(8,128)(2,1)S(1)}, bf16[128,2048]{1,0:T(8,128)(2,1)S(1)}, u32[]{:S(2)}, u32[]{:S(2)}) collective-permute-start(bf16[128,2048]{1,0:T(8,128)(2,1)S(1)} %collective-permute-done.4), channel_id=1, source_target_pairs={{0,1},{1,0},{2,3},{3,2},{4,5},{5,4},{6,7},{7,6},{8,9},{9,8},{10,11... | collective-permute-start | bytes 1572872 | tf_op jit(solution)/shard_map/ppermute | solution.py:94
  173.3 14.3 %collective-permute-start.8 = (bf16[128,2048]{1,0:T(8,128)(2,1)S(1)}, bf16[128,2048]{1,0:T(8,128)(2,1)S(1)}, u32[]{:S(2)}, u32[]{:S(2)}) collective-permute-start(bf16[128,2048]{1,0:T(8,128)(2,1)S(1)} %collective-permute-done.4), channel_id=1, source_target_pairs={{0,2},{1,3},{4,0},{5,1},{8,4},{9,5},{12,8},{13,9},{14,12},{15,13},... | collective-permute-start | bytes 1572872 | tf_op jit(solution)/shard_map/ppermute | solution.py:102
  174.5 14.3 %collective-permute-start.7 = (bf16[128,2048]{1,0:T(8,128)(2,1)S(1)}, bf16[128,2048]{1,0:T(8,128)(2,1)S(1)}, u32[]{:S(2)}, u32[]{:S(2)}) collective-permute-start(bf16[128,2048]{1,0:T(8,128)(2,1)S(1)} %collective-permute-done.3), channel_id=1, source_target_pairs={{0,4},{1,5},{4,8},{5,9},{8,12},{9,13},{12,14},{13,15},{14,10},{15,... | collective-permute-start | bytes 1572872 | tf_op jit(solution)/shard_map/ppermute | solution.py:98
  175.3 15.7 %collective-permute-start.5 = (bf16[128,2048]{1,0:T(8,128)(2,1)S(1)}, bf16[128,2048]{1,0:T(8,128)(2,1)S(1)}, u32[]{:S(2)}, u32[]{:S(2)}) collective-permute-start(bf16[128,2048]{1,0:T(8,128)(2,1)S(1)} %collective-permute-done.3), channel_id=1, source_target_pairs={{0,1},{1,0},{2,3},{3,2},{4,5},{5,4},{6,7},{7,6},{8,9},{9,8},{10,11... | collective-permute-start | bytes 1572872 | tf_op jit(solution)/shard_map/ppermute | solution.py:94
  187.6 17.5 %collective-permute-start.10 = (bf16[128,2048]{1,0:T(8,128)(2,1)S(1)}, bf16[128,2048]{1,0:T(8,128)(2,1)S(1)}, u32[]{:S(2)}, u32[]{:S(2)}) collective-permute-start(bf16[128,2048]{1,0:T(8,128)(2,1)S(1)} %collective-permute-done.8), channel_id=1, source_target_pairs={{0,1},{1,0},{2,3},{3,2},{4,5},{5,4},{6,7},{7,6},{8,9},{9,8},{10,11... | collective-permute-start | bytes 1572872 | tf_op jit(solution)/shard_map/ppermute | solution.py:94
  187.6 16.1 %collective-permute-start.12 = (bf16[128,2048]{1,0:T(8,128)(2,1)S(1)}, bf16[128,2048]{1,0:T(8,128)(2,1)S(1)}, u32[]{:S(2)}, u32[]{:S(2)}) collective-permute-start(bf16[128,2048]{1,0:T(8,128)(2,1)S(1)} %collective-permute-done.8), channel_id=1, source_target_pairs={{0,2},{1,3},{4,0},{5,1},{8,4},{9,5},{12,8},{13,9},{14,12},{15,13},... | collective-permute-start | bytes 1572872 | tf_op jit(solution)/shard_map/ppermute | solution.py:102
  188.8 14.3 %collective-permute-start.11 = (bf16[128,2048]{1,0:T(8,128)(2,1)S(1)}, bf16[128,2048]{1,0:T(8,128)(2,1)S(1)}, u32[]{:S(2)}, u32[]{:S(2)}) collective-permute-start(bf16[128,2048]{1,0:T(8,128)(2,1)S(1)} %collective-permute-done.7), channel_id=1, source_target_pairs={{0,4},{1,5},{4,8},{5,9},{8,12},{9,13},{12,14},{13,15},{14,10},{15,... | collective-permute-start | bytes 1572872 | tf_op jit(solution)/shard_map/ppermute | solution.py:98
  190.5 15.0 %collective-permute-start.9 = (bf16[128,2048]{1,0:T(8,128)(2,1)S(1)}, bf16[128,2048]{1,0:T(8,128)(2,1)S(1)}, u32[]{:S(2)}, u32[]{:S(2)}) collective-permute-start(bf16[128,2048]{1,0:T(8,128)(2,1)S(1)} %collective-permute-done.7), channel_id=1, source_target_pairs={{0,1},{1,0},{2,3},{3,2},{4,5},{5,4},{6,7},{7,6},{8,9},{9,8},{10,11... | collective-permute-start | bytes 1572872 | tf_op jit(solution)/shard_map/ppermute | solution.py:94
  203.1 13.6 %collective-permute-start.15 = (bf16[128,2048]{1,0:T(8,128)(2,1)S(1)}, bf16[128,2048]{1,0:T(8,128)(2,1)S(1)}, u32[]{:S(2)}, u32[]{:S(2)}) collective-permute-start(bf16[128,2048]{1,0:T(8,128)(2,1)S(1)} %collective-permute-done.11), channel_id=1, source_target_pairs={{0,4},{1,5},{4,8},{5,9},{8,12},{9,13},{12,14},{13,15},{14,10},{15,... | collective-permute-start | bytes 1572872 | tf_op jit(solution)/shard_map/ppermute | solution.py:98
  203.7 13.9 %collective-permute-start.13 = (bf16[128,2048]{1,0:T(8,128)(2,1)S(1)}, bf16[128,2048]{1,0:T(8,128)(2,1)S(1)}, u32[]{:S(2)}, u32[]{:S(2)}) collective-permute-start(bf16[128,2048]{1,0:T(8,128)(2,1)S(1)} %collective-permute-done.11), channel_id=1, source_target_pairs={{0,1},{1,0},{2,3},{3,2},{4,5},{5,4},{6,7},{7,6},{8,9},{9,8},{10,11... | collective-permute-start | bytes 1572872 | tf_op jit(solution)/shard_map/ppermute | solution.py:94
  203.7 13.4 %collective-permute-start.14 = (bf16[128,2048]{1,0:T(8,128)(2,1)S(1)}, bf16[128,2048]{1,0:T(8,128)(2,1)S(1)}, u32[]{:S(2)}, u32[]{:S(2)}) collective-permute-start(bf16[128,2048]{1,0:T(8,128)(2,1)S(1)} %collective-permute-done.12), channel_id=1, source_target_pairs={{0,1},{1,0},{2,3},{3,2},{4,5},{5,4},{6,7},{7,6},{8,9},{9,8},{10,11... | collective-permute-start | bytes 1572872 | tf_op jit(solution)/shard_map/ppermute | solution.py:94
  216.7 1.9 collective-permute-start.16
  238.9 4.2 %copy-start.6 = (f32[2048]{0:T(1024)S(1)}, f32[2048]{0:T(1024)}, u32[]{:S(2)}) copy-start(f32[2048]{0:T(1024)} %param.25) | copy-start | bytes 24580
  238.9 4.2 %copy-start.7 = (f32[2048]{0:T(1024)S(1)}, f32[2048]{0:T(1024)}, u32[]{:S(2)}) copy-start(f32[2048]{0:T(1024)} %param.24) | copy-start | bytes 24580
  241.7 2.2 copy-start.2
  244.2 2.0 copy-start.1
Sparse Core Ops, SparseCore 0:
  52.8 99.5 reduce-scatter.1

commit v6 on v4

--- a/solution.py
+++ b/solution.py
@@ -51,7 +51,7 @@
             preferred_element_type=jnp.float32,
         )
         parts.append(lax.psum_scatter(partial, ("zo", "c"), scatter_dimension=0, tiled=True))
-    return jnp.concatenate(parts, axis=1)
+    return parts
 
 
 def ring_codes(weight, rows):
@@ -159,20 +159,32 @@
         jnp.take(keys, send_forward, axis=0), DP, split_axis=0, concat_axis=0, tiled=True
     )
     encoded_rows = jnp.take(moved, receive_forward, axis=0)
-    gradient = pair_gradient(queries, grad_out) * scaling
-    gradient, (encoded_rows, send_back, receive_back) = lax.optimization_barrier(
-        (gradient, (encoded_rows, send_back, receive_back))
-    )
-    new_params, new_first, new_second, new_key = adamw(
-        gradient, params, first_moment, second_moment, key_params
-    )
-    codes = ring_codes(new_key.astype(jnp.bfloat16), encoded_rows)
-    codes = codes.astype(jnp.bfloat16)
-    normed = batch_norm(codes, bn_gain, bn_shift)
-    returned = lax.all_to_all(
-        jnp.take(normed, send_back, axis=0), DP, split_axis=0, concat_axis=0, tiled=True
-    )
-    restored = jnp.take(returned, receive_back, axis=0)
+    halves = pair_gradient(queries, grad_out)
+    halves[0], (encoded_rows, send_back, receive_back) = lax.optimization_barrier(
+        (halves[0], (encoded_rows, send_back, receive_back))
+    )
+    width = params.shape[1] // len(halves)
+    results = []
+    for h, gradient in enumerate(halves):
+        cut = slice(h * width, (h + 1) * width)
+        if results:
+            gradient, results[-1] = lax.optimization_barrier((gradient, results[-1]))
+        updated = adamw(
+            gradient * scaling,
+            params[:, cut],
+            first_moment[:, cut],
+            second_moment[:, cut],
+            key_params[:, cut],
+        )
+        codes = ring_codes(updated[3].astype(jnp.bfloat16), encoded_rows)
+        normed = batch_norm(codes.astype(jnp.bfloat16), bn_gain[cut], bn_shift[cut])
+        returned = lax.all_to_all(
+            jnp.take(normed, send_back, axis=0), DP, split_axis=0, concat_axis=0, tiled=True
+        )
+        results.append(updated + (jnp.take(returned, receive_back, axis=0),))
+    new_params, new_first, new_second, new_key, restored = (
+        jnp.concatenate(parts, axis=1) for parts in zip(*results)
+    )
     new_queue = lax.dynamic_update_slice(
         queue, restored[None], (slot[0], jnp.int32(0), jnp.int32(0))
     )

time: 252 us -> 244 us (0.968)
  waiting for transfers between devices: 177 us -> 139 us
  starting transfers between devices: 21.5 us -> 41.7 us
  other arithmetic: 11.2 us -> 15.7 us
    reduce_scatter x2, waiting for transfers between devices: 63.7 us -> 25.3 us  [pair_gradient(): lax.psum_scatter(partial, ('zo', 'c'), scatter_dimension=0, tiled=True)]
    all_to_all x1, waiting for transfers between devices: 20.9 us -> 0.01 us  [per_device(): lax.all_to_all(jnp.take(keys, send_forward, axis=0), DP, split_axis=0, co...]
    ppermute x4 -> x8, starting transfers between devices: 2.16 us -> 14 us  [ring_codes(): ahead = lax.ppermute(ahead, DP, forward)]
    ppermute x4 -> x8, waiting for transfers between devices: 23.2 us -> 34.2 us  [ring_codes(): ahead = lax.ppermute(ahead, DP, forward)]
    all_to_all x1 -> x2, starting transfers between devices: 3.57 us -> 9.59 us  [per_device(): lax.all_to_all(jnp.take(normed, send_back, axis=0), DP, split_axis=0, con...]
    ppermute x1, waiting for transfers between devices: 11.4 us -> 16.7 us  [pair_gradient(): got_second = lax.ppermute(grad_out[:, half:], 'xl', swap)]
    all_to_all x1 -> x2, waiting for transfers between devices: 13.7 us -> 17.9 us  [per_device(): lax.all_to_all(jnp.take(normed, send_back, axis=0), DP, split_axis=0, con...]
    concatenate x0 -> x4, other arithmetic: none -> 4.17 us  [per_device(): jnp.concatenate(parts, axis=1)]
  transfers between devices with their start and end apart: 22 -> 38, of which waited for: 12 -> 19; matrix products, arithmetic and copies ran while one was open for 7% -> 12% of each run, Pallas kernels for 0% -> 0%
where the time goes in v6:
time: 244 us; the launch traced here: 243 us
  waiting for transfers between devices  139 us (57%)
  starting transfers between devices  41.7 us (17%)
  local copies, waits for them, and re-layouts  15.8 us (6%)
  between operations  15.8 us (6%)
  other arithmetic  15.7 us (6%)
  matrix products  14.8 us (6%)
    ppermute x8, waiting for transfers between devices, ring_codes(): ahead = lax.ppermute(ahead, DP, forward)  34.2 us
    reduce_scatter x2, waiting for transfers between devices, pair_gradient(): lax.psum_scatter(partial, ('zo', 'c'), scatter_dimension=0, tiled=True)  25.3 us
    ppermute x6, waiting for transfers between devices, ring_codes(): behind = lax.ppermute(behind, DP, backward)  23.7 us
    ppermute x2, waiting for transfers between devices, pair_gradient(): lax.ppermute((theirs, grad_out[:, :half]), 'xl', swap)  19.7 us
    all_to_all x2, waiting for transfers between devices, per_device(): lax.all_to_all(jnp.take(normed, send_back, axis=0), DP, split_axis=0, con...  17.9 us
    ppermute x1, waiting for transfers between devices, pair_gradient(): got_second = lax.ppermute(grad_out[:, half:], 'xl', swap)  16.7 us
    ppermute x8, starting transfers between devices, ring_codes(): ahead = lax.ppermute(ahead, DP, forward)  14 us
    all_to_all x2, starting transfers between devices, per_device(): lax.all_to_all(jnp.take(normed, send_back, axis=0), DP, split_axis=0, con...  9.59 us
  transfers between devices with their start and end apart: 38, of which 19 were waited for; matrix products, arithmetic and copies ran while one was open for 12% of the time, Pallas kernels for 0%

profile of v6, /device:TPU:0, one launch (start us, length us, event | category | flops | bytes accessed | tf_op | source)
XLA Modules:
  0.0 243.0 jit_solution(2592259114430772718)
XLA Ops:
  7.2 4.9 %copy.22 = bf16[8,128,2048]{2,1,0:T(8,128)(2,1)} copy(bf16[8,128,2048]{2,1,0:T(8,128)(2,1)} %param.28) | data formatting | bytes 8388608
  14.0 3.0 %collective-permute-start = (bf16[256,1024]{1,0:T(8,128)(2,1)S(1)}, bf16[256,1024]{1,0:T(8,128)(2,1)}, u32[]{:S(2)}, u32[]{:S(2)}) collective-permute-start(bf16[256,1024]{1,0:T(8,128)(2,1)S(1)} %reshape.213), channel_id=1, source_target_pairs={{0,2},{2,0},{1,3},{3,1},{4,6},{6,4},{5,7},{7,5},{8,10},{10,8},{9,1... | collective-permute-start | bytes 1572872 | tf_op jit(solution)/shard_map/ppermute | solution.py:42
  17.0 2.1 fusion.135
  19.5 10.4 %collective-permute-done = bf16[256,1024]{1,0:T(8,128)(2,1)} collective-permute-done((bf16[256,1024]{1,0:T(8,128)(2,1)S(1)}, bf16[256,1024]{1,0:T(8,128)(2,1)}, u32[]{:S(2)}, u32[]{:S(2)}) %collective-permute-start) | collective-permute-done | bytes 524320 | tf_op jit(solution)/shard_map/ppermute | solution.py:42
  31.0 9.3 %collective-permute-done.2 = bf16[256,1024]{1,0:T(8,128)(2,1)} collective-permute-done((bf16[256,1024]{1,0:T(8,128)(2,1)}, bf16[256,1024]{1,0:T(8,128)(2,1)}, u32[]{:S(2)}, u32[]{:S(2)}) %collective-permute-start.2) | collective-permute-done | bytes 524320 | tf_op jit(solution)/shard_map/ppermute | solution.py:42
  40.3 4.4 %fusion.26 = f32[1024,1024]{1,0:T(8,128)} fusion(bf16[512,1024]{1,0:T(8,128)(2,1)S(1)} %constant_dynamic-update-slice_fusion, bf16[256,1024]{1,0:T(8,128)(2,1)} %collective-permute-done.2, bf16[256,1024]{1,0:T(8,128)(2,1)} %get-tuple-element.43), kind=kOutput, calls=%fused_computation.44 | convolution fusion | flops 1075838976 | bytes 6291456 | tf_op jit(solution)/shard_map/dot_general | solution.py:47
  47.5 6.2 %all-to-all-start = ((bf16[16,8,2048]{2,1,0:T(8,128)(2,1)}), bf16[16,8,2048]{2,1,0:T(8,128)(2,1)S(1)}, u32[]{:S(2)}, u32[]{:S(2)}) async-start(bf16[16,8,2048]{2,1,0:T(8,128)(2,1)} %select_bitcast_fusion), calls=%async_computation.2 | async-start | bytes 1048576 | tf_op jit(solution)/shard_map/all_to_all | solution.py:158
  53.7 2.0 collective-permute-start.1
  56.3 16.7 %collective-permute-done.1 = bf16[256,1024]{1,0:T(8,128)(2,1)S(1)} collective-permute-done((bf16[256,1024]{1,0:T(8,128)(2,1)S(1)}, bf16[256,1024]{1,0:T(8,128)(2,1)S(1)}, u32[]{:S(2)}, u32[]{:S(2)}) %collective-permute-start.1) | collective-permute-done | bytes 524320 | tf_op jit(solution)/shard_map/ppermute | solution.py:43
  72.9 3.3 %fusion.22 = f32[1024,1024]{1,0:T(8,128)} fusion(bf16[512,1024]{1,0:T(8,128)(2,1)S(1)} %constant_dynamic-update-slice_fusion, bf16[256,1024]{1,0:T(8,128)(2,1)S(1)} %collective-permute-done.1, bf16[256,1024]{1,0:T(8,128)(2,1)S(1)} %get-tuple-element.44), kind=kOutput, calls=%fused_computation.40 | convolution fusion | flops 1075838976 | bytes 6291456 | tf_op jit(solution)/shard_map/dot_general | solution.py:47
  79.6 25.2 %reduce-scatter.5.cloned.1.call-done = f32[128,1024]{1,0:T(8,128)} async-done(((f32[1024,1024]{1,0:T(8,128)}), f32[128,1024]{1,0:T(8,128)}) %reduce-scatter.5.cloned.1.call-update) | async-done | bytes 524304 | tf_op jit(solution)/shard_map/reduce_scatter | solution.py:53
  104.8 2.2 fusion.130
  107.0 1.5 collective-permute-start.5
  110.0 6.0 %collective-permute-done.5 = bf16[128,1024]{1,0:T(8,128)(2,1)S(1)} collective-permute-done((bf16[128,1024]{1,0:T(8,128)(2,1)S(1)}, bf16[128,1024]{1,0:T(8,128)(2,1)S(1)}, u32[]{:S(2)}, u32[]{:S(2)}) %collective-permute-start.5) | collective-permute-done | bytes 262176 | tf_op jit(solution)/shard_map/ppermute | solution.py:109
  117.8 2.5 %collective-permute-start.8 = (bf16[128,1024]{1,0:T(8,128)(2,1)S(1)}, bf16[128,1024]{1,0:T(8,128)(2,1)S(1)}, u32[]{:S(2)}, u32[]{:S(2)}) collective-permute-start(bf16[128,1024]{1,0:T(8,128)(2,1)S(1)} %collective-permute-done.4), channel_id=1, source_target_pairs={{0,4},{1,5},{4,8},{5,9},{8,12},{9,13},{12,14},{13,15},{14,10},{15,... | collective-permute-start | bytes 786440 | tf_op jit(solution)/shard_map/ppermute | solution.py:105
  121.0 9.7 %collective-permute-done.9 = bf16[128,1024]{1,0:T(8,128)(2,1)S(1)} collective-permute-done((bf16[128,1024]{1,0:T(8,128)(2,1)S(1)}, bf16[128,1024]{1,0:T(8,128)(2,1)S(1)}, u32[]{:S(2)}, u32[]{:S(2)}) %collective-permute-start.9) | collective-permute-done | bytes 262176 | tf_op jit(solution)/shard_map/ppermute | solution.py:109
  132.3 2.5 %collective-permute-start.12 = (bf16[128,1024]{1,0:T(8,128)(2,1)S(1)}, bf16[128,1024]{1,0:T(8,128)(2,1)S(1)}, u32[]{:S(2)}, u32[]{:S(2)}) collective-permute-start(bf16[128,1024]{1,0:T(8,128)(2,1)S(1)} %collective-permute-done.8), channel_id=1, source_target_pairs={{0,4},{1,5},{4,8},{5,9},{8,12},{9,13},{12,14},{13,15},{14,10},{15,... | collective-permute-start | bytes 786440 | tf_op jit(solution)/shard_map/ppermute | solution.py:105
  135.6 11.2 %collective-permute-done.12 = bf16[128,1024]{1,0:T(8,128)(2,1)S(1)} collective-permute-done((bf16[128,1024]{1,0:T(8,128)(2,1)S(1)}, bf16[128,1024]{1,0:T(8,128)(2,1)S(1)}, u32[]{:S(2)}, u32[]{:S(2)}) %collective-permute-start.12) | collective-permute-done | bytes 262176 | tf_op jit(solution)/shard_map/ppermute | solution.py:105
  146.8 2.5 %collective-permute-start.16 = (bf16[128,1024]{1,0:T(8,128)(2,1)S(1)}, bf16[128,1024]{1,0:T(8,128)(2,1)S(1)}, u32[]{:S(2)}, u32[]{:S(2)}) collective-permute-start(bf16[128,1024]{1,0:T(8,128)(2,1)S(1)} %collective-permute-done.12), channel_id=1, source_target_pairs={{0,4},{1,5},{4,8},{5,9},{8,12},{9,13},{12,14},{13,15},{14,10},{15,... | collective-permute-start | bytes 786440 | tf_op jit(solution)/shard_map/ppermute | solution.py:105
  150.7 10.3 %collective-permute-done.16 = bf16[128,1024]{1,0:T(8,128)(2,1)S(1)} collective-permute-done((bf16[128,1024]{1,0:T(8,128)(2,1)S(1)}, bf16[128,1024]{1,0:T(8,128)(2,1)S(1)}, u32[]{:S(2)}, u32[]{:S(2)}) %collective-permute-start.16) | collective-permute-done | bytes 262176 | tf_op jit(solution)/shard_map/ppermute | solution.py:105
  164.6 5.6 %all-to-all-start.1 = ((bf16[16,8,1024]{2,1,0:T(8,128)(2,1)}), bf16[16,8,1024]{2,1,0:T(8,128)(2,1)S(1)}, u32[]{:S(2)}, u32[]{:S(2)}) async-start(bf16[16,8,1024]{2,1,0:T(8,128)(2,1)} %select_bitcast_fusion.2), calls=%async_computation.3 | async-start | bytes 524288 | tf_op jit(solution)/shard_map/all_to_all | solution.py:181
  170.2 10.0 %all-to-all-done.1 = bf16[16,8,1024]{2,1,0:T(8,128)(2,1)S(1)} async-done(((bf16[16,8,1024]{2,1,0:T(8,128)(2,1)}), bf16[16,8,1024]{2,1,0:T(8,128)(2,1)S(1)}, u32[]{:S(2)}, u32[]{:S(2)}) %all-to-all-start.1) | async-done | bytes 262176 | tf_op jit(solution)/shard_map/all_to_all | solution.py:181
  181.2 2.9 %fusion.129 = (bf16[128,1024]{1,0:T(8,128)(2,1)S(1)}, f32[128,1024]{1,0:T(8,128)S(1)}, f32[128,1024]{1,0:T(8,128)S(1)}, f32[128,1024]{1,0:T(8,128)}, f32[128,1024]{1,0:T(8,128)S(1)}) fusion(f32[128,2048]{1,0:T(8,128)} %param.22, f32[128,2048]{1,0:T(8,128)} %param.19, f32[128,1024]{1,0:T(8,128)} %reduce-scatter.3.cloned.1.call-done, f32[128,2048]{1,0:T(8,128)} %param.20, ...), kind=kLoop, calls=%fused_computation.223 | loop fusion | flops 2621440 | bytes 4980736 | tf_op jit(solution)/shard_map/convert_element_type | solution.py:179
  184.2 2.0 collective-permute-start.19
  188.5 3.7 %collective-permute-done.20 = bf16[128,1024]{1,0:T(8,128)(2,1)S(1)} collective-permute-done((bf16[128,1024]{1,0:T(8,128)(2,1)S(1)}, bf16[128,1024]{1,0:T(8,128)(2,1)S(1)}, u32[]{:S(2)}, u32[]{:S(2)}) %collective-permute-start.20) | collective-permute-done | bytes 262176 | tf_op jit(solution)/shard_map/ppermute | solution.py:109
  192.9 1.4 collective-permute-start.23
  195.2 4.2 %collective-permute-done.24 = bf16[128,1024]{1,0:T(8,128)(2,1)S(1)} collective-permute-done((bf16[128,1024]{1,0:T(8,128)(2,1)S(1)}, bf16[128,1024]{1,0:T(8,128)(2,1)S(1)}, u32[]{:S(2)}, u32[]{:S(2)}) %collective-permute-start.24) | collective-permute-done | bytes 262176 | tf_op jit(solution)/shard_map/ppermute | solution.py:109
  199.4 1.4 collective-permute-start.28
  204.0 5.6 %collective-permute-done.27 = bf16[128,1024]{1,0:T(8,128)(2,1)S(1)} collective-permute-done((bf16[128,1024]{1,0:T(8,128)(2,1)S(1)}, bf16[128,1024]{1,0:T(8,128)(2,1)S(1)}, u32[]{:S(2)}, u32[]{:S(2)}) %collective-permute-start.27) | collective-permute-done | bytes 262176 | tf_op jit(solution)/shard_map/ppermute | solution.py:105
  212.5 4.2 %collective-permute-done.31 = bf16[128,1024]{1,0:T(8,128)(2,1)S(1)} collective-permute-done((bf16[128,1024]{1,0:T(8,128)(2,1)S(1)}, bf16[128,1024]{1,0:T(8,128)(2,1)S(1)}, u32[]{:S(2)}, u32[]{:S(2)}) %collective-permute-start.31) | collective-permute-done | bytes 262176 | tf_op jit(solution)/shard_map/ppermute | solution.py:105
  220.3 4.0 %all-to-all-start.2 = ((bf16[16,8,1024]{2,1,0:T(8,128)(2,1)}), bf16[16,8,1024]{2,1,0:T(8,128)(2,1)S(1)}, u32[]{:S(2)}, u32[]{:S(2)}) async-start(bf16[16,8,1024]{2,1,0:T(8,128)(2,1)} %select_bitcast_fusion.1), calls=%async_computation.4 | async-start | bytes 524288 | tf_op jit(solution)/shard_map/all_to_all | solution.py:181
  226.5 7.9 %all-to-all-done.2 = bf16[16,8,1024]{2,1,0:T(8,128)(2,1)S(1)} async-done(((bf16[16,8,1024]{2,1,0:T(8,128)(2,1)}), bf16[16,8,1024]{2,1,0:T(8,128)(2,1)S(1)}, u32[]{:S(2)}, u32[]{:S(2)}) %all-to-all-start.2) | async-done | bytes 262176 | tf_op jit(solution)/shard_map/all_to_all | solution.py:181
  (163 shorter events, 38.5 us)
Async XLA Ops:
  7.2 97.6 %reduce-scatter.5.cloned.1.call-start = ((), (), s32[]{:S(2)}) async-start(), calls=%async_computation.6 | async-start | bytes 4718592 | tf_op jit(solution)/shard_map/reduce_scatter | solution.py:53
  14.0 15.9 %collective-permute-start = (bf16[256,1024]{1,0:T(8,128)(2,1)S(1)}, bf16[256,1024]{1,0:T(8,128)(2,1)}, u32[]{:S(2)}, u32[]{:S(2)}) collective-permute-start(bf16[256,1024]{1,0:T(8,128)(2,1)S(1)} %reshape.213), channel_id=1, source_target_pairs={{0,2},{2,0},{1,3},{3,1},{4,6},{6,4},{5,7},{7,5},{8,10},{10,8},{9,1... | collective-permute-start | bytes 1572872 | tf_op jit(solution)/shard_map/ppermute | solution.py:42
  19.1 21.2 %collective-permute-start.2 = (bf16[256,1024]{1,0:T(8,128)(2,1)}, bf16[256,1024]{1,0:T(8,128)(2,1)}, u32[]{:S(2)}, u32[]{:S(2)}) collective-permute-start(bf16[256,1024]{1,0:T(8,128)(2,1)} %get-tuple-element.43), channel_id=1, source_target_pairs={{0,2},{2,0},{1,3},{3,1},{4,6},{6,4},{5,7},{7,5},{8,10},{10,8},{9,1... | collective-permute-start | bytes 1572872 | tf_op jit(solution)/shard_map/ppermute | solution.py:42
  47.5 31.0 %all-to-all-start = ((bf16[16,8,2048]{2,1,0:T(8,128)(2,1)}), bf16[16,8,2048]{2,1,0:T(8,128)(2,1)S(1)}, u32[]{:S(2)}, u32[]{:S(2)}) async-start(bf16[16,8,2048]{2,1,0:T(8,128)(2,1)} %select_bitcast_fusion), calls=%async_computation.2 | async-start | bytes 1048576 | tf_op jit(solution)/shard_map/all_to_all | solution.py:158
  53.6 127.6 %reduce-scatter.3.cloned.1.call-start = ((), (), s32[]{:S(2)}) async-start(), calls=%async_computation.5 | async-start | bytes 4718592 | tf_op jit(solution)/shard_map/reduce_scatter | solution.py:53
  53.7 19.2 %collective-permute-start.1 = (bf16[256,1024]{1,0:T(8,128)(2,1)S(1)}, bf16[256,1024]{1,0:T(8,128)(2,1)S(1)}, u32[]{:S(2)}, u32[]{:S(2)}) collective-permute-start(bf16[256,1024]{1,0:T(8,128)(2,1)S(1)} %get-tuple-element.44), channel_id=1, source_target_pairs={{0,2},{2,0},{1,3},{3,1},{4,6},{6,4},{5,7},{7,5},{8,10},{10,8},{9,1... | collective-permute-start | bytes 1572872 | tf_op jit(solution)/shard_map/ppermute | solution.py:43
  107.0 9.0 %collective-permute-start.5 = (bf16[128,1024]{1,0:T(8,128)(2,1)S(1)}, bf16[128,1024]{1,0:T(8,128)(2,1)S(1)}, u32[]{:S(2)}, u32[]{:S(2)}) collective-permute-start(bf16[128,1024]{1,0:T(8,128)(2,1)S(1)} %get-tuple-element.32), channel_id=1, source_target_pairs={{0,2},{1,3},{4,0},{5,1},{8,4},{9,5},{12,8},{13,9},{14,12},{15,13},... | collective-permute-start | bytes 786440 | tf_op jit(solution)/shard_map/ppermute | solution.py:109
  108.5 9.3 %collective-permute-start.4 = (bf16[128,1024]{1,0:T(8,128)(2,1)S(1)}, bf16[128,1024]{1,0:T(8,128)(2,1)S(1)}, u32[]{:S(2)}, u32[]{:S(2)}) collective-permute-start(bf16[128,1024]{1,0:T(8,128)(2,1)S(1)} %get-tuple-element.32), channel_id=1, source_target_pairs={{0,4},{1,5},{4,8},{5,9},{8,12},{9,13},{12,14},{13,15},{14,10},{15,... | collective-permute-start | bytes 786440 | tf_op jit(solution)/shard_map/ppermute | solution.py:105
  109.1 11.5 %collective-permute-start.3 = (bf16[128,1024]{1,0:T(8,128)(2,1)S(1)}, bf16[128,1024]{1,0:T(8,128)(2,1)S(1)}, u32[]{:S(2)}, u32[]{:S(2)}) collective-permute-start(bf16[128,1024]{1,0:T(8,128)(2,1)S(1)} %get-tuple-element.32), channel_id=1, source_target_pairs={{0,1},{1,0},{2,3},{3,2},{4,5},{5,4},{6,7},{7,6},{8,9},{9,8},{10,11... | collective-permute-start | bytes 786440 | tf_op jit(solution)/shard_map/ppermute | solution.py:101
  116.0 14.6 %collective-permute-start.9 = (bf16[128,1024]{1,0:T(8,128)(2,1)S(1)}, bf16[128,1024]{1,0:T(8,128)(2,1)S(1)}, u32[]{:S(2)}, u32[]{:S(2)}) collective-permute-start(bf16[128,1024]{1,0:T(8,128)(2,1)S(1)} %collective-permute-done.5), channel_id=1, source_target_pairs={{0,2},{1,3},{4,0},{5,1},{8,4},{9,5},{12,8},{13,9},{14,12},{15,13},... | collective-permute-start | bytes 786440 | tf_op jit(solution)/shard_map/ppermute | solution.py:109
  116.0 19.0 %collective-permute-start.7 = (bf16[128,1024]{1,0:T(8,128)(2,1)S(1)}, bf16[128,1024]{1,0:T(8,128)(2,1)S(1)}, u32[]{:S(2)}, u32[]{:S(2)}) collective-permute-start(bf16[128,1024]{1,0:T(8,128)(2,1)S(1)} %collective-permute-done.5), channel_id=1, source_target_pairs={{0,1},{1,0},{2,3},{3,2},{4,5},{5,4},{6,7},{7,6},{8,9},{9,8},{10,11... | collective-permute-start | bytes 786440 | tf_op jit(solution)/shard_map/ppermute | solution.py:101
  117.8 14.5 %collective-permute-start.8 = (bf16[128,1024]{1,0:T(8,128)(2,1)S(1)}, bf16[128,1024]{1,0:T(8,128)(2,1)S(1)}, u32[]{:S(2)}, u32[]{:S(2)}) collective-permute-start(bf16[128,1024]{1,0:T(8,128)(2,1)S(1)} %collective-permute-done.4), channel_id=1, source_target_pairs={{0,4},{1,5},{4,8},{5,9},{8,12},{9,13},{12,14},{13,15},{14,10},{15,... | collective-permute-start | bytes 786440 | tf_op jit(solution)/shard_map/ppermute | solution.py:105
  120.3 15.0 %collective-permute-start.6 = (bf16[128,1024]{1,0:T(8,128)(2,1)S(1)}, bf16[128,1024]{1,0:T(8,128)(2,1)S(1)}, u32[]{:S(2)}, u32[]{:S(2)}) collective-permute-start(bf16[128,1024]{1,0:T(8,128)(2,1)S(1)} %collective-permute-done.4), channel_id=1, source_target_pairs={{0,1},{1,0},{2,3},{3,2},{4,5},{5,4},{6,7},{7,6},{8,9},{9,8},{10,11... | collective-permute-start | bytes 786440 | tf_op jit(solution)/shard_map/ppermute | solution.py:101
  130.7 18.6 %collective-permute-start.13 = (bf16[128,1024]{1,0:T(8,128)(2,1)S(1)}, bf16[128,1024]{1,0:T(8,128)(2,1)S(1)}, u32[]{:S(2)}, u32[]{:S(2)}) collective-permute-start(bf16[128,1024]{1,0:T(8,128)(2,1)S(1)} %collective-permute-done.9), channel_id=1, source_target_pairs={{0,2},{1,3},{4,0},{5,1},{8,4},{9,5},{12,8},{13,9},{14,12},{15,13},... | collective-permute-start | bytes 786440 | tf_op jit(solution)/shard_map/ppermute | solution.py:109
  130.7 19.6 %collective-permute-start.11 = (bf16[128,1024]{1,0:T(8,128)(2,1)S(1)}, bf16[128,1024]{1,0:T(8,128)(2,1)S(1)}, u32[]{:S(2)}, u32[]{:S(2)}) collective-permute-start(bf16[128,1024]{1,0:T(8,128)(2,1)S(1)} %collective-permute-done.9), channel_id=1, source_target_pairs={{0,1},{1,0},{2,3},{3,2},{4,5},{5,4},{6,7},{7,6},{8,9},{9,8},{10,11... | collective-permute-start | bytes 786440 | tf_op jit(solution)/shard_map/ppermute | solution.py:101
  132.3 14.5 %collective-permute-start.12 = (bf16[128,1024]{1,0:T(8,128)(2,1)S(1)}, bf16[128,1024]{1,0:T(8,128)(2,1)S(1)}, u32[]{:S(2)}, u32[]{:S(2)}) collective-permute-start(bf16[128,1024]{1,0:T(8,128)(2,1)S(1)} %collective-permute-done.8), channel_id=1, source_target_pairs={{0,4},{1,5},{4,8},{5,9},{8,12},{9,13},{12,14},{13,15},{14,10},{15,... | collective-permute-start | bytes 786440 | tf_op jit(solution)/shard_map/ppermute | solution.py:105
  135.0 15.4 %collective-permute-start.10 = (bf16[128,1024]{1,0:T(8,128)(2,1)S(1)}, bf16[128,1024]{1,0:T(8,128)(2,1)S(1)}, u32[]{:S(2)}, u32[]{:S(2)}) collective-permute-start(bf16[128,1024]{1,0:T(8,128)(2,1)S(1)} %collective-permute-done.8), channel_id=1, source_target_pairs={{0,1},{1,0},{2,3},{3,2},{4,5},{5,4},{6,7},{7,6},{8,9},{9,8},{10,11... | collective-permute-start | bytes 786440 | tf_op jit(solution)/shard_map/ppermute | solution.py:101
  146.8 14.2 %collective-permute-start.16 = (bf16[128,1024]{1,0:T(8,128)(2,1)S(1)}, bf16[128,1024]{1,0:T(8,128)(2,1)S(1)}, u32[]{:S(2)}, u32[]{:S(2)}) collective-permute-start(bf16[128,1024]{1,0:T(8,128)(2,1)S(1)} %collective-permute-done.12), channel_id=1, source_target_pairs={{0,4},{1,5},{4,8},{5,9},{8,12},{9,13},{12,14},{13,15},{14,10},{15,... | collective-permute-start | bytes 786440 | tf_op jit(solution)/shard_map/ppermute | solution.py:105
  149.3 12.2 %collective-permute-start.14 = (bf16[128,1024]{1,0:T(8,128)(2,1)S(1)}, bf16[128,1024]{1,0:T(8,128)(2,1)S(1)}, u32[]{:S(2)}, u32[]{:S(2)}) collective-permute-start(bf16[128,1024]{1,0:T(8,128)(2,1)S(1)} %collective-permute-done.12), channel_id=1, source_target_pairs={{0,1},{1,0},{2,3},{3,2},{4,5},{5,4},{6,7},{7,6},{8,9},{9,8},{10,11... | collective-permute-start | bytes 786440 | tf_op jit(solution)/shard_map/ppermute | solution.py:101
  149.3 11.9 %collective-permute-start.15 = (bf16[128,1024]{1,0:T(8,128)(2,1)S(1)}, bf16[128,1024]{1,0:T(8,128)(2,1)S(1)}, u32[]{:S(2)}, u32[]{:S(2)}) collective-permute-start(bf16[128,1024]{1,0:T(8,128)(2,1)S(1)} %collective-permute-done.13), channel_id=1, source_target_pairs={{0,1},{1,0},{2,3},{3,2},{4,5},{5,4},{6,7},{7,6},{8,9},{9,8},{10,11... | collective-permute-start | bytes 786440 | tf_op jit(solution)/shard_map/ppermute | solution.py:101
  164.6 15.6 %all-to-all-start.1 = ((bf16[16,8,1024]{2,1,0:T(8,128)(2,1)}), bf16[16,8,1024]{2,1,0:T(8,128)(2,1)S(1)}, u32[]{:S(2)}, u32[]{:S(2)}) async-start(bf16[16,8,1024]{2,1,0:T(8,128)(2,1)} %select_bitcast_fusion.2), calls=%async_computation.3 | async-start | bytes 524288 | tf_op jit(solution)/shard_map/all_to_all | solution.py:181
  184.2 8.1 %collective-permute-start.20 = (bf16[128,1024]{1,0:T(8,128)(2,1)S(1)}, bf16[128,1024]{1,0:T(8,128)(2,1)S(1)}, u32[]{:S(2)}, u32[]{:S(2)}) collective-permute-start(bf16[128,1024]{1,0:T(8,128)(2,1)S(1)} %get-tuple-element.27), channel_id=1, source_target_pairs={{0,2},{1,3},{4,0},{5,1},{8,4},{9,5},{12,8},{13,9},{14,12},{15,13},... | collective-permute-start | bytes 786440 | tf_op jit(solution)/shard_map/ppermute | solution.py:109
  184.2 8.7 %collective-permute-start.19 = (bf16[128,1024]{1,0:T(8,128)(2,1)S(1)}, bf16[128,1024]{1,0:T(8,128)(2,1)S(1)}, u32[]{:S(2)}, u32[]{:S(2)}) collective-permute-start(bf16[128,1024]{1,0:T(8,128)(2,1)S(1)} %get-tuple-element.27), channel_id=1, source_target_pairs={{0,4},{1,5},{4,8},{5,9},{8,12},{9,13},{12,14},{13,15},{14,10},{15,... | collective-permute-start | bytes 786440 | tf_op jit(solution)/shard_map/ppermute | solution.py:105
  186.2 8.5 %collective-permute-start.18 = (bf16[128,1024]{1,0:T(8,128)(2,1)S(1)}, bf16[128,1024]{1,0:T(8,128)(2,1)S(1)}, u32[]{:S(2)}, u32[]{:S(2)}) collective-permute-start(bf16[128,1024]{1,0:T(8,128)(2,1)S(1)} %get-tuple-element.27), channel_id=1, source_target_pairs={{0,1},{1,0},{2,3},{3,2},{4,5},{5,4},{6,7},{7,6},{8,9},{9,8},{10,11... | collective-permute-start | bytes 786440 | tf_op jit(solution)/shard_map/ppermute | solution.py:101
  192.9 10.5 %collective-permute-start.22 = (bf16[128,1024]{1,0:T(8,128)(2,1)S(1)}, bf16[128,1024]{1,0:T(8,128)(2,1)S(1)}, u32[]{:S(2)}, u32[]{:S(2)}) collective-permute-start(bf16[128,1024]{1,0:T(8,128)(2,1)S(1)} %collective-permute-done.20), channel_id=1, source_target_pairs={{0,1},{1,0},{2,3},{3,2},{4,5},{5,4},{6,7},{7,6},{8,9},{9,8},{10,11... | collective-permute-start | bytes 786440 | tf_op jit(solution)/shard_map/ppermute | solution.py:101
  192.9 8.7 %collective-permute-start.23 = (bf16[128,1024]{1,0:T(8,128)(2,1)S(1)}, bf16[128,1024]{1,0:T(8,128)(2,1)S(1)}, u32[]{:S(2)}, u32[]{:S(2)}) collective-permute-start(bf16[128,1024]{1,0:T(8,128)(2,1)S(1)} %collective-permute-done.19), channel_id=1, source_target_pairs={{0,4},{1,5},{4,8},{5,9},{8,12},{9,13},{12,14},{13,15},{14,10},{15,... | collective-permute-start | bytes 786440 | tf_op jit(solution)/shard_map/ppermute | solution.py:105
  194.3 9.5 %collective-permute-start.21 = (bf16[128,1024]{1,0:T(8,128)(2,1)S(1)}, bf16[128,1024]{1,0:T(8,128)(2,1)S(1)}, u32[]{:S(2)}, u32[]{:S(2)}) collective-permute-start(bf16[128,1024]{1,0:T(8,128)(2,1)S(1)} %collective-permute-done.19), channel_id=1, source_target_pairs={{0,1},{1,0},{2,3},{3,2},{4,5},{5,4},{6,7},{7,6},{8,9},{9,8},{10,11... | collective-permute-start | bytes 786440 | tf_op jit(solution)/shard_map/ppermute | solution.py:101
  199.4 11.7 %collective-permute-start.28 = (bf16[128,1024]{1,0:T(8,128)(2,1)S(1)}, bf16[128,1024]{1,0:T(8,128)(2,1)S(1)}, u32[]{:S(2)}, u32[]{:S(2)}) collective-permute-start(bf16[128,1024]{1,0:T(8,128)(2,1)S(1)} %collective-permute-done.24), channel_id=1, source_target_pairs={{0,2},{1,3},{4,0},{5,1},{8,4},{9,5},{12,8},{13,9},{14,12},{15,13},... | collective-permute-start | bytes 786440 | tf_op jit(solution)/shard_map/ppermute | solution.py:109
  200.9 11.1 %collective-permute-start.26 = (bf16[128,1024]{1,0:T(8,128)(2,1)S(1)}, bf16[128,1024]{1,0:T(8,128)(2,1)S(1)}, u32[]{:S(2)}, u32[]{:S(2)}) collective-permute-start(bf16[128,1024]{1,0:T(8,128)(2,1)S(1)} %collective-permute-done.24), channel_id=1, source_target_pairs={{0,1},{1,0},{2,3},{3,2},{4,5},{5,4},{6,7},{7,6},{8,9},{9,8},{10,11... | collective-permute-start | bytes 786440 | tf_op jit(solution)/shard_map/ppermute | solution.py:101
  201.6 8.0 %collective-permute-start.27 = (bf16[128,1024]{1,0:T(8,128)(2,1)S(1)}, bf16[128,1024]{1,0:T(8,128)(2,1)S(1)}, u32[]{:S(2)}, u32[]{:S(2)}) collective-permute-start(bf16[128,1024]{1,0:T(8,128)(2,1)S(1)} %collective-permute-done.23), channel_id=1, source_target_pairs={{0,4},{1,5},{4,8},{5,9},{8,12},{9,13},{12,14},{13,15},{14,10},{15,... | collective-permute-start | bytes 786440 | tf_op jit(solution)/shard_map/ppermute | solution.py:105
  203.4 8.7 %collective-permute-start.25 = (bf16[128,1024]{1,0:T(8,128)(2,1)S(1)}, bf16[128,1024]{1,0:T(8,128)(2,1)S(1)}, u32[]{:S(2)}, u32[]{:S(2)}) collective-permute-start(bf16[128,1024]{1,0:T(8,128)(2,1)S(1)} %collective-permute-done.23), channel_id=1, source_target_pairs={{0,1},{1,0},{2,3},{3,2},{4,5},{5,4},{6,7},{7,6},{8,9},{9,8},{10,11... | collective-permute-start | bytes 786440 | tf_op jit(solution)/shard_map/ppermute | solution.py:101
  220.3 14.1 %all-to-all-start.2 = ((bf16[16,8,1024]{2,1,0:T(8,128)(2,1)}), bf16[16,8,1024]{2,1,0:T(8,128)(2,1)S(1)}, u32[]{:S(2)}, u32[]{:S(2)}) async-start(bf16[16,8,1024]{2,1,0:T(8,128)(2,1)} %select_bitcast_fusion.1), calls=%async_computation.4 | async-start | bytes 524288 | tf_op jit(solution)/shard_map/all_to_all | solution.py:181
  (14 other events, 121.1 us)
Sparse Core Ops, SparseCore 0:
  44.8 59.9 reduce-scatter.4
  107.1 66.4 reduce-scatter.2

commit v7 on v6

--- a/solution.py
+++ b/solution.py
@@ -31,16 +31,16 @@
 def pair_gradient(queries, grad_out):
     tokens, width = queries.shape
     zo = lax.axis_size("zo")
-    x = lax.axis_index("xl")
+    c = lax.axis_index("c")
     blocks = queries.reshape(tokens, zo, 2, 2, width // (4 * zo))
-    mine = lax.dynamic_index_in_dim(blocks, x, axis=2, keepdims=False)
-    theirs = lax.dynamic_index_in_dim(blocks, 1 - x, axis=2, keepdims=False)
+    mine = lax.dynamic_index_in_dim(blocks, c, axis=3, keepdims=False)
+    theirs = lax.dynamic_index_in_dim(blocks, 1 - c, axis=3, keepdims=False)
     mine = mine.reshape(tokens, width // 2)
     theirs = theirs.reshape(tokens, width // 2)
     swap = [(0, 1), (1, 0)]
     half = grad_out.shape[1] // 2
-    got_queries, got_first = lax.ppermute((theirs, grad_out[:, :half]), "xl", swap)
-    got_second = lax.ppermute(grad_out[:, half:], "xl", swap)
+    got_queries, got_first = lax.ppermute((theirs, grad_out[:, :half]), "c", swap)
+    got_second = lax.ppermute(grad_out[:, half:], "c", swap)
     both_queries = jnp.concatenate([mine, got_queries], axis=0)
     parts = []
     for own, got in ((grad_out[:, :half], got_first), (grad_out[:, half:], got_second)):
@@ -50,7 +50,7 @@
             (((0,), (0,)), ((), ())),
             preferred_element_type=jnp.float32,
         )
-        parts.append(lax.psum_scatter(partial, ("zo", "c"), scatter_dimension=0, tiled=True))
+        parts.append(lax.psum_scatter(partial, ("zo", "xl"), scatter_dimension=0, tiled=True))
     return parts
 
 

time: 244 us -> 295 us (1.21)
  waiting for transfers between devices: 139 us -> 197 us
  local copies, waits for them, and re-layouts: 15.8 us -> 12.4 us
  starting transfers between devices: 41.7 us -> 38.7 us
    reduce_scatter x2, waiting for transfers between devices: 25.3 us -> 95.5 us  [pair_gradient(): lax.psum_scatter(partial, ('zo', 'xl'), scatter_dimension=0, tiled=True)]
    ppermute x3, waiting for transfers between devices: 36.4 us -> 2.64 us  [the longest x2 1.53 us: pair_gradient(): lax.ppermute((theirs, grad_out[:, :half]), 'c', swap)]
    all_to_all x1, waiting for transfers between devices: 0.01 us -> 14.2 us  [per_device(): lax.all_to_all(jnp.take(keys, send_forward, axis=0), DP, split_axis=0, co...]
    ppermute x6, waiting for transfers between devices: 23.7 us -> 30.2 us  [ring_codes(): behind = lax.ppermute(behind, DP, backward)]
    ppermute x8, starting transfers between devices: 14 us -> 8.57 us  [ring_codes(): ahead = lax.ppermute(ahead, DP, forward)]
    ppermute x6, starting transfers between devices: 3.63 us -> 7.41 us  [ring_codes(): behind = lax.ppermute(behind, DP, backward)]
    ppermute x3, starting transfers between devices: 5.01 us -> 1.51 us  [the longest x2 1.04 us: pair_gradient(): lax.ppermute((theirs, grad_out[:, :half]), 'c', swap)]
    unnamed x18 -> x24, local copies, waits for them, and re-layouts: 4.98 us -> 6.71 us
  transfers between devices with their start and end apart: 38 -> 38, of which waited for: 19 -> 19; matrix products, arithmetic and copies ran while one was open for 12% -> 9% of each run, Pallas kernels for 0% -> 0%
where the time goes in v7:
time: 295 us; the launch traced here: 294 us
  waiting for transfers between devices  197 us (67%)
  starting transfers between devices  38.7 us (13%)
  other arithmetic  15.8 us (5%)
  between operations  15.8 us (5%)
  matrix products  14.5 us (5%)
  local copies, waits for them, and re-layouts  12.4 us (4%)
    reduce_scatter x2, waiting for transfers between devices, pair_gradient(): lax.psum_scatter(partial, ('zo', 'xl'), scatter_dimension=0, tiled=True)  95.5 us
    ppermute x8, waiting for transfers between devices, ring_codes(): ahead = lax.ppermute(ahead, DP, forward)  34.5 us
    ppermute x6, waiting for transfers between devices, ring_codes(): behind = lax.ppermute(behind, DP, backward)  30.2 us
    all_to_all x2, waiting for transfers between devices, per_device(): lax.all_to_all(jnp.take(normed, send_back, axis=0), DP, split_axis=0, con...  17.9 us
    all_to_all x1, waiting for transfers between devices, per_device(): lax.all_to_all(jnp.take(keys, send_forward, axis=0), DP, split_axis=0, co...  14.2 us
    all_to_all x2, starting transfers between devices, per_device(): lax.all_to_all(jnp.take(normed, send_back, axis=0), DP, split_axis=0, con...  11.9 us
    ppermute x8, starting transfers between devices, ring_codes(): ahead = lax.ppermute(ahead, DP, forward)  8.57 us
    dot_general x2, matrix products, pair_gradient(): lax.dot_general(both_queries, jnp.concatenate([own, got], axis=0), (((0,)...  7.5 us
  transfers between devices with their start and end apart: 38, of which 19 were waited for; matrix products, arithmetic and copies ran while one was open for 9% of the time, Pallas kernels for 0%

profile of v7, /device:TPU:0, one launch (start us, length us, event | category | flops | bytes accessed | tf_op | source)
XLA Modules:
  0.0 293.9 jit_solution(7360804260059037582)
XLA Ops:
  7.2 4.9 %copy.23 = bf16[8,128,2048]{2,1,0:T(8,128)(2,1)} copy(bf16[8,128,2048]{2,1,0:T(8,128)(2,1)} %param.28) | data formatting | bytes 8388608
  14.8 1.2 collective-permute-done.2
  16.0 3.2 %fusion.26 = f32[1024,1024]{1,0:T(8,128)} fusion(bf16[256,1024]{1,0:T(8,128)(2,1)S(1)} %collective-permute-done.2, bf16[256,1024]{1,0:T(8,128)(2,1)S(1)} %get-tuple-element.43, bf16[256,1024]{0,1:T(8,128)(2,1)S(1)} %collective-permute-done, bf16[256,1024]{0,1:T(8,128)(2,1)S(1)} %bitcast.92), kind=kOutput, calls=%fused_computation.45 | convolution fusion | flops 1077936128 | bytes 6291456 | tf_op jit(solution)/shard_map/dot_general | solution.py:47
  22.7 7.3 %all-to-all-start = ((bf16[16,8,2048]{2,1,0:T(8,128)(2,1)}), bf16[16,8,2048]{2,1,0:T(8,128)(2,1)S(1)}, u32[]{:S(2)}, u32[]{:S(2)}) async-start(bf16[16,8,2048]{2,1,0:T(8,128)(2,1)} %select_bitcast_fusion), calls=%async_computation.2 | async-start | bytes 1048576 | tf_op jit(solution)/shard_map/all_to_all | solution.py:158
  31.0 1.1 collective-permute-done.1
  32.1 4.3 %fusion.22 = f32[1024,1024]{1,0:T(8,128)} fusion(bf16[256,1024]{1,0:T(8,128)(2,1)} %collective-permute-done.1, bf16[256,1024]{1,0:T(8,128)(2,1)S(1)} %get-tuple-element.44, bf16[256,1024]{0,1:T(8,128)(2,1)S(1)} %copy-done.10, bf16[256,1024]{0,1:T(8,128)(2,1)S(1)} %bitcast.93), kind=kOutput, calls=%fused_computation.41 | convolution fusion | flops 1077936128 | bytes 6291456 | tf_op jit(solution)/shard_map/dot_general | solution.py:47
  38.7 14.2 %all-to-all-done = bf16[16,8,2048]{2,1,0:T(8,128)(2,1)S(1)} async-done(((bf16[16,8,2048]{2,1,0:T(8,128)(2,1)}), bf16[16,8,2048]{2,1,0:T(8,128)(2,1)S(1)}, u32[]{:S(2)}, u32[]{:S(2)}) %all-to-all-start) | async-done | bytes 524320 | tf_op jit(solution)/shard_map/all_to_all | solution.py:158
  54.0 66.4 %reduce-scatter.5.cloned.1.call-done = f32[128,1024]{1,0:T(8,128)} async-done(((f32[1024,1024]{1,0:T(8,128)}), f32[128,1024]{1,0:T(8,128)}) %reduce-scatter.5.cloned.1.call-update) | async-done | bytes 524304 | tf_op jit(solution)/shard_map/reduce_scatter | solution.py:53
  120.4 2.2 fusion.130
  122.5 1.5 collective-permute-start.5
  124.9 5.8 %collective-permute-done.5 = bf16[128,1024]{1,0:T(8,128)(2,1)S(1)} collective-permute-done((bf16[128,1024]{1,0:T(8,128)(2,1)S(1)}, bf16[128,1024]{1,0:T(8,128)(2,1)S(1)}, u32[]{:S(2)}, u32[]{:S(2)}) %collective-permute-start.5) | collective-permute-done | bytes 262176 | tf_op jit(solution)/shard_map/ppermute | solution.py:109
  130.7 1.4 collective-permute-start.9
  133.6 16.4 %collective-permute-done.9 = bf16[128,1024]{1,0:T(8,128)(2,1)S(1)} collective-permute-done((bf16[128,1024]{1,0:T(8,128)(2,1)S(1)}, bf16[128,1024]{1,0:T(8,128)(2,1)S(1)}, u32[]{:S(2)}, u32[]{:S(2)}) %collective-permute-start.9) | collective-permute-done | bytes 262176 | tf_op jit(solution)/shard_map/ppermute | solution.py:109
  150.3 2.1 collective-permute-start.12
  153.4 11.2 %collective-permute-done.12 = bf16[128,1024]{1,0:T(8,128)(2,1)S(1)} collective-permute-done((bf16[128,1024]{1,0:T(8,128)(2,1)S(1)}, bf16[128,1024]{1,0:T(8,128)(2,1)S(1)}, u32[]{:S(2)}, u32[]{:S(2)}) %collective-permute-start.12) | collective-permute-done | bytes 262176 | tf_op jit(solution)/shard_map/ppermute | solution.py:105
  164.6 3.2 %collective-permute-start.16 = (bf16[128,1024]{1,0:T(8,128)(2,1)S(1)}, bf16[128,1024]{1,0:T(8,128)(2,1)S(1)}, u32[]{:S(2)}, u32[]{:S(2)}) collective-permute-start(bf16[128,1024]{1,0:T(8,128)(2,1)S(1)} %collective-permute-done.12), channel_id=1, source_target_pairs={{0,4},{1,5},{4,8},{5,9},{8,12},{9,13},{12,14},{13,15},{14,10},{15,... | collective-permute-start | bytes 786440 | tf_op jit(solution)/shard_map/ppermute | solution.py:105
  169.2 10.5 %collective-permute-done.16 = bf16[128,1024]{1,0:T(8,128)(2,1)S(1)} collective-permute-done((bf16[128,1024]{1,0:T(8,128)(2,1)S(1)}, bf16[128,1024]{1,0:T(8,128)(2,1)S(1)}, u32[]{:S(2)}, u32[]{:S(2)}) %collective-permute-start.16) | collective-permute-done | bytes 262176 | tf_op jit(solution)/shard_map/ppermute | solution.py:105
  183.3 8.2 %all-to-all-start.1 = ((bf16[16,8,1024]{2,1,0:T(8,128)(2,1)}), bf16[16,8,1024]{2,1,0:T(8,128)(2,1)S(1)}, u32[]{:S(2)}, u32[]{:S(2)}) async-start(bf16[16,8,1024]{2,1,0:T(8,128)(2,1)} %select_bitcast_fusion.2), calls=%async_computation.3 | async-start | bytes 524288 | tf_op jit(solution)/shard_map/all_to_all | solution.py:181
  191.6 10.0 %all-to-all-done.1 = bf16[16,8,1024]{2,1,0:T(8,128)(2,1)S(1)} async-done(((bf16[16,8,1024]{2,1,0:T(8,128)(2,1)}), bf16[16,8,1024]{2,1,0:T(8,128)(2,1)S(1)}, u32[]{:S(2)}, u32[]{:S(2)}) %all-to-all-start.1) | async-done | bytes 262176 | tf_op jit(solution)/shard_map/all_to_all | solution.py:181
  202.5 29.1 %reduce-scatter.3.cloned.1.call-done = f32[128,1024]{1,0:T(8,128)} async-done(((f32[1024,1024]{1,0:T(8,128)}), f32[128,1024]{1,0:T(8,128)}) %reduce-scatter.3.cloned.1.call-update) | async-done | bytes 524304 | tf_op jit(solution)/shard_map/reduce_scatter | solution.py:53
  231.7 2.9 %fusion.129 = (bf16[128,1024]{1,0:T(8,128)(2,1)S(1)}, f32[128,1024]{1,0:T(8,128)S(1)}, f32[128,1024]{1,0:T(8,128)S(1)}, f32[128,1024]{1,0:T(8,128)}, f32[128,1024]{1,0:T(8,128)S(1)}) fusion(f32[128,2048]{1,0:T(8,128)} %param.22, f32[128,2048]{1,0:T(8,128)} %param.19, f32[128,1024]{1,0:T(8,128)} %reduce-scatter.3.cloned.1.call-done, f32[128,2048]{1,0:T(8,128)} %param.20, ...), kind=kLoop, calls=%fused_computation.222 | loop fusion | flops 2621440 | bytes 4980736 | tf_op jit(solution)/shard_map/convert_element_type | solution.py:179
  234.6 1.5 collective-permute-start.20
  238.9 3.7 %collective-permute-done.20 = bf16[128,1024]{1,0:T(8,128)(2,1)S(1)} collective-permute-done((bf16[128,1024]{1,0:T(8,128)(2,1)S(1)}, bf16[128,1024]{1,0:T(8,128)(2,1)S(1)}, u32[]{:S(2)}, u32[]{:S(2)}) %collective-permute-start.20) | collective-permute-done | bytes 262176 | tf_op jit(solution)/shard_map/ppermute | solution.py:109
  242.7 1.5 collective-permute-start.24
  245.6 4.2 %collective-permute-done.24 = bf16[128,1024]{1,0:T(8,128)(2,1)S(1)} collective-permute-done((bf16[128,1024]{1,0:T(8,128)(2,1)S(1)}, bf16[128,1024]{1,0:T(8,128)(2,1)S(1)}, u32[]{:S(2)}, u32[]{:S(2)}) %collective-permute-start.24) | collective-permute-done | bytes 262176 | tf_op jit(solution)/shard_map/ppermute | solution.py:109
  249.9 1.5 collective-permute-start.28
  251.4 1.5 collective-permute-done.23
  254.5 6.4 %collective-permute-done.27 = bf16[128,1024]{1,0:T(8,128)(2,1)S(1)} collective-permute-done((bf16[128,1024]{1,0:T(8,128)(2,1)S(1)}, bf16[128,1024]{1,0:T(8,128)(2,1)S(1)}, u32[]{:S(2)}, u32[]{:S(2)}) %collective-permute-start.27) | collective-permute-done | bytes 262176 | tf_op jit(solution)/shard_map/ppermute | solution.py:105
  262.9 5.0 %collective-permute-done.31 = bf16[128,1024]{1,0:T(8,128)(2,1)S(1)} collective-permute-done((bf16[128,1024]{1,0:T(8,128)(2,1)S(1)}, bf16[128,1024]{1,0:T(8,128)(2,1)S(1)}, u32[]{:S(2)}, u32[]{:S(2)}) %collective-permute-start.31) | collective-permute-done | bytes 262176 | tf_op jit(solution)/shard_map/ppermute | solution.py:105
  271.5 3.7 %all-to-all-start.2 = ((bf16[16,8,1024]{2,1,0:T(8,128)(2,1)}), bf16[16,8,1024]{2,1,0:T(8,128)(2,1)S(1)}, u32[]{:S(2)}, u32[]{:S(2)}) async-start(bf16[16,8,1024]{2,1,0:T(8,128)(2,1)} %select_bitcast_fusion.1), calls=%async_computation.4 | async-start | bytes 524288 | tf_op jit(solution)/shard_map/all_to_all | solution.py:181
  275.2 1.1 pad_maximum_fusion.2
  277.3 7.9 %all-to-all-done.2 = bf16[16,8,1024]{2,1,0:T(8,128)(2,1)S(1)} async-done(((bf16[16,8,1024]{2,1,0:T(8,128)(2,1)}), bf16[16,8,1024]{2,1,0:T(8,128)(2,1)S(1)}, u32[]{:S(2)}, u32[]{:S(2)}) %all-to-all-start.2) | async-done | bytes 262176 | tf_op jit(solution)/shard_map/all_to_all | solution.py:181
  (165 shorter events, 33.1 us)
Async XLA Ops:
  7.2 113.2 %reduce-scatter.5.cloned.1.call-start = ((), (), s32[]{:S(2)}) async-start(), calls=%async_computation.6 | async-start | bytes 4718592 | tf_op jit(solution)/shard_map/reduce_scatter | solution.py:53
  22.7 30.3 %all-to-all-start = ((bf16[16,8,2048]{2,1,0:T(8,128)(2,1)}), bf16[16,8,2048]{2,1,0:T(8,128)(2,1)S(1)}, u32[]{:S(2)}, u32[]{:S(2)}) async-start(bf16[16,8,2048]{2,1,0:T(8,128)(2,1)} %select_bitcast_fusion), calls=%async_computation.2 | async-start | bytes 1048576 | tf_op jit(solution)/shard_map/all_to_all | solution.py:158
  30.0 201.7 %reduce-scatter.3.cloned.1.call-start = ((), (), s32[]{:S(2)}) async-start(), calls=%async_computation.5 | async-start | bytes 4718592 | tf_op jit(solution)/shard_map/reduce_scatter | solution.py:53
  122.5 8.2 %collective-permute-start.5 = (bf16[128,1024]{1,0:T(8,128)(2,1)S(1)}, bf16[128,1024]{1,0:T(8,128)(2,1)S(1)}, u32[]{:S(2)}, u32[]{:S(2)}) collective-permute-start(bf16[128,1024]{1,0:T(8,128)(2,1)S(1)} %get-tuple-element.32), channel_id=1, source_target_pairs={{0,2},{1,3},{4,0},{5,1},{8,4},{9,5},{12,8},{13,9},{14,12},{15,13},... | collective-permute-start | bytes 786440 | tf_op jit(solution)/shard_map/ppermute | solution.py:109
  124.1 8.1 %collective-permute-start.4 = (bf16[128,1024]{1,0:T(8,128)(2,1)S(1)}, bf16[128,1024]{1,0:T(8,128)(2,1)S(1)}, u32[]{:S(2)}, u32[]{:S(2)}) collective-permute-start(bf16[128,1024]{1,0:T(8,128)(2,1)S(1)} %get-tuple-element.32), channel_id=1, source_target_pairs={{0,4},{1,5},{4,8},{5,9},{8,12},{9,13},{12,14},{13,15},{14,10},{15,... | collective-permute-start | bytes 786440 | tf_op jit(solution)/shard_map/ppermute | solution.py:105
  124.6 8.6 %collective-permute-start.3 = (bf16[128,1024]{1,0:T(8,128)(2,1)S(1)}, bf16[128,1024]{1,0:T(8,128)(2,1)S(1)}, u32[]{:S(2)}, u32[]{:S(2)}) collective-permute-start(bf16[128,1024]{1,0:T(8,128)(2,1)S(1)} %get-tuple-element.32), channel_id=1, source_target_pairs={{0,1},{1,0},{2,3},{3,2},{4,5},{5,4},{6,7},{7,6},{8,9},{9,8},{10,11... | collective-permute-start | bytes 786440 | tf_op jit(solution)/shard_map/ppermute | solution.py:101
  130.7 19.4 %collective-permute-start.9 = (bf16[128,1024]{1,0:T(8,128)(2,1)S(1)}, bf16[128,1024]{1,0:T(8,128)(2,1)S(1)}, u32[]{:S(2)}, u32[]{:S(2)}) collective-permute-start(bf16[128,1024]{1,0:T(8,128)(2,1)S(1)} %collective-permute-done.5), channel_id=1, source_target_pairs={{0,2},{1,3},{4,0},{5,1},{8,4},{9,5},{12,8},{13,9},{14,12},{15,13},... | collective-permute-start | bytes 786440 | tf_op jit(solution)/shard_map/ppermute | solution.py:109
  132.2 20.5 %collective-permute-start.7 = (bf16[128,1024]{1,0:T(8,128)(2,1)S(1)}, bf16[128,1024]{1,0:T(8,128)(2,1)S(1)}, u32[]{:S(2)}, u32[]{:S(2)}) collective-permute-start(bf16[128,1024]{1,0:T(8,128)(2,1)S(1)} %collective-permute-done.5), channel_id=1, source_target_pairs={{0,1},{1,0},{2,3},{3,2},{4,5},{5,4},{6,7},{7,6},{8,9},{9,8},{10,11... | collective-permute-start | bytes 786440 | tf_op jit(solution)/shard_map/ppermute | solution.py:101
  132.2 18.1 %collective-permute-start.8 = (bf16[128,1024]{1,0:T(8,128)(2,1)S(1)}, bf16[128,1024]{1,0:T(8,128)(2,1)S(1)}, u32[]{:S(2)}, u32[]{:S(2)}) collective-permute-start(bf16[128,1024]{1,0:T(8,128)(2,1)S(1)} %collective-permute-done.4), channel_id=1, source_target_pairs={{0,4},{1,5},{4,8},{5,9},{8,12},{9,13},{12,14},{13,15},{14,10},{15,... | collective-permute-start | bytes 786440 | tf_op jit(solution)/shard_map/ppermute | solution.py:105
  132.7 20.4 %collective-permute-start.6 = (bf16[128,1024]{1,0:T(8,128)(2,1)S(1)}, bf16[128,1024]{1,0:T(8,128)(2,1)S(1)}, u32[]{:S(2)}, u32[]{:S(2)}) collective-permute-start(bf16[128,1024]{1,0:T(8,128)(2,1)S(1)} %collective-permute-done.4), channel_id=1, source_target_pairs={{0,1},{1,0},{2,3},{3,2},{4,5},{5,4},{6,7},{7,6},{8,9},{9,8},{10,11... | collective-permute-start | bytes 786440 | tf_op jit(solution)/shard_map/ppermute | solution.py:101
  150.1 17.7 %collective-permute-start.13 = (bf16[128,1024]{1,0:T(8,128)(2,1)S(1)}, bf16[128,1024]{1,0:T(8,128)(2,1)S(1)}, u32[]{:S(2)}, u32[]{:S(2)}) collective-permute-start(bf16[128,1024]{1,0:T(8,128)(2,1)S(1)} %collective-permute-done.9), channel_id=1, source_target_pairs={{0,2},{1,3},{4,0},{5,1},{8,4},{9,5},{12,8},{13,9},{14,12},{15,13},... | collective-permute-start | bytes 786440 | tf_op jit(solution)/shard_map/ppermute | solution.py:109
  150.1 18.6 %collective-permute-start.11 = (bf16[128,1024]{1,0:T(8,128)(2,1)S(1)}, bf16[128,1024]{1,0:T(8,128)(2,1)S(1)}, u32[]{:S(2)}, u32[]{:S(2)}) collective-permute-start(bf16[128,1024]{1,0:T(8,128)(2,1)S(1)} %collective-permute-done.9), channel_id=1, source_target_pairs={{0,1},{1,0},{2,3},{3,2},{4,5},{5,4},{6,7},{7,6},{8,9},{9,8},{10,11... | collective-permute-start | bytes 786440 | tf_op jit(solution)/shard_map/ppermute | solution.py:101
  150.3 14.3 %collective-permute-start.12 = (bf16[128,1024]{1,0:T(8,128)(2,1)S(1)}, bf16[128,1024]{1,0:T(8,128)(2,1)S(1)}, u32[]{:S(2)}, u32[]{:S(2)}) collective-permute-start(bf16[128,1024]{1,0:T(8,128)(2,1)S(1)} %collective-permute-done.8), channel_id=1, source_target_pairs={{0,4},{1,5},{4,8},{5,9},{8,12},{9,13},{12,14},{13,15},{14,10},{15,... | collective-permute-start | bytes 786440 | tf_op jit(solution)/shard_map/ppermute | solution.py:105
  152.6 16.3 %collective-permute-start.10 = (bf16[128,1024]{1,0:T(8,128)(2,1)S(1)}, bf16[128,1024]{1,0:T(8,128)(2,1)S(1)}, u32[]{:S(2)}, u32[]{:S(2)}) collective-permute-start(bf16[128,1024]{1,0:T(8,128)(2,1)S(1)} %collective-permute-done.8), channel_id=1, source_target_pairs={{0,1},{1,0},{2,3},{3,2},{4,5},{5,4},{6,7},{7,6},{8,9},{9,8},{10,11... | collective-permute-start | bytes 786440 | tf_op jit(solution)/shard_map/ppermute | solution.py:101
  164.6 15.1 %collective-permute-start.16 = (bf16[128,1024]{1,0:T(8,128)(2,1)S(1)}, bf16[128,1024]{1,0:T(8,128)(2,1)S(1)}, u32[]{:S(2)}, u32[]{:S(2)}) collective-permute-start(bf16[128,1024]{1,0:T(8,128)(2,1)S(1)} %collective-permute-done.12), channel_id=1, source_target_pairs={{0,4},{1,5},{4,8},{5,9},{8,12},{9,13},{12,14},{13,15},{14,10},{15,... | collective-permute-start | bytes 786440 | tf_op jit(solution)/shard_map/ppermute | solution.py:105
  167.8 12.4 %collective-permute-start.14 = (bf16[128,1024]{1,0:T(8,128)(2,1)S(1)}, bf16[128,1024]{1,0:T(8,128)(2,1)S(1)}, u32[]{:S(2)}, u32[]{:S(2)}) collective-permute-start(bf16[128,1024]{1,0:T(8,128)(2,1)S(1)} %collective-permute-done.12), channel_id=1, source_target_pairs={{0,1},{1,0},{2,3},{3,2},{4,5},{5,4},{6,7},{7,6},{8,9},{9,8},{10,11... | collective-permute-start | bytes 786440 | tf_op jit(solution)/shard_map/ppermute | solution.py:101
  167.8 12.1 %collective-permute-start.15 = (bf16[128,1024]{1,0:T(8,128)(2,1)S(1)}, bf16[128,1024]{1,0:T(8,128)(2,1)S(1)}, u32[]{:S(2)}, u32[]{:S(2)}) collective-permute-start(bf16[128,1024]{1,0:T(8,128)(2,1)S(1)} %collective-permute-done.13), channel_id=1, source_target_pairs={{0,1},{1,0},{2,3},{3,2},{4,5},{5,4},{6,7},{7,6},{8,9},{9,8},{10,11... | collective-permute-start | bytes 786440 | tf_op jit(solution)/shard_map/ppermute | solution.py:101
  183.3 18.3 %all-to-all-start.1 = ((bf16[16,8,1024]{2,1,0:T(8,128)(2,1)}), bf16[16,8,1024]{2,1,0:T(8,128)(2,1)S(1)}, u32[]{:S(2)}, u32[]{:S(2)}) async-start(bf16[16,8,1024]{2,1,0:T(8,128)(2,1)} %select_bitcast_fusion.2), calls=%async_computation.3 | async-start | bytes 524288 | tf_op jit(solution)/shard_map/all_to_all | solution.py:181
  234.6 8.1 %collective-permute-start.20 = (bf16[128,1024]{1,0:T(8,128)(2,1)S(1)}, bf16[128,1024]{1,0:T(8,128)(2,1)S(1)}, u32[]{:S(2)}, u32[]{:S(2)}) collective-permute-start(bf16[128,1024]{1,0:T(8,128)(2,1)S(1)} %get-tuple-element.27), channel_id=1, source_target_pairs={{0,2},{1,3},{4,0},{5,1},{8,4},{9,5},{12,8},{13,9},{14,12},{15,13},... | collective-permute-start | bytes 786440 | tf_op jit(solution)/shard_map/ppermute | solution.py:109
  236.1 8.1 %collective-permute-start.19 = (bf16[128,1024]{1,0:T(8,128)(2,1)S(1)}, bf16[128,1024]{1,0:T(8,128)(2,1)S(1)}, u32[]{:S(2)}, u32[]{:S(2)}) collective-permute-start(bf16[128,1024]{1,0:T(8,128)(2,1)S(1)} %get-tuple-element.27), channel_id=1, source_target_pairs={{0,4},{1,5},{4,8},{5,9},{8,12},{9,13},{12,14},{13,15},{14,10},{15,... | collective-permute-start | bytes 786440 | tf_op jit(solution)/shard_map/ppermute | solution.py:105
  236.6 8.5 %collective-permute-start.18 = (bf16[128,1024]{1,0:T(8,128)(2,1)S(1)}, bf16[128,1024]{1,0:T(8,128)(2,1)S(1)}, u32[]{:S(2)}, u32[]{:S(2)}) collective-permute-start(bf16[128,1024]{1,0:T(8,128)(2,1)S(1)} %get-tuple-element.27), channel_id=1, source_target_pairs={{0,1},{1,0},{2,3},{3,2},{4,5},{5,4},{6,7},{7,6},{8,9},{9,8},{10,11... | collective-permute-start | bytes 786440 | tf_op jit(solution)/shard_map/ppermute | solution.py:101
  242.7 7.2 %collective-permute-start.24 = (bf16[128,1024]{1,0:T(8,128)(2,1)S(1)}, bf16[128,1024]{1,0:T(8,128)(2,1)S(1)}, u32[]{:S(2)}, u32[]{:S(2)}) collective-permute-start(bf16[128,1024]{1,0:T(8,128)(2,1)S(1)} %collective-permute-done.20), channel_id=1, source_target_pairs={{0,2},{1,3},{4,0},{5,1},{8,4},{9,5},{12,8},{13,9},{14,12},{15,13},... | collective-permute-start | bytes 786440 | tf_op jit(solution)/shard_map/ppermute | solution.py:109
  244.2 9.7 %collective-permute-start.22 = (bf16[128,1024]{1,0:T(8,128)(2,1)S(1)}, bf16[128,1024]{1,0:T(8,128)(2,1)S(1)}, u32[]{:S(2)}, u32[]{:S(2)}) collective-permute-start(bf16[128,1024]{1,0:T(8,128)(2,1)S(1)} %collective-permute-done.20), channel_id=1, source_target_pairs={{0,1},{1,0},{2,3},{3,2},{4,5},{5,4},{6,7},{7,6},{8,9},{9,8},{10,11... | collective-permute-start | bytes 786440 | tf_op jit(solution)/shard_map/ppermute | solution.py:101
  244.2 8.7 %collective-permute-start.23 = (bf16[128,1024]{1,0:T(8,128)(2,1)S(1)}, bf16[128,1024]{1,0:T(8,128)(2,1)S(1)}, u32[]{:S(2)}, u32[]{:S(2)}) collective-permute-start(bf16[128,1024]{1,0:T(8,128)(2,1)S(1)} %collective-permute-done.19), channel_id=1, source_target_pairs={{0,4},{1,5},{4,8},{5,9},{8,12},{9,13},{12,14},{13,15},{14,10},{15,... | collective-permute-start | bytes 786440 | tf_op jit(solution)/shard_map/ppermute | solution.py:105
  244.7 9.5 %collective-permute-start.21 = (bf16[128,1024]{1,0:T(8,128)(2,1)S(1)}, bf16[128,1024]{1,0:T(8,128)(2,1)S(1)}, u32[]{:S(2)}, u32[]{:S(2)}) collective-permute-start(bf16[128,1024]{1,0:T(8,128)(2,1)S(1)} %collective-permute-done.19), channel_id=1, source_target_pairs={{0,1},{1,0},{2,3},{3,2},{4,5},{5,4},{6,7},{7,6},{8,9},{9,8},{10,11... | collective-permute-start | bytes 786440 | tf_op jit(solution)/shard_map/ppermute | solution.py:101
  249.9 11.7 %collective-permute-start.28 = (bf16[128,1024]{1,0:T(8,128)(2,1)S(1)}, bf16[128,1024]{1,0:T(8,128)(2,1)S(1)}, u32[]{:S(2)}, u32[]{:S(2)}) collective-permute-start(bf16[128,1024]{1,0:T(8,128)(2,1)S(1)} %collective-permute-done.24), channel_id=1, source_target_pairs={{0,2},{1,3},{4,0},{5,1},{8,4},{9,5},{12,8},{13,9},{14,12},{15,13},... | collective-permute-start | bytes 786440 | tf_op jit(solution)/shard_map/ppermute | solution.py:109
  251.4 11.0 %collective-permute-start.26 = (bf16[128,1024]{1,0:T(8,128)(2,1)S(1)}, bf16[128,1024]{1,0:T(8,128)(2,1)S(1)}, u32[]{:S(2)}, u32[]{:S(2)}) collective-permute-start(bf16[128,1024]{1,0:T(8,128)(2,1)S(1)} %collective-permute-done.24), channel_id=1, source_target_pairs={{0,1},{1,0},{2,3},{3,2},{4,5},{5,4},{6,7},{7,6},{8,9},{9,8},{10,11... | collective-permute-start | bytes 786440 | tf_op jit(solution)/shard_map/ppermute | solution.py:101
  252.9 7.9 %collective-permute-start.27 = (bf16[128,1024]{1,0:T(8,128)(2,1)S(1)}, bf16[128,1024]{1,0:T(8,128)(2,1)S(1)}, u32[]{:S(2)}, u32[]{:S(2)}) collective-permute-start(bf16[128,1024]{1,0:T(8,128)(2,1)S(1)} %collective-permute-done.23), channel_id=1, source_target_pairs={{0,4},{1,5},{4,8},{5,9},{8,12},{9,13},{12,14},{13,15},{14,10},{15,... | collective-permute-start | bytes 786440 | tf_op jit(solution)/shard_map/ppermute | solution.py:105
  253.9 8.7 %collective-permute-start.25 = (bf16[128,1024]{1,0:T(8,128)(2,1)S(1)}, bf16[128,1024]{1,0:T(8,128)(2,1)S(1)}, u32[]{:S(2)}, u32[]{:S(2)}) collective-permute-start(bf16[128,1024]{1,0:T(8,128)(2,1)S(1)} %collective-permute-done.23), channel_id=1, source_target_pairs={{0,1},{1,0},{2,3},{3,2},{4,5},{5,4},{6,7},{7,6},{8,9},{9,8},{10,11... | collective-permute-start | bytes 786440 | tf_op jit(solution)/shard_map/ppermute | solution.py:101
  260.8 7.0 %collective-permute-start.31 = (bf16[128,1024]{1,0:T(8,128)(2,1)S(1)}, bf16[128,1024]{1,0:T(8,128)(2,1)S(1)}, u32[]{:S(2)}, u32[]{:S(2)}) collective-permute-start(bf16[128,1024]{1,0:T(8,128)(2,1)S(1)} %collective-permute-done.27), channel_id=1, source_target_pairs={{0,4},{1,5},{4,8},{5,9},{8,12},{9,13},{12,14},{13,15},{14,10},{15,... | collective-permute-start | bytes 786440 | tf_op jit(solution)/shard_map/ppermute | solution.py:105
  261.4 7.0 %collective-permute-start.29 = (bf16[128,1024]{1,0:T(8,128)(2,1)S(1)}, bf16[128,1024]{1,0:T(8,128)(2,1)S(1)}, u32[]{:S(2)}, u32[]{:S(2)}) collective-permute-start(bf16[128,1024]{1,0:T(8,128)(2,1)S(1)} %collective-permute-done.27), channel_id=1, source_target_pairs={{0,1},{1,0},{2,3},{3,2},{4,5},{5,4},{6,7},{7,6},{8,9},{9,8},{10,11... | collective-permute-start | bytes 786440 | tf_op jit(solution)/shard_map/ppermute | solution.py:101
  271.5 13.7 %all-to-all-start.2 = ((bf16[16,8,1024]{2,1,0:T(8,128)(2,1)}), bf16[16,8,1024]{2,1,0:T(8,128)(2,1)S(1)}, u32[]{:S(2)}, u32[]{:S(2)}) async-start(bf16[16,8,1024]{2,1,0:T(8,128)(2,1)} %select_bitcast_fusion.1), calls=%async_computation.4 | async-start | bytes 524288 | tf_op jit(solution)/shard_map/all_to_all | solution.py:181
  (17 other events, 77.5 us)
Sparse Core Ops, SparseCore 0:
  19.4 100.9 reduce-scatter.4
  124.4 107.1 reduce-scatter.2

commit v8 on v6

--- a/solution.py
+++ b/solution.py
@@ -178,13 +178,14 @@
         )
         codes = ring_codes(updated[3].astype(jnp.bfloat16), encoded_rows)
         normed = batch_norm(codes.astype(jnp.bfloat16), bn_gain[cut], bn_shift[cut])
-        returned = lax.all_to_all(
-            jnp.take(normed, send_back, axis=0), DP, split_axis=0, concat_axis=0, tiled=True
-        )
-        results.append(updated + (jnp.take(returned, receive_back, axis=0),))
-    new_params, new_first, new_second, new_key, restored = (
+        results.append(updated + (normed,))
+    new_params, new_first, new_second, new_key, normed = (
         jnp.concatenate(parts, axis=1) for parts in zip(*results)
     )
+    returned = lax.all_to_all(
+        jnp.take(normed, send_back, axis=0), DP, split_axis=0, concat_axis=0, tiled=True
+    )
+    restored = jnp.take(returned, receive_back, axis=0)
     new_queue = lax.dynamic_update_slice(
         queue, restored[None], (slot[0], jnp.int32(0), jnp.int32(0))
     )

time: 244 us -> 244 us (level)
  waiting for transfers between devices: 139 us -> 145 us
  starting transfers between devices: 41.7 us -> 36.6 us
    reduce_scatter x2, waiting for transfers between devices: 25.3 us -> 35.4 us  [pair_gradient(): lax.psum_scatter(partial, ('zo', 'c'), scatter_dimension=0, tiled=True)]
    all_to_all x2 -> x1, waiting for transfers between devices: 17.9 us -> 9.11 us  [per_device(): lax.all_to_all(jnp.take(normed, send_back, axis=0), DP, split_axis=0, con...]
    all_to_all x2 -> x1, starting transfers between devices: 9.59 us -> 3.78 us  [per_device(): lax.all_to_all(jnp.take(normed, send_back, axis=0), DP, split_axis=0, con...]
    ppermute x6, starting transfers between devices: 3.63 us -> 9.23 us  [ring_codes(): behind = lax.ppermute(behind, DP, backward)]
    ppermute x8, starting transfers between devices: 14 us -> 8.77 us  [ring_codes(): ahead = lax.ppermute(ahead, DP, forward)]
    concatenate x4 -> x5, other arithmetic: 4.17 us -> 5.36 us  [per_device(): jnp.concatenate(parts, axis=1)]
    unnamed x18 -> x22, local copies, waits for them, and re-layouts: 4.98 us -> 4.99 us
  transfers between devices with their start and end apart: 38 -> 37, of which waited for: 19 -> 19; matrix products, arithmetic and copies ran while one was open for 12% -> 11% of each run, Pallas kernels for 0% -> 0%
where the time goes in v8:
time: 244 us; the launch traced here: 243 us
  waiting for transfers between devices  145 us (59%)
  starting transfers between devices  36.6 us (15%)
  other arithmetic  16.6 us (7%)
  between operations  15.8 us (6%)
  local copies, waits for them, and re-layouts  15 us (6%)
  matrix products  14.7 us (6%)
    ppermute x8, waiting for transfers between devices, ring_codes(): ahead = lax.ppermute(ahead, DP, forward)  36.4 us
    reduce_scatter x2, waiting for transfers between devices, pair_gradient(): lax.psum_scatter(partial, ('zo', 'c'), scatter_dimension=0, tiled=True)  35.4 us
    ppermute x6, waiting for transfers between devices, ring_codes(): behind = lax.ppermute(behind, DP, backward)  25.3 us
    ppermute x2, waiting for transfers between devices, pair_gradient(): lax.ppermute((theirs, grad_out[:, :half]), 'xl', swap)  19.9 us
    ppermute x1, waiting for transfers between devices, pair_gradient(): got_second = lax.ppermute(grad_out[:, half:], 'xl', swap)  16.9 us
    ppermute x6, starting transfers between devices, ring_codes(): behind = lax.ppermute(behind, DP, backward)  9.23 us
    all_to_all x1, waiting for transfers between devices, per_device(): lax.all_to_all(jnp.take(normed, send_back, axis=0), DP, split_axis=0, con...  9.11 us
    ppermute x8, starting transfers between devices, ring_codes(): ahead = lax.ppermute(ahead, DP, forward)  8.77 us
  transfers between devices with their start and end apart: 37, of which 19 were waited for; matrix products, arithmetic and copies ran while one was open for 11% of the time, Pallas kernels for 0%

profile of v8, /device:TPU:0, one launch (start us, length us, event | category | flops | bytes accessed | tf_op | source)
XLA Modules:
  0.0 243.5 jit_solution(13859270903878770513)
XLA Ops:
  7.2 4.9 %copy.22 = bf16[8,128,2048]{2,1,0:T(8,128)(2,1)} copy(bf16[8,128,2048]{2,1,0:T(8,128)(2,1)} %param.26) | data formatting | bytes 8388608
  14.8 2.9 %collective-permute-start = (bf16[256,1024]{1,0:T(8,128)(2,1)}, bf16[256,1024]{1,0:T(8,128)(2,1)}, u32[]{:S(2)}, u32[]{:S(2)}) collective-permute-start(bf16[256,1024]{1,0:T(8,128)(2,1)} %reshape.206), channel_id=1, source_target_pairs={{0,2},{2,0},{1,3},{3,1},{4,6},{6,4},{5,7},{7,5},{8,10},{10,8},{9,1... | collective-permute-start | bytes 1572872 | tf_op jit(solution)/shard_map/ppermute | solution.py:42
  17.7 2.1 fusion.134
  20.2 10.6 %collective-permute-done = bf16[256,1024]{1,0:T(8,128)(2,1)} collective-permute-done((bf16[256,1024]{1,0:T(8,128)(2,1)}, bf16[256,1024]{1,0:T(8,128)(2,1)}, u32[]{:S(2)}, u32[]{:S(2)}) %collective-permute-start) | collective-permute-done | bytes 524320 | tf_op jit(solution)/shard_map/ppermute | solution.py:42
  31.9 9.3 %collective-permute-done.2 = bf16[256,1024]{1,0:T(8,128)(2,1)} collective-permute-done((bf16[256,1024]{1,0:T(8,128)(2,1)}, bf16[256,1024]{1,0:T(8,128)(2,1)}, u32[]{:S(2)}, u32[]{:S(2)}) %collective-permute-start.2) | collective-permute-done | bytes 524320 | tf_op jit(solution)/shard_map/ppermute | solution.py:42
  41.2 4.4 %fusion.26 = f32[1024,1024]{1,0:T(8,128)} fusion(bf16[512,1024]{1,0:T(8,128)(2,1)S(1)} %constant_dynamic-update-slice_fusion, bf16[256,1024]{1,0:T(8,128)(2,1)} %collective-permute-done.2, bf16[256,1024]{1,0:T(8,128)(2,1)} %get-tuple-element.42), kind=kOutput, calls=%fused_computation.42 | convolution fusion | flops 1075838976 | bytes 6291456 | tf_op jit(solution)/shard_map/dot_general | solution.py:47
  48.4 6.2 %all-to-all-start = ((bf16[16,8,2048]{2,1,0:T(8,128)(2,1)}), bf16[16,8,2048]{2,1,0:T(8,128)(2,1)S(1)}, u32[]{:S(2)}, u32[]{:S(2)}) async-start(bf16[16,8,2048]{2,1,0:T(8,128)(2,1)} %select_bitcast_fusion.1), calls=%async_computation.2 | async-start | bytes 1048576 | tf_op jit(solution)/shard_map/all_to_all | solution.py:158
  54.6 2.0 collective-permute-start.1
  56.9 16.9 %collective-permute-done.1 = bf16[256,1024]{1,0:T(8,128)(2,1)S(1)} collective-permute-done((bf16[256,1024]{1,0:T(8,128)(2,1)S(1)}, bf16[256,1024]{1,0:T(8,128)(2,1)S(1)}, u32[]{:S(2)}, u32[]{:S(2)}) %collective-permute-start.1) | collective-permute-done | bytes 524320 | tf_op jit(solution)/shard_map/ppermute | solution.py:43
  73.9 3.3 %fusion.22 = f32[1024,1024]{1,0:T(8,128)} fusion(bf16[512,1024]{1,0:T(8,128)(2,1)S(1)} %constant_dynamic-update-slice_fusion, bf16[256,1024]{1,0:T(8,128)(2,1)S(1)} %collective-permute-done.1, bf16[256,1024]{1,0:T(8,128)(2,1)S(1)} %get-tuple-element.43), kind=kOutput, calls=%fused_computation.38 | convolution fusion | flops 1075838976 | bytes 6291456 | tf_op jit(solution)/shard_map/dot_general | solution.py:47
  80.8 25.0 %reduce-scatter.5.cloned.1.call-done = f32[128,1024]{1,0:T(8,128)} async-done(((f32[1024,1024]{1,0:T(8,128)}), f32[128,1024]{1,0:T(8,128)}) %reduce-scatter.5.cloned.1.call-update) | async-done | bytes 524304 | tf_op jit(solution)/shard_map/reduce_scatter | solution.py:53
  105.8 2.2 fusion.129
  107.9 1.5 collective-permute-start.5
  111.0 6.0 %collective-permute-done.5 = bf16[128,1024]{1,0:T(8,128)(2,1)S(1)} collective-permute-done((bf16[128,1024]{1,0:T(8,128)(2,1)S(1)}, bf16[128,1024]{1,0:T(8,128)(2,1)S(1)}, u32[]{:S(2)}, u32[]{:S(2)}) %collective-permute-start.5) | collective-permute-done | bytes 262176 | tf_op jit(solution)/shard_map/ppermute | solution.py:109
  118.8 2.5 %collective-permute-start.8 = (bf16[128,1024]{1,0:T(8,128)(2,1)S(1)}, bf16[128,1024]{1,0:T(8,128)(2,1)S(1)}, u32[]{:S(2)}, u32[]{:S(2)}) collective-permute-start(bf16[128,1024]{1,0:T(8,128)(2,1)S(1)} %collective-permute-done.4), channel_id=1, source_target_pairs={{0,4},{1,5},{4,8},{5,9},{8,12},{9,13},{12,14},{13,15},{14,10},{15,... | collective-permute-start | bytes 786440 | tf_op jit(solution)/shard_map/ppermute | solution.py:105
  121.9 9.7 %collective-permute-done.9 = bf16[128,1024]{1,0:T(8,128)(2,1)S(1)} collective-permute-done((bf16[128,1024]{1,0:T(8,128)(2,1)S(1)}, bf16[128,1024]{1,0:T(8,128)(2,1)S(1)}, u32[]{:S(2)}, u32[]{:S(2)}) %collective-permute-start.9) | collective-permute-done | bytes 262176 | tf_op jit(solution)/shard_map/ppermute | solution.py:109
  133.2 2.5 %collective-permute-start.12 = (bf16[128,1024]{1,0:T(8,128)(2,1)S(1)}, bf16[128,1024]{1,0:T(8,128)(2,1)S(1)}, u32[]{:S(2)}, u32[]{:S(2)}) collective-permute-start(bf16[128,1024]{1,0:T(8,128)(2,1)S(1)} %collective-permute-done.8), channel_id=1, source_target_pairs={{0,4},{1,5},{4,8},{5,9},{8,12},{9,13},{12,14},{13,15},{14,10},{15,... | collective-permute-start | bytes 786440 | tf_op jit(solution)/shard_map/ppermute | solution.py:105
  136.5 11.2 %collective-permute-done.12 = bf16[128,1024]{1,0:T(8,128)(2,1)S(1)} collective-permute-done((bf16[128,1024]{1,0:T(8,128)(2,1)S(1)}, bf16[128,1024]{1,0:T(8,128)(2,1)S(1)}, u32[]{:S(2)}, u32[]{:S(2)}) %collective-permute-start.12) | collective-permute-done | bytes 262176 | tf_op jit(solution)/shard_map/ppermute | solution.py:105
  147.7 2.5 %collective-permute-start.16 = (bf16[128,1024]{1,0:T(8,128)(2,1)S(1)}, bf16[128,1024]{1,0:T(8,128)(2,1)S(1)}, u32[]{:S(2)}, u32[]{:S(2)}) collective-permute-start(bf16[128,1024]{1,0:T(8,128)(2,1)S(1)} %collective-permute-done.12), channel_id=1, source_target_pairs={{0,4},{1,5},{4,8},{5,9},{8,12},{9,13},{12,14},{13,15},{14,10},{15,... | collective-permute-start | bytes 786440 | tf_op jit(solution)/shard_map/ppermute | solution.py:105
  151.6 10.3 %collective-permute-done.16 = bf16[128,1024]{1,0:T(8,128)(2,1)S(1)} collective-permute-done((bf16[128,1024]{1,0:T(8,128)(2,1)S(1)}, bf16[128,1024]{1,0:T(8,128)(2,1)S(1)}, u32[]{:S(2)}, u32[]{:S(2)}) %collective-permute-start.16) | collective-permute-done | bytes 262176 | tf_op jit(solution)/shard_map/ppermute | solution.py:105
  163.9 10.4 %reduce-scatter.3.cloned.1.call-done = f32[128,1024]{1,0:T(8,128)} async-done(((f32[1024,1024]{1,0:T(8,128)}), f32[128,1024]{1,0:T(8,128)}) %reduce-scatter.3.cloned.1.call-update) | async-done | bytes 524304 | tf_op jit(solution)/shard_map/reduce_scatter | solution.py:53
  174.3 3.4 %fusion.128 = (bf16[128,1024]{1,0:T(8,128)(2,1)S(1)}, f32[128,1024]{1,0:T(8,128)}, f32[128,1024]{1,0:T(8,128)}, f32[128,1024]{1,0:T(8,128)}, f32[128,1024]{1,0:T(8,128)}) fusion(f32[128,2048]{1,0:T(8,128)} %param.20, f32[128,2048]{1,0:T(8,128)} %param.17, f32[128,1024]{1,0:T(8,128)} %reduce-scatter.3.cloned.1.call-done, f32[128,2048]{1,0:T(8,128)} %param.18, ...), kind=kLoop, calls=%fused_computation.218 | loop fusion | flops 2621440 | bytes 4980736 | tf_op jit(solution)/shard_map/convert_element_type | solution.py:179
  177.7 2.8 %collective-permute-start.20 = (bf16[128,1024]{1,0:T(8,128)(2,1)S(1)}, bf16[128,1024]{1,0:T(8,128)(2,1)S(1)}, u32[]{:S(2)}, u32[]{:S(2)}) collective-permute-start(bf16[128,1024]{1,0:T(8,128)(2,1)S(1)} %get-tuple-element.26), channel_id=1, source_target_pairs={{0,2},{1,3},{4,0},{5,1},{8,4},{9,5},{12,8},{13,9},{14,12},{15,13},... | collective-permute-start | bytes 786440 | tf_op jit(solution)/shard_map/ppermute | solution.py:109
  180.7 5.7 %collective-permute-done.20 = bf16[128,1024]{1,0:T(8,128)(2,1)S(1)} collective-permute-done((bf16[128,1024]{1,0:T(8,128)(2,1)S(1)}, bf16[128,1024]{1,0:T(8,128)(2,1)S(1)}, u32[]{:S(2)}, u32[]{:S(2)}) %collective-permute-start.20) | collective-permute-done | bytes 262176 | tf_op jit(solution)/shard_map/ppermute | solution.py:109
  186.4 2.5 %collective-permute-start.24 = (bf16[128,1024]{1,0:T(8,128)(2,1)S(1)}, bf16[128,1024]{1,0:T(8,128)(2,1)S(1)}, u32[]{:S(2)}, u32[]{:S(2)}) collective-permute-start(bf16[128,1024]{1,0:T(8,128)(2,1)S(1)} %collective-permute-done.20), channel_id=1, source_target_pairs={{0,2},{1,3},{4,0},{5,1},{8,4},{9,5},{12,8},{13,9},{14,12},{15,13},... | collective-permute-start | bytes 786440 | tf_op jit(solution)/shard_map/ppermute | solution.py:109
  190.1 4.0 %collective-permute-done.24 = bf16[128,1024]{1,0:T(8,128)(2,1)S(1)} collective-permute-done((bf16[128,1024]{1,0:T(8,128)(2,1)S(1)}, bf16[128,1024]{1,0:T(8,128)(2,1)S(1)}, u32[]{:S(2)}, u32[]{:S(2)}) %collective-permute-start.24) | collective-permute-done | bytes 262176 | tf_op jit(solution)/shard_map/ppermute | solution.py:109
  194.0 2.5 %collective-permute-start.28 = (bf16[128,1024]{1,0:T(8,128)(2,1)S(1)}, bf16[128,1024]{1,0:T(8,128)(2,1)S(1)}, u32[]{:S(2)}, u32[]{:S(2)}) collective-permute-start(bf16[128,1024]{1,0:T(8,128)(2,1)S(1)} %collective-permute-done.24), channel_id=1, source_target_pairs={{0,2},{1,3},{4,0},{5,1},{8,4},{9,5},{12,8},{13,9},{14,12},{15,13},... | collective-permute-start | bytes 786440 | tf_op jit(solution)/shard_map/ppermute | solution.py:109
  198.9 6.7 %collective-permute-done.27 = bf16[128,1024]{1,0:T(8,128)(2,1)S(1)} collective-permute-done((bf16[128,1024]{1,0:T(8,128)(2,1)S(1)}, bf16[128,1024]{1,0:T(8,128)(2,1)S(1)}, u32[]{:S(2)}, u32[]{:S(2)}) %collective-permute-start.27) | collective-permute-done | bytes 262176 | tf_op jit(solution)/shard_map/ppermute | solution.py:105
  207.5 5.1 %collective-permute-done.31 = bf16[128,1024]{1,0:T(8,128)(2,1)S(1)} collective-permute-done((bf16[128,1024]{1,0:T(8,128)(2,1)S(1)}, bf16[128,1024]{1,0:T(8,128)(2,1)S(1)}, u32[]{:S(2)}, u32[]{:S(2)}) %collective-permute-start.31) | collective-permute-done | bytes 262176 | tf_op jit(solution)/shard_map/ppermute | solution.py:105
  216.5 3.8 %all-to-all-start.1 = ((bf16[16,8,2048]{2,1,0:T(8,128)(2,1)}), bf16[16,8,2048]{2,1,0:T(8,128)(2,1)S(1)}, u32[]{:S(2)}, u32[]{:S(2)}) async-start(bf16[16,8,2048]{2,1,0:T(8,128)(2,1)} %select_bitcast_fusion), calls=%async_computation.3 | async-start | bytes 1048576 | tf_op jit(solution)/shard_map/all_to_all | solution.py:185
  220.3 2.2 pad_maximum_fusion.3
  225.6 9.1 %all-to-all-done.1 = bf16[16,8,2048]{2,1,0:T(8,128)(2,1)S(1)} async-done(((bf16[16,8,2048]{2,1,0:T(8,128)(2,1)}), bf16[16,8,2048]{2,1,0:T(8,128)(2,1)S(1)}, u32[]{:S(2)}, u32[]{:S(2)}) %all-to-all-start.1) | async-done | bytes 524320 | tf_op jit(solution)/shard_map/all_to_all | solution.py:185
  (161 shorter events, 34.0 us)
Async XLA Ops:
  7.2 98.6 %reduce-scatter.5.cloned.1.call-start = ((), (), s32[]{:S(2)}) async-start(), calls=%async_computation.5 | async-start | bytes 4718592 | tf_op jit(solution)/shard_map/reduce_scatter | solution.py:53
  14.8 16.0 %collective-permute-start = (bf16[256,1024]{1,0:T(8,128)(2,1)}, bf16[256,1024]{1,0:T(8,128)(2,1)}, u32[]{:S(2)}, u32[]{:S(2)}) collective-permute-start(bf16[256,1024]{1,0:T(8,128)(2,1)} %reshape.206), channel_id=1, source_target_pairs={{0,2},{2,0},{1,3},{3,1},{4,6},{6,4},{5,7},{7,5},{8,10},{10,8},{9,1... | collective-permute-start | bytes 1572872 | tf_op jit(solution)/shard_map/ppermute | solution.py:42
  19.8 21.4 %collective-permute-start.2 = (bf16[256,1024]{1,0:T(8,128)(2,1)}, bf16[256,1024]{1,0:T(8,128)(2,1)}, u32[]{:S(2)}, u32[]{:S(2)}) collective-permute-start(bf16[256,1024]{1,0:T(8,128)(2,1)} %get-tuple-element.42), channel_id=1, source_target_pairs={{0,2},{2,0},{1,3},{3,1},{4,6},{6,4},{5,7},{7,5},{8,10},{10,8},{9,1... | collective-permute-start | bytes 1572872 | tf_op jit(solution)/shard_map/ppermute | solution.py:42
  48.4 31.3 %all-to-all-start = ((bf16[16,8,2048]{2,1,0:T(8,128)(2,1)}), bf16[16,8,2048]{2,1,0:T(8,128)(2,1)S(1)}, u32[]{:S(2)}, u32[]{:S(2)}) async-start(bf16[16,8,2048]{2,1,0:T(8,128)(2,1)} %select_bitcast_fusion.1), calls=%async_computation.2 | async-start | bytes 1048576 | tf_op jit(solution)/shard_map/all_to_all | solution.py:158
  54.6 119.7 %reduce-scatter.3.cloned.1.call-start = ((), (), s32[]{:S(2)}) async-start(), calls=%async_computation.4 | async-start | bytes 4718592 | tf_op jit(solution)/shard_map/reduce_scatter | solution.py:53
  54.6 19.2 %collective-permute-start.1 = (bf16[256,1024]{1,0:T(8,128)(2,1)S(1)}, bf16[256,1024]{1,0:T(8,128)(2,1)S(1)}, u32[]{:S(2)}, u32[]{:S(2)}) collective-permute-start(bf16[256,1024]{1,0:T(8,128)(2,1)S(1)} %get-tuple-element.43), channel_id=1, source_target_pairs={{0,2},{2,0},{1,3},{3,1},{4,6},{6,4},{5,7},{7,5},{8,10},{10,8},{9,1... | collective-permute-start | bytes 1572872 | tf_op jit(solution)/shard_map/ppermute | solution.py:43
  107.9 9.0 %collective-permute-start.5 = (bf16[128,1024]{1,0:T(8,128)(2,1)S(1)}, bf16[128,1024]{1,0:T(8,128)(2,1)S(1)}, u32[]{:S(2)}, u32[]{:S(2)}) collective-permute-start(bf16[128,1024]{1,0:T(8,128)(2,1)S(1)} %get-tuple-element.31), channel_id=1, source_target_pairs={{0,2},{1,3},{4,0},{5,1},{8,4},{9,5},{12,8},{13,9},{14,12},{15,13},... | collective-permute-start | bytes 786440 | tf_op jit(solution)/shard_map/ppermute | solution.py:109
  109.4 9.3 %collective-permute-start.4 = (bf16[128,1024]{1,0:T(8,128)(2,1)S(1)}, bf16[128,1024]{1,0:T(8,128)(2,1)S(1)}, u32[]{:S(2)}, u32[]{:S(2)}) collective-permute-start(bf16[128,1024]{1,0:T(8,128)(2,1)S(1)} %get-tuple-element.31), channel_id=1, source_target_pairs={{0,4},{1,5},{4,8},{5,9},{8,12},{9,13},{12,14},{13,15},{14,10},{15,... | collective-permute-start | bytes 786440 | tf_op jit(solution)/shard_map/ppermute | solution.py:105
  110.0 11.5 %collective-permute-start.3 = (bf16[128,1024]{1,0:T(8,128)(2,1)S(1)}, bf16[128,1024]{1,0:T(8,128)(2,1)S(1)}, u32[]{:S(2)}, u32[]{:S(2)}) collective-permute-start(bf16[128,1024]{1,0:T(8,128)(2,1)S(1)} %get-tuple-element.31), channel_id=1, source_target_pairs={{0,1},{1,0},{2,3},{3,2},{4,5},{5,4},{6,7},{7,6},{8,9},{9,8},{10,11... | collective-permute-start | bytes 786440 | tf_op jit(solution)/shard_map/ppermute | solution.py:101
  116.9 14.6 %collective-permute-start.9 = (bf16[128,1024]{1,0:T(8,128)(2,1)S(1)}, bf16[128,1024]{1,0:T(8,128)(2,1)S(1)}, u32[]{:S(2)}, u32[]{:S(2)}) collective-permute-start(bf16[128,1024]{1,0:T(8,128)(2,1)S(1)} %collective-permute-done.5), channel_id=1, source_target_pairs={{0,2},{1,3},{4,0},{5,1},{8,4},{9,5},{12,8},{13,9},{14,12},{15,13},... | collective-permute-start | bytes 786440 | tf_op jit(solution)/shard_map/ppermute | solution.py:109
  116.9 19.0 %collective-permute-start.7 = (bf16[128,1024]{1,0:T(8,128)(2,1)S(1)}, bf16[128,1024]{1,0:T(8,128)(2,1)S(1)}, u32[]{:S(2)}, u32[]{:S(2)}) collective-permute-start(bf16[128,1024]{1,0:T(8,128)(2,1)S(1)} %collective-permute-done.5), channel_id=1, source_target_pairs={{0,1},{1,0},{2,3},{3,2},{4,5},{5,4},{6,7},{7,6},{8,9},{9,8},{10,11... | collective-permute-start | bytes 786440 | tf_op jit(solution)/shard_map/ppermute | solution.py:101
  118.8 14.5 %collective-permute-start.8 = (bf16[128,1024]{1,0:T(8,128)(2,1)S(1)}, bf16[128,1024]{1,0:T(8,128)(2,1)S(1)}, u32[]{:S(2)}, u32[]{:S(2)}) collective-permute-start(bf16[128,1024]{1,0:T(8,128)(2,1)S(1)} %collective-permute-done.4), channel_id=1, source_target_pairs={{0,4},{1,5},{4,8},{5,9},{8,12},{9,13},{12,14},{13,15},{14,10},{15,... | collective-permute-start | bytes 786440 | tf_op jit(solution)/shard_map/ppermute | solution.py:105
  121.2 15.0 %collective-permute-start.6 = (bf16[128,1024]{1,0:T(8,128)(2,1)S(1)}, bf16[128,1024]{1,0:T(8,128)(2,1)S(1)}, u32[]{:S(2)}, u32[]{:S(2)}) collective-permute-start(bf16[128,1024]{1,0:T(8,128)(2,1)S(1)} %collective-permute-done.4), channel_id=1, source_target_pairs={{0,1},{1,0},{2,3},{3,2},{4,5},{5,4},{6,7},{7,6},{8,9},{9,8},{10,11... | collective-permute-start | bytes 786440 | tf_op jit(solution)/shard_map/ppermute | solution.py:101
  131.6 18.6 %collective-permute-start.13 = (bf16[128,1024]{1,0:T(8,128)(2,1)S(1)}, bf16[128,1024]{1,0:T(8,128)(2,1)S(1)}, u32[]{:S(2)}, u32[]{:S(2)}) collective-permute-start(bf16[128,1024]{1,0:T(8,128)(2,1)S(1)} %collective-permute-done.9), channel_id=1, source_target_pairs={{0,2},{1,3},{4,0},{5,1},{8,4},{9,5},{12,8},{13,9},{14,12},{15,13},... | collective-permute-start | bytes 786440 | tf_op jit(solution)/shard_map/ppermute | solution.py:109
  131.6 19.6 %collective-permute-start.11 = (bf16[128,1024]{1,0:T(8,128)(2,1)S(1)}, bf16[128,1024]{1,0:T(8,128)(2,1)S(1)}, u32[]{:S(2)}, u32[]{:S(2)}) collective-permute-start(bf16[128,1024]{1,0:T(8,128)(2,1)S(1)} %collective-permute-done.9), channel_id=1, source_target_pairs={{0,1},{1,0},{2,3},{3,2},{4,5},{5,4},{6,7},{7,6},{8,9},{9,8},{10,11... | collective-permute-start | bytes 786440 | tf_op jit(solution)/shard_map/ppermute | solution.py:101
  133.2 14.5 %collective-permute-start.12 = (bf16[128,1024]{1,0:T(8,128)(2,1)S(1)}, bf16[128,1024]{1,0:T(8,128)(2,1)S(1)}, u32[]{:S(2)}, u32[]{:S(2)}) collective-permute-start(bf16[128,1024]{1,0:T(8,128)(2,1)S(1)} %collective-permute-done.8), channel_id=1, source_target_pairs={{0,4},{1,5},{4,8},{5,9},{8,12},{9,13},{12,14},{13,15},{14,10},{15,... | collective-permute-start | bytes 786440 | tf_op jit(solution)/shard_map/ppermute | solution.py:105
  136.0 15.4 %collective-permute-start.10 = (bf16[128,1024]{1,0:T(8,128)(2,1)S(1)}, bf16[128,1024]{1,0:T(8,128)(2,1)S(1)}, u32[]{:S(2)}, u32[]{:S(2)}) collective-permute-start(bf16[128,1024]{1,0:T(8,128)(2,1)S(1)} %collective-permute-done.8), channel_id=1, source_target_pairs={{0,1},{1,0},{2,3},{3,2},{4,5},{5,4},{6,7},{7,6},{8,9},{9,8},{10,11... | collective-permute-start | bytes 786440 | tf_op jit(solution)/shard_map/ppermute | solution.py:101
  147.7 14.2 %collective-permute-start.16 = (bf16[128,1024]{1,0:T(8,128)(2,1)S(1)}, bf16[128,1024]{1,0:T(8,128)(2,1)S(1)}, u32[]{:S(2)}, u32[]{:S(2)}) collective-permute-start(bf16[128,1024]{1,0:T(8,128)(2,1)S(1)} %collective-permute-done.12), channel_id=1, source_target_pairs={{0,4},{1,5},{4,8},{5,9},{8,12},{9,13},{12,14},{13,15},{14,10},{15,... | collective-permute-start | bytes 786440 | tf_op jit(solution)/shard_map/ppermute | solution.py:105
  150.2 12.2 %collective-permute-start.14 = (bf16[128,1024]{1,0:T(8,128)(2,1)S(1)}, bf16[128,1024]{1,0:T(8,128)(2,1)S(1)}, u32[]{:S(2)}, u32[]{:S(2)}) collective-permute-start(bf16[128,1024]{1,0:T(8,128)(2,1)S(1)} %collective-permute-done.12), channel_id=1, source_target_pairs={{0,1},{1,0},{2,3},{3,2},{4,5},{5,4},{6,7},{7,6},{8,9},{9,8},{10,11... | collective-permute-start | bytes 786440 | tf_op jit(solution)/shard_map/ppermute | solution.py:101
  150.2 11.9 %collective-permute-start.15 = (bf16[128,1024]{1,0:T(8,128)(2,1)S(1)}, bf16[128,1024]{1,0:T(8,128)(2,1)S(1)}, u32[]{:S(2)}, u32[]{:S(2)}) collective-permute-start(bf16[128,1024]{1,0:T(8,128)(2,1)S(1)} %collective-permute-done.13), channel_id=1, source_target_pairs={{0,1},{1,0},{2,3},{3,2},{4,5},{5,4},{6,7},{7,6},{8,9},{9,8},{10,11... | collective-permute-start | bytes 786440 | tf_op jit(solution)/shard_map/ppermute | solution.py:101
  177.7 8.7 %collective-permute-start.20 = (bf16[128,1024]{1,0:T(8,128)(2,1)S(1)}, bf16[128,1024]{1,0:T(8,128)(2,1)S(1)}, u32[]{:S(2)}, u32[]{:S(2)}) collective-permute-start(bf16[128,1024]{1,0:T(8,128)(2,1)S(1)} %get-tuple-element.26), channel_id=1, source_target_pairs={{0,2},{1,3},{4,0},{5,1},{8,4},{9,5},{12,8},{13,9},{14,12},{15,13},... | collective-permute-start | bytes 786440 | tf_op jit(solution)/shard_map/ppermute | solution.py:109
  180.4 8.5 %collective-permute-start.19 = (bf16[128,1024]{1,0:T(8,128)(2,1)S(1)}, bf16[128,1024]{1,0:T(8,128)(2,1)S(1)}, u32[]{:S(2)}, u32[]{:S(2)}) collective-permute-start(bf16[128,1024]{1,0:T(8,128)(2,1)S(1)} %get-tuple-element.26), channel_id=1, source_target_pairs={{0,4},{1,5},{4,8},{5,9},{8,12},{9,13},{12,14},{13,15},{14,10},{15,... | collective-permute-start | bytes 786440 | tf_op jit(solution)/shard_map/ppermute | solution.py:105
  180.4 9.2 %collective-permute-start.18 = (bf16[128,1024]{1,0:T(8,128)(2,1)S(1)}, bf16[128,1024]{1,0:T(8,128)(2,1)S(1)}, u32[]{:S(2)}, u32[]{:S(2)}) collective-permute-start(bf16[128,1024]{1,0:T(8,128)(2,1)S(1)} %get-tuple-element.26), channel_id=1, source_target_pairs={{0,1},{1,0},{2,3},{3,2},{4,5},{5,4},{6,7},{7,6},{8,9},{9,8},{10,11... | collective-permute-start | bytes 786440 | tf_op jit(solution)/shard_map/ppermute | solution.py:101
  186.4 7.6 %collective-permute-start.24 = (bf16[128,1024]{1,0:T(8,128)(2,1)S(1)}, bf16[128,1024]{1,0:T(8,128)(2,1)S(1)}, u32[]{:S(2)}, u32[]{:S(2)}) collective-permute-start(bf16[128,1024]{1,0:T(8,128)(2,1)S(1)} %collective-permute-done.20), channel_id=1, source_target_pairs={{0,2},{1,3},{4,0},{5,1},{8,4},{9,5},{12,8},{13,9},{14,12},{15,13},... | collective-permute-start | bytes 786440 | tf_op jit(solution)/shard_map/ppermute | solution.py:109
  188.9 9.5 %collective-permute-start.22 = (bf16[128,1024]{1,0:T(8,128)(2,1)S(1)}, bf16[128,1024]{1,0:T(8,128)(2,1)S(1)}, u32[]{:S(2)}, u32[]{:S(2)}) collective-permute-start(bf16[128,1024]{1,0:T(8,128)(2,1)S(1)} %collective-permute-done.20), channel_id=1, source_target_pairs={{0,1},{1,0},{2,3},{3,2},{4,5},{5,4},{6,7},{7,6},{8,9},{9,8},{10,11... | collective-permute-start | bytes 786440 | tf_op jit(solution)/shard_map/ppermute | solution.py:101
  188.9 8.7 %collective-permute-start.23 = (bf16[128,1024]{1,0:T(8,128)(2,1)S(1)}, bf16[128,1024]{1,0:T(8,128)(2,1)S(1)}, u32[]{:S(2)}, u32[]{:S(2)}) collective-permute-start(bf16[128,1024]{1,0:T(8,128)(2,1)S(1)} %collective-permute-done.19), channel_id=1, source_target_pairs={{0,4},{1,5},{4,8},{5,9},{8,12},{9,13},{12,14},{13,15},{14,10},{15,... | collective-permute-start | bytes 786440 | tf_op jit(solution)/shard_map/ppermute | solution.py:105
  188.9 9.7 %collective-permute-start.21 = (bf16[128,1024]{1,0:T(8,128)(2,1)S(1)}, bf16[128,1024]{1,0:T(8,128)(2,1)S(1)}, u32[]{:S(2)}, u32[]{:S(2)}) collective-permute-start(bf16[128,1024]{1,0:T(8,128)(2,1)S(1)} %collective-permute-done.19), channel_id=1, source_target_pairs={{0,1},{1,0},{2,3},{3,2},{4,5},{5,4},{6,7},{7,6},{8,9},{9,8},{10,11... | collective-permute-start | bytes 786440 | tf_op jit(solution)/shard_map/ppermute | solution.py:101
  194.0 12.2 %collective-permute-start.28 = (bf16[128,1024]{1,0:T(8,128)(2,1)S(1)}, bf16[128,1024]{1,0:T(8,128)(2,1)S(1)}, u32[]{:S(2)}, u32[]{:S(2)}) collective-permute-start(bf16[128,1024]{1,0:T(8,128)(2,1)S(1)} %collective-permute-done.24), channel_id=1, source_target_pairs={{0,2},{1,3},{4,0},{5,1},{8,4},{9,5},{12,8},{13,9},{14,12},{15,13},... | collective-permute-start | bytes 786440 | tf_op jit(solution)/shard_map/ppermute | solution.py:109
  196.5 10.5 %collective-permute-start.26 = (bf16[128,1024]{1,0:T(8,128)(2,1)S(1)}, bf16[128,1024]{1,0:T(8,128)(2,1)S(1)}, u32[]{:S(2)}, u32[]{:S(2)}) collective-permute-start(bf16[128,1024]{1,0:T(8,128)(2,1)S(1)} %collective-permute-done.24), channel_id=1, source_target_pairs={{0,1},{1,0},{2,3},{3,2},{4,5},{5,4},{6,7},{7,6},{8,9},{9,8},{10,11... | collective-permute-start | bytes 786440 | tf_op jit(solution)/shard_map/ppermute | solution.py:101
  197.6 7.9 %collective-permute-start.27 = (bf16[128,1024]{1,0:T(8,128)(2,1)S(1)}, bf16[128,1024]{1,0:T(8,128)(2,1)S(1)}, u32[]{:S(2)}, u32[]{:S(2)}) collective-permute-start(bf16[128,1024]{1,0:T(8,128)(2,1)S(1)} %collective-permute-done.23), channel_id=1, source_target_pairs={{0,4},{1,5},{4,8},{5,9},{8,12},{9,13},{12,14},{13,15},{14,10},{15,... | collective-permute-start | bytes 786440 | tf_op jit(solution)/shard_map/ppermute | solution.py:105
  198.3 8.9 %collective-permute-start.25 = (bf16[128,1024]{1,0:T(8,128)(2,1)S(1)}, bf16[128,1024]{1,0:T(8,128)(2,1)S(1)}, u32[]{:S(2)}, u32[]{:S(2)}) collective-permute-start(bf16[128,1024]{1,0:T(8,128)(2,1)S(1)} %collective-permute-done.23), channel_id=1, source_target_pairs={{0,1},{1,0},{2,3},{3,2},{4,5},{5,4},{6,7},{7,6},{8,9},{9,8},{10,11... | collective-permute-start | bytes 786440 | tf_op jit(solution)/shard_map/ppermute | solution.py:101
  216.5 18.3 %all-to-all-start.1 = ((bf16[16,8,2048]{2,1,0:T(8,128)(2,1)}), bf16[16,8,2048]{2,1,0:T(8,128)(2,1)S(1)}, u32[]{:S(2)}, u32[]{:S(2)}) async-start(bf16[16,8,2048]{2,1,0:T(8,128)(2,1)} %select_bitcast_fusion), calls=%async_computation.3 | async-start | bytes 1048576 | tf_op jit(solution)/shard_map/all_to_all | solution.py:185
  (15 other events, 125.5 us)
Sparse Core Ops, SparseCore 0:
  45.8 59.9 reduce-scatter.4
  108.1 66.2 reduce-scatter.2

commit v9 on v8

--- a/solution.py
+++ b/solution.py
@@ -163,6 +163,8 @@
     halves[0], (encoded_rows, send_back, receive_back) = lax.optimization_barrier(
         (halves[0], (encoded_rows, send_back, receive_back))
     )
+    kept = encoded_rows[0, 0] == encoded_rows[0, 0]
+    queue = lax.optimization_barrier(jnp.where(kept, queue, jnp.zeros_like(queue)))
     width = params.shape[1] // len(halves)
     results = []
     for h, gradient in enumerate(halves):

time: 244 us -> 242 us (level)
  waiting for transfers between devices: 145 us -> 140 us
  other arithmetic: 16.6 us -> 19.9 us
  local copies, waits for them, and re-layouts: 15 us -> 11.8 us
    unnamed x22 -> x23, local copies, waits for them, and re-layouts: 4.99 us -> 0.1 us
    ppermute x6, waiting for transfers between devices: 25.3 us -> 21.8 us  [ring_codes(): behind = lax.ppermute(behind, DP, backward)]
  transfers between devices with their start and end apart: 37 -> 37, of which waited for: 19 -> 20; matrix products, arithmetic and copies ran while one was open for 11% -> 13% of each run, Pallas kernels for 0% -> 0%
where the time goes in v9:
time: 242 us; the launch traced here: 241 us
  waiting for transfers between devices  140 us (58%)
  starting transfers between devices  38.3 us (16%)
  other arithmetic  19.9 us (8%)
  between operations  16.9 us (7%)
  matrix products  14.8 us (6%)
  local copies, waits for them, and re-layouts  11.8 us (5%)
    reduce_scatter x2, waiting for transfers between devices, pair_gradient(): lax.psum_scatter(partial, ('zo', 'c'), scatter_dimension=0, tiled=True)  36.5 us
    ppermute x8, waiting for transfers between devices, ring_codes(): ahead = lax.ppermute(ahead, DP, forward)  35.5 us
    ppermute x6, waiting for transfers between devices, ring_codes(): behind = lax.ppermute(behind, DP, backward)  21.8 us
    ppermute x2, waiting for transfers between devices, pair_gradient(): lax.ppermute((theirs, grad_out[:, :half]), 'xl', swap)  19.9 us
    ppermute x1, waiting for transfers between devices, pair_gradient(): got_second = lax.ppermute(grad_out[:, half:], 'xl', swap)  15.1 us
    ppermute x6, starting transfers between devices, ring_codes(): behind = lax.ppermute(behind, DP, backward)  9.45 us
    ppermute x8, starting transfers between devices, ring_codes(): ahead = lax.ppermute(ahead, DP, forward)  9.05 us
    all_to_all x1, waiting for transfers between devices, per_device(): lax.all_to_all(jnp.take(normed, send_back, axis=0), DP, split_axis=0, con...  9.05 us
  transfers between devices with their start and end apart: 37, of which 20 were waited for; matrix products, arithmetic and copies ran while one was open for 13% of the time, Pallas kernels for 0%

profile of v9, /device:TPU:0, one launch (start us, length us, event | category | flops | bytes accessed | tf_op | source)
XLA Modules:
  0.0 241.3 jit_solution(7053208808273329153)
XLA Ops:
  11.0 2.9 %collective-permute-start = (bf16[256,1024]{1,0:T(8,128)(2,1)}, bf16[256,1024]{1,0:T(8,128)(2,1)}, u32[]{:S(2)}, u32[]{:S(2)}) collective-permute-start(bf16[256,1024]{1,0:T(8,128)(2,1)} %reshape.207), channel_id=1, source_target_pairs={{0,2},{2,0},{1,3},{3,1},{4,6},{6,4},{5,7},{7,5},{8,10},{10,8},{9,1... | collective-permute-start | bytes 1572872 | tf_op jit(solution)/shard_map/ppermute | solution.py:42
  13.9 2.1 fusion.134
  16.4 10.6 %collective-permute-done = bf16[256,1024]{1,0:T(8,128)(2,1)} collective-permute-done((bf16[256,1024]{1,0:T(8,128)(2,1)}, bf16[256,1024]{1,0:T(8,128)(2,1)}, u32[]{:S(2)}, u32[]{:S(2)}) %collective-permute-start) | collective-permute-done | bytes 524320 | tf_op jit(solution)/shard_map/ppermute | solution.py:42
  28.1 9.3 %collective-permute-done.2 = bf16[256,1024]{1,0:T(8,128)(2,1)} collective-permute-done((bf16[256,1024]{1,0:T(8,128)(2,1)}, bf16[256,1024]{1,0:T(8,128)(2,1)}, u32[]{:S(2)}, u32[]{:S(2)}) %collective-permute-start.2) | collective-permute-done | bytes 524320 | tf_op jit(solution)/shard_map/ppermute | solution.py:42
  37.4 4.5 %fusion.26 = f32[1024,1024]{1,0:T(8,128)} fusion(bf16[512,1024]{1,0:T(8,128)(2,1)S(1)} %constant_dynamic-update-slice_fusion, bf16[256,1024]{1,0:T(8,128)(2,1)} %collective-permute-done.2, bf16[256,1024]{1,0:T(8,128)(2,1)} %get-tuple-element.42), kind=kOutput, calls=%fused_computation.43 | convolution fusion | flops 1075838976 | bytes 6291456 | tf_op jit(solution)/shard_map/dot_general | solution.py:47
  44.7 6.2 %all-to-all-start = ((bf16[16,8,2048]{2,1,0:T(8,128)(2,1)}), bf16[16,8,2048]{2,1,0:T(8,128)(2,1)S(1)}, u32[]{:S(2)}, u32[]{:S(2)}) async-start(bf16[16,8,2048]{2,1,0:T(8,128)(2,1)} %select_bitcast_fusion.1), calls=%async_computation.2 | async-start | bytes 1048576 | tf_op jit(solution)/shard_map/all_to_all | solution.py:158
  50.9 2.0 collective-permute-start.1
  55.0 15.1 %collective-permute-done.1 = bf16[256,1024]{1,0:T(8,128)(2,1)S(1)} collective-permute-done((bf16[256,1024]{1,0:T(8,128)(2,1)S(1)}, bf16[256,1024]{1,0:T(8,128)(2,1)S(1)}, u32[]{:S(2)}, u32[]{:S(2)}) %collective-permute-start.1) | collective-permute-done | bytes 524320 | tf_op jit(solution)/shard_map/ppermute | solution.py:43
  70.1 3.2 %fusion.22 = f32[1024,1024]{1,0:T(8,128)} fusion(bf16[512,1024]{1,0:T(8,128)(2,1)S(1)} %constant_dynamic-update-slice_fusion, bf16[256,1024]{1,0:T(8,128)(2,1)S(1)} %collective-permute-done.1, bf16[256,1024]{1,0:T(8,128)(2,1)S(1)} %get-tuple-element.43), kind=kOutput, calls=%fused_computation.39 | convolution fusion | flops 1075838976 | bytes 6291456 | tf_op jit(solution)/shard_map/dot_general | solution.py:47
  74.9 27.1 %reduce-scatter.5.cloned.1.call-done = f32[128,1024]{1,0:T(8,128)} async-done(((f32[1024,1024]{1,0:T(8,128)}), f32[128,1024]{1,0:T(8,128)}) %reduce-scatter.5.cloned.1.call-update) | async-done | bytes 524304 | tf_op jit(solution)/shard_map/reduce_scatter | solution.py:53
  102.0 3.1 %fusion.129 = (bf16[128,1024]{1,0:T(8,128)(2,1)S(1)}, f32[128,1024]{1,0:T(8,128)}, f32[128,1024]{1,0:T(8,128)S(1)}, f32[128,1024]{1,0:T(8,128)S(1)}, f32[128,1024]{1,0:T(8,128)S(1)}) fusion(f32[128,2048]{1,0:T(8,128)} %param.20, f32[128,2048]{1,0:T(8,128)} %param.17, f32[128,1024]{1,0:T(8,128)} %reduce-scatter.5.cloned.1.call-done, f32[128,2048]{1,0:T(8,128)} %param.18, ...), kind=kLoop, calls=%fused_computation.220 | loop fusion | flops 2621440 | bytes 4980736 | tf_op jit(solution)/shard_map/convert_element_type | solution.py:181
  109.8 2.3 broadcast_select_fusion
  112.1 2.3 collective-permute-done.5
  114.5 2.1 collective-permute-start.7
  116.7 2.5 %collective-permute-start.8 = (bf16[128,1024]{1,0:T(8,128)(2,1)S(1)}, bf16[128,1024]{1,0:T(8,128)(2,1)S(1)}, u32[]{:S(2)}, u32[]{:S(2)}) collective-permute-start(bf16[128,1024]{1,0:T(8,128)(2,1)S(1)} %collective-permute-done.4), channel_id=1, source_target_pairs={{0,4},{1,5},{4,8},{5,9},{8,12},{9,13},{12,14},{13,15},{14,10},{15,... | collective-permute-start | bytes 786440 | tf_op jit(solution)/shard_map/ppermute | solution.py:105
  119.9 9.3 %collective-permute-done.9 = bf16[128,1024]{1,0:T(8,128)(2,1)S(1)} collective-permute-done((bf16[128,1024]{1,0:T(8,128)(2,1)S(1)}, bf16[128,1024]{1,0:T(8,128)(2,1)S(1)}, u32[]{:S(2)}, u32[]{:S(2)}) %collective-permute-start.9) | collective-permute-done | bytes 262176 | tf_op jit(solution)/shard_map/ppermute | solution.py:109
  131.2 2.5 %collective-permute-start.12 = (bf16[128,1024]{1,0:T(8,128)(2,1)S(1)}, bf16[128,1024]{1,0:T(8,128)(2,1)S(1)}, u32[]{:S(2)}, u32[]{:S(2)}) collective-permute-start(bf16[128,1024]{1,0:T(8,128)(2,1)S(1)} %collective-permute-done.8), channel_id=1, source_target_pairs={{0,4},{1,5},{4,8},{5,9},{8,12},{9,13},{12,14},{13,15},{14,10},{15,... | collective-permute-start | bytes 786440 | tf_op jit(solution)/shard_map/ppermute | solution.py:105
  134.4 11.2 %collective-permute-done.12 = bf16[128,1024]{1,0:T(8,128)(2,1)S(1)} collective-permute-done((bf16[128,1024]{1,0:T(8,128)(2,1)S(1)}, bf16[128,1024]{1,0:T(8,128)(2,1)S(1)}, u32[]{:S(2)}, u32[]{:S(2)}) %collective-permute-start.12) | collective-permute-done | bytes 262176 | tf_op jit(solution)/shard_map/ppermute | solution.py:105
  145.6 2.5 %collective-permute-start.16 = (bf16[128,1024]{1,0:T(8,128)(2,1)S(1)}, bf16[128,1024]{1,0:T(8,128)(2,1)S(1)}, u32[]{:S(2)}, u32[]{:S(2)}) collective-permute-start(bf16[128,1024]{1,0:T(8,128)(2,1)S(1)} %collective-permute-done.12), channel_id=1, source_target_pairs={{0,4},{1,5},{4,8},{5,9},{8,12},{9,13},{12,14},{13,15},{14,10},{15,... | collective-permute-start | bytes 786440 | tf_op jit(solution)/shard_map/ppermute | solution.py:105
  149.6 10.3 %collective-permute-done.16 = bf16[128,1024]{1,0:T(8,128)(2,1)S(1)} collective-permute-done((bf16[128,1024]{1,0:T(8,128)(2,1)S(1)}, bf16[128,1024]{1,0:T(8,128)(2,1)S(1)}, u32[]{:S(2)}, u32[]{:S(2)}) %collective-permute-start.16) | collective-permute-done | bytes 262176 | tf_op jit(solution)/shard_map/ppermute | solution.py:105
  161.9 9.5 %reduce-scatter.3.cloned.1.call-done = f32[128,1024]{1,0:T(8,128)} async-done(((f32[1024,1024]{1,0:T(8,128)}), f32[128,1024]{1,0:T(8,128)}) %reduce-scatter.3.cloned.1.call-update) | async-done | bytes 524304 | tf_op jit(solution)/shard_map/reduce_scatter | solution.py:53
  171.4 3.4 %fusion.128 = (bf16[128,1024]{1,0:T(8,128)(2,1)S(1)}, f32[128,1024]{1,0:T(8,128)}, f32[128,1024]{1,0:T(8,128)}, f32[128,1024]{1,0:T(8,128)}, f32[128,1024]{1,0:T(8,128)}) fusion(f32[128,2048]{1,0:T(8,128)} %param.20, f32[128,2048]{1,0:T(8,128)} %param.17, f32[128,1024]{1,0:T(8,128)} %reduce-scatter.3.cloned.1.call-done, f32[128,2048]{1,0:T(8,128)} %param.18, ...), kind=kLoop, calls=%fused_computation.219 | loop fusion | flops 2621440 | bytes 4980736 | tf_op jit(solution)/shard_map/convert_element_type | solution.py:181
  174.7 2.0 collective-permute-start.20
  177.8 5.4 %collective-permute-done.20 = bf16[128,1024]{1,0:T(8,128)(2,1)S(1)} collective-permute-done((bf16[128,1024]{1,0:T(8,128)(2,1)S(1)}, bf16[128,1024]{1,0:T(8,128)(2,1)S(1)}, u32[]{:S(2)}, u32[]{:S(2)}) %collective-permute-start.20) | collective-permute-done | bytes 262176 | tf_op jit(solution)/shard_map/ppermute | solution.py:109
  183.2 2.5 %collective-permute-start.24 = (bf16[128,1024]{1,0:T(8,128)(2,1)S(1)}, bf16[128,1024]{1,0:T(8,128)(2,1)S(1)}, u32[]{:S(2)}, u32[]{:S(2)}) collective-permute-start(bf16[128,1024]{1,0:T(8,128)(2,1)S(1)} %collective-permute-done.20), channel_id=1, source_target_pairs={{0,2},{1,3},{4,0},{5,1},{8,4},{9,5},{12,8},{13,9},{14,12},{15,13},... | collective-permute-start | bytes 786440 | tf_op jit(solution)/shard_map/ppermute | solution.py:109
  186.9 4.8 %collective-permute-done.24 = bf16[128,1024]{1,0:T(8,128)(2,1)S(1)} collective-permute-done((bf16[128,1024]{1,0:T(8,128)(2,1)S(1)}, bf16[128,1024]{1,0:T(8,128)(2,1)S(1)}, u32[]{:S(2)}, u32[]{:S(2)}) %collective-permute-start.24) | collective-permute-done | bytes 262176 | tf_op jit(solution)/shard_map/ppermute | solution.py:109
  191.7 2.5 %collective-permute-start.28 = (bf16[128,1024]{1,0:T(8,128)(2,1)S(1)}, bf16[128,1024]{1,0:T(8,128)(2,1)S(1)}, u32[]{:S(2)}, u32[]{:S(2)}) collective-permute-start(bf16[128,1024]{1,0:T(8,128)(2,1)S(1)} %collective-permute-done.24), channel_id=1, source_target_pairs={{0,2},{1,3},{4,0},{5,1},{8,4},{9,5},{12,8},{13,9},{14,12},{15,13},... | collective-permute-start | bytes 786440 | tf_op jit(solution)/shard_map/ppermute | solution.py:109
  195.7 7.2 %collective-permute-done.27 = bf16[128,1024]{1,0:T(8,128)(2,1)S(1)} collective-permute-done((bf16[128,1024]{1,0:T(8,128)(2,1)S(1)}, bf16[128,1024]{1,0:T(8,128)(2,1)S(1)}, u32[]{:S(2)}, u32[]{:S(2)}) %collective-permute-start.27) | collective-permute-done | bytes 262176 | tf_op jit(solution)/shard_map/ppermute | solution.py:105
  204.8 5.9 %collective-permute-done.31 = bf16[128,1024]{1,0:T(8,128)(2,1)S(1)} collective-permute-done((bf16[128,1024]{1,0:T(8,128)(2,1)S(1)}, bf16[128,1024]{1,0:T(8,128)(2,1)S(1)}, u32[]{:S(2)}, u32[]{:S(2)}) %collective-permute-start.31) | collective-permute-done | bytes 262176 | tf_op jit(solution)/shard_map/ppermute | solution.py:105
  214.5 3.6 %all-to-all-start.1 = ((bf16[16,8,2048]{2,1,0:T(8,128)(2,1)}), bf16[16,8,2048]{2,1,0:T(8,128)(2,1)S(1)}, u32[]{:S(2)}, u32[]{:S(2)}) async-start(bf16[16,8,2048]{2,1,0:T(8,128)(2,1)} %select_bitcast_fusion), calls=%async_computation.3 | async-start | bytes 1048576 | tf_op jit(solution)/shard_map/all_to_all | solution.py:187
  218.1 2.2 pad_maximum_fusion.3
  223.5 9.0 %all-to-all-done.1 = bf16[16,8,2048]{2,1,0:T(8,128)(2,1)S(1)} async-done(((bf16[16,8,2048]{2,1,0:T(8,128)(2,1)}), bf16[16,8,2048]{2,1,0:T(8,128)(2,1)S(1)}, u32[]{:S(2)}, u32[]{:S(2)}) %all-to-all-start.1) | async-done | bytes 524320 | tf_op jit(solution)/shard_map/all_to_all | solution.py:187
  (164 shorter events, 35.6 us)
Async XLA Ops:
  7.2 94.8 %reduce-scatter.5.cloned.1.call-start = ((), (), s32[]{:S(2)}) async-start(), calls=%async_computation.5 | async-start | bytes 4718592 | tf_op jit(solution)/shard_map/reduce_scatter | solution.py:53
  11.0 16.0 %collective-permute-start = (bf16[256,1024]{1,0:T(8,128)(2,1)}, bf16[256,1024]{1,0:T(8,128)(2,1)}, u32[]{:S(2)}, u32[]{:S(2)}) collective-permute-start(bf16[256,1024]{1,0:T(8,128)(2,1)} %reshape.207), channel_id=1, source_target_pairs={{0,2},{2,0},{1,3},{3,1},{4,6},{6,4},{5,7},{7,5},{8,10},{10,8},{9,1... | collective-permute-start | bytes 1572872 | tf_op jit(solution)/shard_map/ppermute | solution.py:42
  16.0 21.4 %collective-permute-start.2 = (bf16[256,1024]{1,0:T(8,128)(2,1)}, bf16[256,1024]{1,0:T(8,128)(2,1)}, u32[]{:S(2)}, u32[]{:S(2)}) collective-permute-start(bf16[256,1024]{1,0:T(8,128)(2,1)} %get-tuple-element.42), channel_id=1, source_target_pairs={{0,2},{2,0},{1,3},{3,1},{4,6},{6,4},{5,7},{7,5},{8,10},{10,8},{9,1... | collective-permute-start | bytes 1572872 | tf_op jit(solution)/shard_map/ppermute | solution.py:42
  44.7 29.2 %all-to-all-start = ((bf16[16,8,2048]{2,1,0:T(8,128)(2,1)}), bf16[16,8,2048]{2,1,0:T(8,128)(2,1)S(1)}, u32[]{:S(2)}, u32[]{:S(2)}) async-start(bf16[16,8,2048]{2,1,0:T(8,128)(2,1)} %select_bitcast_fusion.1), calls=%async_computation.2 | async-start | bytes 1048576 | tf_op jit(solution)/shard_map/all_to_all | solution.py:158
  50.8 120.5 %reduce-scatter.3.cloned.1.call-start = ((), (), s32[]{:S(2)}) async-start(), calls=%async_computation.4 | async-start | bytes 4718592 | tf_op jit(solution)/shard_map/reduce_scatter | solution.py:53
  50.9 19.2 %collective-permute-start.1 = (bf16[256,1024]{1,0:T(8,128)(2,1)S(1)}, bf16[256,1024]{1,0:T(8,128)(2,1)S(1)}, u32[]{:S(2)}, u32[]{:S(2)}) collective-permute-start(bf16[256,1024]{1,0:T(8,128)(2,1)S(1)} %get-tuple-element.43), channel_id=1, source_target_pairs={{0,2},{2,0},{1,3},{3,1},{4,6},{6,4},{5,7},{7,5},{8,10},{10,8},{9,1... | collective-permute-start | bytes 1572872 | tf_op jit(solution)/shard_map/ppermute | solution.py:43
  105.1 9.3 %collective-permute-start.5 = (bf16[128,1024]{1,0:T(8,128)(2,1)S(1)}, bf16[128,1024]{1,0:T(8,128)(2,1)S(1)}, u32[]{:S(2)}, u32[]{:S(2)}) collective-permute-start(bf16[128,1024]{1,0:T(8,128)(2,1)S(1)} %get-tuple-element.31), channel_id=1, source_target_pairs={{0,2},{1,3},{4,0},{5,1},{8,4},{9,5},{12,8},{13,9},{14,12},{15,13},... | collective-permute-start | bytes 786440 | tf_op jit(solution)/shard_map/ppermute | solution.py:109
  106.6 10.1 %collective-permute-start.4 = (bf16[128,1024]{1,0:T(8,128)(2,1)S(1)}, bf16[128,1024]{1,0:T(8,128)(2,1)S(1)}, u32[]{:S(2)}, u32[]{:S(2)}) collective-permute-start(bf16[128,1024]{1,0:T(8,128)(2,1)S(1)} %get-tuple-element.31), channel_id=1, source_target_pairs={{0,4},{1,5},{4,8},{5,9},{8,12},{9,13},{12,14},{13,15},{14,10},{15,... | collective-permute-start | bytes 786440 | tf_op jit(solution)/shard_map/ppermute | solution.py:105
  107.2 12.3 %collective-permute-start.3 = (bf16[128,1024]{1,0:T(8,128)(2,1)S(1)}, bf16[128,1024]{1,0:T(8,128)(2,1)S(1)}, u32[]{:S(2)}, u32[]{:S(2)}) collective-permute-start(bf16[128,1024]{1,0:T(8,128)(2,1)S(1)} %get-tuple-element.31), channel_id=1, source_target_pairs={{0,1},{1,0},{2,3},{3,2},{4,5},{5,4},{6,7},{7,6},{8,9},{9,8},{10,11... | collective-permute-start | bytes 786440 | tf_op jit(solution)/shard_map/ppermute | solution.py:101
  114.5 14.7 %collective-permute-start.9 = (bf16[128,1024]{1,0:T(8,128)(2,1)S(1)}, bf16[128,1024]{1,0:T(8,128)(2,1)S(1)}, u32[]{:S(2)}, u32[]{:S(2)}) collective-permute-start(bf16[128,1024]{1,0:T(8,128)(2,1)S(1)} %collective-permute-done.5), channel_id=1, source_target_pairs={{0,2},{1,3},{4,0},{5,1},{8,4},{9,5},{12,8},{13,9},{14,12},{15,13},... | collective-permute-start | bytes 786440 | tf_op jit(solution)/shard_map/ppermute | solution.py:109
  114.5 19.4 %collective-permute-start.7 = (bf16[128,1024]{1,0:T(8,128)(2,1)S(1)}, bf16[128,1024]{1,0:T(8,128)(2,1)S(1)}, u32[]{:S(2)}, u32[]{:S(2)}) collective-permute-start(bf16[128,1024]{1,0:T(8,128)(2,1)S(1)} %collective-permute-done.5), channel_id=1, source_target_pairs={{0,1},{1,0},{2,3},{3,2},{4,5},{5,4},{6,7},{7,6},{8,9},{9,8},{10,11... | collective-permute-start | bytes 786440 | tf_op jit(solution)/shard_map/ppermute | solution.py:101
  116.7 14.4 %collective-permute-start.8 = (bf16[128,1024]{1,0:T(8,128)(2,1)S(1)}, bf16[128,1024]{1,0:T(8,128)(2,1)S(1)}, u32[]{:S(2)}, u32[]{:S(2)}) collective-permute-start(bf16[128,1024]{1,0:T(8,128)(2,1)S(1)} %collective-permute-done.4), channel_id=1, source_target_pairs={{0,4},{1,5},{4,8},{5,9},{8,12},{9,13},{12,14},{13,15},{14,10},{15,... | collective-permute-start | bytes 786440 | tf_op jit(solution)/shard_map/ppermute | solution.py:105
  119.2 15.0 %collective-permute-start.6 = (bf16[128,1024]{1,0:T(8,128)(2,1)S(1)}, bf16[128,1024]{1,0:T(8,128)(2,1)S(1)}, u32[]{:S(2)}, u32[]{:S(2)}) collective-permute-start(bf16[128,1024]{1,0:T(8,128)(2,1)S(1)} %collective-permute-done.4), channel_id=1, source_target_pairs={{0,1},{1,0},{2,3},{3,2},{4,5},{5,4},{6,7},{7,6},{8,9},{9,8},{10,11... | collective-permute-start | bytes 786440 | tf_op jit(solution)/shard_map/ppermute | solution.py:101
  129.2 19.0 %collective-permute-start.13 = (bf16[128,1024]{1,0:T(8,128)(2,1)S(1)}, bf16[128,1024]{1,0:T(8,128)(2,1)S(1)}, u32[]{:S(2)}, u32[]{:S(2)}) collective-permute-start(bf16[128,1024]{1,0:T(8,128)(2,1)S(1)} %collective-permute-done.9), channel_id=1, source_target_pairs={{0,2},{1,3},{4,0},{5,1},{8,4},{9,5},{12,8},{13,9},{14,12},{15,13},... | collective-permute-start | bytes 786440 | tf_op jit(solution)/shard_map/ppermute | solution.py:109
  130.2 18.9 %collective-permute-start.11 = (bf16[128,1024]{1,0:T(8,128)(2,1)S(1)}, bf16[128,1024]{1,0:T(8,128)(2,1)S(1)}, u32[]{:S(2)}, u32[]{:S(2)}) collective-permute-start(bf16[128,1024]{1,0:T(8,128)(2,1)S(1)} %collective-permute-done.9), channel_id=1, source_target_pairs={{0,1},{1,0},{2,3},{3,2},{4,5},{5,4},{6,7},{7,6},{8,9},{9,8},{10,11... | collective-permute-start | bytes 786440 | tf_op jit(solution)/shard_map/ppermute | solution.py:101
  131.2 14.5 %collective-permute-start.12 = (bf16[128,1024]{1,0:T(8,128)(2,1)S(1)}, bf16[128,1024]{1,0:T(8,128)(2,1)S(1)}, u32[]{:S(2)}, u32[]{:S(2)}) collective-permute-start(bf16[128,1024]{1,0:T(8,128)(2,1)S(1)} %collective-permute-done.8), channel_id=1, source_target_pairs={{0,4},{1,5},{4,8},{5,9},{8,12},{9,13},{12,14},{13,15},{14,10},{15,... | collective-permute-start | bytes 786440 | tf_op jit(solution)/shard_map/ppermute | solution.py:105
  133.9 15.4 %collective-permute-start.10 = (bf16[128,1024]{1,0:T(8,128)(2,1)S(1)}, bf16[128,1024]{1,0:T(8,128)(2,1)S(1)}, u32[]{:S(2)}, u32[]{:S(2)}) collective-permute-start(bf16[128,1024]{1,0:T(8,128)(2,1)S(1)} %collective-permute-done.8), channel_id=1, source_target_pairs={{0,1},{1,0},{2,3},{3,2},{4,5},{5,4},{6,7},{7,6},{8,9},{9,8},{10,11... | collective-permute-start | bytes 786440 | tf_op jit(solution)/shard_map/ppermute | solution.py:101
  145.6 14.3 %collective-permute-start.16 = (bf16[128,1024]{1,0:T(8,128)(2,1)S(1)}, bf16[128,1024]{1,0:T(8,128)(2,1)S(1)}, u32[]{:S(2)}, u32[]{:S(2)}) collective-permute-start(bf16[128,1024]{1,0:T(8,128)(2,1)S(1)} %collective-permute-done.12), channel_id=1, source_target_pairs={{0,4},{1,5},{4,8},{5,9},{8,12},{9,13},{12,14},{13,15},{14,10},{15,... | collective-permute-start | bytes 786440 | tf_op jit(solution)/shard_map/ppermute | solution.py:105
  148.1 12.2 %collective-permute-start.14 = (bf16[128,1024]{1,0:T(8,128)(2,1)S(1)}, bf16[128,1024]{1,0:T(8,128)(2,1)S(1)}, u32[]{:S(2)}, u32[]{:S(2)}) collective-permute-start(bf16[128,1024]{1,0:T(8,128)(2,1)S(1)} %collective-permute-done.12), channel_id=1, source_target_pairs={{0,1},{1,0},{2,3},{3,2},{4,5},{5,4},{6,7},{7,6},{8,9},{9,8},{10,11... | collective-permute-start | bytes 786440 | tf_op jit(solution)/shard_map/ppermute | solution.py:101
  148.1 12.0 %collective-permute-start.15 = (bf16[128,1024]{1,0:T(8,128)(2,1)S(1)}, bf16[128,1024]{1,0:T(8,128)(2,1)S(1)}, u32[]{:S(2)}, u32[]{:S(2)}) collective-permute-start(bf16[128,1024]{1,0:T(8,128)(2,1)S(1)} %collective-permute-done.13), channel_id=1, source_target_pairs={{0,1},{1,0},{2,3},{3,2},{4,5},{5,4},{6,7},{7,6},{8,9},{9,8},{10,11... | collective-permute-start | bytes 786440 | tf_op jit(solution)/shard_map/ppermute | solution.py:101
  174.7 8.5 %collective-permute-start.20 = (bf16[128,1024]{1,0:T(8,128)(2,1)S(1)}, bf16[128,1024]{1,0:T(8,128)(2,1)S(1)}, u32[]{:S(2)}, u32[]{:S(2)}) collective-permute-start(bf16[128,1024]{1,0:T(8,128)(2,1)S(1)} %get-tuple-element.26), channel_id=1, source_target_pairs={{0,2},{1,3},{4,0},{5,1},{8,4},{9,5},{12,8},{13,9},{14,12},{15,13},... | collective-permute-start | bytes 786440 | tf_op jit(solution)/shard_map/ppermute | solution.py:109
  176.7 9.1 %collective-permute-start.19 = (bf16[128,1024]{1,0:T(8,128)(2,1)S(1)}, bf16[128,1024]{1,0:T(8,128)(2,1)S(1)}, u32[]{:S(2)}, u32[]{:S(2)}) collective-permute-start(bf16[128,1024]{1,0:T(8,128)(2,1)S(1)} %get-tuple-element.26), channel_id=1, source_target_pairs={{0,4},{1,5},{4,8},{5,9},{8,12},{9,13},{12,14},{13,15},{14,10},{15,... | collective-permute-start | bytes 786440 | tf_op jit(solution)/shard_map/ppermute | solution.py:105
  176.9 9.5 %collective-permute-start.18 = (bf16[128,1024]{1,0:T(8,128)(2,1)S(1)}, bf16[128,1024]{1,0:T(8,128)(2,1)S(1)}, u32[]{:S(2)}, u32[]{:S(2)}) collective-permute-start(bf16[128,1024]{1,0:T(8,128)(2,1)S(1)} %get-tuple-element.26), channel_id=1, source_target_pairs={{0,1},{1,0},{2,3},{3,2},{4,5},{5,4},{6,7},{7,6},{8,9},{9,8},{10,11... | collective-permute-start | bytes 786440 | tf_op jit(solution)/shard_map/ppermute | solution.py:101
  183.2 8.5 %collective-permute-start.24 = (bf16[128,1024]{1,0:T(8,128)(2,1)S(1)}, bf16[128,1024]{1,0:T(8,128)(2,1)S(1)}, u32[]{:S(2)}, u32[]{:S(2)}) collective-permute-start(bf16[128,1024]{1,0:T(8,128)(2,1)S(1)} %collective-permute-done.20), channel_id=1, source_target_pairs={{0,2},{1,3},{4,0},{5,1},{8,4},{9,5},{12,8},{13,9},{14,12},{15,13},... | collective-permute-start | bytes 786440 | tf_op jit(solution)/shard_map/ppermute | solution.py:109
  185.7 9.5 %collective-permute-start.22 = (bf16[128,1024]{1,0:T(8,128)(2,1)S(1)}, bf16[128,1024]{1,0:T(8,128)(2,1)S(1)}, u32[]{:S(2)}, u32[]{:S(2)}) collective-permute-start(bf16[128,1024]{1,0:T(8,128)(2,1)S(1)} %collective-permute-done.20), channel_id=1, source_target_pairs={{0,1},{1,0},{2,3},{3,2},{4,5},{5,4},{6,7},{7,6},{8,9},{9,8},{10,11... | collective-permute-start | bytes 786440 | tf_op jit(solution)/shard_map/ppermute | solution.py:101
  185.8 8.6 %collective-permute-start.23 = (bf16[128,1024]{1,0:T(8,128)(2,1)S(1)}, bf16[128,1024]{1,0:T(8,128)(2,1)S(1)}, u32[]{:S(2)}, u32[]{:S(2)}) collective-permute-start(bf16[128,1024]{1,0:T(8,128)(2,1)S(1)} %collective-permute-done.19), channel_id=1, source_target_pairs={{0,4},{1,5},{4,8},{5,9},{8,12},{9,13},{12,14},{13,15},{14,10},{15,... | collective-permute-start | bytes 786440 | tf_op jit(solution)/shard_map/ppermute | solution.py:105
  186.0 9.4 %collective-permute-start.21 = (bf16[128,1024]{1,0:T(8,128)(2,1)S(1)}, bf16[128,1024]{1,0:T(8,128)(2,1)S(1)}, u32[]{:S(2)}, u32[]{:S(2)}) collective-permute-start(bf16[128,1024]{1,0:T(8,128)(2,1)S(1)} %collective-permute-done.19), channel_id=1, source_target_pairs={{0,1},{1,0},{2,3},{3,2},{4,5},{5,4},{6,7},{7,6},{8,9},{9,8},{10,11... | collective-permute-start | bytes 786440 | tf_op jit(solution)/shard_map/ppermute | solution.py:101
  191.7 11.7 %collective-permute-start.28 = (bf16[128,1024]{1,0:T(8,128)(2,1)S(1)}, bf16[128,1024]{1,0:T(8,128)(2,1)S(1)}, u32[]{:S(2)}, u32[]{:S(2)}) collective-permute-start(bf16[128,1024]{1,0:T(8,128)(2,1)S(1)} %collective-permute-done.24), channel_id=1, source_target_pairs={{0,2},{1,3},{4,0},{5,1},{8,4},{9,5},{12,8},{13,9},{14,12},{15,13},... | collective-permute-start | bytes 786440 | tf_op jit(solution)/shard_map/ppermute | solution.py:109
  194.2 10.0 %collective-permute-start.26 = (bf16[128,1024]{1,0:T(8,128)(2,1)S(1)}, bf16[128,1024]{1,0:T(8,128)(2,1)S(1)}, u32[]{:S(2)}, u32[]{:S(2)}) collective-permute-start(bf16[128,1024]{1,0:T(8,128)(2,1)S(1)} %collective-permute-done.24), channel_id=1, source_target_pairs={{0,1},{1,0},{2,3},{3,2},{4,5},{5,4},{6,7},{7,6},{8,9},{9,8},{10,11... | collective-permute-start | bytes 786440 | tf_op jit(solution)/shard_map/ppermute | solution.py:101
  194.4 8.5 %collective-permute-start.27 = (bf16[128,1024]{1,0:T(8,128)(2,1)S(1)}, bf16[128,1024]{1,0:T(8,128)(2,1)S(1)}, u32[]{:S(2)}, u32[]{:S(2)}) collective-permute-start(bf16[128,1024]{1,0:T(8,128)(2,1)S(1)} %collective-permute-done.23), channel_id=1, source_target_pairs={{0,4},{1,5},{4,8},{5,9},{8,12},{9,13},{12,14},{13,15},{14,10},{15,... | collective-permute-start | bytes 786440 | tf_op jit(solution)/shard_map/ppermute | solution.py:105
  195.1 9.3 %collective-permute-start.25 = (bf16[128,1024]{1,0:T(8,128)(2,1)S(1)}, bf16[128,1024]{1,0:T(8,128)(2,1)S(1)}, u32[]{:S(2)}, u32[]{:S(2)}) collective-permute-start(bf16[128,1024]{1,0:T(8,128)(2,1)S(1)} %collective-permute-done.23), channel_id=1, source_target_pairs={{0,1},{1,0},{2,3},{3,2},{4,5},{5,4},{6,7},{7,6},{8,9},{9,8},{10,11... | collective-permute-start | bytes 786440 | tf_op jit(solution)/shard_map/ppermute | solution.py:101
  214.5 18.0 %all-to-all-start.1 = ((bf16[16,8,2048]{2,1,0:T(8,128)(2,1)}), bf16[16,8,2048]{2,1,0:T(8,128)(2,1)S(1)}, u32[]{:S(2)}, u32[]{:S(2)}) async-start(bf16[16,8,2048]{2,1,0:T(8,128)(2,1)} %select_bitcast_fusion), calls=%async_computation.3 | async-start | bytes 1048576 | tf_op jit(solution)/shard_map/all_to_all | solution.py:187
  (16 other events, 165.7 us)
Sparse Core Ops, SparseCore 0:
  42.0 59.9 reduce-scatter.4
  104.3 66.9 reduce-scatter.2

commit v10 on v9

--- a/solution.py
+++ b/solution.py
@@ -41,14 +41,12 @@
     half = grad_out.shape[1] // 2
     got_queries, got_first = lax.ppermute((theirs, grad_out[:, :half]), "xl", swap)
     got_second = lax.ppermute(grad_out[:, half:], "xl", swap)
-    both_queries = jnp.concatenate([mine, got_queries], axis=0)
     parts = []
     for own, got in ((grad_out[:, :half], got_first), (grad_out[:, half:], got_second)):
         partial = lax.dot_general(
-            both_queries,
-            jnp.concatenate([own, got], axis=0),
-            (((0,), (0,)), ((), ())),
-            preferred_element_type=jnp.float32,
+            mine, own, (((0,), (0,)), ((), ())), preferred_element_type=jnp.float32
+        ) + lax.dot_general(
+            got_queries, got, (((0,), (0,)), ((), ())), preferred_element_type=jnp.float32
         )
         parts.append(lax.psum_scatter(partial, ("zo", "c"), scatter_dimension=0, tiled=True))
     return parts

time: 242 us -> 243 us (level)
    dot_general x2 -> x4, matrix products: 7.73 us -> 8 us  [the longest x2 6.51 us: pair_gradient(): lax.dot_general(got_queries, got, (((0,), (0,)), ((), ())), preferred_ele...]
where the time goes in v10:
time: 243 us
  waiting for transfers between devices  139 us (57%)
  starting transfers between devices  38.7 us (16%)
  other arithmetic  21.1 us (9%)
  between operations  16.8 us (7%)
  matrix products  15.1 us (6%)
  local copies, waits for them, and re-layouts  12.4 us (5%)
    reduce_scatter x2, waiting for transfers between devices, pair_gradient(): lax.psum_scatter(partial, ('zo', 'c'), scatter_dimension=0, tiled=True)  35.7 us
    ppermute x8, waiting for transfers between devices, ring_codes(): ahead = lax.ppermute(ahead, DP, forward)  35.7 us
    ppermute x6, waiting for transfers between devices, ring_codes(): behind = lax.ppermute(behind, DP, backward)  21.6 us
    ppermute x2, waiting for transfers between devices, pair_gradient(): lax.ppermute((theirs, grad_out[:, :half]), 'xl', swap)  21.3 us
    ppermute x1, waiting for transfers between devices, pair_gradient(): got_second = lax.ppermute(grad_out[:, half:], 'xl', swap)  14.4 us
    ppermute x8, starting transfers between devices, ring_codes(): ahead = lax.ppermute(ahead, DP, forward)  9.35 us
    ppermute x6, starting transfers between devices, ring_codes(): behind = lax.ppermute(behind, DP, backward)  9.14 us
    all_to_all x1, waiting for transfers between devices, per_device(): lax.all_to_all(jnp.take(normed, send_back, axis=0), DP, split_axis=0, con...  8 us
  transfers between devices with their start and end apart: 37, of which 20 were waited for; matrix products, arithmetic and copies ran while one was open for 13% of the time, Pallas kernels for 0%

profile of v10, /device:TPU:0, one launch (start us, length us, event | category | flops | bytes accessed | tf_op | source)
XLA Modules:
  0.0 242.8 jit_solution(10631604651301408884)
XLA Ops:
  10.7 2.2 reshape.207
  12.9 2.9 %collective-permute-start = (bf16[256,1024]{1,0:T(8,128)(2,1)}, bf16[256,1024]{1,0:T(8,128)(2,1)S(1)}, u32[]{:S(2)}, u32[]{:S(2)}) collective-permute-start(bf16[256,1024]{1,0:T(8,128)(2,1)} %reshape.207), channel_id=1, source_target_pairs={{0,2},{2,0},{1,3},{3,1},{4,6},{6,4},{5,7},{7,5},{8,10},{10,8},{9,1... | collective-permute-start | bytes 1572872 | tf_op jit(solution)/shard_map/ppermute | solution.py:42
  18.0 10.8 %collective-permute-done = bf16[256,1024]{1,0:T(8,128)(2,1)S(1)} collective-permute-done((bf16[256,1024]{1,0:T(8,128)(2,1)}, bf16[256,1024]{1,0:T(8,128)(2,1)S(1)}, u32[]{:S(2)}, u32[]{:S(2)}) %collective-permute-start) | collective-permute-done | bytes 524320 | tf_op jit(solution)/shard_map/ppermute | solution.py:42
  28.8 10.5 %collective-permute-done.2 = bf16[256,1024]{1,0:T(8,128)(2,1)} collective-permute-done((bf16[256,1024]{1,0:T(8,128)(2,1)}, bf16[256,1024]{1,0:T(8,128)(2,1)}, u32[]{:S(2)}, u32[]{:S(2)}) %collective-permute-start.2) | collective-permute-done | bytes 524320 | tf_op jit(solution)/shard_map/ppermute | solution.py:42
  39.3 3.8 %convolution_add_fusion = f32[1024,1024]{1,0:T(8,128)} fusion(f32[1024,1024]{1,0:T(8,128)S(1)} %fusion.118, bf16[256,1024]{1,0:T(8,128)(2,1)S(1)} %collective-permute-done, bf16[256,1024]{1,0:T(8,128)(2,1)} %collective-permute-done.2), kind=kOutput, calls=%fused_computation.5 | convolution fusion | flops 537919488 | bytes 9437184 | tf_op jit(solution)/shard_map/dot_general | solution.py:48
  46.5 6.2 %all-to-all-start = ((bf16[16,8,2048]{2,1,0:T(8,128)(2,1)}), bf16[16,8,2048]{2,1,0:T(8,128)(2,1)S(1)}, u32[]{:S(2)}, u32[]{:S(2)}) async-start(bf16[16,8,2048]{2,1,0:T(8,128)(2,1)} %select_bitcast_fusion.1), calls=%async_computation.2 | async-start | bytes 1048576 | tf_op jit(solution)/shard_map/all_to_all | solution.py:156
  52.7 2.0 collective-permute-start.1
  57.6 14.4 %collective-permute-done.1 = bf16[256,1024]{1,0:T(8,128)(2,1)S(1)} collective-permute-done((bf16[256,1024]{1,0:T(8,128)(2,1)}, bf16[256,1024]{1,0:T(8,128)(2,1)S(1)}, u32[]{:S(2)}, u32[]{:S(2)}) %collective-permute-start.1) | collective-permute-done | bytes 524320 | tf_op jit(solution)/shard_map/ppermute | solution.py:43
  71.9 2.7 %convolution_add_fusion.1 = f32[1024,1024]{1,0:T(8,128)} fusion(f32[1024,1024]{1,0:T(8,128)S(1)} %fusion.120, bf16[256,1024]{1,0:T(8,128)(2,1)S(1)} %collective-permute-done, bf16[256,1024]{1,0:T(8,128)(2,1)S(1)} %collective-permute-done.1), kind=kOutput, calls=%fused_computation.6 | convolution fusion | flops 537919488 | bytes 9437184 | tf_op jit(solution)/shard_map/dot_general | solution.py:48
  76.7 26.5 %reduce-scatter.5.cloned.1.call-done = f32[128,1024]{1,0:T(8,128)} async-done(((f32[1024,1024]{1,0:T(8,128)}), f32[128,1024]{1,0:T(8,128)}) %reduce-scatter.5.cloned.1.call-update) | async-done | bytes 524304 | tf_op jit(solution)/shard_map/reduce_scatter | solution.py:51
  103.2 3.3 %fusion.123 = (bf16[128,1024]{1,0:T(8,128)(2,1)S(1)}, f32[128,1024]{1,0:T(8,128)}, f32[128,1024]{1,0:T(8,128)}, f32[128,1024]{1,0:T(8,128)}, f32[128,1024]{1,0:T(8,128)S(1)}) fusion(f32[128,2048]{1,0:T(8,128)S(1)} %copy-done.9, f32[128,2048]{1,0:T(8,128)} %param.17, f32[128,1024]{1,0:T(8,128)} %reduce-scatter.5.cloned.1.call-done, f32[128,2048]{1,0:T(8,128)} %param.18, ...), kind=kLoop, calls=%fused_computation.214 | loop fusion | flops 2621440 | bytes 4980736 | tf_op jit(solution)/shard_map/convert_element_type | solution.py:179
  111.2 2.3 broadcast_select_fusion
  113.5 2.4 collective-permute-done.5
  115.9 2.1 collective-permute-start.7
  118.3 2.5 %collective-permute-start.8 = (bf16[128,1024]{1,0:T(8,128)(2,1)S(1)}, bf16[128,1024]{1,0:T(8,128)(2,1)S(1)}, u32[]{:S(2)}, u32[]{:S(2)}) collective-permute-start(bf16[128,1024]{1,0:T(8,128)(2,1)S(1)} %collective-permute-done.4), channel_id=1, source_target_pairs={{0,4},{1,5},{4,8},{5,9},{8,12},{9,13},{12,14},{13,15},{14,10},{15,... | collective-permute-start | bytes 786440 | tf_op jit(solution)/shard_map/ppermute | solution.py:103
  121.4 9.2 %collective-permute-done.9 = bf16[128,1024]{1,0:T(8,128)(2,1)S(1)} collective-permute-done((bf16[128,1024]{1,0:T(8,128)(2,1)S(1)}, bf16[128,1024]{1,0:T(8,128)(2,1)S(1)}, u32[]{:S(2)}, u32[]{:S(2)}) %collective-permute-start.9) | collective-permute-done | bytes 262176 | tf_op jit(solution)/shard_map/ppermute | solution.py:107
  132.8 2.5 %collective-permute-start.12 = (bf16[128,1024]{1,0:T(8,128)(2,1)S(1)}, bf16[128,1024]{1,0:T(8,128)(2,1)S(1)}, u32[]{:S(2)}, u32[]{:S(2)}) collective-permute-start(bf16[128,1024]{1,0:T(8,128)(2,1)S(1)} %collective-permute-done.8), channel_id=1, source_target_pairs={{0,4},{1,5},{4,8},{5,9},{8,12},{9,13},{12,14},{13,15},{14,10},{15,... | collective-permute-start | bytes 786440 | tf_op jit(solution)/shard_map/ppermute | solution.py:103
  136.1 11.2 %collective-permute-done.12 = bf16[128,1024]{1,0:T(8,128)(2,1)S(1)} collective-permute-done((bf16[128,1024]{1,0:T(8,128)(2,1)S(1)}, bf16[128,1024]{1,0:T(8,128)(2,1)S(1)}, u32[]{:S(2)}, u32[]{:S(2)}) %collective-permute-start.12) | collective-permute-done | bytes 262176 | tf_op jit(solution)/shard_map/ppermute | solution.py:103
  147.2 2.5 %collective-permute-start.16 = (bf16[128,1024]{1,0:T(8,128)(2,1)S(1)}, bf16[128,1024]{1,0:T(8,128)(2,1)S(1)}, u32[]{:S(2)}, u32[]{:S(2)}) collective-permute-start(bf16[128,1024]{1,0:T(8,128)(2,1)S(1)} %collective-permute-done.12), channel_id=1, source_target_pairs={{0,4},{1,5},{4,8},{5,9},{8,12},{9,13},{12,14},{13,15},{14,10},{15,... | collective-permute-start | bytes 786440 | tf_op jit(solution)/shard_map/ppermute | solution.py:103
  151.2 10.3 %collective-permute-done.16 = bf16[128,1024]{1,0:T(8,128)(2,1)S(1)} collective-permute-done((bf16[128,1024]{1,0:T(8,128)(2,1)S(1)}, bf16[128,1024]{1,0:T(8,128)(2,1)S(1)}, u32[]{:S(2)}, u32[]{:S(2)}) %collective-permute-start.16) | collective-permute-done | bytes 262176 | tf_op jit(solution)/shard_map/ppermute | solution.py:103
  163.5 9.2 %reduce-scatter.3.cloned.1.call-done = f32[128,1024]{1,0:T(8,128)} async-done(((f32[1024,1024]{1,0:T(8,128)}), f32[128,1024]{1,0:T(8,128)}) %reduce-scatter.3.cloned.1.call-update) | async-done | bytes 524304 | tf_op jit(solution)/shard_map/reduce_scatter | solution.py:51
  172.7 3.4 %fusion.122 = (bf16[128,1024]{1,0:T(8,128)(2,1)S(1)}, f32[128,1024]{1,0:T(8,128)}, f32[128,1024]{1,0:T(8,128)}, f32[128,1024]{1,0:T(8,128)}, f32[128,1024]{1,0:T(8,128)}) fusion(f32[128,2048]{1,0:T(8,128)} %param.20, f32[128,2048]{1,0:T(8,128)} %param.17, f32[128,1024]{1,0:T(8,128)} %reduce-scatter.3.cloned.1.call-done, f32[128,2048]{1,0:T(8,128)} %param.18, ...), kind=kLoop, calls=%fused_computation.213 | loop fusion | flops 2621440 | bytes 4980736 | tf_op jit(solution)/shard_map/convert_element_type | solution.py:179
  179.2 5.1 %collective-permute-done.20 = bf16[128,1024]{1,0:T(8,128)(2,1)S(1)} collective-permute-done((bf16[128,1024]{1,0:T(8,128)(2,1)S(1)}, bf16[128,1024]{1,0:T(8,128)(2,1)S(1)}, u32[]{:S(2)}, u32[]{:S(2)}) %collective-permute-start.20) | collective-permute-done | bytes 262176 | tf_op jit(solution)/shard_map/ppermute | solution.py:107
  184.3 2.4 collective-permute-start.24
  188.1 4.8 %collective-permute-done.24 = bf16[128,1024]{1,0:T(8,128)(2,1)S(1)} collective-permute-done((bf16[128,1024]{1,0:T(8,128)(2,1)S(1)}, bf16[128,1024]{1,0:T(8,128)(2,1)S(1)}, u32[]{:S(2)}, u32[]{:S(2)}) %collective-permute-start.24) | collective-permute-done | bytes 262176 | tf_op jit(solution)/shard_map/ppermute | solution.py:107
  192.9 2.5 %collective-permute-start.28 = (bf16[128,1024]{1,0:T(8,128)(2,1)S(1)}, bf16[128,1024]{1,0:T(8,128)(2,1)S(1)}, u32[]{:S(2)}, u32[]{:S(2)}) collective-permute-start(bf16[128,1024]{1,0:T(8,128)(2,1)S(1)} %collective-permute-done.24), channel_id=1, source_target_pairs={{0,2},{1,3},{4,0},{5,1},{8,4},{9,5},{12,8},{13,9},{14,12},{15,13},... | collective-permute-start | bytes 786440 | tf_op jit(solution)/shard_map/ppermute | solution.py:107
  196.9 7.2 %collective-permute-done.27 = bf16[128,1024]{1,0:T(8,128)(2,1)S(1)} collective-permute-done((bf16[128,1024]{1,0:T(8,128)(2,1)S(1)}, bf16[128,1024]{1,0:T(8,128)(2,1)S(1)}, u32[]{:S(2)}, u32[]{:S(2)}) %collective-permute-start.27) | collective-permute-done | bytes 262176 | tf_op jit(solution)/shard_map/ppermute | solution.py:103
  205.9 6.1 %collective-permute-done.31 = bf16[128,1024]{1,0:T(8,128)(2,1)S(1)} collective-permute-done((bf16[128,1024]{1,0:T(8,128)(2,1)S(1)}, bf16[128,1024]{1,0:T(8,128)(2,1)S(1)}, u32[]{:S(2)}, u32[]{:S(2)}) %collective-permute-start.31) | collective-permute-done | bytes 262176 | tf_op jit(solution)/shard_map/ppermute | solution.py:103
  215.9 3.7 %all-to-all-start.1 = ((bf16[16,8,2048]{2,1,0:T(8,128)(2,1)}), bf16[16,8,2048]{2,1,0:T(8,128)(2,1)S(1)}, u32[]{:S(2)}, u32[]{:S(2)}) async-start(bf16[16,8,2048]{2,1,0:T(8,128)(2,1)} %select_bitcast_fusion), calls=%async_computation.3 | async-start | bytes 1048576 | tf_op jit(solution)/shard_map/all_to_all | solution.py:185
  219.6 2.2 pad_maximum_fusion.3
  221.8 2.1 pad_maximum_fusion
  226.0 8.0 %all-to-all-done.1 = bf16[16,8,2048]{2,1,0:T(8,128)(2,1)S(1)} async-done(((bf16[16,8,2048]{2,1,0:T(8,128)(2,1)}), bf16[16,8,2048]{2,1,0:T(8,128)(2,1)S(1)}, u32[]{:S(2)}, u32[]{:S(2)}) %all-to-all-start.1) | async-done | bytes 524320 | tf_op jit(solution)/shard_map/all_to_all | solution.py:185
  (170 shorter events, 39.1 us)
Async XLA Ops:
  7.2 96.0 %reduce-scatter.5.cloned.1.call-start = ((), (), s32[]{:S(2)}) async-start(), calls=%async_computation.5 | async-start | bytes 4718592 | tf_op jit(solution)/shard_map/reduce_scatter | solution.py:51
  12.9 15.9 %collective-permute-start = (bf16[256,1024]{1,0:T(8,128)(2,1)}, bf16[256,1024]{1,0:T(8,128)(2,1)S(1)}, u32[]{:S(2)}, u32[]{:S(2)}) collective-permute-start(bf16[256,1024]{1,0:T(8,128)(2,1)} %reshape.207), channel_id=1, source_target_pairs={{0,2},{2,0},{1,3},{3,1},{4,6},{6,4},{5,7},{7,5},{8,10},{10,8},{9,1... | collective-permute-start | bytes 1572872 | tf_op jit(solution)/shard_map/ppermute | solution.py:42
  16.9 22.4 %collective-permute-start.2 = (bf16[256,1024]{1,0:T(8,128)(2,1)}, bf16[256,1024]{1,0:T(8,128)(2,1)}, u32[]{:S(2)}, u32[]{:S(2)}) collective-permute-start(bf16[256,1024]{1,0:T(8,128)(2,1)} %get-tuple-element.42), channel_id=1, source_target_pairs={{0,2},{2,0},{1,3},{3,1},{4,6},{6,4},{5,7},{7,5},{8,10},{10,8},{9,1... | collective-permute-start | bytes 1572872 | tf_op jit(solution)/shard_map/ppermute | solution.py:42
  46.5 29.2 %all-to-all-start = ((bf16[16,8,2048]{2,1,0:T(8,128)(2,1)}), bf16[16,8,2048]{2,1,0:T(8,128)(2,1)S(1)}, u32[]{:S(2)}, u32[]{:S(2)}) async-start(bf16[16,8,2048]{2,1,0:T(8,128)(2,1)} %select_bitcast_fusion.1), calls=%async_computation.2 | async-start | bytes 1048576 | tf_op jit(solution)/shard_map/all_to_all | solution.py:156
  52.7 120.0 %reduce-scatter.3.cloned.1.call-start = ((), (), s32[]{:S(2)}) async-start(), calls=%async_computation.4 | async-start | bytes 4718592 | tf_op jit(solution)/shard_map/reduce_scatter | solution.py:51
  52.7 19.2 %collective-permute-start.1 = (bf16[256,1024]{1,0:T(8,128)(2,1)}, bf16[256,1024]{1,0:T(8,128)(2,1)S(1)}, u32[]{:S(2)}, u32[]{:S(2)}) collective-permute-start(bf16[256,1024]{1,0:T(8,128)(2,1)} %get-tuple-element.43), channel_id=1, source_target_pairs={{0,2},{2,0},{1,3},{3,1},{4,6},{6,4},{5,7},{7,5},{8,10},{10,8},{9,1... | collective-permute-start | bytes 1572872 | tf_op jit(solution)/shard_map/ppermute | solution.py:43
  106.5 9.4 %collective-permute-start.5 = (bf16[128,1024]{1,0:T(8,128)(2,1)S(1)}, bf16[128,1024]{1,0:T(8,128)(2,1)S(1)}, u32[]{:S(2)}, u32[]{:S(2)}) collective-permute-start(bf16[128,1024]{1,0:T(8,128)(2,1)S(1)} %get-tuple-element.31), channel_id=1, source_target_pairs={{0,2},{1,3},{4,0},{5,1},{8,4},{9,5},{12,8},{13,9},{14,12},{15,13},... | collective-permute-start | bytes 786440 | tf_op jit(solution)/shard_map/ppermute | solution.py:107
  108.0 10.3 %collective-permute-start.4 = (bf16[128,1024]{1,0:T(8,128)(2,1)S(1)}, bf16[128,1024]{1,0:T(8,128)(2,1)S(1)}, u32[]{:S(2)}, u32[]{:S(2)}) collective-permute-start(bf16[128,1024]{1,0:T(8,128)(2,1)S(1)} %get-tuple-element.31), channel_id=1, source_target_pairs={{0,4},{1,5},{4,8},{5,9},{8,12},{9,13},{12,14},{13,15},{14,10},{15,... | collective-permute-start | bytes 786440 | tf_op jit(solution)/shard_map/ppermute | solution.py:103
  108.5 12.5 %collective-permute-start.3 = (bf16[128,1024]{1,0:T(8,128)(2,1)S(1)}, bf16[128,1024]{1,0:T(8,128)(2,1)S(1)}, u32[]{:S(2)}, u32[]{:S(2)}) collective-permute-start(bf16[128,1024]{1,0:T(8,128)(2,1)S(1)} %get-tuple-element.31), channel_id=1, source_target_pairs={{0,1},{1,0},{2,3},{3,2},{4,5},{5,4},{6,7},{7,6},{8,9},{9,8},{10,11... | collective-permute-start | bytes 786440 | tf_op jit(solution)/shard_map/ppermute | solution.py:99
  115.9 14.8 %collective-permute-start.9 = (bf16[128,1024]{1,0:T(8,128)(2,1)S(1)}, bf16[128,1024]{1,0:T(8,128)(2,1)S(1)}, u32[]{:S(2)}, u32[]{:S(2)}) collective-permute-start(bf16[128,1024]{1,0:T(8,128)(2,1)S(1)} %collective-permute-done.5), channel_id=1, source_target_pairs={{0,2},{1,3},{4,0},{5,1},{8,4},{9,5},{12,8},{13,9},{14,12},{15,13},... | collective-permute-start | bytes 786440 | tf_op jit(solution)/shard_map/ppermute | solution.py:107
  115.9 19.6 %collective-permute-start.7 = (bf16[128,1024]{1,0:T(8,128)(2,1)S(1)}, bf16[128,1024]{1,0:T(8,128)(2,1)S(1)}, u32[]{:S(2)}, u32[]{:S(2)}) collective-permute-start(bf16[128,1024]{1,0:T(8,128)(2,1)S(1)} %collective-permute-done.5), channel_id=1, source_target_pairs={{0,1},{1,0},{2,3},{3,2},{4,5},{5,4},{6,7},{7,6},{8,9},{9,8},{10,11... | collective-permute-start | bytes 786440 | tf_op jit(solution)/shard_map/ppermute | solution.py:99
  118.3 14.5 %collective-permute-start.8 = (bf16[128,1024]{1,0:T(8,128)(2,1)S(1)}, bf16[128,1024]{1,0:T(8,128)(2,1)S(1)}, u32[]{:S(2)}, u32[]{:S(2)}) collective-permute-start(bf16[128,1024]{1,0:T(8,128)(2,1)S(1)} %collective-permute-done.4), channel_id=1, source_target_pairs={{0,4},{1,5},{4,8},{5,9},{8,12},{9,13},{12,14},{13,15},{14,10},{15,... | collective-permute-start | bytes 786440 | tf_op jit(solution)/shard_map/ppermute | solution.py:103
  120.7 15.0 %collective-permute-start.6 = (bf16[128,1024]{1,0:T(8,128)(2,1)S(1)}, bf16[128,1024]{1,0:T(8,128)(2,1)S(1)}, u32[]{:S(2)}, u32[]{:S(2)}) collective-permute-start(bf16[128,1024]{1,0:T(8,128)(2,1)S(1)} %collective-permute-done.4), channel_id=1, source_target_pairs={{0,1},{1,0},{2,3},{3,2},{4,5},{5,4},{6,7},{7,6},{8,9},{9,8},{10,11... | collective-permute-start | bytes 786440 | tf_op jit(solution)/shard_map/ppermute | solution.py:99
  130.7 19.1 %collective-permute-start.13 = (bf16[128,1024]{1,0:T(8,128)(2,1)S(1)}, bf16[128,1024]{1,0:T(8,128)(2,1)S(1)}, u32[]{:S(2)}, u32[]{:S(2)}) collective-permute-start(bf16[128,1024]{1,0:T(8,128)(2,1)S(1)} %collective-permute-done.9), channel_id=1, source_target_pairs={{0,2},{1,3},{4,0},{5,1},{8,4},{9,5},{12,8},{13,9},{14,12},{15,13},... | collective-permute-start | bytes 786440 | tf_op jit(solution)/shard_map/ppermute | solution.py:107
  131.7 19.0 %collective-permute-start.11 = (bf16[128,1024]{1,0:T(8,128)(2,1)S(1)}, bf16[128,1024]{1,0:T(8,128)(2,1)S(1)}, u32[]{:S(2)}, u32[]{:S(2)}) collective-permute-start(bf16[128,1024]{1,0:T(8,128)(2,1)S(1)} %collective-permute-done.9), channel_id=1, source_target_pairs={{0,1},{1,0},{2,3},{3,2},{4,5},{5,4},{6,7},{7,6},{8,9},{9,8},{10,11... | collective-permute-start | bytes 786440 | tf_op jit(solution)/shard_map/ppermute | solution.py:99
  132.8 14.5 %collective-permute-start.12 = (bf16[128,1024]{1,0:T(8,128)(2,1)S(1)}, bf16[128,1024]{1,0:T(8,128)(2,1)S(1)}, u32[]{:S(2)}, u32[]{:S(2)}) collective-permute-start(bf16[128,1024]{1,0:T(8,128)(2,1)S(1)} %collective-permute-done.8), channel_id=1, source_target_pairs={{0,4},{1,5},{4,8},{5,9},{8,12},{9,13},{12,14},{13,15},{14,10},{15,... | collective-permute-start | bytes 786440 | tf_op jit(solution)/shard_map/ppermute | solution.py:103
  135.5 15.4 %collective-permute-start.10 = (bf16[128,1024]{1,0:T(8,128)(2,1)S(1)}, bf16[128,1024]{1,0:T(8,128)(2,1)S(1)}, u32[]{:S(2)}, u32[]{:S(2)}) collective-permute-start(bf16[128,1024]{1,0:T(8,128)(2,1)S(1)} %collective-permute-done.8), channel_id=1, source_target_pairs={{0,1},{1,0},{2,3},{3,2},{4,5},{5,4},{6,7},{7,6},{8,9},{9,8},{10,11... | collective-permute-start | bytes 786440 | tf_op jit(solution)/shard_map/ppermute | solution.py:99
  147.2 14.3 %collective-permute-start.16 = (bf16[128,1024]{1,0:T(8,128)(2,1)S(1)}, bf16[128,1024]{1,0:T(8,128)(2,1)S(1)}, u32[]{:S(2)}, u32[]{:S(2)}) collective-permute-start(bf16[128,1024]{1,0:T(8,128)(2,1)S(1)} %collective-permute-done.12), channel_id=1, source_target_pairs={{0,4},{1,5},{4,8},{5,9},{8,12},{9,13},{12,14},{13,15},{14,10},{15,... | collective-permute-start | bytes 786440 | tf_op jit(solution)/shard_map/ppermute | solution.py:103
  149.7 12.2 %collective-permute-start.14 = (bf16[128,1024]{1,0:T(8,128)(2,1)S(1)}, bf16[128,1024]{1,0:T(8,128)(2,1)S(1)}, u32[]{:S(2)}, u32[]{:S(2)}) collective-permute-start(bf16[128,1024]{1,0:T(8,128)(2,1)S(1)} %collective-permute-done.12), channel_id=1, source_target_pairs={{0,1},{1,0},{2,3},{3,2},{4,5},{5,4},{6,7},{7,6},{8,9},{9,8},{10,11... | collective-permute-start | bytes 786440 | tf_op jit(solution)/shard_map/ppermute | solution.py:99
  149.7 12.0 %collective-permute-start.15 = (bf16[128,1024]{1,0:T(8,128)(2,1)S(1)}, bf16[128,1024]{1,0:T(8,128)(2,1)S(1)}, u32[]{:S(2)}, u32[]{:S(2)}) collective-permute-start(bf16[128,1024]{1,0:T(8,128)(2,1)S(1)} %collective-permute-done.13), channel_id=1, source_target_pairs={{0,1},{1,0},{2,3},{3,2},{4,5},{5,4},{6,7},{7,6},{8,9},{9,8},{10,11... | collective-permute-start | bytes 786440 | tf_op jit(solution)/shard_map/ppermute | solution.py:99
  176.1 8.2 %collective-permute-start.20 = (bf16[128,1024]{1,0:T(8,128)(2,1)S(1)}, bf16[128,1024]{1,0:T(8,128)(2,1)S(1)}, u32[]{:S(2)}, u32[]{:S(2)}) collective-permute-start(bf16[128,1024]{1,0:T(8,128)(2,1)S(1)} %get-tuple-element.26), channel_id=1, source_target_pairs={{0,2},{1,3},{4,0},{5,1},{8,4},{9,5},{12,8},{13,9},{14,12},{15,13},... | collective-permute-start | bytes 786440 | tf_op jit(solution)/shard_map/ppermute | solution.py:107
  177.9 9.1 %collective-permute-start.19 = (bf16[128,1024]{1,0:T(8,128)(2,1)S(1)}, bf16[128,1024]{1,0:T(8,128)(2,1)S(1)}, u32[]{:S(2)}, u32[]{:S(2)}) collective-permute-start(bf16[128,1024]{1,0:T(8,128)(2,1)S(1)} %get-tuple-element.26), channel_id=1, source_target_pairs={{0,4},{1,5},{4,8},{5,9},{8,12},{9,13},{12,14},{13,15},{14,10},{15,... | collective-permute-start | bytes 786440 | tf_op jit(solution)/shard_map/ppermute | solution.py:103
  178.2 9.4 %collective-permute-start.18 = (bf16[128,1024]{1,0:T(8,128)(2,1)S(1)}, bf16[128,1024]{1,0:T(8,128)(2,1)S(1)}, u32[]{:S(2)}, u32[]{:S(2)}) collective-permute-start(bf16[128,1024]{1,0:T(8,128)(2,1)S(1)} %get-tuple-element.26), channel_id=1, source_target_pairs={{0,1},{1,0},{2,3},{3,2},{4,5},{5,4},{6,7},{7,6},{8,9},{9,8},{10,11... | collective-permute-start | bytes 786440 | tf_op jit(solution)/shard_map/ppermute | solution.py:99
  184.3 8.6 %collective-permute-start.24 = (bf16[128,1024]{1,0:T(8,128)(2,1)S(1)}, bf16[128,1024]{1,0:T(8,128)(2,1)S(1)}, u32[]{:S(2)}, u32[]{:S(2)}) collective-permute-start(bf16[128,1024]{1,0:T(8,128)(2,1)S(1)} %collective-permute-done.20), channel_id=1, source_target_pairs={{0,2},{1,3},{4,0},{5,1},{8,4},{9,5},{12,8},{13,9},{14,12},{15,13},... | collective-permute-start | bytes 786440 | tf_op jit(solution)/shard_map/ppermute | solution.py:107
  186.7 9.5 %collective-permute-start.22 = (bf16[128,1024]{1,0:T(8,128)(2,1)S(1)}, bf16[128,1024]{1,0:T(8,128)(2,1)S(1)}, u32[]{:S(2)}, u32[]{:S(2)}) collective-permute-start(bf16[128,1024]{1,0:T(8,128)(2,1)S(1)} %collective-permute-done.20), channel_id=1, source_target_pairs={{0,1},{1,0},{2,3},{3,2},{4,5},{5,4},{6,7},{7,6},{8,9},{9,8},{10,11... | collective-permute-start | bytes 786440 | tf_op jit(solution)/shard_map/ppermute | solution.py:99
  187.0 8.4 %collective-permute-start.23 = (bf16[128,1024]{1,0:T(8,128)(2,1)S(1)}, bf16[128,1024]{1,0:T(8,128)(2,1)S(1)}, u32[]{:S(2)}, u32[]{:S(2)}) collective-permute-start(bf16[128,1024]{1,0:T(8,128)(2,1)S(1)} %collective-permute-done.19), channel_id=1, source_target_pairs={{0,4},{1,5},{4,8},{5,9},{8,12},{9,13},{12,14},{13,15},{14,10},{15,... | collective-permute-start | bytes 786440 | tf_op jit(solution)/shard_map/ppermute | solution.py:103
  187.4 9.2 %collective-permute-start.21 = (bf16[128,1024]{1,0:T(8,128)(2,1)S(1)}, bf16[128,1024]{1,0:T(8,128)(2,1)S(1)}, u32[]{:S(2)}, u32[]{:S(2)}) collective-permute-start(bf16[128,1024]{1,0:T(8,128)(2,1)S(1)} %collective-permute-done.19), channel_id=1, source_target_pairs={{0,1},{1,0},{2,3},{3,2},{4,5},{5,4},{6,7},{7,6},{8,9},{9,8},{10,11... | collective-permute-start | bytes 786440 | tf_op jit(solution)/shard_map/ppermute | solution.py:99
  192.9 11.7 %collective-permute-start.28 = (bf16[128,1024]{1,0:T(8,128)(2,1)S(1)}, bf16[128,1024]{1,0:T(8,128)(2,1)S(1)}, u32[]{:S(2)}, u32[]{:S(2)}) collective-permute-start(bf16[128,1024]{1,0:T(8,128)(2,1)S(1)} %collective-permute-done.24), channel_id=1, source_target_pairs={{0,2},{1,3},{4,0},{5,1},{8,4},{9,5},{12,8},{13,9},{14,12},{15,13},... | collective-permute-start | bytes 786440 | tf_op jit(solution)/shard_map/ppermute | solution.py:107
  195.4 10.0 %collective-permute-start.26 = (bf16[128,1024]{1,0:T(8,128)(2,1)S(1)}, bf16[128,1024]{1,0:T(8,128)(2,1)S(1)}, u32[]{:S(2)}, u32[]{:S(2)}) collective-permute-start(bf16[128,1024]{1,0:T(8,128)(2,1)S(1)} %collective-permute-done.24), channel_id=1, source_target_pairs={{0,1},{1,0},{2,3},{3,2},{4,5},{5,4},{6,7},{7,6},{8,9},{9,8},{10,11... | collective-permute-start | bytes 786440 | tf_op jit(solution)/shard_map/ppermute | solution.py:99
  195.4 8.7 %collective-permute-start.27 = (bf16[128,1024]{1,0:T(8,128)(2,1)S(1)}, bf16[128,1024]{1,0:T(8,128)(2,1)S(1)}, u32[]{:S(2)}, u32[]{:S(2)}) collective-permute-start(bf16[128,1024]{1,0:T(8,128)(2,1)S(1)} %collective-permute-done.23), channel_id=1, source_target_pairs={{0,4},{1,5},{4,8},{5,9},{8,12},{9,13},{12,14},{13,15},{14,10},{15,... | collective-permute-start | bytes 786440 | tf_op jit(solution)/shard_map/ppermute | solution.py:103
  196.1 9.5 %collective-permute-start.25 = (bf16[128,1024]{1,0:T(8,128)(2,1)S(1)}, bf16[128,1024]{1,0:T(8,128)(2,1)S(1)}, u32[]{:S(2)}, u32[]{:S(2)}) collective-permute-start(bf16[128,1024]{1,0:T(8,128)(2,1)S(1)} %collective-permute-done.23), channel_id=1, source_target_pairs={{0,1},{1,0},{2,3},{3,2},{4,5},{5,4},{6,7},{7,6},{8,9},{9,8},{10,11... | collective-permute-start | bytes 786440 | tf_op jit(solution)/shard_map/ppermute | solution.py:99
  215.9 18.1 %all-to-all-start.1 = ((bf16[16,8,2048]{2,1,0:T(8,128)(2,1)}), bf16[16,8,2048]{2,1,0:T(8,128)(2,1)S(1)}, u32[]{:S(2)}, u32[]{:S(2)}) async-start(bf16[16,8,2048]{2,1,0:T(8,128)(2,1)} %select_bitcast_fusion), calls=%async_computation.3 | async-start | bytes 1048576 | tf_op jit(solution)/shard_map/all_to_all | solution.py:185
  (19 other events, 171.5 us)
Sparse Core Ops, SparseCore 0:
  43.2 59.9 reduce-scatter.4
  105.5 67.1 reduce-scatter.2

commit v11 on v9

--- a/solution.py
+++ b/solution.py
@@ -38,7 +38,7 @@
     mine = mine.reshape(tokens, width // 2)
     theirs = theirs.reshape(tokens, width // 2)
     swap = [(0, 1), (1, 0)]
-    half = grad_out.shape[1] // 2
+    half = grad_out.shape[1] * 9 // 16
     got_queries, got_first = lax.ppermute((theirs, grad_out[:, :half]), "xl", swap)
     got_second = lax.ppermute(grad_out[:, half:], "xl", swap)
     both_queries = jnp.concatenate([mine, got_queries], axis=0)
@@ -165,10 +165,11 @@
     )
     kept = encoded_rows[0, 0] == encoded_rows[0, 0]
     queue = lax.optimization_barrier(jnp.where(kept, queue, jnp.zeros_like(queue)))
-    width = params.shape[1] // len(halves)
     results = []
-    for h, gradient in enumerate(halves):
-        cut = slice(h * width, (h + 1) * width)
+    start = 0
+    for gradient in halves:
+        cut = slice(start, start + gradient.shape[1])
+        start += gradient.shape[1]
         if results:
             gradient, results[-1] = lax.optimization_barrier((gradient, results[-1]))
         updated = adamw(

time: 242 us -> 242 us (level)
    all_to_all x1, waiting for transfers between devices: 0.01 us -> 16.9 us  [per_device(): lax.all_to_all(jnp.take(keys, send_forward, axis=0), DP, split_axis=0, co...]
    ppermute x1, waiting for transfers between devices: 15.1 us -> 0.01 us  [pair_gradient(): got_second = lax.ppermute(grad_out[:, half:], 'xl', swap)]
    reduce_scatter x2, waiting for transfers between devices: 36.5 us -> 30.8 us  [pair_gradient(): lax.psum_scatter(partial, ('zo', 'c'), scatter_dimension=0, tiled=True)]
    ppermute x6, waiting for transfers between devices: 21.8 us -> 25.5 us  [ring_codes(): behind = lax.ppermute(behind, DP, backward)]
  transfers between devices with their start and end apart: 37 -> 37, of which waited for: 20 -> 18; matrix products, arithmetic and copies ran while one was open for 13% -> 13% of each run, Pallas kernels for 0% -> 0%
where the time goes in v11:
time: 242 us
  waiting for transfers between devices  141 us (58%)
  starting transfers between devices  36.4 us (15%)
  other arithmetic  21 us (9%)
  between operations  17.1 us (7%)
  matrix products  13.9 us (6%)
  local copies, waits for them, and re-layouts  11.9 us (5%)
    ppermute x8, waiting for transfers between devices, ring_codes(): ahead = lax.ppermute(ahead, DP, forward)  36.5 us
    reduce_scatter x2, waiting for transfers between devices, pair_gradient(): lax.psum_scatter(partial, ('zo', 'c'), scatter_dimension=0, tiled=True)  30.8 us
    ppermute x6, waiting for transfers between devices, ring_codes(): behind = lax.ppermute(behind, DP, backward)  25.5 us
    ppermute x2, waiting for transfers between devices, pair_gradient(): lax.ppermute((theirs, grad_out[:, :half]), 'xl', swap)  22.1 us
    all_to_all x1, waiting for transfers between devices, per_device(): lax.all_to_all(jnp.take(keys, send_forward, axis=0), DP, split_axis=0, co...  16.9 us
    ppermute x6, starting transfers between devices, ring_codes(): behind = lax.ppermute(behind, DP, backward)  9.79 us
    ppermute x8, starting transfers between devices, ring_codes(): ahead = lax.ppermute(ahead, DP, forward)  8.62 us
    all_to_all x1, waiting for transfers between devices, per_device(): lax.all_to_all(jnp.take(normed, send_back, axis=0), DP, split_axis=0, con...  7.93 us
  transfers between devices with their start and end apart: 37, of which 18 were waited for; matrix products, arithmetic and copies ran while one was open for 13% of the time, Pallas kernels for 0%

profile of v11, /device:TPU:0, one launch (start us, length us, event | category | flops | bytes accessed | tf_op | source)
XLA Modules:
  0.0 241.7 jit_solution(4418963955880831688)
XLA Ops:
  7.2 1.8 reshape.205
  11.0 2.9 %collective-permute-start = (bf16[256,1024]{1,0:T(8,128)(2,1)}, bf16[256,1024]{1,0:T(8,128)(2,1)}, u32[]{:S(2)}, u32[]{:S(2)}) collective-permute-start(bf16[256,1024]{1,0:T(8,128)(2,1)} %reshape.207), channel_id=1, source_target_pairs={{0,2},{2,0},{1,3},{3,1},{4,6},{6,4},{5,7},{7,5},{8,10},{10,8},{9,1... | collective-permute-start | bytes 1572872 | tf_op jit(solution)/shard_map/ppermute | solution.py:42
  15.5 11.5 %collective-permute-done = bf16[256,1024]{1,0:T(8,128)(2,1)} collective-permute-done((bf16[256,1024]{1,0:T(8,128)(2,1)}, bf16[256,1024]{1,0:T(8,128)(2,1)}, u32[]{:S(2)}, u32[]{:S(2)}) %collective-permute-start) | collective-permute-done | bytes 524320 | tf_op jit(solution)/shard_map/ppermute | solution.py:42
  28.1 10.6 %collective-permute-done.2 = bf16[256,1152]{1,0:T(8,128)(2,1)S(1)} collective-permute-done((bf16[256,1152]{1,0:T(8,128)(2,1)S(1)}, bf16[256,1152]{1,0:T(8,128)(2,1)S(1)}, u32[]{:S(2)}, u32[]{:S(2)}) %collective-permute-start.2) | collective-permute-done | bytes 589856 | tf_op jit(solution)/shard_map/ppermute | solution.py:42
  38.7 3.7 %fusion.22 = f32[1024,1152]{1,0:T(8,128)} fusion(bf16[512,1024]{1,0:T(8,128)(2,1)S(1)} %constant_dynamic-update-slice_fusion, bf16[256,1152]{1,0:T(8,128)(2,1)S(1)} %collective-permute-done.2, bf16[256,1152]{1,0:T(8,128)(2,1)S(1)} %slice.51), kind=kOutput, calls=%fused_computation.39 | convolution fusion | flops 1210318848 | bytes 6946816 | tf_op jit(solution)/shard_map/dot_general | solution.py:47
  43.5 1.8 collective-permute-start.1
  48.0 5.0 %all-to-all-start = ((bf16[16,8,2048]{2,1,0:T(8,128)(2,1)}), bf16[16,8,2048]{2,1,0:T(8,128)(2,1)S(1)}, u32[]{:S(2)}, u32[]{:S(2)}) async-start(bf16[16,8,2048]{2,1,0:T(8,128)(2,1)} %select_bitcast_fusion.1), calls=%async_computation.2 | async-start | bytes 1048576 | tf_op jit(solution)/shard_map/all_to_all | solution.py:158
  56.0 3.1 %fusion.26 = f32[1024,896]{1,0:T(8,128)} fusion(bf16[512,1024]{1,0:T(8,128)(2,1)S(1)} %constant_dynamic-update-slice_fusion, bf16[256,896]{1,0:T(8,128)(2,1)S(1)} %collective-permute-done.1, bf16[256,896]{1,0:T(8,128)(2,1)S(1)} %slice.48), kind=kOutput, calls=%fused_computation.47 | convolution fusion | flops 941359104 | bytes 5636096 | tf_op jit(solution)/shard_map/dot_general | solution.py:47
  59.1 16.9 %all-to-all-done = bf16[16,8,2048]{2,1,0:T(8,128)(2,1)S(1)} async-done(((bf16[16,8,2048]{2,1,0:T(8,128)(2,1)}), bf16[16,8,2048]{2,1,0:T(8,128)(2,1)S(1)}, u32[]{:S(2)}, u32[]{:S(2)}) %all-to-all-start) | async-done | bytes 524320 | tf_op jit(solution)/shard_map/all_to_all | solution.py:158
  77.1 30.3 %reduce-scatter.5.cloned.1.call-done = f32[128,1152]{1,0:T(8,128)} async-done(((f32[1024,1152]{1,0:T(8,128)}), f32[128,1152]{1,0:T(8,128)}) %reduce-scatter.5.cloned.1.call-update) | async-done | bytes 589840 | tf_op jit(solution)/shard_map/reduce_scatter | solution.py:53
  107.4 3.3 %fusion.129 = (bf16[128,1152]{1,0:T(8,128)(2,1)S(1)}, f32[128,1152]{1,0:T(8,128)}, f32[128,1152]{1,0:T(8,128)S(1)}, f32[128,1152]{1,0:T(8,128)S(1)}, f32[128,1152]{1,0:T(8,128)S(1)}) fusion(f32[128,2048]{1,0:T(8,128)} %param.20, f32[128,2048]{1,0:T(8,128)} %param.17, f32[128,1152]{1,0:T(8,128)} %reduce-scatter.5.cloned.1.call-done, f32[128,2048]{1,0:T(8,128)} %param.18, ...), kind=kLoop, calls=%fused_computation.220 | loop fusion | flops 2949120 | bytes 5603328 | tf_op jit(solution)/shard_map/convert_element_type | solution.py:182
  110.7 1.5 collective-permute-start.5
  115.3 2.3 broadcast_select_fusion
  117.8 5.0 %collective-permute-done.5 = bf16[128,1152]{1,0:T(8,128)(2,1)S(1)} collective-permute-done((bf16[128,1152]{1,0:T(8,128)(2,1)S(1)}, bf16[128,1152]{1,0:T(8,128)(2,1)S(1)}, u32[]{:S(2)}, u32[]{:S(2)}) %collective-permute-start.5) | collective-permute-done | bytes 294944 | tf_op jit(solution)/shard_map/ppermute | solution.py:109
  124.3 2.5 %collective-permute-start.8 = (bf16[128,1152]{1,0:T(8,128)(2,1)S(1)}, bf16[128,1152]{1,0:T(8,128)(2,1)S(1)}, u32[]{:S(2)}, u32[]{:S(2)}) collective-permute-start(bf16[128,1152]{1,0:T(8,128)(2,1)S(1)} %collective-permute-done.4), channel_id=1, source_target_pairs={{0,4},{1,5},{4,8},{5,9},{8,12},{9,13},{12,14},{13,15},{14,10},{15,... | collective-permute-start | bytes 884744 | tf_op jit(solution)/shard_map/ppermute | solution.py:105
  127.5 12.4 %collective-permute-done.9 = bf16[128,1152]{1,0:T(8,128)(2,1)S(1)} collective-permute-done((bf16[128,1152]{1,0:T(8,128)(2,1)S(1)}, bf16[128,1152]{1,0:T(8,128)(2,1)S(1)}, u32[]{:S(2)}, u32[]{:S(2)}) %collective-permute-start.9) | collective-permute-done | bytes 294944 | tf_op jit(solution)/shard_map/ppermute | solution.py:109
  140.4 2.3 collective-permute-start.12
  143.5 12.6 %collective-permute-done.12 = bf16[128,1152]{1,0:T(8,128)(2,1)S(1)} collective-permute-done((bf16[128,1152]{1,0:T(8,128)(2,1)S(1)}, bf16[128,1152]{1,0:T(8,128)(2,1)S(1)}, u32[]{:S(2)}, u32[]{:S(2)}) %collective-permute-start.12) | collective-permute-done | bytes 294944 | tf_op jit(solution)/shard_map/ppermute | solution.py:105
  156.2 2.5 %collective-permute-start.16 = (bf16[128,1152]{1,0:T(8,128)(2,1)S(1)}, bf16[128,1152]{1,0:T(8,128)(2,1)S(1)}, u32[]{:S(2)}, u32[]{:S(2)}) collective-permute-start(bf16[128,1152]{1,0:T(8,128)(2,1)S(1)} %collective-permute-done.12), channel_id=1, source_target_pairs={{0,4},{1,5},{4,8},{5,9},{8,12},{9,13},{12,14},{13,15},{14,10},{15,... | collective-permute-start | bytes 884744 | tf_op jit(solution)/shard_map/ppermute | solution.py:105
  160.1 11.9 %collective-permute-done.16 = bf16[128,1152]{1,0:T(8,128)(2,1)S(1)} collective-permute-done((bf16[128,1152]{1,0:T(8,128)(2,1)S(1)}, bf16[128,1152]{1,0:T(8,128)(2,1)S(1)}, u32[]{:S(2)}, u32[]{:S(2)}) %collective-permute-start.16) | collective-permute-done | bytes 294944 | tf_op jit(solution)/shard_map/ppermute | solution.py:105
  174.5 3.1 %fusion.128 = (bf16[128,896]{1,0:T(8,128)(2,1)S(1)}, f32[128,896]{1,0:T(8,128)}, f32[128,896]{1,0:T(8,128)}, f32[128,896]{1,0:T(8,128)}, f32[128,896]{1,0:T(8,128)}) fusion(f32[128,2048]{1,0:T(8,128)} %param.20, f32[128,2048]{1,0:T(8,128)} %param.17, f32[128,896]{1,0:T(8,128)} %reduce-scatter.3.cloned.1.call-done, f32[128,2048]{1,0:T(8,128)} %param.18, ...), kind=kLoop, calls=%fused_computation.219 | loop fusion | flops 2293760 | bytes 4358144 | tf_op jit(solution)/shard_map/convert_element_type | solution.py:182
  177.6 3.3 %collective-permute-start.20 = (bf16[128,896]{1,0:T(8,128)(2,1)S(1)}, bf16[128,896]{1,0:T(8,128)(2,1)S(1)}, u32[]{:S(2)}, u32[]{:S(2)}) collective-permute-start(bf16[128,896]{1,0:T(8,128)(2,1)S(1)} %get-tuple-element.26), channel_id=1, source_target_pairs={{0,2},{1,3},{4,0},{5,1},{8,4},{9,5},{12,8},{13,9},{14,12},{15,13},... | collective-permute-start | bytes 688136 | tf_op jit(solution)/shard_map/ppermute | solution.py:109
  181.2 5.0 %collective-permute-done.20 = bf16[128,896]{1,0:T(8,128)(2,1)S(1)} collective-permute-done((bf16[128,896]{1,0:T(8,128)(2,1)S(1)}, bf16[128,896]{1,0:T(8,128)(2,1)S(1)}, u32[]{:S(2)}, u32[]{:S(2)}) %collective-permute-start.20) | collective-permute-done | bytes 229408 | tf_op jit(solution)/shard_map/ppermute | solution.py:109
  186.1 2.5 %collective-permute-start.24 = (bf16[128,896]{1,0:T(8,128)(2,1)S(1)}, bf16[128,896]{1,0:T(8,128)(2,1)S(1)}, u32[]{:S(2)}, u32[]{:S(2)}) collective-permute-start(bf16[128,896]{1,0:T(8,128)(2,1)S(1)} %collective-permute-done.20), channel_id=1, source_target_pairs={{0,2},{1,3},{4,0},{5,1},{8,4},{9,5},{12,8},{13,9},{14,12},{15,13},... | collective-permute-start | bytes 688136 | tf_op jit(solution)/shard_map/ppermute | solution.py:109
  189.8 3.1 %collective-permute-done.24 = bf16[128,896]{1,0:T(8,128)(2,1)S(1)} collective-permute-done((bf16[128,896]{1,0:T(8,128)(2,1)S(1)}, bf16[128,896]{1,0:T(8,128)(2,1)S(1)}, u32[]{:S(2)}, u32[]{:S(2)}) %collective-permute-start.24) | collective-permute-done | bytes 229408 | tf_op jit(solution)/shard_map/ppermute | solution.py:109
  192.9 2.5 %collective-permute-start.28 = (bf16[128,896]{1,0:T(8,128)(2,1)S(1)}, bf16[128,896]{1,0:T(8,128)(2,1)S(1)}, u32[]{:S(2)}, u32[]{:S(2)}) collective-permute-start(bf16[128,896]{1,0:T(8,128)(2,1)S(1)} %collective-permute-done.24), channel_id=1, source_target_pairs={{0,2},{1,3},{4,0},{5,1},{8,4},{9,5},{12,8},{13,9},{14,12},{15,13},... | collective-permute-start | bytes 688136 | tf_op jit(solution)/shard_map/ppermute | solution.py:109
  197.9 5.9 %collective-permute-done.27 = bf16[128,896]{1,0:T(8,128)(2,1)S(1)} collective-permute-done((bf16[128,896]{1,0:T(8,128)(2,1)S(1)}, bf16[128,896]{1,0:T(8,128)(2,1)S(1)}, u32[]{:S(2)}, u32[]{:S(2)}) %collective-permute-start.27) | collective-permute-done | bytes 229408 | tf_op jit(solution)/shard_map/ppermute | solution.py:105
  205.9 4.3 %collective-permute-done.31 = bf16[128,896]{1,0:T(8,128)(2,1)S(1)} collective-permute-done((bf16[128,896]{1,0:T(8,128)(2,1)S(1)}, bf16[128,896]{1,0:T(8,128)(2,1)S(1)}, u32[]{:S(2)}, u32[]{:S(2)}) %collective-permute-start.31) | collective-permute-done | bytes 229408 | tf_op jit(solution)/shard_map/ppermute | solution.py:105
  214.0 4.4 %all-to-all-start.1 = ((bf16[16,8,2048]{2,1,0:T(8,128)(2,1)}), bf16[16,8,2048]{2,1,0:T(8,128)(2,1)S(1)}, u32[]{:S(2)}, u32[]{:S(2)}) async-start(bf16[16,8,2048]{2,1,0:T(8,128)(2,1)} %select_bitcast_fusion), calls=%async_computation.3 | async-start | bytes 1048576 | tf_op jit(solution)/shard_map/all_to_all | solution.py:188
  218.4 2.3 pad_maximum_fusion.3
  220.7 2.1 pad_maximum_fusion
  225.0 7.9 %all-to-all-done.1 = bf16[16,8,2048]{2,1,0:T(8,128)(2,1)S(1)} async-done(((bf16[16,8,2048]{2,1,0:T(8,128)(2,1)}), bf16[16,8,2048]{2,1,0:T(8,128)(2,1)S(1)}, u32[]{:S(2)}, u32[]{:S(2)}) %all-to-all-start.1) | async-done | bytes 524320 | tf_op jit(solution)/shard_map/all_to_all | solution.py:188
  (162 shorter events, 34.1 us)
Async XLA Ops:
  7.2 100.3 %reduce-scatter.5.cloned.1.call-start = ((), (), s32[]{:S(2)}) async-start(), calls=%async_computation.5 | async-start | bytes 5308416 | tf_op jit(solution)/shard_map/reduce_scatter | solution.py:53
  11.0 16.0 %collective-permute-start = (bf16[256,1024]{1,0:T(8,128)(2,1)}, bf16[256,1024]{1,0:T(8,128)(2,1)}, u32[]{:S(2)}, u32[]{:S(2)}) collective-permute-start(bf16[256,1024]{1,0:T(8,128)(2,1)} %reshape.207), channel_id=1, source_target_pairs={{0,2},{2,0},{1,3},{3,1},{4,6},{6,4},{5,7},{7,5},{8,10},{10,8},{9,1... | collective-permute-start | bytes 1572872 | tf_op jit(solution)/shard_map/ppermute | solution.py:42
  15.0 23.7 %collective-permute-start.2 = (bf16[256,1152]{1,0:T(8,128)(2,1)S(1)}, bf16[256,1152]{1,0:T(8,128)(2,1)S(1)}, u32[]{:S(2)}, u32[]{:S(2)}) collective-permute-start(bf16[256,1152]{1,0:T(8,128)(2,1)S(1)} %slice.51), channel_id=1, source_target_pairs={{0,2},{2,0},{1,3},{3,1},{4,6},{6,4},{5,7},{7,5},{8,10},{10,8},{9,1... | collective-permute-start | bytes 1769480 | tf_op jit(solution)/shard_map/ppermute | solution.py:42
  43.5 12.5 %collective-permute-start.1 = (bf16[256,896]{1,0:T(8,128)(2,1)S(1)}, bf16[256,896]{1,0:T(8,128)(2,1)S(1)}, u32[]{:S(2)}, u32[]{:S(2)}) collective-permute-start(bf16[256,896]{1,0:T(8,128)(2,1)S(1)} %slice.48), channel_id=1, source_target_pairs={{0,2},{2,0},{1,3},{3,1},{4,6},{6,4},{5,7},{7,5},{8,10},{10,8},{9,1... | collective-permute-start | bytes 1376264 | tf_op jit(solution)/shard_map/ppermute | solution.py:43
  48.0 28.0 %all-to-all-start = ((bf16[16,8,2048]{2,1,0:T(8,128)(2,1)}), bf16[16,8,2048]{2,1,0:T(8,128)(2,1)S(1)}, u32[]{:S(2)}, u32[]{:S(2)}) async-start(bf16[16,8,2048]{2,1,0:T(8,128)(2,1)} %select_bitcast_fusion.1), calls=%async_computation.2 | async-start | bytes 1048576 | tf_op jit(solution)/shard_map/all_to_all | solution.py:158
  53.0 121.5 %reduce-scatter.3.cloned.1.call-start = ((), (), s32[]{:S(2)}) async-start(), calls=%async_computation.4 | async-start | bytes 4128768 | tf_op jit(solution)/shard_map/reduce_scatter | solution.py:53
  110.7 12.0 %collective-permute-start.5 = (bf16[128,1152]{1,0:T(8,128)(2,1)S(1)}, bf16[128,1152]{1,0:T(8,128)(2,1)S(1)}, u32[]{:S(2)}, u32[]{:S(2)}) collective-permute-start(bf16[128,1152]{1,0:T(8,128)(2,1)S(1)} %get-tuple-element.31), channel_id=1, source_target_pairs={{0,2},{1,3},{4,0},{5,1},{8,4},{9,5},{12,8},{13,9},{14,12},{15,13},... | collective-permute-start | bytes 884744 | tf_op jit(solution)/shard_map/ppermute | solution.py:109
  112.2 12.1 %collective-permute-start.4 = (bf16[128,1152]{1,0:T(8,128)(2,1)S(1)}, bf16[128,1152]{1,0:T(8,128)(2,1)S(1)}, u32[]{:S(2)}, u32[]{:S(2)}) collective-permute-start(bf16[128,1152]{1,0:T(8,128)(2,1)S(1)} %get-tuple-element.31), channel_id=1, source_target_pairs={{0,4},{1,5},{4,8},{5,9},{8,12},{9,13},{12,14},{13,15},{14,10},{15,... | collective-permute-start | bytes 884744 | tf_op jit(solution)/shard_map/ppermute | solution.py:105
  112.8 14.0 %collective-permute-start.3 = (bf16[128,1152]{1,0:T(8,128)(2,1)S(1)}, bf16[128,1152]{1,0:T(8,128)(2,1)S(1)}, u32[]{:S(2)}, u32[]{:S(2)}) collective-permute-start(bf16[128,1152]{1,0:T(8,128)(2,1)S(1)} %get-tuple-element.31), channel_id=1, source_target_pairs={{0,1},{1,0},{2,3},{3,2},{4,5},{5,4},{6,7},{7,6},{8,9},{9,8},{10,11... | collective-permute-start | bytes 884744 | tf_op jit(solution)/shard_map/ppermute | solution.py:101
  122.8 17.1 %collective-permute-start.9 = (bf16[128,1152]{1,0:T(8,128)(2,1)S(1)}, bf16[128,1152]{1,0:T(8,128)(2,1)S(1)}, u32[]{:S(2)}, u32[]{:S(2)}) collective-permute-start(bf16[128,1152]{1,0:T(8,128)(2,1)S(1)} %collective-permute-done.5), channel_id=1, source_target_pairs={{0,2},{1,3},{4,0},{5,1},{8,4},{9,5},{12,8},{13,9},{14,12},{15,13},... | collective-permute-start | bytes 884744 | tf_op jit(solution)/shard_map/ppermute | solution.py:109
  122.8 20.2 %collective-permute-start.7 = (bf16[128,1152]{1,0:T(8,128)(2,1)S(1)}, bf16[128,1152]{1,0:T(8,128)(2,1)S(1)}, u32[]{:S(2)}, u32[]{:S(2)}) collective-permute-start(bf16[128,1152]{1,0:T(8,128)(2,1)S(1)} %collective-permute-done.5), channel_id=1, source_target_pairs={{0,1},{1,0},{2,3},{3,2},{4,5},{5,4},{6,7},{7,6},{8,9},{9,8},{10,11... | collective-permute-start | bytes 884744 | tf_op jit(solution)/shard_map/ppermute | solution.py:101
  124.3 16.1 %collective-permute-start.8 = (bf16[128,1152]{1,0:T(8,128)(2,1)S(1)}, bf16[128,1152]{1,0:T(8,128)(2,1)S(1)}, u32[]{:S(2)}, u32[]{:S(2)}) collective-permute-start(bf16[128,1152]{1,0:T(8,128)(2,1)S(1)} %collective-permute-done.4), channel_id=1, source_target_pairs={{0,4},{1,5},{4,8},{5,9},{8,12},{9,13},{12,14},{13,15},{14,10},{15,... | collective-permute-start | bytes 884744 | tf_op jit(solution)/shard_map/ppermute | solution.py:105
  126.8 16.5 %collective-permute-start.6 = (bf16[128,1152]{1,0:T(8,128)(2,1)S(1)}, bf16[128,1152]{1,0:T(8,128)(2,1)S(1)}, u32[]{:S(2)}, u32[]{:S(2)}) collective-permute-start(bf16[128,1152]{1,0:T(8,128)(2,1)S(1)} %collective-permute-done.4), channel_id=1, source_target_pairs={{0,1},{1,0},{2,3},{3,2},{4,5},{5,4},{6,7},{7,6},{8,9},{9,8},{10,11... | collective-permute-start | bytes 884744 | tf_op jit(solution)/shard_map/ppermute | solution.py:101
  139.9 18.8 %collective-permute-start.13 = (bf16[128,1152]{1,0:T(8,128)(2,1)S(1)}, bf16[128,1152]{1,0:T(8,128)(2,1)S(1)}, u32[]{:S(2)}, u32[]{:S(2)}) collective-permute-start(bf16[128,1152]{1,0:T(8,128)(2,1)S(1)} %collective-permute-done.9), channel_id=1, source_target_pairs={{0,2},{1,3},{4,0},{5,1},{8,4},{9,5},{12,8},{13,9},{14,12},{15,13},... | collective-permute-start | bytes 884744 | tf_op jit(solution)/shard_map/ppermute | solution.py:109
  139.9 19.7 %collective-permute-start.11 = (bf16[128,1152]{1,0:T(8,128)(2,1)S(1)}, bf16[128,1152]{1,0:T(8,128)(2,1)S(1)}, u32[]{:S(2)}, u32[]{:S(2)}) collective-permute-start(bf16[128,1152]{1,0:T(8,128)(2,1)S(1)} %collective-permute-done.9), channel_id=1, source_target_pairs={{0,1},{1,0},{2,3},{3,2},{4,5},{5,4},{6,7},{7,6},{8,9},{9,8},{10,11... | collective-permute-start | bytes 884744 | tf_op jit(solution)/shard_map/ppermute | solution.py:101
  140.4 15.8 %collective-permute-start.12 = (bf16[128,1152]{1,0:T(8,128)(2,1)S(1)}, bf16[128,1152]{1,0:T(8,128)(2,1)S(1)}, u32[]{:S(2)}, u32[]{:S(2)}) collective-permute-start(bf16[128,1152]{1,0:T(8,128)(2,1)S(1)} %collective-permute-done.8), channel_id=1, source_target_pairs={{0,4},{1,5},{4,8},{5,9},{8,12},{9,13},{12,14},{13,15},{14,10},{15,... | collective-permute-start | bytes 884744 | tf_op jit(solution)/shard_map/ppermute | solution.py:105
  142.9 16.9 %collective-permute-start.10 = (bf16[128,1152]{1,0:T(8,128)(2,1)S(1)}, bf16[128,1152]{1,0:T(8,128)(2,1)S(1)}, u32[]{:S(2)}, u32[]{:S(2)}) collective-permute-start(bf16[128,1152]{1,0:T(8,128)(2,1)S(1)} %collective-permute-done.8), channel_id=1, source_target_pairs={{0,1},{1,0},{2,3},{3,2},{4,5},{5,4},{6,7},{7,6},{8,9},{9,8},{10,11... | collective-permute-start | bytes 884744 | tf_op jit(solution)/shard_map/ppermute | solution.py:101
  156.2 15.9 %collective-permute-start.16 = (bf16[128,1152]{1,0:T(8,128)(2,1)S(1)}, bf16[128,1152]{1,0:T(8,128)(2,1)S(1)}, u32[]{:S(2)}, u32[]{:S(2)}) collective-permute-start(bf16[128,1152]{1,0:T(8,128)(2,1)S(1)} %collective-permute-done.12), channel_id=1, source_target_pairs={{0,4},{1,5},{4,8},{5,9},{8,12},{9,13},{12,14},{13,15},{14,10},{15,... | collective-permute-start | bytes 884744 | tf_op jit(solution)/shard_map/ppermute | solution.py:105
  158.6 13.8 %collective-permute-start.14 = (bf16[128,1152]{1,0:T(8,128)(2,1)S(1)}, bf16[128,1152]{1,0:T(8,128)(2,1)S(1)}, u32[]{:S(2)}, u32[]{:S(2)}) collective-permute-start(bf16[128,1152]{1,0:T(8,128)(2,1)S(1)} %collective-permute-done.12), channel_id=1, source_target_pairs={{0,1},{1,0},{2,3},{3,2},{4,5},{5,4},{6,7},{7,6},{8,9},{9,8},{10,11... | collective-permute-start | bytes 884744 | tf_op jit(solution)/shard_map/ppermute | solution.py:101
  158.6 13.6 %collective-permute-start.15 = (bf16[128,1152]{1,0:T(8,128)(2,1)S(1)}, bf16[128,1152]{1,0:T(8,128)(2,1)S(1)}, u32[]{:S(2)}, u32[]{:S(2)}) collective-permute-start(bf16[128,1152]{1,0:T(8,128)(2,1)S(1)} %collective-permute-done.13), channel_id=1, source_target_pairs={{0,1},{1,0},{2,3},{3,2},{4,5},{5,4},{6,7},{7,6},{8,9},{9,8},{10,11... | collective-permute-start | bytes 884744 | tf_op jit(solution)/shard_map/ppermute | solution.py:101
  177.6 8.5 %collective-permute-start.20 = (bf16[128,896]{1,0:T(8,128)(2,1)S(1)}, bf16[128,896]{1,0:T(8,128)(2,1)S(1)}, u32[]{:S(2)}, u32[]{:S(2)}) collective-permute-start(bf16[128,896]{1,0:T(8,128)(2,1)S(1)} %get-tuple-element.26), channel_id=1, source_target_pairs={{0,2},{1,3},{4,0},{5,1},{8,4},{9,5},{12,8},{13,9},{14,12},{15,13},... | collective-permute-start | bytes 688136 | tf_op jit(solution)/shard_map/ppermute | solution.py:109
  180.9 7.7 %collective-permute-start.19 = (bf16[128,896]{1,0:T(8,128)(2,1)S(1)}, bf16[128,896]{1,0:T(8,128)(2,1)S(1)}, u32[]{:S(2)}, u32[]{:S(2)}) collective-permute-start(bf16[128,896]{1,0:T(8,128)(2,1)S(1)} %get-tuple-element.26), channel_id=1, source_target_pairs={{0,4},{1,5},{4,8},{5,9},{8,12},{9,13},{12,14},{13,15},{14,10},{15,... | collective-permute-start | bytes 688136 | tf_op jit(solution)/shard_map/ppermute | solution.py:105
  180.9 8.4 %collective-permute-start.18 = (bf16[128,896]{1,0:T(8,128)(2,1)S(1)}, bf16[128,896]{1,0:T(8,128)(2,1)S(1)}, u32[]{:S(2)}, u32[]{:S(2)}) collective-permute-start(bf16[128,896]{1,0:T(8,128)(2,1)S(1)} %get-tuple-element.26), channel_id=1, source_target_pairs={{0,1},{1,0},{2,3},{3,2},{4,5},{5,4},{6,7},{7,6},{8,9},{9,8},{10,11... | collective-permute-start | bytes 688136 | tf_op jit(solution)/shard_map/ppermute | solution.py:101
  186.1 6.8 %collective-permute-start.24 = (bf16[128,896]{1,0:T(8,128)(2,1)S(1)}, bf16[128,896]{1,0:T(8,128)(2,1)S(1)}, u32[]{:S(2)}, u32[]{:S(2)}) collective-permute-start(bf16[128,896]{1,0:T(8,128)(2,1)S(1)} %collective-permute-done.20), channel_id=1, source_target_pairs={{0,2},{1,3},{4,0},{5,1},{8,4},{9,5},{12,8},{13,9},{14,12},{15,13},... | collective-permute-start | bytes 688136 | tf_op jit(solution)/shard_map/ppermute | solution.py:109
  188.6 8.7 %collective-permute-start.22 = (bf16[128,896]{1,0:T(8,128)(2,1)S(1)}, bf16[128,896]{1,0:T(8,128)(2,1)S(1)}, u32[]{:S(2)}, u32[]{:S(2)}) collective-permute-start(bf16[128,896]{1,0:T(8,128)(2,1)S(1)} %collective-permute-done.20), channel_id=1, source_target_pairs={{0,1},{1,0},{2,3},{3,2},{4,5},{5,4},{6,7},{7,6},{8,9},{9,8},{10,11... | collective-permute-start | bytes 688136 | tf_op jit(solution)/shard_map/ppermute | solution.py:101
  188.6 8.0 %collective-permute-start.23 = (bf16[128,896]{1,0:T(8,128)(2,1)S(1)}, bf16[128,896]{1,0:T(8,128)(2,1)S(1)}, u32[]{:S(2)}, u32[]{:S(2)}) collective-permute-start(bf16[128,896]{1,0:T(8,128)(2,1)S(1)} %collective-permute-done.19), channel_id=1, source_target_pairs={{0,4},{1,5},{4,8},{5,9},{8,12},{9,13},{12,14},{13,15},{14,10},{15,... | collective-permute-start | bytes 688136 | tf_op jit(solution)/shard_map/ppermute | solution.py:105
  188.6 9.0 %collective-permute-start.21 = (bf16[128,896]{1,0:T(8,128)(2,1)S(1)}, bf16[128,896]{1,0:T(8,128)(2,1)S(1)}, u32[]{:S(2)}, u32[]{:S(2)}) collective-permute-start(bf16[128,896]{1,0:T(8,128)(2,1)S(1)} %collective-permute-done.19), channel_id=1, source_target_pairs={{0,1},{1,0},{2,3},{3,2},{4,5},{5,4},{6,7},{7,6},{8,9},{9,8},{10,11... | collective-permute-start | bytes 688136 | tf_op jit(solution)/shard_map/ppermute | solution.py:101
  192.9 11.6 %collective-permute-start.28 = (bf16[128,896]{1,0:T(8,128)(2,1)S(1)}, bf16[128,896]{1,0:T(8,128)(2,1)S(1)}, u32[]{:S(2)}, u32[]{:S(2)}) collective-permute-start(bf16[128,896]{1,0:T(8,128)(2,1)S(1)} %collective-permute-done.24), channel_id=1, source_target_pairs={{0,2},{1,3},{4,0},{5,1},{8,4},{9,5},{12,8},{13,9},{14,12},{15,13},... | collective-permute-start | bytes 688136 | tf_op jit(solution)/shard_map/ppermute | solution.py:109
  195.4 9.9 %collective-permute-start.26 = (bf16[128,896]{1,0:T(8,128)(2,1)S(1)}, bf16[128,896]{1,0:T(8,128)(2,1)S(1)}, u32[]{:S(2)}, u32[]{:S(2)}) collective-permute-start(bf16[128,896]{1,0:T(8,128)(2,1)S(1)} %collective-permute-done.24), channel_id=1, source_target_pairs={{0,1},{1,0},{2,3},{3,2},{4,5},{5,4},{6,7},{7,6},{8,9},{9,8},{10,11... | collective-permute-start | bytes 688136 | tf_op jit(solution)/shard_map/ppermute | solution.py:101
  196.6 7.2 %collective-permute-start.27 = (bf16[128,896]{1,0:T(8,128)(2,1)S(1)}, bf16[128,896]{1,0:T(8,128)(2,1)S(1)}, u32[]{:S(2)}, u32[]{:S(2)}) collective-permute-start(bf16[128,896]{1,0:T(8,128)(2,1)S(1)} %collective-permute-done.23), channel_id=1, source_target_pairs={{0,4},{1,5},{4,8},{5,9},{8,12},{9,13},{12,14},{13,15},{14,10},{15,... | collective-permute-start | bytes 688136 | tf_op jit(solution)/shard_map/ppermute | solution.py:105
  197.4 8.2 %collective-permute-start.25 = (bf16[128,896]{1,0:T(8,128)(2,1)S(1)}, bf16[128,896]{1,0:T(8,128)(2,1)S(1)}, u32[]{:S(2)}, u32[]{:S(2)}) collective-permute-start(bf16[128,896]{1,0:T(8,128)(2,1)S(1)} %collective-permute-done.23), channel_id=1, source_target_pairs={{0,1},{1,0},{2,3},{3,2},{4,5},{5,4},{6,7},{7,6},{8,9},{9,8},{10,11... | collective-permute-start | bytes 688136 | tf_op jit(solution)/shard_map/ppermute | solution.py:101
  214.0 18.9 %all-to-all-start.1 = ((bf16[16,8,2048]{2,1,0:T(8,128)(2,1)}), bf16[16,8,2048]{2,1,0:T(8,128)(2,1)S(1)}, u32[]{:S(2)}, u32[]{:S(2)}) async-start(bf16[16,8,2048]{2,1,0:T(8,128)(2,1)} %select_bitcast_fusion), calls=%async_computation.3 | async-start | bytes 1048576 | tf_op jit(solution)/shard_map/all_to_all | solution.py:188
  (14 other events, 129.9 us)
Sparse Core Ops, SparseCore 0:
  42.5 64.8 reduce-scatter.4
  109.7 64.7 reduce-scatter.2

commit v12 on v11

--- a/solution.py
+++ b/solution.py
@@ -38,7 +38,7 @@
     mine = mine.reshape(tokens, width // 2)
     theirs = theirs.reshape(tokens, width // 2)
     swap = [(0, 1), (1, 0)]
-    half = grad_out.shape[1] * 9 // 16
+    half = grad_out.shape[1] * 7 // 16
     got_queries, got_first = lax.ppermute((theirs, grad_out[:, :half]), "xl", swap)
     got_second = lax.ppermute(grad_out[:, half:], "xl", swap)
     both_queries = jnp.concatenate([mine, got_queries], axis=0)

time: 242 us -> 239 us (0.988)
  waiting for transfers between devices: 141 us -> 137 us
    reduce_scatter x2, waiting for transfers between devices: 30.8 us -> 38.2 us  [pair_gradient(): lax.psum_scatter(partial, ('zo', 'c'), scatter_dimension=0, tiled=True)]
    all_to_all x1, waiting for transfers between devices: 16.9 us -> 10.1 us  [per_device(): lax.all_to_all(jnp.take(keys, send_forward, axis=0), DP, split_axis=0, co...]
    ppermute x1, waiting for transfers between devices: 0.01 us -> 5.56 us  [pair_gradient(): got_second = lax.ppermute(grad_out[:, half:], 'xl', swap)]
    ppermute x6, waiting for transfers between devices: 25.5 us -> 21 us  [ring_codes(): behind = lax.ppermute(behind, DP, backward)]
    ppermute x8, waiting for transfers between devices: 36.5 us -> 32.9 us  [ring_codes(): ahead = lax.ppermute(ahead, DP, forward)]
    ppermute x2, waiting for transfers between devices: 22.1 us -> 19.2 us  [pair_gradient(): lax.ppermute((theirs, grad_out[:, :half]), 'xl', swap)]
  transfers between devices with their start and end apart: 37 -> 37, of which waited for: 18 -> 19; matrix products, arithmetic and copies ran while one was open for 13% -> 14% of each run, Pallas kernels for 0% -> 0%
where the time goes in v12:
time: 239 us; the launch traced here: 238 us
  waiting for transfers between devices  137 us (57%)
  starting transfers between devices  36.7 us (15%)
  other arithmetic  20.9 us (9%)
  between operations  17 us (7%)
  matrix products  15 us (6%)
  local copies, waits for them, and re-layouts  11.7 us (5%)
    reduce_scatter x2, waiting for transfers between devices, pair_gradient(): lax.psum_scatter(partial, ('zo', 'c'), scatter_dimension=0, tiled=True)  38.2 us
    ppermute x8, waiting for transfers between devices, ring_codes(): ahead = lax.ppermute(ahead, DP, forward)  32.9 us
    ppermute x6, waiting for transfers between devices, ring_codes(): behind = lax.ppermute(behind, DP, backward)  21 us
    ppermute x2, waiting for transfers between devices, pair_gradient(): lax.ppermute((theirs, grad_out[:, :half]), 'xl', swap)  19.2 us
    ppermute x6, starting transfers between devices, ring_codes(): behind = lax.ppermute(behind, DP, backward)  10.5 us
    all_to_all x1, waiting for transfers between devices, per_device(): lax.all_to_all(jnp.take(keys, send_forward, axis=0), DP, split_axis=0, co...  10.1 us
    ppermute x8, starting transfers between devices, ring_codes(): ahead = lax.ppermute(ahead, DP, forward)  8.41 us
    all_to_all x1, waiting for transfers between devices, per_device(): lax.all_to_all(jnp.take(normed, send_back, axis=0), DP, split_axis=0, con...  7.94 us
  transfers between devices with their start and end apart: 37, of which 19 were waited for; matrix products, arithmetic and copies ran while one was open for 14% of the time, Pallas kernels for 0%

profile of v12, /device:TPU:0, one launch (start us, length us, event | category | flops | bytes accessed | tf_op | source)
XLA Modules:
  0.0 238.1 jit_solution(905666881022604498)
XLA Ops:
  7.2 1.8 reshape.205
  10.2 3.0 %collective-permute-start = (bf16[256,1024]{1,0:T(8,128)(2,1)S(1)}, bf16[256,1024]{1,0:T(8,128)(2,1)}, u32[]{:S(2)}, u32[]{:S(2)}) collective-permute-start(bf16[256,1024]{1,0:T(8,128)(2,1)S(1)} %reshape.207), channel_id=1, source_target_pairs={{0,2},{2,0},{1,3},{3,1},{4,6},{6,4},{5,7},{7,5},{8,10},{10,8},{9,1... | collective-permute-start | bytes 1572872 | tf_op jit(solution)/shard_map/ppermute | solution.py:42
  14.7 11.3 %collective-permute-done = bf16[256,1024]{1,0:T(8,128)(2,1)} collective-permute-done((bf16[256,1024]{1,0:T(8,128)(2,1)S(1)}, bf16[256,1024]{1,0:T(8,128)(2,1)}, u32[]{:S(2)}, u32[]{:S(2)}) %collective-permute-start) | collective-permute-done | bytes 524320 | tf_op jit(solution)/shard_map/ppermute | solution.py:42
  27.1 7.9 %collective-permute-done.2 = bf16[256,896]{1,0:T(8,128)(2,1)} collective-permute-done((bf16[256,896]{1,0:T(8,128)(2,1)S(1)}, bf16[256,896]{1,0:T(8,128)(2,1)}, u32[]{:S(2)}, u32[]{:S(2)}) %collective-permute-start.2) | collective-permute-done | bytes 458784 | tf_op jit(solution)/shard_map/ppermute | solution.py:42
  35.0 4.1 %fusion.26 = f32[1024,896]{1,0:T(8,128)} fusion(bf16[512,1024]{1,0:T(8,128)(2,1)S(1)} %constant_dynamic-update-slice_fusion, bf16[256,896]{1,0:T(8,128)(2,1)} %collective-permute-done.2, bf16[256,896]{1,0:T(8,128)(2,1)S(1)} %slice.51), kind=kOutput, calls=%fused_computation.47 | convolution fusion | flops 941359104 | bytes 5636096 | tf_op jit(solution)/shard_map/dot_general | solution.py:47
  40.3 1.8 collective-permute-start.1
  44.9 5.0 %all-to-all-start = ((bf16[16,8,2048]{2,1,0:T(8,128)(2,1)}), bf16[16,8,2048]{2,1,0:T(8,128)(2,1)S(1)}, u32[]{:S(2)}, u32[]{:S(2)}) async-start(bf16[16,8,2048]{2,1,0:T(8,128)(2,1)} %select_bitcast_fusion.1), calls=%async_computation.2 | async-start | bytes 1048576 | tf_op jit(solution)/shard_map/all_to_all | solution.py:158
  50.8 5.6 %collective-permute-done.1 = bf16[256,1152]{1,0:T(8,128)(2,1)S(1)} collective-permute-done((bf16[256,1152]{1,0:T(8,128)(2,1)S(1)}, bf16[256,1152]{1,0:T(8,128)(2,1)S(1)}, u32[]{:S(2)}, u32[]{:S(2)}) %collective-permute-start.1) | collective-permute-done | bytes 589856 | tf_op jit(solution)/shard_map/ppermute | solution.py:43
  56.4 3.7 %fusion.22 = f32[1024,1152]{1,0:T(8,128)} fusion(bf16[512,1024]{1,0:T(8,128)(2,1)S(1)} %constant_dynamic-update-slice_fusion, bf16[256,1152]{1,0:T(8,128)(2,1)S(1)} %collective-permute-done.1, bf16[256,1152]{1,0:T(8,128)(2,1)S(1)} %slice.48), kind=kOutput, calls=%fused_computation.39 | convolution fusion | flops 1210318848 | bytes 6946816 | tf_op jit(solution)/shard_map/dot_general | solution.py:47
  62.7 10.1 %all-to-all-done = bf16[16,8,2048]{2,1,0:T(8,128)(2,1)S(1)} async-done(((bf16[16,8,2048]{2,1,0:T(8,128)(2,1)}), bf16[16,8,2048]{2,1,0:T(8,128)(2,1)S(1)}, u32[]{:S(2)}, u32[]{:S(2)}) %all-to-all-start) | async-done | bytes 524320 | tf_op jit(solution)/shard_map/all_to_all | solution.py:158
  73.9 20.4 %reduce-scatter.5.cloned.1.call-done = f32[128,896]{1,0:T(8,128)} async-done(((f32[1024,896]{1,0:T(8,128)}), f32[128,896]{1,0:T(8,128)}) %reduce-scatter.5.cloned.1.call-update) | async-done | bytes 458768 | tf_op jit(solution)/shard_map/reduce_scatter | solution.py:53
  94.4 3.2 %fusion.129 = (bf16[128,896]{1,0:T(8,128)(2,1)S(1)}, f32[128,896]{1,0:T(8,128)}, f32[128,896]{1,0:T(8,128)}, f32[128,896]{1,0:T(8,128)}, f32[128,896]{1,0:T(8,128)S(1)}) fusion(f32[128,2048]{1,0:T(8,128)} %param.20, f32[128,2048]{1,0:T(8,128)} %param.17, f32[128,896]{1,0:T(8,128)} %reduce-scatter.5.cloned.1.call-done, f32[128,2048]{1,0:T(8,128)} %param.18, ...), kind=kLoop, calls=%fused_computation.220 | loop fusion | flops 2293760 | bytes 4358144 | tf_op jit(solution)/shard_map/convert_element_type | solution.py:182
  102.2 2.3 broadcast_select_fusion
  107.6 2.1 collective-permute-start.8
  110.4 9.0 %collective-permute-done.9 = bf16[128,896]{1,0:T(8,128)(2,1)S(1)} collective-permute-done((bf16[128,896]{1,0:T(8,128)(2,1)S(1)}, bf16[128,896]{1,0:T(8,128)(2,1)S(1)}, u32[]{:S(2)}, u32[]{:S(2)}) %collective-permute-start.9) | collective-permute-done | bytes 229408 | tf_op jit(solution)/shard_map/ppermute | solution.py:109
  120.3 2.5 %collective-permute-start.12 = (bf16[128,896]{1,0:T(8,128)(2,1)S(1)}, bf16[128,896]{1,0:T(8,128)(2,1)S(1)}, u32[]{:S(2)}, u32[]{:S(2)}) collective-permute-start(bf16[128,896]{1,0:T(8,128)(2,1)S(1)} %collective-permute-done.8), channel_id=1, source_target_pairs={{0,4},{1,5},{4,8},{5,9},{8,12},{9,13},{12,14},{13,15},{14,10},{15,... | collective-permute-start | bytes 688136 | tf_op jit(solution)/shard_map/ppermute | solution.py:105
  123.8 9.5 %collective-permute-done.12 = bf16[128,896]{1,0:T(8,128)(2,1)S(1)} collective-permute-done((bf16[128,896]{1,0:T(8,128)(2,1)S(1)}, bf16[128,896]{1,0:T(8,128)(2,1)S(1)}, u32[]{:S(2)}, u32[]{:S(2)}) %collective-permute-start.12) | collective-permute-done | bytes 229408 | tf_op jit(solution)/shard_map/ppermute | solution.py:105
  133.2 2.5 %collective-permute-start.16 = (bf16[128,896]{1,0:T(8,128)(2,1)S(1)}, bf16[128,896]{1,0:T(8,128)(2,1)S(1)}, u32[]{:S(2)}, u32[]{:S(2)}) collective-permute-start(bf16[128,896]{1,0:T(8,128)(2,1)S(1)} %collective-permute-done.12), channel_id=1, source_target_pairs={{0,4},{1,5},{4,8},{5,9},{8,12},{9,13},{12,14},{13,15},{14,10},{15,... | collective-permute-start | bytes 688136 | tf_op jit(solution)/shard_map/ppermute | solution.py:105
  137.2 8.8 %collective-permute-done.16 = bf16[128,896]{1,0:T(8,128)(2,1)S(1)} collective-permute-done((bf16[128,896]{1,0:T(8,128)(2,1)S(1)}, bf16[128,896]{1,0:T(8,128)(2,1)S(1)}, u32[]{:S(2)}, u32[]{:S(2)}) %collective-permute-start.16) | collective-permute-done | bytes 229408 | tf_op jit(solution)/shard_map/ppermute | solution.py:105
  147.9 17.7 %reduce-scatter.3.cloned.1.call-done = f32[128,1152]{1,0:T(8,128)} async-done(((f32[1024,1152]{1,0:T(8,128)}), f32[128,1152]{1,0:T(8,128)}) %reduce-scatter.3.cloned.1.call-update) | async-done | bytes 589840 | tf_op jit(solution)/shard_map/reduce_scatter | solution.py:53
  165.6 3.1 %fusion.128 = (bf16[128,1152]{1,0:T(8,128)(2,1)S(1)}, f32[128,1152]{1,0:T(8,128)}, f32[128,1152]{1,0:T(8,128)S(1)}, f32[128,1152]{1,0:T(8,128)S(1)}, f32[128,1152]{1,0:T(8,128)S(1)}) fusion(f32[128,2048]{1,0:T(8,128)} %param.20, f32[128,2048]{1,0:T(8,128)} %param.17, f32[128,1152]{1,0:T(8,128)} %reduce-scatter.3.cloned.1.call-done, f32[128,2048]{1,0:T(8,128)} %param.18, ...), kind=kLoop, calls=%fused_computation.219 | loop fusion | flops 2949120 | bytes 5603328 | tf_op jit(solution)/shard_map/convert_element_type | solution.py:182
  168.8 3.4 %collective-permute-start.20 = (bf16[128,1152]{1,0:T(8,128)(2,1)S(1)}, bf16[128,1152]{1,0:T(8,128)(2,1)S(1)}, u32[]{:S(2)}, u32[]{:S(2)}) collective-permute-start(bf16[128,1152]{1,0:T(8,128)(2,1)S(1)} %get-tuple-element.26), channel_id=1, source_target_pairs={{0,2},{1,3},{4,0},{5,1},{8,4},{9,5},{12,8},{13,9},{14,12},{15,13},... | collective-permute-start | bytes 884744 | tf_op jit(solution)/shard_map/ppermute | solution.py:109
  172.4 6.3 %collective-permute-done.20 = bf16[128,1152]{1,0:T(8,128)(2,1)S(1)} collective-permute-done((bf16[128,1152]{1,0:T(8,128)(2,1)S(1)}, bf16[128,1152]{1,0:T(8,128)(2,1)S(1)}, u32[]{:S(2)}, u32[]{:S(2)}) %collective-permute-start.20) | collective-permute-done | bytes 294944 | tf_op jit(solution)/shard_map/ppermute | solution.py:109
  178.7 2.5 %collective-permute-start.24 = (bf16[128,1152]{1,0:T(8,128)(2,1)S(1)}, bf16[128,1152]{1,0:T(8,128)(2,1)S(1)}, u32[]{:S(2)}, u32[]{:S(2)}) collective-permute-start(bf16[128,1152]{1,0:T(8,128)(2,1)S(1)} %collective-permute-done.20), channel_id=1, source_target_pairs={{0,2},{1,3},{4,0},{5,1},{8,4},{9,5},{12,8},{13,9},{14,12},{15,13},... | collective-permute-start | bytes 884744 | tf_op jit(solution)/shard_map/ppermute | solution.py:109
  182.4 4.5 %collective-permute-done.24 = bf16[128,1152]{1,0:T(8,128)(2,1)S(1)} collective-permute-done((bf16[128,1152]{1,0:T(8,128)(2,1)S(1)}, bf16[128,1152]{1,0:T(8,128)(2,1)S(1)}, u32[]{:S(2)}, u32[]{:S(2)}) %collective-permute-start.24) | collective-permute-done | bytes 294944 | tf_op jit(solution)/shard_map/ppermute | solution.py:109
  186.9 2.5 %collective-permute-start.28 = (bf16[128,1152]{1,0:T(8,128)(2,1)S(1)}, bf16[128,1152]{1,0:T(8,128)(2,1)S(1)}, u32[]{:S(2)}, u32[]{:S(2)}) collective-permute-start(bf16[128,1152]{1,0:T(8,128)(2,1)S(1)} %collective-permute-done.24), channel_id=1, source_target_pairs={{0,2},{1,3},{4,0},{5,1},{8,4},{9,5},{12,8},{13,9},{14,12},{15,13},... | collective-permute-start | bytes 884744 | tf_op jit(solution)/shard_map/ppermute | solution.py:109
  192.0 7.3 %collective-permute-done.27 = bf16[128,1152]{1,0:T(8,128)(2,1)S(1)} collective-permute-done((bf16[128,1152]{1,0:T(8,128)(2,1)S(1)}, bf16[128,1152]{1,0:T(8,128)(2,1)S(1)}, u32[]{:S(2)}, u32[]{:S(2)}) %collective-permute-start.27) | collective-permute-done | bytes 294944 | tf_op jit(solution)/shard_map/ppermute | solution.py:105
  201.3 5.7 %collective-permute-done.31 = bf16[128,1152]{1,0:T(8,128)(2,1)S(1)} collective-permute-done((bf16[128,1152]{1,0:T(8,128)(2,1)S(1)}, bf16[128,1152]{1,0:T(8,128)(2,1)S(1)}, u32[]{:S(2)}, u32[]{:S(2)}) %collective-permute-start.31) | collective-permute-done | bytes 294944 | tf_op jit(solution)/shard_map/ppermute | solution.py:105
  211.0 3.8 %all-to-all-start.1 = ((bf16[16,8,2048]{2,1,0:T(8,128)(2,1)}), bf16[16,8,2048]{2,1,0:T(8,128)(2,1)S(1)}, u32[]{:S(2)}, u32[]{:S(2)}) async-start(bf16[16,8,2048]{2,1,0:T(8,128)(2,1)} %select_bitcast_fusion), calls=%async_computation.3 | async-start | bytes 1048576 | tf_op jit(solution)/shard_map/all_to_all | solution.py:188
  214.9 2.3 pad_maximum_fusion.3
  217.1 2.1 pad_maximum_fusion
  221.4 7.9 %all-to-all-done.1 = bf16[16,8,2048]{2,1,0:T(8,128)(2,1)S(1)} async-done(((bf16[16,8,2048]{2,1,0:T(8,128)(2,1)}), bf16[16,8,2048]{2,1,0:T(8,128)(2,1)S(1)}, u32[]{:S(2)}, u32[]{:S(2)}) %all-to-all-start.1) | async-done | bytes 524320 | tf_op jit(solution)/shard_map/all_to_all | solution.py:188
  (164 shorter events, 37.2 us)
Async XLA Ops:
  7.2 87.2 %reduce-scatter.5.cloned.1.call-start = ((), (), s32[]{:S(2)}) async-start(), calls=%async_computation.5 | async-start | bytes 4128768 | tf_op jit(solution)/shard_map/reduce_scatter | solution.py:53
  10.2 15.9 %collective-permute-start = (bf16[256,1024]{1,0:T(8,128)(2,1)S(1)}, bf16[256,1024]{1,0:T(8,128)(2,1)}, u32[]{:S(2)}, u32[]{:S(2)}) collective-permute-start(bf16[256,1024]{1,0:T(8,128)(2,1)S(1)} %reshape.207), channel_id=1, source_target_pairs={{0,2},{2,0},{1,3},{3,1},{4,6},{6,4},{5,7},{7,5},{8,10},{10,8},{9,1... | collective-permute-start | bytes 1572872 | tf_op jit(solution)/shard_map/ppermute | solution.py:42
  14.2 20.8 %collective-permute-start.2 = (bf16[256,896]{1,0:T(8,128)(2,1)S(1)}, bf16[256,896]{1,0:T(8,128)(2,1)}, u32[]{:S(2)}, u32[]{:S(2)}) collective-permute-start(bf16[256,896]{1,0:T(8,128)(2,1)S(1)} %slice.51), channel_id=1, source_target_pairs={{0,2},{2,0},{1,3},{3,1},{4,6},{6,4},{5,7},{7,5},{8,10},{10,8},{9,1... | collective-permute-start | bytes 1376264 | tf_op jit(solution)/shard_map/ppermute | solution.py:42
  40.3 16.1 %collective-permute-start.1 = (bf16[256,1152]{1,0:T(8,128)(2,1)S(1)}, bf16[256,1152]{1,0:T(8,128)(2,1)S(1)}, u32[]{:S(2)}, u32[]{:S(2)}) collective-permute-start(bf16[256,1152]{1,0:T(8,128)(2,1)S(1)} %slice.48), channel_id=1, source_target_pairs={{0,2},{2,0},{1,3},{3,1},{4,6},{6,4},{5,7},{7,5},{8,10},{10,8},{9,1... | collective-permute-start | bytes 1769480 | tf_op jit(solution)/shard_map/ppermute | solution.py:43
  44.9 28.0 %all-to-all-start = ((bf16[16,8,2048]{2,1,0:T(8,128)(2,1)}), bf16[16,8,2048]{2,1,0:T(8,128)(2,1)S(1)}, u32[]{:S(2)}, u32[]{:S(2)}) async-start(bf16[16,8,2048]{2,1,0:T(8,128)(2,1)} %select_bitcast_fusion.1), calls=%async_computation.2 | async-start | bytes 1048576 | tf_op jit(solution)/shard_map/all_to_all | solution.py:158
  49.9 115.8 %reduce-scatter.3.cloned.1.call-start = ((), (), s32[]{:S(2)}) async-start(), calls=%async_computation.4 | async-start | bytes 5308416 | tf_op jit(solution)/shard_map/reduce_scatter | solution.py:53
  97.5 8.3 %collective-permute-start.5 = (bf16[128,896]{1,0:T(8,128)(2,1)S(1)}, bf16[128,896]{1,0:T(8,128)(2,1)S(1)}, u32[]{:S(2)}, u32[]{:S(2)}) collective-permute-start(bf16[128,896]{1,0:T(8,128)(2,1)S(1)} %get-tuple-element.31), channel_id=1, source_target_pairs={{0,2},{1,3},{4,0},{5,1},{8,4},{9,5},{12,8},{13,9},{14,12},{15,13},... | collective-permute-start | bytes 688136 | tf_op jit(solution)/shard_map/ppermute | solution.py:109
  99.0 8.6 %collective-permute-start.4 = (bf16[128,896]{1,0:T(8,128)(2,1)S(1)}, bf16[128,896]{1,0:T(8,128)(2,1)S(1)}, u32[]{:S(2)}, u32[]{:S(2)}) collective-permute-start(bf16[128,896]{1,0:T(8,128)(2,1)S(1)} %get-tuple-element.31), channel_id=1, source_target_pairs={{0,4},{1,5},{4,8},{5,9},{8,12},{9,13},{12,14},{13,15},{14,10},{15,... | collective-permute-start | bytes 688136 | tf_op jit(solution)/shard_map/ppermute | solution.py:105
  99.6 10.4 %collective-permute-start.3 = (bf16[128,896]{1,0:T(8,128)(2,1)S(1)}, bf16[128,896]{1,0:T(8,128)(2,1)S(1)}, u32[]{:S(2)}, u32[]{:S(2)}) collective-permute-start(bf16[128,896]{1,0:T(8,128)(2,1)S(1)} %get-tuple-element.31), channel_id=1, source_target_pairs={{0,1},{1,0},{2,3},{3,2},{4,5},{5,4},{6,7},{7,6},{8,9},{9,8},{10,11... | collective-permute-start | bytes 688136 | tf_op jit(solution)/shard_map/ppermute | solution.py:101
  105.8 13.6 %collective-permute-start.9 = (bf16[128,896]{1,0:T(8,128)(2,1)S(1)}, bf16[128,896]{1,0:T(8,128)(2,1)S(1)}, u32[]{:S(2)}, u32[]{:S(2)}) collective-permute-start(bf16[128,896]{1,0:T(8,128)(2,1)S(1)} %collective-permute-done.5), channel_id=1, source_target_pairs={{0,2},{1,3},{4,0},{5,1},{8,4},{9,5},{12,8},{13,9},{14,12},{15,13},... | collective-permute-start | bytes 688136 | tf_op jit(solution)/shard_map/ppermute | solution.py:109
  106.5 16.7 %collective-permute-start.7 = (bf16[128,896]{1,0:T(8,128)(2,1)S(1)}, bf16[128,896]{1,0:T(8,128)(2,1)S(1)}, u32[]{:S(2)}, u32[]{:S(2)}) collective-permute-start(bf16[128,896]{1,0:T(8,128)(2,1)S(1)} %collective-permute-done.5), channel_id=1, source_target_pairs={{0,1},{1,0},{2,3},{3,2},{4,5},{5,4},{6,7},{7,6},{8,9},{9,8},{10,11... | collective-permute-start | bytes 688136 | tf_op jit(solution)/shard_map/ppermute | solution.py:101
  107.6 12.7 %collective-permute-start.8 = (bf16[128,896]{1,0:T(8,128)(2,1)S(1)}, bf16[128,896]{1,0:T(8,128)(2,1)S(1)}, u32[]{:S(2)}, u32[]{:S(2)}) collective-permute-start(bf16[128,896]{1,0:T(8,128)(2,1)S(1)} %collective-permute-done.4), channel_id=1, source_target_pairs={{0,4},{1,5},{4,8},{5,9},{8,12},{9,13},{12,14},{13,15},{14,10},{15,... | collective-permute-start | bytes 688136 | tf_op jit(solution)/shard_map/ppermute | solution.py:105
  109.7 13.8 %collective-permute-start.6 = (bf16[128,896]{1,0:T(8,128)(2,1)S(1)}, bf16[128,896]{1,0:T(8,128)(2,1)S(1)}, u32[]{:S(2)}, u32[]{:S(2)}) collective-permute-start(bf16[128,896]{1,0:T(8,128)(2,1)S(1)} %collective-permute-done.4), channel_id=1, source_target_pairs={{0,1},{1,0},{2,3},{3,2},{4,5},{5,4},{6,7},{7,6},{8,9},{9,8},{10,11... | collective-permute-start | bytes 688136 | tf_op jit(solution)/shard_map/ppermute | solution.py:101
  119.4 16.4 %collective-permute-start.13 = (bf16[128,896]{1,0:T(8,128)(2,1)S(1)}, bf16[128,896]{1,0:T(8,128)(2,1)S(1)}, u32[]{:S(2)}, u32[]{:S(2)}) collective-permute-start(bf16[128,896]{1,0:T(8,128)(2,1)S(1)} %collective-permute-done.9), channel_id=1, source_target_pairs={{0,2},{1,3},{4,0},{5,1},{8,4},{9,5},{12,8},{13,9},{14,12},{15,13},... | collective-permute-start | bytes 688136 | tf_op jit(solution)/shard_map/ppermute | solution.py:109
  119.4 17.3 %collective-permute-start.11 = (bf16[128,896]{1,0:T(8,128)(2,1)S(1)}, bf16[128,896]{1,0:T(8,128)(2,1)S(1)}, u32[]{:S(2)}, u32[]{:S(2)}) collective-permute-start(bf16[128,896]{1,0:T(8,128)(2,1)S(1)} %collective-permute-done.9), channel_id=1, source_target_pairs={{0,1},{1,0},{2,3},{3,2},{4,5},{5,4},{6,7},{7,6},{8,9},{9,8},{10,11... | collective-permute-start | bytes 688136 | tf_op jit(solution)/shard_map/ppermute | solution.py:101
  120.3 13.0 %collective-permute-start.12 = (bf16[128,896]{1,0:T(8,128)(2,1)S(1)}, bf16[128,896]{1,0:T(8,128)(2,1)S(1)}, u32[]{:S(2)}, u32[]{:S(2)}) collective-permute-start(bf16[128,896]{1,0:T(8,128)(2,1)S(1)} %collective-permute-done.8), channel_id=1, source_target_pairs={{0,4},{1,5},{4,8},{5,9},{8,12},{9,13},{12,14},{13,15},{14,10},{15,... | collective-permute-start | bytes 688136 | tf_op jit(solution)/shard_map/ppermute | solution.py:105
  123.2 13.7 %collective-permute-start.10 = (bf16[128,896]{1,0:T(8,128)(2,1)S(1)}, bf16[128,896]{1,0:T(8,128)(2,1)S(1)}, u32[]{:S(2)}, u32[]{:S(2)}) collective-permute-start(bf16[128,896]{1,0:T(8,128)(2,1)S(1)} %collective-permute-done.8), channel_id=1, source_target_pairs={{0,1},{1,0},{2,3},{3,2},{4,5},{5,4},{6,7},{7,6},{8,9},{9,8},{10,11... | collective-permute-start | bytes 688136 | tf_op jit(solution)/shard_map/ppermute | solution.py:101
  133.2 12.7 %collective-permute-start.16 = (bf16[128,896]{1,0:T(8,128)(2,1)S(1)}, bf16[128,896]{1,0:T(8,128)(2,1)S(1)}, u32[]{:S(2)}, u32[]{:S(2)}) collective-permute-start(bf16[128,896]{1,0:T(8,128)(2,1)S(1)} %collective-permute-done.12), channel_id=1, source_target_pairs={{0,4},{1,5},{4,8},{5,9},{8,12},{9,13},{12,14},{13,15},{14,10},{15,... | collective-permute-start | bytes 688136 | tf_op jit(solution)/shard_map/ppermute | solution.py:105
  135.7 10.7 %collective-permute-start.14 = (bf16[128,896]{1,0:T(8,128)(2,1)S(1)}, bf16[128,896]{1,0:T(8,128)(2,1)S(1)}, u32[]{:S(2)}, u32[]{:S(2)}) collective-permute-start(bf16[128,896]{1,0:T(8,128)(2,1)S(1)} %collective-permute-done.12), channel_id=1, source_target_pairs={{0,1},{1,0},{2,3},{3,2},{4,5},{5,4},{6,7},{7,6},{8,9},{9,8},{10,11... | collective-permute-start | bytes 688136 | tf_op jit(solution)/shard_map/ppermute | solution.py:101
  135.7 10.5 %collective-permute-start.15 = (bf16[128,896]{1,0:T(8,128)(2,1)S(1)}, bf16[128,896]{1,0:T(8,128)(2,1)S(1)}, u32[]{:S(2)}, u32[]{:S(2)}) collective-permute-start(bf16[128,896]{1,0:T(8,128)(2,1)S(1)} %collective-permute-done.13), channel_id=1, source_target_pairs={{0,1},{1,0},{2,3},{3,2},{4,5},{5,4},{6,7},{7,6},{8,9},{9,8},{10,11... | collective-permute-start | bytes 688136 | tf_op jit(solution)/shard_map/ppermute | solution.py:101
  168.8 10.0 %collective-permute-start.20 = (bf16[128,1152]{1,0:T(8,128)(2,1)S(1)}, bf16[128,1152]{1,0:T(8,128)(2,1)S(1)}, u32[]{:S(2)}, u32[]{:S(2)}) collective-permute-start(bf16[128,1152]{1,0:T(8,128)(2,1)S(1)} %get-tuple-element.26), channel_id=1, source_target_pairs={{0,2},{1,3},{4,0},{5,1},{8,4},{9,5},{12,8},{13,9},{14,12},{15,13},... | collective-permute-start | bytes 884744 | tf_op jit(solution)/shard_map/ppermute | solution.py:109
  172.2 9.0 %collective-permute-start.19 = (bf16[128,1152]{1,0:T(8,128)(2,1)S(1)}, bf16[128,1152]{1,0:T(8,128)(2,1)S(1)}, u32[]{:S(2)}, u32[]{:S(2)}) collective-permute-start(bf16[128,1152]{1,0:T(8,128)(2,1)S(1)} %get-tuple-element.26), channel_id=1, source_target_pairs={{0,4},{1,5},{4,8},{5,9},{8,12},{9,13},{12,14},{13,15},{14,10},{15,... | collective-permute-start | bytes 884744 | tf_op jit(solution)/shard_map/ppermute | solution.py:105
  172.2 9.5 %collective-permute-start.18 = (bf16[128,1152]{1,0:T(8,128)(2,1)S(1)}, bf16[128,1152]{1,0:T(8,128)(2,1)S(1)}, u32[]{:S(2)}, u32[]{:S(2)}) collective-permute-start(bf16[128,1152]{1,0:T(8,128)(2,1)S(1)} %get-tuple-element.26), channel_id=1, source_target_pairs={{0,1},{1,0},{2,3},{3,2},{4,5},{5,4},{6,7},{7,6},{8,9},{9,8},{10,11... | collective-permute-start | bytes 884744 | tf_op jit(solution)/shard_map/ppermute | solution.py:101
  178.7 8.2 %collective-permute-start.24 = (bf16[128,1152]{1,0:T(8,128)(2,1)S(1)}, bf16[128,1152]{1,0:T(8,128)(2,1)S(1)}, u32[]{:S(2)}, u32[]{:S(2)}) collective-permute-start(bf16[128,1152]{1,0:T(8,128)(2,1)S(1)} %collective-permute-done.20), channel_id=1, source_target_pairs={{0,2},{1,3},{4,0},{5,1},{8,4},{9,5},{12,8},{13,9},{14,12},{15,13},... | collective-permute-start | bytes 884744 | tf_op jit(solution)/shard_map/ppermute | solution.py:109
  181.2 10.2 %collective-permute-start.22 = (bf16[128,1152]{1,0:T(8,128)(2,1)S(1)}, bf16[128,1152]{1,0:T(8,128)(2,1)S(1)}, u32[]{:S(2)}, u32[]{:S(2)}) collective-permute-start(bf16[128,1152]{1,0:T(8,128)(2,1)S(1)} %collective-permute-done.20), channel_id=1, source_target_pairs={{0,1},{1,0},{2,3},{3,2},{4,5},{5,4},{6,7},{7,6},{8,9},{9,8},{10,11... | collective-permute-start | bytes 884744 | tf_op jit(solution)/shard_map/ppermute | solution.py:101
  181.2 9.4 %collective-permute-start.23 = (bf16[128,1152]{1,0:T(8,128)(2,1)S(1)}, bf16[128,1152]{1,0:T(8,128)(2,1)S(1)}, u32[]{:S(2)}, u32[]{:S(2)}) collective-permute-start(bf16[128,1152]{1,0:T(8,128)(2,1)S(1)} %collective-permute-done.19), channel_id=1, source_target_pairs={{0,4},{1,5},{4,8},{5,9},{8,12},{9,13},{12,14},{13,15},{14,10},{15,... | collective-permute-start | bytes 884744 | tf_op jit(solution)/shard_map/ppermute | solution.py:105
  181.2 10.5 %collective-permute-start.21 = (bf16[128,1152]{1,0:T(8,128)(2,1)S(1)}, bf16[128,1152]{1,0:T(8,128)(2,1)S(1)}, u32[]{:S(2)}, u32[]{:S(2)}) collective-permute-start(bf16[128,1152]{1,0:T(8,128)(2,1)S(1)} %collective-permute-done.19), channel_id=1, source_target_pairs={{0,1},{1,0},{2,3},{3,2},{4,5},{5,4},{6,7},{7,6},{8,9},{9,8},{10,11... | collective-permute-start | bytes 884744 | tf_op jit(solution)/shard_map/ppermute | solution.py:101
  186.9 13.1 %collective-permute-start.28 = (bf16[128,1152]{1,0:T(8,128)(2,1)S(1)}, bf16[128,1152]{1,0:T(8,128)(2,1)S(1)}, u32[]{:S(2)}, u32[]{:S(2)}) collective-permute-start(bf16[128,1152]{1,0:T(8,128)(2,1)S(1)} %collective-permute-done.24), channel_id=1, source_target_pairs={{0,2},{1,3},{4,0},{5,1},{8,4},{9,5},{12,8},{13,9},{14,12},{15,13},... | collective-permute-start | bytes 884744 | tf_op jit(solution)/shard_map/ppermute | solution.py:109
  189.4 11.4 %collective-permute-start.26 = (bf16[128,1152]{1,0:T(8,128)(2,1)S(1)}, bf16[128,1152]{1,0:T(8,128)(2,1)S(1)}, u32[]{:S(2)}, u32[]{:S(2)}) collective-permute-start(bf16[128,1152]{1,0:T(8,128)(2,1)S(1)} %collective-permute-done.24), channel_id=1, source_target_pairs={{0,1},{1,0},{2,3},{3,2},{4,5},{5,4},{6,7},{7,6},{8,9},{9,8},{10,11... | collective-permute-start | bytes 884744 | tf_op jit(solution)/shard_map/ppermute | solution.py:101
  190.6 8.6 %collective-permute-start.27 = (bf16[128,1152]{1,0:T(8,128)(2,1)S(1)}, bf16[128,1152]{1,0:T(8,128)(2,1)S(1)}, u32[]{:S(2)}, u32[]{:S(2)}) collective-permute-start(bf16[128,1152]{1,0:T(8,128)(2,1)S(1)} %collective-permute-done.23), channel_id=1, source_target_pairs={{0,4},{1,5},{4,8},{5,9},{8,12},{9,13},{12,14},{13,15},{14,10},{15,... | collective-permute-start | bytes 884744 | tf_op jit(solution)/shard_map/ppermute | solution.py:105
  191.4 9.6 %collective-permute-start.25 = (bf16[128,1152]{1,0:T(8,128)(2,1)S(1)}, bf16[128,1152]{1,0:T(8,128)(2,1)S(1)}, u32[]{:S(2)}, u32[]{:S(2)}) collective-permute-start(bf16[128,1152]{1,0:T(8,128)(2,1)S(1)} %collective-permute-done.23), channel_id=1, source_target_pairs={{0,1},{1,0},{2,3},{3,2},{4,5},{5,4},{6,7},{7,6},{8,9},{9,8},{10,11... | collective-permute-start | bytes 884744 | tf_op jit(solution)/shard_map/ppermute | solution.py:101
  211.0 18.3 %all-to-all-start.1 = ((bf16[16,8,2048]{2,1,0:T(8,128)(2,1)}), bf16[16,8,2048]{2,1,0:T(8,128)(2,1)S(1)}, u32[]{:S(2)}, u32[]{:S(2)}) async-start(bf16[16,8,2048]{2,1,0:T(8,128)(2,1)} %select_bitcast_fusion), calls=%async_computation.3 | async-start | bytes 1048576 | tf_op jit(solution)/shard_map/all_to_all | solution.py:188
  (15 other events, 130.5 us)
Sparse Core Ops, SparseCore 0:
  39.3 54.9 reduce-scatter.4
  96.7 68.9 reduce-scatter.2

commit v13 on v12

--- a/solution.py
+++ b/solution.py
@@ -38,7 +38,7 @@
     mine = mine.reshape(tokens, width // 2)
     theirs = theirs.reshape(tokens, width // 2)
     swap = [(0, 1), (1, 0)]
-    half = grad_out.shape[1] * 7 // 16
+    half = grad_out.shape[1] * 3 // 8
     got_queries, got_first = lax.ppermute((theirs, grad_out[:, :half]), "xl", swap)
     got_second = lax.ppermute(grad_out[:, half:], "xl", swap)
     both_queries = jnp.concatenate([mine, got_queries], axis=0)

time: 239 us -> 240 us (level)
  waiting for transfers between devices: 137 us -> 140 us
  other arithmetic: 20.9 us -> 23.3 us
    reduce_scatter x2, waiting for transfers between devices: 38.2 us -> 23.1 us  [pair_gradient(): lax.psum_scatter(partial, ('zo', 'c'), scatter_dimension=0, tiled=True)]
    ppermute x6, waiting for transfers between devices: 21 us -> 30.6 us  [ring_codes(): behind = lax.ppermute(behind, DP, backward)]
    ppermute x1, waiting for transfers between devices: 5.56 us -> 13.9 us  [pair_gradient(): got_second = lax.ppermute(grad_out[:, half:], 'xl', swap)]
    all_to_all x1, waiting for transfers between devices: 10.1 us -> 18.1 us  [per_device(): lax.all_to_all(jnp.take(keys, send_forward, axis=0), DP, split_axis=0, co...]
    ppermute x8, waiting for transfers between devices: 32.9 us -> 26.8 us  [ring_codes(): ahead = lax.ppermute(ahead, DP, forward)]
    select_n x1, other arithmetic: 2.29 us -> 4.96 us  [per_device(): jnp.where(kept, queue, jnp.zeros_like(queue))]
    ppermute x16, starting transfers between devices: 3.99 us -> 1.5 us  [ring_codes(): sent = lax.ppermute(tuple((s for _, s in handed)), DP, partner)]
  transfers between devices with their start and end apart: 37 -> 37, of which waited for: 19 -> 16; matrix products, arithmetic and copies ran while one was open for 14% -> 14% of each run, Pallas kernels for 0% -> 0%
where the time goes in v13:
time: 240 us
  waiting for transfers between devices  140 us (58%)
  starting transfers between devices  34.7 us (14%)
  other arithmetic  23.3 us (10%)
  between operations  17.1 us (7%)
  matrix products  13.5 us (6%)
  local copies, waits for them, and re-layouts  11.1 us (5%)
    ppermute x6, waiting for transfers between devices, ring_codes(): behind = lax.ppermute(behind, DP, backward)  30.6 us
    ppermute x8, waiting for transfers between devices, ring_codes(): ahead = lax.ppermute(ahead, DP, forward)  26.8 us
    reduce_scatter x2, waiting for transfers between devices, pair_gradient(): lax.psum_scatter(partial, ('zo', 'c'), scatter_dimension=0, tiled=True)  23.1 us
    all_to_all x1, waiting for transfers between devices, per_device(): lax.all_to_all(jnp.take(keys, send_forward, axis=0), DP, split_axis=0, co...  18.1 us
    ppermute x2, waiting for transfers between devices, pair_gradient(): lax.ppermute((theirs, grad_out[:, :half]), 'xl', swap)  17.8 us
    ppermute x1, waiting for transfers between devices, pair_gradient(): got_second = lax.ppermute(grad_out[:, half:], 'xl', swap)  13.9 us
    ppermute x6, starting transfers between devices, ring_codes(): behind = lax.ppermute(behind, DP, backward)  9.96 us
    ppermute x8, starting transfers between devices, ring_codes(): ahead = lax.ppermute(ahead, DP, forward)  8.5 us
  transfers between devices with their start and end apart: 37, of which 16 were waited for; matrix products, arithmetic and copies ran while one was open for 14% of the time, Pallas kernels for 0%

profile of v13, /device:TPU:0, one launch (start us, length us, event | category | flops | bytes accessed | tf_op | source)
XLA Modules:
  0.0 239.8 jit_solution(8550762842438528413)
XLA Ops:
  7.2 1.8 reshape.205
  10.2 3.0 %collective-permute-start = (bf16[256,1024]{1,0:T(8,128)(2,1)S(1)}, bf16[256,1024]{1,0:T(8,128)(2,1)}, u32[]{:S(2)}, u32[]{:S(2)}) collective-permute-start(bf16[256,1024]{1,0:T(8,128)(2,1)S(1)} %reshape.207), channel_id=1, source_target_pairs={{0,2},{2,0},{1,3},{3,1},{4,6},{6,4},{5,7},{7,5},{8,10},{10,8},{9,1... | collective-permute-start | bytes 1572872 | tf_op jit(solution)/shard_map/ppermute | solution.py:42
  14.7 11.3 %collective-permute-done = bf16[256,1024]{1,0:T(8,128)(2,1)} collective-permute-done((bf16[256,1024]{1,0:T(8,128)(2,1)S(1)}, bf16[256,1024]{1,0:T(8,128)(2,1)}, u32[]{:S(2)}, u32[]{:S(2)}) %collective-permute-start) | collective-permute-done | bytes 524320 | tf_op jit(solution)/shard_map/ppermute | solution.py:42
  27.1 6.4 %collective-permute-done.2 = bf16[256,768]{1,0:T(8,128)(2,1)S(1)} collective-permute-done((bf16[256,768]{1,0:T(8,128)(2,1)S(1)}, bf16[256,768]{1,0:T(8,128)(2,1)S(1)}, u32[]{:S(2)}, u32[]{:S(2)}) %collective-permute-start.2) | collective-permute-done | bytes 393248 | tf_op jit(solution)/shard_map/ppermute | solution.py:42
  33.5 2.7 %fusion.26 = f32[1024,768]{1,0:T(8,128)} fusion(bf16[512,1024]{1,0:T(8,128)(2,1)S(1)} %constant_dynamic-update-slice_fusion, bf16[256,768]{1,0:T(8,128)(2,1)S(1)} %collective-permute-done.2, bf16[256,768]{1,0:T(8,128)(2,1)S(1)} %slice.51), kind=kOutput, calls=%fused_computation.47 | convolution fusion | flops 806879232 | bytes 4980736 | tf_op jit(solution)/shard_map/dot_general | solution.py:47
  37.5 1.8 collective-permute-start.1
  39.6 13.9 %collective-permute-done.1 = bf16[256,1280]{1,0:T(8,128)(2,1)S(1)} collective-permute-done((bf16[256,1280]{1,0:T(8,128)(2,1)S(1)}, bf16[256,1280]{1,0:T(8,128)(2,1)S(1)}, u32[]{:S(2)}, u32[]{:S(2)}) %collective-permute-start.1) | collective-permute-done | bytes 655392 | tf_op jit(solution)/shard_map/ppermute | solution.py:43
  53.5 3.9 %fusion.11 = f32[1024,1280]{1,0:T(8,128)} fusion(bf16[512,1024]{1,0:T(8,128)(2,1)S(1)} %constant_dynamic-update-slice_fusion, bf16[256,1280]{1,0:T(8,128)(2,1)S(1)} %collective-permute-done.1, bf16[256,1280]{1,0:T(8,128)(2,1)S(1)} %slice.48), kind=kOutput, calls=%fused_computation.22 | convolution fusion | flops 1344798720 | bytes 7602176 | tf_op jit(solution)/shard_map/dot_general | solution.py:47
  59.9 5.8 %all-to-all-start = ((bf16[16,8,2048]{2,1,0:T(8,128)(2,1)}), bf16[16,8,2048]{2,1,0:T(8,128)(2,1)S(1)}, u32[]{:S(2)}, u32[]{:S(2)}) async-start(bf16[16,8,2048]{2,1,0:T(8,128)(2,1)} %select_bitcast_fusion.1), calls=%async_computation.2 | async-start | bytes 1048576 | tf_op jit(solution)/shard_map/all_to_all | solution.py:158
  68.6 18.1 %all-to-all-done = bf16[16,8,2048]{2,1,0:T(8,128)(2,1)S(1)} async-done(((bf16[16,8,2048]{2,1,0:T(8,128)(2,1)}), bf16[16,8,2048]{2,1,0:T(8,128)(2,1)S(1)}, u32[]{:S(2)}, u32[]{:S(2)}) %all-to-all-start) | async-done | bytes 524320 | tf_op jit(solution)/shard_map/all_to_all | solution.py:158
  87.7 2.7 %fusion.129 = (bf16[128,768]{1,0:T(8,128)(2,1)S(1)}, f32[128,768]{1,0:T(8,128)}, f32[128,768]{1,0:T(8,128)S(1)}, f32[128,768]{1,0:T(8,128)}, f32[128,768]{1,0:T(8,128)}) fusion(f32[128,2048]{1,0:T(8,128)} %param.20, f32[128,2048]{1,0:T(8,128)} %param.17, f32[128,768]{1,0:T(8,128)} %reduce-scatter.5.cloned.1.call-done, f32[128,2048]{1,0:T(8,128)} %param.18, ...), kind=kLoop, calls=%fused_computation.220 | loop fusion | flops 1966080 | bytes 3735552 | tf_op jit(solution)/shard_map/convert_element_type | solution.py:182
  90.9 1.6 collective-permute-start.4
  94.3 5.0 %broadcast_select_fusion = bf16[8,128,2048]{2,1,0:T(8,128)(2,1)} fusion(bf16[8,128,2048]{2,1,0:T(8,128)(2,1)} %param.26, pred[]{:T(512)} %bitcast.4), kind=kLoop, calls=%fused_computation.4 | loop fusion | flops 2097152 | bytes 8388609 | tf_op jit(solution)/shard_map/jit(_where)/select_n | solution.py:167
  102.4 9.8 %collective-permute-done.9 = bf16[128,768]{1,0:T(8,128)(2,1)S(1)} collective-permute-done((bf16[128,768]{1,0:T(8,128)(2,1)S(1)}, bf16[128,768]{1,0:T(8,128)(2,1)S(1)}, u32[]{:S(2)}, u32[]{:S(2)}) %collective-permute-start.9) | collective-permute-done | bytes 196640 | tf_op jit(solution)/shard_map/ppermute | solution.py:109
  112.1 2.0 collective-permute-start.12
  115.1 8.4 %collective-permute-done.12 = bf16[128,768]{1,0:T(8,128)(2,1)S(1)} collective-permute-done((bf16[128,768]{1,0:T(8,128)(2,1)S(1)}, bf16[128,768]{1,0:T(8,128)(2,1)S(1)}, u32[]{:S(2)}, u32[]{:S(2)}) %collective-permute-start.12) | collective-permute-done | bytes 196640 | tf_op jit(solution)/shard_map/ppermute | solution.py:105
  123.5 2.5 %collective-permute-start.16 = (bf16[128,768]{1,0:T(8,128)(2,1)S(1)}, bf16[128,768]{1,0:T(8,128)(2,1)S(1)}, u32[]{:S(2)}, u32[]{:S(2)}) collective-permute-start(bf16[128,768]{1,0:T(8,128)(2,1)S(1)} %collective-permute-done.12), channel_id=1, source_target_pairs={{0,4},{1,5},{4,8},{5,9},{8,12},{9,13},{12,14},{13,15},{14,10},{15,... | collective-permute-start | bytes 589832 | tf_op jit(solution)/shard_map/ppermute | solution.py:105
  127.3 7.8 %collective-permute-done.16 = bf16[128,768]{1,0:T(8,128)(2,1)S(1)} collective-permute-done((bf16[128,768]{1,0:T(8,128)(2,1)S(1)}, bf16[128,768]{1,0:T(8,128)(2,1)S(1)}, u32[]{:S(2)}, u32[]{:S(2)}) %collective-permute-start.16) | collective-permute-done | bytes 196640 | tf_op jit(solution)/shard_map/ppermute | solution.py:105
  137.0 23.0 %reduce-scatter.3.cloned.1.call-done = f32[128,1280]{1,0:T(8,128)} async-done(((f32[1024,1280]{1,0:T(8,128)}), f32[128,1280]{1,0:T(8,128)}) %reduce-scatter.3.cloned.1.call-update) | async-done | bytes 655376 | tf_op jit(solution)/shard_map/reduce_scatter | solution.py:53
  160.0 3.3 %fusion.128 = (bf16[128,1280]{1,0:T(8,128)(2,1)S(1)}, f32[128,1280]{1,0:T(8,128)}, f32[128,1280]{1,0:T(8,128)S(1)}, f32[128,1280]{1,0:T(8,128)S(1)}, f32[128,1280]{1,0:T(8,128)S(1)}) fusion(f32[128,2048]{1,0:T(8,128)} %param.20, f32[128,2048]{1,0:T(8,128)} %param.17, f32[128,1280]{1,0:T(8,128)} %reduce-scatter.3.cloned.1.call-done, f32[128,2048]{1,0:T(8,128)} %param.18, ...), kind=kLoop, calls=%fused_computation.219 | loop fusion | flops 3276800 | bytes 6225920 | tf_op jit(solution)/shard_map/convert_element_type | solution.py:182
  163.5 4.4 %collective-permute-start.20 = (bf16[128,1280]{1,0:T(8,128)(2,1)S(1)}, bf16[128,1280]{1,0:T(8,128)(2,1)S(1)}, u32[]{:S(2)}, u32[]{:S(2)}) collective-permute-start(bf16[128,1280]{1,0:T(8,128)(2,1)S(1)} %get-tuple-element.26), channel_id=1, source_target_pairs={{0,2},{1,3},{4,0},{5,1},{8,4},{9,5},{12,8},{13,9},{14,12},{15,13},... | collective-permute-start | bytes 983048 | tf_op jit(solution)/shard_map/ppermute | solution.py:109
  168.2 7.4 %collective-permute-done.20 = bf16[128,1280]{1,0:T(8,128)(2,1)S(1)} collective-permute-done((bf16[128,1280]{1,0:T(8,128)(2,1)S(1)}, bf16[128,1280]{1,0:T(8,128)(2,1)S(1)}, u32[]{:S(2)}, u32[]{:S(2)}) %collective-permute-start.20) | collective-permute-done | bytes 327712 | tf_op jit(solution)/shard_map/ppermute | solution.py:109
  175.6 2.5 %collective-permute-start.24 = (bf16[128,1280]{1,0:T(8,128)(2,1)S(1)}, bf16[128,1280]{1,0:T(8,128)(2,1)S(1)}, u32[]{:S(2)}, u32[]{:S(2)}) collective-permute-start(bf16[128,1280]{1,0:T(8,128)(2,1)S(1)} %collective-permute-done.20), channel_id=1, source_target_pairs={{0,2},{1,3},{4,0},{5,1},{8,4},{9,5},{12,8},{13,9},{14,12},{15,13},... | collective-permute-start | bytes 983048 | tf_op jit(solution)/shard_map/ppermute | solution.py:109
  179.0 6.7 %collective-permute-done.24 = bf16[128,1280]{1,0:T(8,128)(2,1)S(1)} collective-permute-done((bf16[128,1280]{1,0:T(8,128)(2,1)S(1)}, bf16[128,1280]{1,0:T(8,128)(2,1)S(1)}, u32[]{:S(2)}, u32[]{:S(2)}) %collective-permute-start.24) | collective-permute-done | bytes 327712 | tf_op jit(solution)/shard_map/ppermute | solution.py:109
  186.0 1.9 collective-permute-done.23
  188.5 1.7 collective-permute-start.28
  190.8 6.8 %collective-permute-done.28 = bf16[128,1280]{1,0:T(8,128)(2,1)S(1)} collective-permute-done((bf16[128,1280]{1,0:T(8,128)(2,1)S(1)}, bf16[128,1280]{1,0:T(8,128)(2,1)S(1)}, u32[]{:S(2)}, u32[]{:S(2)}) %collective-permute-start.28) | collective-permute-done | bytes 327712 | tf_op jit(solution)/shard_map/ppermute | solution.py:109
  199.6 8.6 %collective-permute-done.31 = bf16[128,1280]{1,0:T(8,128)(2,1)S(1)} collective-permute-done((bf16[128,1280]{1,0:T(8,128)(2,1)S(1)}, bf16[128,1280]{1,0:T(8,128)(2,1)S(1)}, u32[]{:S(2)}, u32[]{:S(2)}) %collective-permute-start.31) | collective-permute-done | bytes 327712 | tf_op jit(solution)/shard_map/ppermute | solution.py:105
  212.6 3.9 %all-to-all-start.1 = ((bf16[16,8,2048]{2,1,0:T(8,128)(2,1)}), bf16[16,8,2048]{2,1,0:T(8,128)(2,1)S(1)}, u32[]{:S(2)}, u32[]{:S(2)}) async-start(bf16[16,8,2048]{2,1,0:T(8,128)(2,1)} %select_bitcast_fusion), calls=%async_computation.3 | async-start | bytes 1048576 | tf_op jit(solution)/shard_map/all_to_all | solution.py:188
  216.6 2.3 pad_maximum_fusion.3
  218.8 2.1 pad_maximum_fusion.2
  223.1 8.0 %all-to-all-done.1 = bf16[16,8,2048]{2,1,0:T(8,128)(2,1)S(1)} async-done(((bf16[16,8,2048]{2,1,0:T(8,128)(2,1)}), bf16[16,8,2048]{2,1,0:T(8,128)(2,1)S(1)}, u32[]{:S(2)}, u32[]{:S(2)}) %all-to-all-start.1) | async-done | bytes 524320 | tf_op jit(solution)/shard_map/all_to_all | solution.py:188
  (164 shorter events, 31.5 us)
Async XLA Ops:
  7.2 80.5 %reduce-scatter.5.cloned.1.call-start = ((), (), s32[]{:S(2)}) async-start(), calls=%async_computation.5 | async-start | bytes 3538944 | tf_op jit(solution)/shard_map/reduce_scatter | solution.py:53
  10.2 15.9 %collective-permute-start = (bf16[256,1024]{1,0:T(8,128)(2,1)S(1)}, bf16[256,1024]{1,0:T(8,128)(2,1)}, u32[]{:S(2)}, u32[]{:S(2)}) collective-permute-start(bf16[256,1024]{1,0:T(8,128)(2,1)S(1)} %reshape.207), channel_id=1, source_target_pairs={{0,2},{2,0},{1,3},{3,1},{4,6},{6,4},{5,7},{7,5},{8,10},{10,8},{9,1... | collective-permute-start | bytes 1572872 | tf_op jit(solution)/shard_map/ppermute | solution.py:42
  14.2 19.3 %collective-permute-start.2 = (bf16[256,768]{1,0:T(8,128)(2,1)S(1)}, bf16[256,768]{1,0:T(8,128)(2,1)S(1)}, u32[]{:S(2)}, u32[]{:S(2)}) collective-permute-start(bf16[256,768]{1,0:T(8,128)(2,1)S(1)} %slice.51), channel_id=1, source_target_pairs={{0,2},{2,0},{1,3},{3,1},{4,6},{6,4},{5,7},{7,5},{8,10},{10,8},{9,1... | collective-permute-start | bytes 1179656 | tf_op jit(solution)/shard_map/ppermute | solution.py:42
  36.2 123.8 %reduce-scatter.3.cloned.1.call-start = ((), (), s32[]{:S(2)}) async-start(), calls=%async_computation.4 | async-start | bytes 5898240 | tf_op jit(solution)/shard_map/reduce_scatter | solution.py:53
  37.5 16.0 %collective-permute-start.1 = (bf16[256,1280]{1,0:T(8,128)(2,1)S(1)}, bf16[256,1280]{1,0:T(8,128)(2,1)S(1)}, u32[]{:S(2)}, u32[]{:S(2)}) collective-permute-start(bf16[256,1280]{1,0:T(8,128)(2,1)S(1)} %slice.48), channel_id=1, source_target_pairs={{0,2},{2,0},{1,3},{3,1},{4,6},{6,4},{5,7},{7,5},{8,10},{10,8},{9,1... | collective-permute-start | bytes 1966088 | tf_op jit(solution)/shard_map/ppermute | solution.py:43
  59.9 26.8 %all-to-all-start = ((bf16[16,8,2048]{2,1,0:T(8,128)(2,1)}), bf16[16,8,2048]{2,1,0:T(8,128)(2,1)S(1)}, u32[]{:S(2)}, u32[]{:S(2)}) async-start(bf16[16,8,2048]{2,1,0:T(8,128)(2,1)} %select_bitcast_fusion.1), calls=%async_computation.2 | async-start | bytes 1048576 | tf_op jit(solution)/shard_map/all_to_all | solution.py:158
  90.4 11.5 %collective-permute-start.3 = (bf16[128,768]{1,0:T(8,128)(2,1)S(1)}, bf16[128,768]{1,0:T(8,128)(2,1)S(1)}, u32[]{:S(2)}, u32[]{:S(2)}) collective-permute-start(bf16[128,768]{1,0:T(8,128)(2,1)S(1)} %get-tuple-element.31), channel_id=1, source_target_pairs={{0,1},{1,0},{2,3},{3,2},{4,5},{5,4},{6,7},{7,6},{8,9},{9,8},{10,11... | collective-permute-start | bytes 589832 | tf_op jit(solution)/shard_map/ppermute | solution.py:101
  90.9 9.6 %collective-permute-start.4 = (bf16[128,768]{1,0:T(8,128)(2,1)S(1)}, bf16[128,768]{1,0:T(8,128)(2,1)S(1)}, u32[]{:S(2)}, u32[]{:S(2)}) collective-permute-start(bf16[128,768]{1,0:T(8,128)(2,1)S(1)} %get-tuple-element.31), channel_id=1, source_target_pairs={{0,4},{1,5},{4,8},{5,9},{8,12},{9,13},{12,14},{13,15},{14,10},{15,... | collective-permute-start | bytes 589832 | tf_op jit(solution)/shard_map/ppermute | solution.py:105
  99.5 15.0 %collective-permute-start.7 = (bf16[128,768]{1,0:T(8,128)(2,1)S(1)}, bf16[128,768]{1,0:T(8,128)(2,1)S(1)}, u32[]{:S(2)}, u32[]{:S(2)}) collective-permute-start(bf16[128,768]{1,0:T(8,128)(2,1)S(1)} %collective-permute-done.5), channel_id=1, source_target_pairs={{0,1},{1,0},{2,3},{3,2},{4,5},{5,4},{6,7},{7,6},{8,9},{9,8},{10,11... | collective-permute-start | bytes 589832 | tf_op jit(solution)/shard_map/ppermute | solution.py:101
  99.6 12.5 %collective-permute-start.9 = (bf16[128,768]{1,0:T(8,128)(2,1)S(1)}, bf16[128,768]{1,0:T(8,128)(2,1)S(1)}, u32[]{:S(2)}, u32[]{:S(2)}) collective-permute-start(bf16[128,768]{1,0:T(8,128)(2,1)S(1)} %collective-permute-done.5), channel_id=1, source_target_pairs={{0,2},{1,3},{4,0},{5,1},{8,4},{9,5},{12,8},{13,9},{14,12},{15,13},... | collective-permute-start | bytes 589832 | tf_op jit(solution)/shard_map/ppermute | solution.py:109
  100.5 11.6 %collective-permute-start.8 = (bf16[128,768]{1,0:T(8,128)(2,1)S(1)}, bf16[128,768]{1,0:T(8,128)(2,1)S(1)}, u32[]{:S(2)}, u32[]{:S(2)}) collective-permute-start(bf16[128,768]{1,0:T(8,128)(2,1)S(1)} %collective-permute-done.4), channel_id=1, source_target_pairs={{0,4},{1,5},{4,8},{5,9},{8,12},{9,13},{12,14},{13,15},{14,10},{15,... | collective-permute-start | bytes 589832 | tf_op jit(solution)/shard_map/ppermute | solution.py:105
  101.7 13.1 %collective-permute-start.6 = (bf16[128,768]{1,0:T(8,128)(2,1)S(1)}, bf16[128,768]{1,0:T(8,128)(2,1)S(1)}, u32[]{:S(2)}, u32[]{:S(2)}) collective-permute-start(bf16[128,768]{1,0:T(8,128)(2,1)S(1)} %collective-permute-done.4), channel_id=1, source_target_pairs={{0,1},{1,0},{2,3},{3,2},{4,5},{5,4},{6,7},{7,6},{8,9},{9,8},{10,11... | collective-permute-start | bytes 589832 | tf_op jit(solution)/shard_map/ppermute | solution.py:101
  112.1 14.7 %collective-permute-start.11 = (bf16[128,768]{1,0:T(8,128)(2,1)S(1)}, bf16[128,768]{1,0:T(8,128)(2,1)S(1)}, u32[]{:S(2)}, u32[]{:S(2)}) collective-permute-start(bf16[128,768]{1,0:T(8,128)(2,1)S(1)} %collective-permute-done.9), channel_id=1, source_target_pairs={{0,1},{1,0},{2,3},{3,2},{4,5},{5,4},{6,7},{7,6},{8,9},{9,8},{10,11... | collective-permute-start | bytes 589832 | tf_op jit(solution)/shard_map/ppermute | solution.py:101
  112.1 13.8 %collective-permute-start.13 = (bf16[128,768]{1,0:T(8,128)(2,1)S(1)}, bf16[128,768]{1,0:T(8,128)(2,1)S(1)}, u32[]{:S(2)}, u32[]{:S(2)}) collective-permute-start(bf16[128,768]{1,0:T(8,128)(2,1)S(1)} %collective-permute-done.9), channel_id=1, source_target_pairs={{0,2},{1,3},{4,0},{5,1},{8,4},{9,5},{12,8},{13,9},{14,12},{15,13},... | collective-permute-start | bytes 589832 | tf_op jit(solution)/shard_map/ppermute | solution.py:109
  112.1 11.3 %collective-permute-start.12 = (bf16[128,768]{1,0:T(8,128)(2,1)S(1)}, bf16[128,768]{1,0:T(8,128)(2,1)S(1)}, u32[]{:S(2)}, u32[]{:S(2)}) collective-permute-start(bf16[128,768]{1,0:T(8,128)(2,1)S(1)} %collective-permute-done.8), channel_id=1, source_target_pairs={{0,4},{1,5},{4,8},{5,9},{8,12},{9,13},{12,14},{13,15},{14,10},{15,... | collective-permute-start | bytes 589832 | tf_op jit(solution)/shard_map/ppermute | solution.py:105
  114.6 12.5 %collective-permute-start.10 = (bf16[128,768]{1,0:T(8,128)(2,1)S(1)}, bf16[128,768]{1,0:T(8,128)(2,1)S(1)}, u32[]{:S(2)}, u32[]{:S(2)}) collective-permute-start(bf16[128,768]{1,0:T(8,128)(2,1)S(1)} %collective-permute-done.8), channel_id=1, source_target_pairs={{0,1},{1,0},{2,3},{3,2},{4,5},{5,4},{6,7},{7,6},{8,9},{9,8},{10,11... | collective-permute-start | bytes 589832 | tf_op jit(solution)/shard_map/ppermute | solution.py:101
  123.5 11.7 %collective-permute-start.16 = (bf16[128,768]{1,0:T(8,128)(2,1)S(1)}, bf16[128,768]{1,0:T(8,128)(2,1)S(1)}, u32[]{:S(2)}, u32[]{:S(2)}) collective-permute-start(bf16[128,768]{1,0:T(8,128)(2,1)S(1)} %collective-permute-done.12), channel_id=1, source_target_pairs={{0,4},{1,5},{4,8},{5,9},{8,12},{9,13},{12,14},{13,15},{14,10},{15,... | collective-permute-start | bytes 589832 | tf_op jit(solution)/shard_map/ppermute | solution.py:105
  125.9 9.6 %collective-permute-start.14 = (bf16[128,768]{1,0:T(8,128)(2,1)S(1)}, bf16[128,768]{1,0:T(8,128)(2,1)S(1)}, u32[]{:S(2)}, u32[]{:S(2)}) collective-permute-start(bf16[128,768]{1,0:T(8,128)(2,1)S(1)} %collective-permute-done.12), channel_id=1, source_target_pairs={{0,1},{1,0},{2,3},{3,2},{4,5},{5,4},{6,7},{7,6},{8,9},{9,8},{10,11... | collective-permute-start | bytes 589832 | tf_op jit(solution)/shard_map/ppermute | solution.py:101
  126.0 9.4 %collective-permute-start.15 = (bf16[128,768]{1,0:T(8,128)(2,1)S(1)}, bf16[128,768]{1,0:T(8,128)(2,1)S(1)}, u32[]{:S(2)}, u32[]{:S(2)}) collective-permute-start(bf16[128,768]{1,0:T(8,128)(2,1)S(1)} %collective-permute-done.13), channel_id=1, source_target_pairs={{0,1},{1,0},{2,3},{3,2},{4,5},{5,4},{6,7},{7,6},{8,9},{9,8},{10,11... | collective-permute-start | bytes 589832 | tf_op jit(solution)/shard_map/ppermute | solution.py:101
  163.3 15.0 %collective-permute-start.18 = (bf16[128,1280]{1,0:T(8,128)(2,1)S(1)}, bf16[128,1280]{1,0:T(8,128)(2,1)S(1)}, u32[]{:S(2)}, u32[]{:S(2)}) collective-permute-start(bf16[128,1280]{1,0:T(8,128)(2,1)S(1)} %get-tuple-element.26), channel_id=1, source_target_pairs={{0,1},{1,0},{2,3},{3,2},{4,5},{5,4},{6,7},{7,6},{8,9},{9,8},{10,11... | collective-permute-start | bytes 983048 | tf_op jit(solution)/shard_map/ppermute | solution.py:101
  163.5 12.1 %collective-permute-start.20 = (bf16[128,1280]{1,0:T(8,128)(2,1)S(1)}, bf16[128,1280]{1,0:T(8,128)(2,1)S(1)}, u32[]{:S(2)}, u32[]{:S(2)}) collective-permute-start(bf16[128,1280]{1,0:T(8,128)(2,1)S(1)} %get-tuple-element.26), channel_id=1, source_target_pairs={{0,2},{1,3},{4,0},{5,1},{8,4},{9,5},{12,8},{13,9},{14,12},{15,13},... | collective-permute-start | bytes 983048 | tf_op jit(solution)/shard_map/ppermute | solution.py:109
  167.9 10.1 %collective-permute-start.19 = (bf16[128,1280]{1,0:T(8,128)(2,1)S(1)}, bf16[128,1280]{1,0:T(8,128)(2,1)S(1)}, u32[]{:S(2)}, u32[]{:S(2)}) collective-permute-start(bf16[128,1280]{1,0:T(8,128)(2,1)S(1)} %get-tuple-element.26), channel_id=1, source_target_pairs={{0,4},{1,5},{4,8},{5,9},{8,12},{9,13},{12,14},{13,15},{14,10},{15,... | collective-permute-start | bytes 983048 | tf_op jit(solution)/shard_map/ppermute | solution.py:105
  175.6 14.6 %collective-permute-start.22 = (bf16[128,1280]{1,0:T(8,128)(2,1)S(1)}, bf16[128,1280]{1,0:T(8,128)(2,1)S(1)}, u32[]{:S(2)}, u32[]{:S(2)}) collective-permute-start(bf16[128,1280]{1,0:T(8,128)(2,1)S(1)} %collective-permute-done.20), channel_id=1, source_target_pairs={{0,1},{1,0},{2,3},{3,2},{4,5},{5,4},{6,7},{7,6},{8,9},{9,8},{10,11... | collective-permute-start | bytes 983048 | tf_op jit(solution)/shard_map/ppermute | solution.py:101
  175.6 10.1 %collective-permute-start.24 = (bf16[128,1280]{1,0:T(8,128)(2,1)S(1)}, bf16[128,1280]{1,0:T(8,128)(2,1)S(1)}, u32[]{:S(2)}, u32[]{:S(2)}) collective-permute-start(bf16[128,1280]{1,0:T(8,128)(2,1)S(1)} %collective-permute-done.20), channel_id=1, source_target_pairs={{0,2},{1,3},{4,0},{5,1},{8,4},{9,5},{12,8},{13,9},{14,12},{15,13},... | collective-permute-start | bytes 983048 | tf_op jit(solution)/shard_map/ppermute | solution.py:109
  178.1 9.8 %collective-permute-start.23 = (bf16[128,1280]{1,0:T(8,128)(2,1)S(1)}, bf16[128,1280]{1,0:T(8,128)(2,1)S(1)}, u32[]{:S(2)}, u32[]{:S(2)}) collective-permute-start(bf16[128,1280]{1,0:T(8,128)(2,1)S(1)} %collective-permute-done.19), channel_id=1, source_target_pairs={{0,4},{1,5},{4,8},{5,9},{8,12},{9,13},{12,14},{13,15},{14,10},{15,... | collective-permute-start | bytes 983048 | tf_op jit(solution)/shard_map/ppermute | solution.py:105
  178.1 12.4 %collective-permute-start.21 = (bf16[128,1280]{1,0:T(8,128)(2,1)S(1)}, bf16[128,1280]{1,0:T(8,128)(2,1)S(1)}, u32[]{:S(2)}, u32[]{:S(2)}) collective-permute-start(bf16[128,1280]{1,0:T(8,128)(2,1)S(1)} %collective-permute-done.19), channel_id=1, source_target_pairs={{0,1},{1,0},{2,3},{3,2},{4,5},{5,4},{6,7},{7,6},{8,9},{9,8},{10,11... | collective-permute-start | bytes 983048 | tf_op jit(solution)/shard_map/ppermute | solution.py:101
  185.9 13.2 %collective-permute-start.26 = (bf16[128,1280]{1,0:T(8,128)(2,1)S(1)}, bf16[128,1280]{1,0:T(8,128)(2,1)S(1)}, u32[]{:S(2)}, u32[]{:S(2)}) collective-permute-start(bf16[128,1280]{1,0:T(8,128)(2,1)S(1)} %collective-permute-done.24), channel_id=1, source_target_pairs={{0,1},{1,0},{2,3},{3,2},{4,5},{5,4},{6,7},{7,6},{8,9},{9,8},{10,11... | collective-permute-start | bytes 983048 | tf_op jit(solution)/shard_map/ppermute | solution.py:101
  188.1 9.7 %collective-permute-start.27 = (bf16[128,1280]{1,0:T(8,128)(2,1)S(1)}, bf16[128,1280]{1,0:T(8,128)(2,1)S(1)}, u32[]{:S(2)}, u32[]{:S(2)}) collective-permute-start(bf16[128,1280]{1,0:T(8,128)(2,1)S(1)} %collective-permute-done.23), channel_id=1, source_target_pairs={{0,4},{1,5},{4,8},{5,9},{8,12},{9,13},{12,14},{13,15},{14,10},{15,... | collective-permute-start | bytes 983048 | tf_op jit(solution)/shard_map/ppermute | solution.py:105
  197.8 10.8 %collective-permute-start.30 = (bf16[128,1280]{1,0:T(8,128)(2,1)S(1)}, bf16[128,1280]{1,0:T(8,128)(2,1)S(1)}, u32[]{:S(2)}, u32[]{:S(2)}) collective-permute-start(bf16[128,1280]{1,0:T(8,128)(2,1)S(1)} %collective-permute-done.28), channel_id=1, source_target_pairs={{0,1},{1,0},{2,3},{3,2},{4,5},{5,4},{6,7},{7,6},{8,9},{9,8},{10,11... | collective-permute-start | bytes 983048 | tf_op jit(solution)/shard_map/ppermute | solution.py:101
  198.1 10.2 %collective-permute-start.31 = (bf16[128,1280]{1,0:T(8,128)(2,1)S(1)}, bf16[128,1280]{1,0:T(8,128)(2,1)S(1)}, u32[]{:S(2)}, u32[]{:S(2)}) collective-permute-start(bf16[128,1280]{1,0:T(8,128)(2,1)S(1)} %collective-permute-done.27), channel_id=1, source_target_pairs={{0,4},{1,5},{4,8},{5,9},{8,12},{9,13},{12,14},{13,15},{14,10},{15,... | collective-permute-start | bytes 983048 | tf_op jit(solution)/shard_map/ppermute | solution.py:105
  198.9 9.9 %collective-permute-start.29 = (bf16[128,1280]{1,0:T(8,128)(2,1)S(1)}, bf16[128,1280]{1,0:T(8,128)(2,1)S(1)}, u32[]{:S(2)}, u32[]{:S(2)}) collective-permute-start(bf16[128,1280]{1,0:T(8,128)(2,1)S(1)} %collective-permute-done.27), channel_id=1, source_target_pairs={{0,1},{1,0},{2,3},{3,2},{4,5},{5,4},{6,7},{7,6},{8,9},{9,8},{10,11... | collective-permute-start | bytes 983048 | tf_op jit(solution)/shard_map/ppermute | solution.py:101
  212.6 18.4 %all-to-all-start.1 = ((bf16[16,8,2048]{2,1,0:T(8,128)(2,1)}), bf16[16,8,2048]{2,1,0:T(8,128)(2,1)S(1)}, u32[]{:S(2)}, u32[]{:S(2)}) async-start(bf16[16,8,2048]{2,1,0:T(8,128)(2,1)} %select_bitcast_fusion), calls=%async_computation.3 | async-start | bytes 1048576 | tf_op jit(solution)/shard_map/all_to_all | solution.py:188
  (15 other events, 150.2 us)
Sparse Core Ops, SparseCore 0:
  36.4 48.2 reduce-scatter.4
  87.0 73.0 reduce-scatter.2
